TPU v7x, 512 devices: a whole 4x4x16 slice. The times are simulated.
512 devices in a mesh: seq: 64 (over y, z), head: 8 (over x, core).
Axes of the slice: x: 4, y: 4, z: 16, core: 2. Of those that a mesh axis runs over, the one named last changes fastest.
Arguments:
- q_delta: bfloat16 [16384, 2048], P('seq', 'head'), may hold values from -6 to 6
- k_delta: bfloat16 [16384, 2048], P('seq', 'head'), may hold values from -6 to 6
- v_delta: bfloat16 [16384, 2048], P('seq', 'head'), may hold values from -6 to 6
- write_rate: float32 [16384, 16], P('seq', 'head'), may hold values from 0 to 1
- q_attn: bfloat16 [16384, 2048], P('seq', 'head'), may hold values from -200 to 200
- k_attn: bfloat16 [16384, 2048], P('seq', 'head'), may hold values from -6 to 6
- out_gain: float32 [2048], P('head'), may hold values from 0.5 to 1.5
Outputs:
- delta_out: bfloat16 [16384, 2048], P('seq', 'head')
- normed_out: bfloat16 [16384, 2048], P('seq', 'head')
All inputs are finite; a program needn't handle non-finite values.
Results may differ from a plain program's by a relative error of at most 0.0058.
Values may be sent and summed in bfloat16 or wider, within the bound.
No kernel may reach another device: no remote copies, remote signals or barrier semaphores. Data moves between devices by JAX's collectives and lax.ppermute only.
A program may use at most 64 MiB of HBM per device.

v0:
```python
import math

import jax
import jax.numpy as jnp
from jax import lax
from jax.sharding import PartitionSpec as P

GROUP_TOKENS = 64
WINDOW = 2048


highest = lax.Precision.HIGHEST


def shifted(value, axis, by):
    size = lax.axis_size(axis)
    pairs = [(i, i + by) for i in range(size) if 0 <= i + by < size]
    return lax.ppermute(value, axis, pairs)


def unit_rows(entries):
    entries = entries.astype(jnp.float32)
    return entries * lax.rsqrt(jnp.sum(entries * entries, axis=-1, keepdims=True) + 1e-06)


def lower_inverse(below_part):
    length = below_part.shape[-1]
    identity = jnp.eye(length, dtype=jnp.float32)
    result = identity - below_part
    raised = below_part
    doubled = 2
    while doubled < length:
        raised = jnp.einsum("nij,njk->nik", raised, raised, precision=highest)
        result = jnp.einsum("nij,njk->nik", result, identity + raised, precision=highest)
        doubled = doubled * 2
    return result


def prepare(queries, key_rows, values, rate_rows):
    n_groups = queries.shape[0] // GROUP_TOKENS
    q_unit = unit_rows(queries).reshape(n_groups, GROUP_TOKENS, -1)
    k_unit = unit_rows(key_rows).reshape(n_groups, GROUP_TOKENS, -1)
    val_units = values.astype(jnp.float32).reshape(n_groups, GROUP_TOKENS, -1)
    rate_col = rate_rows.reshape(n_groups, GROUP_TOKENS, 1)
    key_inner = jnp.einsum("nik,njk->nij", k_unit, k_unit, precision=highest)
    positions = jnp.arange(GROUP_TOKENS)
    is_below = positions[:, None] > positions[None, :]
    on_or_below = positions[:, None] >= positions[None, :]
    below_part = jnp.where(is_below[None], rate_col * key_inner, 0.0)
    inverse = lower_inverse(below_part)
    writes = jnp.einsum("nij,njk->nik", inverse, rate_col * k_unit, precision=highest)
    updates = jnp.einsum("nij,njk->nik", inverse, rate_col * val_units, precision=highest)
    query_key = jnp.where(
        on_or_below[None], jnp.einsum("nik,njk->nij", q_unit, k_unit, precision=highest), 0.0
    )
    return (q_unit, k_unit, writes, updates, query_key)


def local_pair(k_unit, writes, updates):
    head_size = k_unit.shape[-1]
    identity = jnp.eye(head_size, dtype=jnp.float32)

    def stride(carry, inputs_now):
        transit, carried = carry
        k_block, w_block, u_block = inputs_now
        stepped = identity - jnp.dot(k_block.T, w_block, precision=highest)
        transit = jnp.dot(stepped, transit, precision=highest)
        carried = jnp.dot(stepped, carried, precision=highest) + jnp.dot(
            k_block.T, u_block, precision=highest
        )
        return ((transit, carried), None)

    start_pair = (identity, jnp.zeros((head_size, head_size), jnp.float32))
    (transit, carried), _ = lax.scan(stride, start_pair, (k_unit, writes, updates))
    return (transit, carried)


def advance(carried, inputs_now):
    q_block, k_block, w_block, u_block, cross_block = inputs_now
    corrected = u_block - jnp.dot(w_block, carried, precision=highest)
    result_now = jnp.dot(q_block, carried, precision=highest) + jnp.dot(
        cross_block, corrected, precision=highest
    )
    return (carried + jnp.dot(k_block.T, corrected, precision=highest), result_now)


def run_blocks(carried_in, q_unit, k_unit, writes, updates, query_key):
    _, results = lax.scan(advance, carried_in, (q_unit, k_unit, writes, updates, query_key))
    return results


def batched_dot(left, right):
    return jnp.einsum("hij,hjk->hik", left, right, precision=highest)


def on_device(q_delta, k_delta, v_delta, write_rate, q_attn, k_attn, out_gain):
    tok_rows, features = q_delta.shape
    heads_here = write_rate.shape[1]
    head_size = features // heads_here

    def by_head(entries):
        return entries.reshape(tok_rows, heads_here, head_size).transpose(1, 0, 2)

    q_unit, k_unit, writes, updates, query_key = jax.vmap(prepare)(
        by_head(q_delta), by_head(k_delta), by_head(v_delta), write_rate.T
    )
    transit, carried = jax.vmap(local_pair)(k_unit, writes, updates)
    position = lax.axis_index("seq")

    def relay(loop_index, received):
        leaving = batched_dot(transit, received) + carried
        arrived = shifted(leaving, "seq", 1)
        return jnp.where(position == loop_index + 1, arrived, received)

    incoming = lax.fori_loop(0, lax.axis_size("seq") - 1, relay, jnp.zeros_like(carried))
    results = jax.vmap(run_blocks)(incoming, q_unit, k_unit, writes, updates, query_key)
    delta_out = (
        results.reshape(heads_here, tok_rows, head_size)
        .transpose(1, 0, 2)
        .reshape(tok_rows, features)
        .astype(jnp.bfloat16)
    )
    own_rows = jnp.stack((k_attn, delta_out))
    shard_reach = WINDOW // tok_rows
    pieces = [own_rows]
    for hop_count in range(1, shard_reach + 1):
        pieces = [shifted(own_rows, "seq", hop_count)] + pieces
    rows_all = jnp.concatenate(pieces, axis=1)
    block_rows = min(512, tok_rows)
    first_row = lax.axis_index("seq") * tok_rows
    score_scale = 1.0 / math.sqrt(head_size)

    def attend_block(block_start):
        queries = q_attn.reshape(block_rows, heads_here, head_size)
        near_keys = rows_all[0].reshape(WINDOW + block_rows, heads_here, head_size)
        near_values = rows_all[1].reshape(WINDOW + block_rows, heads_here, head_size)
        scores = (
            jnp.einsum("qhd,khd->hqk", queries, near_keys, preferred_element_type=jnp.float32)
            * score_scale
        )
        q_index = jnp.arange(block_rows)[:, None]
        k_index = jnp.arange(WINDOW + block_rows)[None, :]
        allowed = (
            (k_index > q_index)
            & (k_index <= q_index + WINDOW)
            & (first_row + block_start + k_index >= WINDOW)
        )
        row_top = jnp.max(jnp.where(allowed[None], scores, -1e30), axis=2, keepdims=True)
        exps = jnp.exp(jnp.where(allowed[None], scores - row_top, -1e30))
        weights = (exps / jnp.sum(exps, axis=2, keepdims=True)).astype(jnp.bfloat16)
        mixed_rows = jnp.einsum(
            "hqk,khd->qhd", weights, near_values, preferred_element_type=jnp.float32
        )
        return mixed_rows.reshape(block_rows, features)

    starts = jnp.arange(tok_rows // block_rows) * block_rows
    attended = lax.map(attend_block, starts).reshape(tok_rows, features)
    squares = jnp.sum(attended * attended, axis=1)
    total_sq = lax.psum(squares, "head")
    scale_rows = lax.rsqrt(total_sq / (features * lax.axis_size("head")) + 1e-06)
    normed_out = (attended * out_gain[None, :] * scale_rows[:, None]).astype(jnp.bfloat16)
    return (delta_out, normed_out)


def solution(mesh):
    placed = (
        P("seq", "head"),
        P("seq", "head"),
        P("seq", "head"),
        P("seq", "head"),
        P("seq", "head"),
        P("seq", "head"),
        P("head"),
    )
    return jax.shard_map(
        on_device,
        mesh=mesh,
        in_specs=placed,
        out_specs=(P("seq", "head"), P("seq", "head")),
        check_vma=False,
    )
```

profile of v0, /device:TPU:25, one launch (start us, length us, event | category | flops | bytes accessed | tf_op | source)
XLA Modules:
  0.0 801.5 jit_solution(1470932131062995595)
XLA Ops:
  16.1 536.2 %while.45 = (s32[]{:T(128)}, f32[2,128,128]{2,1,0:T(8,128)S(1)}, s32[]{:T(128)}, f32[2,128,128]{2,1,0:T(8,128)S(1)}, f32[2,128,128]{2,1,0:T(8,128)S(1)}, /*index=5*/s32[]{:T(128)}, s32[]{:T(128)}) while((s32[]{:T(128)}, f32[2,128,128]{2,1,0:T(8,128)S(1)}, s32[]{:T(128)}, f32[2,128,128]{2,1,0:T(8,128)S(1)}, ...), condition=%wide.region_4.5_spmd.clone, body=%wide.region_3.4_spmd.clone.sunk | while | flops 50462720 | bytes 1441930 | solution.py:115
  20.0 11.0 %collective-permute-done = f32[2,128,128]{2,1,0:T(8,128)S(1)} collective-permute-done((f32[2,128,128]{2,1,0:T(8,128)S(1)}, f32[2,128,128]{2,1,0:T(8,128)S(1)}, u32[]{:S(2)}, u32[]{:S(2)}) %collective-permute-start) | collective-permute-done | bytes 131104 | tf_op jit(solution)/shard_map/while/body/eval_jaxpr/ppermute | solution.py:18
  33.2 5.9 collective-permute-done
  49.5 5.9 collective-permute-done
  74.0 5.9 collective-permute-done
  82.2 6.6 collective-permute-done
  91.0 7.2 collective-permute-done
  100.5 6.3 collective-permute-done
  117.2 5.9 collective-permute-done
  149.8 5.9 collective-permute-done
  158.0 7.0 collective-permute-done
  167.3 6.7 collective-permute-done
  176.3 5.9 collective-permute-done
  184.5 5.9 collective-permute-done
  208.9 5.9 collective-permute-done
  225.2 6.6 collective-permute-done
  234.1 7.2 collective-permute-done
  243.5 6.3 collective-permute-done
  260.3 5.9 collective-permute-done
  284.7 5.9 collective-permute-done
  301.0 7.0 collective-permute-done
  310.4 6.7 collective-permute-done
  327.5 5.9 collective-permute-done
  335.7 5.9 collective-permute-done
  352.0 5.9 collective-permute-done
  360.2 5.9 collective-permute-done
  368.3 6.6 collective-permute-done
  377.2 7.2 collective-permute-done
  386.6 6.3 collective-permute-done
  395.2 5.9 collective-permute-done
  403.4 5.9 collective-permute-done
  419.7 5.9 collective-permute-done
  436.0 5.9 collective-permute-done
  444.1 7.0 collective-permute-done
  453.4 6.7 collective-permute-done
  462.5 5.9 collective-permute-done
  478.8 5.9 collective-permute-done
  495.1 5.9 collective-permute-done
  511.4 6.6 collective-permute-done
  520.2 7.2 collective-permute-done
  529.7 6.3 collective-permute-done
  538.3 5.9 collective-permute-done
  546.4 5.9 collective-permute-done
  568.7 56.5 %collective-permute-done.1 = bf16[2,256,256]{1,2,0:T(8,128)(2,1)S(1)} collective-permute-done((bf16[2,256,256]{1,2,0:T(8,128)(2,1)S(1)}, bf16[2,256,256]{1,2,0:T(8,128)(2,1)S(1)}, u32[]{:S(2)}, u32[]{:S(2)}) %collective-permute-start.1) | collective-permute-done | bytes 262176 | tf_op jit(solution)/shard_map/ppermute | solution.py:18
  631.3 10.9 %collective-permute-done.4 = bf16[2,256,256]{1,2,0:T(8,128)(2,1)S(1)} collective-permute-done((bf16[2,256,256]{1,2,0:T(8,128)(2,1)S(1)}, bf16[2,256,256]{1,2,0:T(8,128)(2,1)S(1)}, u32[]{:S(2)}, u32[]{:S(2)}) %collective-permute-start.4) | collective-permute-done | bytes 262176 | tf_op jit(solution)/shard_map/ppermute | solution.py:18
  642.2 7.5 collective-permute-done.5
  649.8 10.8 %collective-permute-done.6 = bf16[2,256,256]{1,2,0:T(8,128)(2,1)S(1)} collective-permute-done((bf16[2,256,256]{1,2,0:T(8,128)(2,1)S(1)}, bf16[2,256,256]{1,2,0:T(8,128)(2,1)S(1)}, u32[]{:S(2)}, u32[]{:S(2)}) %collective-permute-start.6) | collective-permute-done | bytes 262176 | tf_op jit(solution)/shard_map/ppermute | solution.py:18
  664.6 135.9 %psum.7 = f32[256]{0:T(256)S(1)} all-reduce(f32[256]{0:T(256)S(1)} %get-tuple-element.322), channel_id=1, replica_groups=mesh['seq'=64,'head'=8] {'head'}, use_global_device_ids=true, to_apply=%region_11.12 | all-reduce | flops 256 | bytes 2048 | tf_op jit(solution)/shard_map/psum | solution.py:159
  (334 shorter events, 317.5 us)
Async XLA Ops:
  16.4 14.5 %collective-permute-start = (f32[2,128,128]{2,1,0:T(8,128)S(1)}, f32[2,128,128]{2,1,0:T(8,128)S(1)}, u32[]{:S(2)}, u32[]{:S(2)}) collective-permute-start(f32[2,128,128]{2,1,0:T(8,128)S(1)} %convolution_add_fusion.10), channel_id=1, source_target_pairs={{0,8},{8,16},{16,24},{24,32},{32,40},{40,48},{48,56},{56,64},{64,7... | collective-permute-start | bytes 393224 | tf_op jit(solution)/shard_map/while/body/eval_jaxpr/ppermute | solution.py:18
  31.3 7.8 collective-permute-start
  39.5 7.8 collective-permute-start
  47.6 7.8 collective-permute-start
  63.9 7.8 collective-permute-start
  72.1 7.8 collective-permute-start
  80.2 8.5 %collective-permute-start = (f32[2,128,128]{2,1,0:T(8,128)S(1)}, f32[2,128,128]{2,1,0:T(8,128)S(1)}, u32[]{:S(2)}, u32[]{:S(2)}) collective-permute-start(f32[2,128,128]{2,1,0:T(8,128)S(1)} %convolution_add_fusion.10), channel_id=1, source_target_pairs={{0,8},{8,16},{16,24},{24,32},{32,40},{40,48},{48,56},{56,64},{64,7... | collective-permute-start | bytes 393224 | tf_op jit(solution)/shard_map/while/body/eval_jaxpr/ppermute | solution.py:18
  89.1 9.1 %collective-permute-start = (f32[2,128,128]{2,1,0:T(8,128)S(1)}, f32[2,128,128]{2,1,0:T(8,128)S(1)}, u32[]{:S(2)}, u32[]{:S(2)}) collective-permute-start(f32[2,128,128]{2,1,0:T(8,128)S(1)} %convolution_add_fusion.10), channel_id=1, source_target_pairs={{0,8},{8,16},{16,24},{24,32},{32,40},{40,48},{48,56},{56,64},{64,7... | collective-permute-start | bytes 393224 | tf_op jit(solution)/shard_map/while/body/eval_jaxpr/ppermute | solution.py:18
  98.5 8.2 %collective-permute-start = (f32[2,128,128]{2,1,0:T(8,128)S(1)}, f32[2,128,128]{2,1,0:T(8,128)S(1)}, u32[]{:S(2)}, u32[]{:S(2)}) collective-permute-start(f32[2,128,128]{2,1,0:T(8,128)S(1)} %convolution_add_fusion.10), channel_id=1, source_target_pairs={{0,8},{8,16},{16,24},{24,32},{32,40},{40,48},{48,56},{56,64},{64,7... | collective-permute-start | bytes 393224 | tf_op jit(solution)/shard_map/while/body/eval_jaxpr/ppermute | solution.py:18
  107.1 7.8 collective-permute-start
  115.3 7.8 collective-permute-start
  131.6 7.8 collective-permute-start
  139.7 7.8 collective-permute-start
  147.9 7.8 collective-permute-start
  156.0 9.0 %collective-permute-start = (f32[2,128,128]{2,1,0:T(8,128)S(1)}, f32[2,128,128]{2,1,0:T(8,128)S(1)}, u32[]{:S(2)}, u32[]{:S(2)}) collective-permute-start(f32[2,128,128]{2,1,0:T(8,128)S(1)} %convolution_add_fusion.10), channel_id=1, source_target_pairs={{0,8},{8,16},{16,24},{24,32},{32,40},{40,48},{48,56},{56,64},{64,7... | collective-permute-start | bytes 393224 | tf_op jit(solution)/shard_map/while/body/eval_jaxpr/ppermute | solution.py:18
  165.3 8.7 %collective-permute-start = (f32[2,128,128]{2,1,0:T(8,128)S(1)}, f32[2,128,128]{2,1,0:T(8,128)S(1)}, u32[]{:S(2)}, u32[]{:S(2)}) collective-permute-start(f32[2,128,128]{2,1,0:T(8,128)S(1)} %convolution_add_fusion.10), channel_id=1, source_target_pairs={{0,8},{8,16},{16,24},{24,32},{32,40},{40,48},{48,56},{56,64},{64,7... | collective-permute-start | bytes 393224 | tf_op jit(solution)/shard_map/while/body/eval_jaxpr/ppermute | solution.py:18
  174.4 7.8 collective-permute-start
  182.5 7.8 collective-permute-start
  190.7 7.8 collective-permute-start
  207.0 7.8 collective-permute-start
  215.1 7.8 collective-permute-start
  223.3 8.5 %collective-permute-start = (f32[2,128,128]{2,1,0:T(8,128)S(1)}, f32[2,128,128]{2,1,0:T(8,128)S(1)}, u32[]{:S(2)}, u32[]{:S(2)}) collective-permute-start(f32[2,128,128]{2,1,0:T(8,128)S(1)} %convolution_add_fusion.10), channel_id=1, source_target_pairs={{0,8},{8,16},{16,24},{24,32},{32,40},{40,48},{48,56},{56,64},{64,7... | collective-permute-start | bytes 393224 | tf_op jit(solution)/shard_map/while/body/eval_jaxpr/ppermute | solution.py:18
  232.1 9.1 %collective-permute-start = (f32[2,128,128]{2,1,0:T(8,128)S(1)}, f32[2,128,128]{2,1,0:T(8,128)S(1)}, u32[]{:S(2)}, u32[]{:S(2)}) collective-permute-start(f32[2,128,128]{2,1,0:T(8,128)S(1)} %convolution_add_fusion.10), channel_id=1, source_target_pairs={{0,8},{8,16},{16,24},{24,32},{32,40},{40,48},{48,56},{56,64},{64,7... | collective-permute-start | bytes 393224 | tf_op jit(solution)/shard_map/while/body/eval_jaxpr/ppermute | solution.py:18
  241.6 8.2 %collective-permute-start = (f32[2,128,128]{2,1,0:T(8,128)S(1)}, f32[2,128,128]{2,1,0:T(8,128)S(1)}, u32[]{:S(2)}, u32[]{:S(2)}) collective-permute-start(f32[2,128,128]{2,1,0:T(8,128)S(1)} %convolution_add_fusion.10), channel_id=1, source_target_pairs={{0,8},{8,16},{16,24},{24,32},{32,40},{40,48},{48,56},{56,64},{64,7... | collective-permute-start | bytes 393224 | tf_op jit(solution)/shard_map/while/body/eval_jaxpr/ppermute | solution.py:18
  258.3 7.8 collective-permute-start
  266.5 7.8 collective-permute-start
  274.6 7.8 collective-permute-start
  282.8 7.8 collective-permute-start
  291.0 7.8 collective-permute-start
  299.1 9.0 %collective-permute-start = (f32[2,128,128]{2,1,0:T(8,128)S(1)}, f32[2,128,128]{2,1,0:T(8,128)S(1)}, u32[]{:S(2)}, u32[]{:S(2)}) collective-permute-start(f32[2,128,128]{2,1,0:T(8,128)S(1)} %convolution_add_fusion.10), channel_id=1, source_target_pairs={{0,8},{8,16},{16,24},{24,32},{32,40},{40,48},{48,56},{56,64},{64,7... | collective-permute-start | bytes 393224 | tf_op jit(solution)/shard_map/while/body/eval_jaxpr/ppermute | solution.py:18
  308.4 8.7 %collective-permute-start = (f32[2,128,128]{2,1,0:T(8,128)S(1)}, f32[2,128,128]{2,1,0:T(8,128)S(1)}, u32[]{:S(2)}, u32[]{:S(2)}) collective-permute-start(f32[2,128,128]{2,1,0:T(8,128)S(1)} %convolution_add_fusion.10), channel_id=1, source_target_pairs={{0,8},{8,16},{16,24},{24,32},{32,40},{40,48},{48,56},{56,64},{64,7... | collective-permute-start | bytes 393224 | tf_op jit(solution)/shard_map/while/body/eval_jaxpr/ppermute | solution.py:18
  317.4 7.8 collective-permute-start
  366.4 8.5 %collective-permute-start = (f32[2,128,128]{2,1,0:T(8,128)S(1)}, f32[2,128,128]{2,1,0:T(8,128)S(1)}, u32[]{:S(2)}, u32[]{:S(2)}) collective-permute-start(f32[2,128,128]{2,1,0:T(8,128)S(1)} %convolution_add_fusion.10), channel_id=1, source_target_pairs={{0,8},{8,16},{16,24},{24,32},{32,40},{40,48},{48,56},{56,64},{64,7... | collective-permute-start | bytes 393224 | tf_op jit(solution)/shard_map/while/body/eval_jaxpr/ppermute | solution.py:18
  375.2 9.1 %collective-permute-start = (f32[2,128,128]{2,1,0:T(8,128)S(1)}, f32[2,128,128]{2,1,0:T(8,128)S(1)}, u32[]{:S(2)}, u32[]{:S(2)}) collective-permute-start(f32[2,128,128]{2,1,0:T(8,128)S(1)} %convolution_add_fusion.10), channel_id=1, source_target_pairs={{0,8},{8,16},{16,24},{24,32},{32,40},{40,48},{48,56},{56,64},{64,7... | collective-permute-start | bytes 393224 | tf_op jit(solution)/shard_map/while/body/eval_jaxpr/ppermute | solution.py:18
  384.7 8.2 %collective-permute-start = (f32[2,128,128]{2,1,0:T(8,128)S(1)}, f32[2,128,128]{2,1,0:T(8,128)S(1)}, u32[]{:S(2)}, u32[]{:S(2)}) collective-permute-start(f32[2,128,128]{2,1,0:T(8,128)S(1)} %convolution_add_fusion.10), channel_id=1, source_target_pairs={{0,8},{8,16},{16,24},{24,32},{32,40},{40,48},{48,56},{56,64},{64,7... | collective-permute-start | bytes 393224 | tf_op jit(solution)/shard_map/while/body/eval_jaxpr/ppermute | solution.py:18
  442.2 9.0 %collective-permute-start = (f32[2,128,128]{2,1,0:T(8,128)S(1)}, f32[2,128,128]{2,1,0:T(8,128)S(1)}, u32[]{:S(2)}, u32[]{:S(2)}) collective-permute-start(f32[2,128,128]{2,1,0:T(8,128)S(1)} %convolution_add_fusion.10), channel_id=1, source_target_pairs={{0,8},{8,16},{16,24},{24,32},{32,40},{40,48},{48,56},{56,64},{64,7... | collective-permute-start | bytes 393224 | tf_op jit(solution)/shard_map/while/body/eval_jaxpr/ppermute | solution.py:18
  451.5 8.7 %collective-permute-start = (f32[2,128,128]{2,1,0:T(8,128)S(1)}, f32[2,128,128]{2,1,0:T(8,128)S(1)}, u32[]{:S(2)}, u32[]{:S(2)}) collective-permute-start(f32[2,128,128]{2,1,0:T(8,128)S(1)} %convolution_add_fusion.10), channel_id=1, source_target_pairs={{0,8},{8,16},{16,24},{24,32},{32,40},{40,48},{48,56},{56,64},{64,7... | collective-permute-start | bytes 393224 | tf_op jit(solution)/shard_map/while/body/eval_jaxpr/ppermute | solution.py:18
  509.5 8.5 %collective-permute-start = (f32[2,128,128]{2,1,0:T(8,128)S(1)}, f32[2,128,128]{2,1,0:T(8,128)S(1)}, u32[]{:S(2)}, u32[]{:S(2)}) collective-permute-start(f32[2,128,128]{2,1,0:T(8,128)S(1)} %convolution_add_fusion.10), channel_id=1, source_target_pairs={{0,8},{8,16},{16,24},{24,32},{32,40},{40,48},{48,56},{56,64},{64,7... | collective-permute-start | bytes 393224 | tf_op jit(solution)/shard_map/while/body/eval_jaxpr/ppermute | solution.py:18
  518.3 9.1 %collective-permute-start = (f32[2,128,128]{2,1,0:T(8,128)S(1)}, f32[2,128,128]{2,1,0:T(8,128)S(1)}, u32[]{:S(2)}, u32[]{:S(2)}) collective-permute-start(f32[2,128,128]{2,1,0:T(8,128)S(1)} %convolution_add_fusion.10), channel_id=1, source_target_pairs={{0,8},{8,16},{16,24},{24,32},{32,40},{40,48},{48,56},{56,64},{64,7... | collective-permute-start | bytes 393224 | tf_op jit(solution)/shard_map/while/body/eval_jaxpr/ppermute | solution.py:18
  527.8 8.2 %collective-permute-start = (f32[2,128,128]{2,1,0:T(8,128)S(1)}, f32[2,128,128]{2,1,0:T(8,128)S(1)}, u32[]{:S(2)}, u32[]{:S(2)}) collective-permute-start(f32[2,128,128]{2,1,0:T(8,128)S(1)} %convolution_add_fusion.10), channel_id=1, source_target_pairs={{0,8},{8,16},{16,24},{24,32},{32,40},{40,48},{48,56},{56,64},{64,7... | collective-permute-start | bytes 393224 | tf_op jit(solution)/shard_map/while/body/eval_jaxpr/ppermute | solution.py:18
  557.0 103.6 %collective-permute-start.8 = (bf16[2,256,256]{1,2,0:T(8,128)(2,1)S(1)}, bf16[2,256,256]{1,2,0:T(8,128)(2,1)S(1)}, u32[]{:S(2)}, u32[]{:S(2)}) collective-permute-start(bf16[2,256,256]{1,2,0:T(8,128)(2,1)S(1)} %pad_maximum_fusion), channel_id=1, source_target_pairs={{0,8},{8,16},{16,24},{24,32},{32,40},{40,48},{48,56},{56,64},{64,7... | collective-permute-start | bytes 786440 | tf_op jit(solution)/shard_map/ppermute | solution.py:18
  558.9 101.7 %collective-permute-start.7 = (bf16[2,256,256]{1,2,0:T(8,128)(2,1)S(1)}, bf16[2,256,256]{1,2,0:T(8,128)(2,1)S(1)}, u32[]{:S(2)}, u32[]{:S(2)}) collective-permute-start(bf16[2,256,256]{1,2,0:T(8,128)(2,1)S(1)} %pad_maximum_fusion), channel_id=1, source_target_pairs={{0,16},{8,24},{16,32},{24,40},{32,48},{40,56},{48,64},{56,72},{64,... | collective-permute-start | bytes 786440 | tf_op jit(solution)/shard_map/ppermute | solution.py:18
  560.9 68.3 %collective-permute-start.3 = (bf16[2,256,256]{1,2,0:T(8,128)(2,1)S(1)}, bf16[2,256,256]{1,2,0:T(8,128)(2,1)S(1)}, u32[]{:S(2)}, u32[]{:S(2)}) collective-permute-start(bf16[2,256,256]{1,2,0:T(8,128)(2,1)S(1)} %pad_maximum_fusion), channel_id=1, source_target_pairs={{0,48},{8,56},{16,64},{24,72},{32,80},{40,88},{48,96},{56,104},{64... | collective-permute-start | bytes 786440 | tf_op jit(solution)/shard_map/ppermute | solution.py:18
  562.8 64.4 %collective-permute-start.2 = (bf16[2,256,256]{1,2,0:T(8,128)(2,1)S(1)}, bf16[2,256,256]{1,2,0:T(8,128)(2,1)S(1)}, u32[]{:S(2)}, u32[]{:S(2)}) collective-permute-start(bf16[2,256,256]{1,2,0:T(8,128)(2,1)S(1)} %pad_maximum_fusion), channel_id=1, source_target_pairs={{0,56},{8,64},{16,72},{24,80},{32,88},{40,96},{48,104},{56,112},{6... | collective-permute-start | bytes 786440 | tf_op jit(solution)/shard_map/ppermute | solution.py:18
  564.7 60.5 %collective-permute-start.1 = (bf16[2,256,256]{1,2,0:T(8,128)(2,1)S(1)}, bf16[2,256,256]{1,2,0:T(8,128)(2,1)S(1)}, u32[]{:S(2)}, u32[]{:S(2)}) collective-permute-start(bf16[2,256,256]{1,2,0:T(8,128)(2,1)S(1)} %pad_maximum_fusion), channel_id=1, source_target_pairs={{0,64},{8,72},{16,80},{24,88},{32,96},{40,104},{48,112},{56,120},{... | collective-permute-start | bytes 786440 | tf_op jit(solution)/shard_map/ppermute | solution.py:18
  625.2 16.9 %collective-permute-start.4 = (bf16[2,256,256]{1,2,0:T(8,128)(2,1)S(1)}, bf16[2,256,256]{1,2,0:T(8,128)(2,1)S(1)}, u32[]{:S(2)}, u32[]{:S(2)}) collective-permute-start(bf16[2,256,256]{1,2,0:T(8,128)(2,1)S(1)} %pad_maximum_fusion), channel_id=1, source_target_pairs={{0,40},{8,48},{16,56},{24,64},{32,72},{40,80},{48,88},{56,96},{64,... | collective-permute-start | bytes 786440 | tf_op jit(solution)/shard_map/ppermute | solution.py:18
  627.2 22.5 %collective-permute-start.5 = (bf16[2,256,256]{1,2,0:T(8,128)(2,1)S(1)}, bf16[2,256,256]{1,2,0:T(8,128)(2,1)S(1)}, u32[]{:S(2)}, u32[]{:S(2)}) collective-permute-start(bf16[2,256,256]{1,2,0:T(8,128)(2,1)S(1)} %pad_maximum_fusion), channel_id=1, source_target_pairs={{0,32},{8,40},{16,48},{24,56},{32,64},{40,72},{48,80},{56,88},{64,... | collective-permute-start | bytes 786440 | tf_op jit(solution)/shard_map/ppermute | solution.py:18
  629.2 31.4 %collective-permute-start.6 = (bf16[2,256,256]{1,2,0:T(8,128)(2,1)S(1)}, bf16[2,256,256]{1,2,0:T(8,128)(2,1)S(1)}, u32[]{:S(2)}, u32[]{:S(2)}) collective-permute-start(bf16[2,256,256]{1,2,0:T(8,128)(2,1)S(1)} %pad_maximum_fusion), channel_id=1, source_target_pairs={{0,24},{8,32},{16,40},{24,48},{32,56},{40,64},{48,72},{56,80},{64,... | collective-permute-start | bytes 786440 | tf_op jit(solution)/shard_map/ppermute | solution.py:18
  (27 other events, 983.8 us)
where the time goes:
time: 805 us; the launch traced here: 801 us
  waiting for transfers between devices  477 us (59%)
  starting transfers between devices  138 us (17%)
  blocking collectives  136 us (17%)
  matrix products  33.8 us (4%)
    ppermute x71, waiting for transfers between devices, shifted(): return lax.ppermute(value, axis, pairs)  477 us
    ppermute x71, starting transfers between devices, shifted(): return lax.ppermute(value, axis, pairs)  138 us
    psum x1, blocking collectives, on_device(): total_sq = lax.psum(squares, 'head')  136 us
    dot_general x63, matrix products, batched_dot(): return jnp.einsum('hij,hjk->hik', left, right, precision=highest)  17 us
  transfers between devices with their start and end apart: 71, of which 67 were waited for; matrix products, arithmetic and copies ran while one was open for 0% of the time, Pallas kernels for 0%

commit v1 on v0

--- a/solution.py
+++ b/solution.py
@@ -106,13 +106,20 @@
     )
     transit, carried = jax.vmap(local_pair)(k_unit, writes, updates)
     position = lax.axis_index("seq")
-
-    def relay(loop_index, received):
-        leaving = batched_dot(transit, received) + carried
-        arrived = shifted(leaving, "seq", 1)
-        return jnp.where(position == loop_index + 1, arrived, received)
-
-    incoming = lax.fori_loop(0, lax.axis_size("seq") - 1, relay, jnp.zeros_like(carried))
+    seq_size = lax.axis_size("seq")
+    distance = 1
+    while distance < seq_size:
+        final = 2 * distance >= seq_size
+        if final:
+            carried_prev = shifted(carried, "seq", distance)
+        else:
+            transit_prev, carried_prev = shifted((transit, carried), "seq", distance)
+        has_prev = position >= distance
+        carried = jnp.where(has_prev, batched_dot(transit, carried_prev) + carried, carried)
+        if not final:
+            transit = jnp.where(has_prev, batched_dot(transit, transit_prev), transit)
+        distance *= 2
+    incoming = shifted(carried, "seq", 1)
     results = jax.vmap(run_blocks)(incoming, q_unit, k_unit, writes, updates, query_key)
     delta_out = (
         results.reshape(heads_here, tok_rows, head_size)
@@ -120,12 +127,15 @@
         .reshape(tok_rows, features)
         .astype(jnp.bfloat16)
     )
-    own_rows = jnp.stack((k_attn, delta_out))
     shard_reach = WINDOW // tok_rows
-    pieces = [own_rows]
-    for hop_count in range(1, shard_reach + 1):
-        pieces = [shifted(own_rows, "seq", hop_count)] + pieces
-    rows_all = jnp.concatenate(pieces, axis=1)
+
+    def window_rows(own):
+        pieces = [own]
+        for _ in range(shard_reach):
+            pieces = [shifted(pieces[0], "seq", 1)] + pieces
+        return jnp.concatenate(pieces, axis=0)
+
+    rows_all = (window_rows(k_attn), window_rows(delta_out))
     block_rows = min(512, tok_rows)
     first_row = lax.axis_index("seq") * tok_rows
     score_scale = 1.0 / math.sqrt(head_size)

time: 805 us -> 219 us (0.27)
  waiting for transfers between devices: 477 us -> 84.4 us
  blocking collectives: 136 us -> 25.6 us
  starting transfers between devices: 138 us -> 77 us
  matrix products: 33.8 us -> 19.8 us
    ppermute x71 -> x28, waiting for transfers between devices: 477 us -> 84.4 us  [shifted(): return lax.ppermute(value, axis, pairs)]
    psum x1, blocking collectives: 136 us -> 25.6 us  [on_device(): total_sq = lax.psum(squares, 'head')]
    ppermute x71 -> x28, starting transfers between devices: 138 us -> 77 us  [shifted(): return lax.ppermute(value, axis, pairs)]
    dot_general x63 -> x11, matrix products: 17 us -> 2.93 us  [batched_dot(): return jnp.einsum('hij,hjk->hik', left, right, precision=highest)]
  transfers between devices with their start and end apart: 71 -> 28, of which waited for: 67 -> 21; matrix products, arithmetic and copies ran while one was open for 0% -> 12% of each run, Pallas kernels for 0% -> 0%
where the time goes in v1:
time: 219 us; the launch traced here: 218 us
  waiting for transfers between devices  84.4 us (39%)
  starting transfers between devices  77 us (35%)
  blocking collectives  25.6 us (12%)
  matrix products  19.8 us (9%)
  local copies, waits for them, and re-layouts  4.72 us (2%)
  other arithmetic  4.65 us (2%)
    ppermute x28, waiting for transfers between devices, shifted(): return lax.ppermute(value, axis, pairs)  84.4 us
    ppermute x28, starting transfers between devices, shifted(): return lax.ppermute(value, axis, pairs)  77 us
    psum x1, blocking collectives, on_device(): total_sq = lax.psum(squares, 'head')  25.6 us
  transfers between devices with their start and end apart: 28, of which 21 were waited for; matrix products, arithmetic and copies ran while one was open for 12% of the time, Pallas kernels for 0%

profile of v1, /device:TPU:25, one launch (start us, length us, event | category | flops | bytes accessed | tf_op | source)
XLA Modules:
  0.0 218.1 jit_solution(3363750031757542944)
XLA Ops:
  1.7 3.5 %collective-permute-start.20 = (bf16[256,256]{0,1:T(8,128)(2,1)S(1)}, bf16[256,256]{0,1:T(8,128)(2,1)S(1)}, u32[]{:S(2)}, u32[]{:S(2)}) collective-permute-start(bf16[256,256]{0,1:T(8,128)(2,1)S(1)} %copy.57), channel_id=1, source_target_pairs={{0,8},{8,16},{16,24},{24,32},{32,40},{40,48},{48,56},{56,64},{64,7... | collective-permute-start | bytes 393224 | tf_op jit(solution)/shard_map/ppermute | solution.py:18
  13.1 5.7 %while.30 = (s32[]{:T(128)}, f32[2,128,128]{2,1,0:T(8,128)S(1)}, f32[2,128,128]{2,1,0:T(8,128)S(1)}, f32[4,2,64,128]{3,2,1,0:T(8,128)S(1)}, f32[4,2,64,128]{3,2,...) while((s32[]{:T(128)}, f32[2,128,128]{2,1,0:T(8,128)S(1)}, ...), condition=%wide.region_2.3_spmd.clone, body=%wide.region_1.0_spmd.clone.sunk | while | flops 151126016 | bytes 1837159 | solution.py:74
  18.8 3.6 %collective-permute-start.5 = (f32[2,128,128]{2,1,0:T(8,128)S(1)}, f32[2,128,128]{2,1,0:T(8,128)S(1)}, u32[]{:S(2)}, u32[]{:S(2)}) collective-permute-start(f32[2,128,128]{2,1,0:T(8,128)S(1)} %get-tuple-element.101), channel_id=1, source_target_pairs={{0,8},{8,16},{16,24},{24,32},{32,40},{40,48},{48,56},{56,64},{64,7... | collective-permute-start | bytes 393224 | tf_op jit(solution)/shard_map/ppermute | solution.py:18
  22.3 3.5 %collective-permute-start = (f32[2,128,128]{2,1,0:T(8,128)S(1)}, f32[2,128,128]{2,1,0:T(8,128)S(1)}, u32[]{:S(2)}, u32[]{:S(2)}) collective-permute-start(f32[2,128,128]{2,1,0:T(8,128)S(1)} %get-tuple-element.100), channel_id=1, source_target_pairs={{0,8},{8,16},{16,24},{24,32},{32,40},{40,48},{48,56},{56,64},{64,7... | collective-permute-start | bytes 393224 | tf_op jit(solution)/shard_map/ppermute | solution.py:18
  26.3 5.4 %collective-permute-done.5 = f32[2,128,128]{2,1,0:T(8,128)S(1)} collective-permute-done((f32[2,128,128]{2,1,0:T(8,128)S(1)}, f32[2,128,128]{2,1,0:T(8,128)S(1)}, u32[]{:S(2)}, u32[]{:S(2)}) %collective-permute-start.5) | collective-permute-done | bytes 131104 | tf_op jit(solution)/shard_map/ppermute | solution.py:18
  31.9 1.9 collective-permute-start.6
  34.8 3.1 %collective-permute-start.1 = (f32[2,128,128]{2,1,0:T(8,128)S(1)}, f32[2,128,128]{2,1,0:T(8,128)S(1)}, u32[]{:S(2)}, u32[]{:S(2)}) collective-permute-start(f32[2,128,128]{2,1,0:T(8,128)S(1)} %convolution_select_fusion.5), channel_id=1, source_target_pairs={{0,16},{8,24},{16,32},{24,40},{32,48},{40,56},{48,64},{56,72},{64,... | collective-permute-start | bytes 393224 | tf_op jit(solution)/shard_map/ppermute | solution.py:18
  37.9 4.8 %collective-permute-start.21 = (bf16[256,256]{0,1:T(8,128)(2,1)S(1)}, bf16[256,256]{0,1:T(8,128)(2,1)S(1)}, u32[]{:S(2)}, u32[]{:S(2)}) collective-permute-start(bf16[256,256]{0,1:T(8,128)(2,1)S(1)} %collective-permute-done.20), channel_id=1, source_target_pairs={{0,8},{8,16},{16,24},{24,32},{32,40},{40,48},{48,56},{56,64},{64,7... | collective-permute-start | bytes 393224 | tf_op jit(solution)/shard_map/ppermute | solution.py:18
  43.5 3.9 %collective-permute-start.7 = (f32[2,128,128]{2,1,0:T(8,128)S(1)}, f32[2,128,128]{2,1,0:T(8,128)S(1)}, u32[]{:S(2)}, u32[]{:S(2)}) collective-permute-start(f32[2,128,128]{2,1,0:T(8,128)S(1)} %fusion.54), channel_id=1, source_target_pairs={{0,32},{8,40},{16,48},{24,56},{32,64},{40,72},{48,80},{56,88},{64,... | collective-permute-start | bytes 393224 | tf_op jit(solution)/shard_map/ppermute | solution.py:18
  48.7 3.7 %collective-permute-start.2 = (f32[2,128,128]{2,1,0:T(8,128)S(1)}, f32[2,128,128]{2,1,0:T(8,128)S(1)}, u32[]{:S(2)}, u32[]{:S(2)}) collective-permute-start(f32[2,128,128]{2,1,0:T(8,128)S(1)} %convolution_select_fusion.4), channel_id=1, source_target_pairs={{0,32},{8,40},{16,48},{24,56},{32,64},{40,72},{48,80},{56,88},{64,... | collective-permute-start | bytes 393224 | tf_op jit(solution)/shard_map/ppermute | solution.py:18
  52.4 2.6 %collective-permute-start.22 = (bf16[256,256]{0,1:T(8,128)(2,1)S(1)}, bf16[256,256]{0,1:T(8,128)(2,1)S(1)}, u32[]{:S(2)}, u32[]{:S(2)}) collective-permute-start(bf16[256,256]{0,1:T(8,128)(2,1)S(1)} %collective-permute-done.21), channel_id=1, source_target_pairs={{0,8},{8,16},{16,24},{24,32},{32,40},{40,48},{48,56},{56,64},{64,7... | collective-permute-start | bytes 393224 | tf_op jit(solution)/shard_map/ppermute | solution.py:18
  55.1 1.3 collective-permute-done.7
  56.7 8.6 %collective-permute-start.8 = (f32[2,128,128]{2,1,0:T(8,128)S(1)}, f32[2,128,128]{2,1,0:T(8,128)S(1)}, u32[]{:S(2)}, u32[]{:S(2)}) collective-permute-start(f32[2,128,128]{2,1,0:T(8,128)S(1)} %fusion.53), channel_id=1, source_target_pairs={{0,64},{8,72},{16,80},{24,88},{32,96},{40,104},{48,112},{56,120},{... | collective-permute-start | bytes 393224 | tf_op jit(solution)/shard_map/ppermute | solution.py:18
  66.3 7.0 %collective-permute-start.3 = (f32[2,128,128]{2,1,0:T(8,128)S(1)}, f32[2,128,128]{2,1,0:T(8,128)S(1)}, u32[]{:S(2)}, u32[]{:S(2)}) collective-permute-start(f32[2,128,128]{2,1,0:T(8,128)S(1)} %convolution_select_fusion.3), channel_id=1, source_target_pairs={{0,64},{8,72},{16,80},{24,88},{32,96},{40,104},{48,112},{56,120},{... | collective-permute-start | bytes 393224 | tf_op jit(solution)/shard_map/ppermute | solution.py:18
  73.3 2.6 %collective-permute-done.22 = bf16[256,256]{0,1:T(8,128)(2,1)S(1)} collective-permute-done((bf16[256,256]{0,1:T(8,128)(2,1)S(1)}, bf16[256,256]{0,1:T(8,128)(2,1)S(1)}, u32[]{:S(2)}, u32[]{:S(2)}) %collective-permute-start.22) | collective-permute-done | bytes 131104 | tf_op jit(solution)/shard_map/ppermute | solution.py:18
  75.9 1.9 collective-permute-start.23
  77.8 6.1 %collective-permute-done.8 = f32[2,128,128]{2,1,0:T(8,128)S(1)} collective-permute-done((f32[2,128,128]{2,1,0:T(8,128)S(1)}, f32[2,128,128]{2,1,0:T(8,128)S(1)}, u32[]{:S(2)}, u32[]{:S(2)}) %collective-permute-start.8) | collective-permute-done | bytes 131104 | tf_op jit(solution)/shard_map/ppermute | solution.py:18
  84.2 1.3 collective-permute-start.9
  85.5 3.8 %collective-permute-done.3 = f32[2,128,128]{2,1,0:T(8,128)S(1)} collective-permute-done((f32[2,128,128]{2,1,0:T(8,128)S(1)}, f32[2,128,128]{2,1,0:T(8,128)S(1)}, u32[]{:S(2)}, u32[]{:S(2)}) %collective-permute-start.3) | collective-permute-done | bytes 131104 | tf_op jit(solution)/shard_map/ppermute | solution.py:18
  89.5 1.3 collective-permute-start.4
  90.8 11.4 %collective-permute-done.23 = bf16[256,256]{0,1:T(8,128)(2,1)S(1)} collective-permute-done((bf16[256,256]{0,1:T(8,128)(2,1)S(1)}, bf16[256,256]{0,1:T(8,128)(2,1)S(1)}, u32[]{:S(2)}, u32[]{:S(2)}) %collective-permute-start.23) | collective-permute-done | bytes 131104 | tf_op jit(solution)/shard_map/ppermute | solution.py:18
  102.2 1.9 collective-permute-start.24
  104.4 1.3 collective-permute-start.10
  105.7 4.3 %collective-permute-done.24 = bf16[256,256]{0,1:T(8,128)(2,1)S(1)} collective-permute-done((bf16[256,256]{0,1:T(8,128)(2,1)S(1)}, bf16[256,256]{0,1:T(8,128)(2,1)S(1)}, u32[]{:S(2)}, u32[]{:S(2)}) %collective-permute-start.24) | collective-permute-done | bytes 131104 | tf_op jit(solution)/shard_map/ppermute | solution.py:18
  110.0 1.9 collective-permute-start.25
  112.5 1.9 collective-permute-start.11
  115.0 2.8 %collective-permute-done.25 = bf16[256,256]{0,1:T(8,128)(2,1)S(1)} collective-permute-done((bf16[256,256]{0,1:T(8,128)(2,1)S(1)}, bf16[256,256]{0,1:T(8,128)(2,1)S(1)}, u32[]{:S(2)}, u32[]{:S(2)}) %collective-permute-start.25) | collective-permute-done | bytes 131104 | tf_op jit(solution)/shard_map/ppermute | solution.py:18
  117.9 1.9 collective-permute-start.26
  120.4 4.5 %while.29 = (s32[]{:T(128)}, f32[2,128,128]{2,1,0:T(8,128)S(1)}, bf16[4,2,64,128]{3,2,0,1:T(8,128)(2,1)S(1)}, f32[4,2,64,128]{3,2,1,0:T(8,128)S(1)}, f32[4,2,64,...) while((s32[]{:T(128)}, f32[2,128,128]{2,1,0:T(8,128)S(1)}, ...), condition=%wide.region_5.6_spmd, body=%wide.region_4.5_spmd.sunk | while | flops 88145920 | bytes 1247341 | solution.py:88
  125.0 1.9 collective-permute-start.12
  126.9 1.9 collective-permute-start.27
  128.9 4.0 %collective-permute-done.12 = bf16[256,256]{0,1:T(8,128)(2,1)S(1)} collective-permute-done((bf16[256,256]{0,1:T(8,128)(2,1)S(1)}, bf16[256,256]{0,1:T(8,128)(2,1)S(1)}, u32[]{:S(2)}, u32[]{:S(2)}) %collective-permute-start.12) | collective-permute-done | bytes 131104 | tf_op jit(solution)/shard_map/ppermute | solution.py:18
  132.8 2.1 collective-permute-start.13
  137.0 4.5 %collective-permute-done.13 = bf16[256,256]{0,1:T(8,128)(2,1)S(1)} collective-permute-done((bf16[256,256]{0,1:T(8,128)(2,1)S(1)}, bf16[256,256]{0,1:T(8,128)(2,1)S(1)}, u32[]{:S(2)}, u32[]{:S(2)}) %collective-permute-start.13) | collective-permute-done | bytes 131104 | tf_op jit(solution)/shard_map/ppermute | solution.py:18
  141.4 1.9 collective-permute-start.14
  143.4 6.3 %collective-permute-done.14 = bf16[256,256]{0,1:T(8,128)(2,1)S(1)} collective-permute-done((bf16[256,256]{0,1:T(8,128)(2,1)S(1)}, bf16[256,256]{0,1:T(8,128)(2,1)S(1)}, u32[]{:S(2)}, u32[]{:S(2)}) %collective-permute-start.14) | collective-permute-done | bytes 131104 | tf_op jit(solution)/shard_map/ppermute | solution.py:18
  149.6 1.9 collective-permute-start.15
  151.6 7.4 %collective-permute-done.15 = bf16[256,256]{0,1:T(8,128)(2,1)S(1)} collective-permute-done((bf16[256,256]{0,1:T(8,128)(2,1)S(1)}, bf16[256,256]{0,1:T(8,128)(2,1)S(1)}, u32[]{:S(2)}, u32[]{:S(2)}) %collective-permute-start.15) | collective-permute-done | bytes 131104 | tf_op jit(solution)/shard_map/ppermute | solution.py:18
  159.0 1.9 collective-permute-start.16
  160.9 6.5 %collective-permute-done.16 = bf16[256,256]{0,1:T(8,128)(2,1)S(1)} collective-permute-done((bf16[256,256]{0,1:T(8,128)(2,1)S(1)}, bf16[256,256]{0,1:T(8,128)(2,1)S(1)}, u32[]{:S(2)}, u32[]{:S(2)}) %collective-permute-start.16) | collective-permute-done | bytes 131104 | tf_op jit(solution)/shard_map/ppermute | solution.py:18
  167.5 1.9 collective-permute-start.17
  169.4 5.9 %collective-permute-done.17 = bf16[256,256]{0,1:T(8,128)(2,1)S(1)} collective-permute-done((bf16[256,256]{0,1:T(8,128)(2,1)S(1)}, bf16[256,256]{0,1:T(8,128)(2,1)S(1)}, u32[]{:S(2)}, u32[]{:S(2)}) %collective-permute-start.17) | collective-permute-done | bytes 131104 | tf_op jit(solution)/shard_map/ppermute | solution.py:18
  175.3 1.9 collective-permute-start.18
  178.1 5.0 %collective-permute-done.18 = bf16[256,256]{0,1:T(8,128)(2,1)S(1)} collective-permute-done((bf16[256,256]{0,1:T(8,128)(2,1)S(1)}, bf16[256,256]{0,1:T(8,128)(2,1)S(1)}, u32[]{:S(2)}, u32[]{:S(2)}) %collective-permute-start.18) | collective-permute-done | bytes 131104 | tf_op jit(solution)/shard_map/ppermute | solution.py:18
  183.1 1.9 collective-permute-start.19
  185.0 2.4 %fusion.85 = (f32[2,256]{1,0:T(2,128)S(1)}, f32[2,256,2304]{1,2,0:T(8,128)S(1)}) fusion(f32[2,256,2304]{1,2,0:T(8,128)S(1)} %fusion.39, pred[256,2304]{0,1:T(8,128)(4,1)S(1)} %fusion.46), kind=kOutput, calls=%fused_computation.139 | output fusion | flops 4720895 | bytes 10029056 | tf_op jit(solution)/shard_map/while/body/eval_jaxpr/sub | solution.py:159
  187.4 3.5 %collective-permute-done.19 = bf16[256,256]{0,1:T(8,128)(2,1)S(1)} collective-permute-done((bf16[256,256]{0,1:T(8,128)(2,1)S(1)}, bf16[256,256]{0,1:T(8,128)(2,1)S(1)}, u32[]{:S(2)}, u32[]{:S(2)}) %collective-permute-start.19) | collective-permute-done | bytes 131104 | tf_op jit(solution)/shard_map/ppermute | solution.py:18
  191.6 25.6 %psum.7 = f32[256]{0:T(256)S(1)} all-reduce(f32[256]{0:T(256)S(1)} %get-tuple-element.200), channel_id=1, replica_groups=mesh['seq'=64,'head'=8] {'head'}, use_global_device_ids=true, to_apply=%region_9.10 | all-reduce | flops 256 | bytes 2048 | tf_op jit(solution)/shard_map/psum | solution.py:169
  (138 shorter events, 30.4 us)
Async XLA Ops:
  0.6 176.6 %copy-start = (bf16[256,256]{1,0:T(8,128)(2,1)S(1)}, bf16[256,256]{1,0:T(8,128)(2,1)}, u32[]{:S(2)}) copy-start(bf16[256,256]{1,0:T(8,128)(2,1)} %param.15) | copy-start | bytes 393220
  0.6 6.7 %copy-start.1 = (bf16[256,256]{1,0:T(8,128)(2,1)S(1)}, bf16[256,256]{1,0:T(8,128)(2,1)}, u32[]{:S(2)}) copy-start(bf16[256,256]{1,0:T(8,128)(2,1)} %param.13) | copy-start | bytes 393220
  1.7 36.2 %collective-permute-start.20 = (bf16[256,256]{0,1:T(8,128)(2,1)S(1)}, bf16[256,256]{0,1:T(8,128)(2,1)S(1)}, u32[]{:S(2)}, u32[]{:S(2)}) collective-permute-start(bf16[256,256]{0,1:T(8,128)(2,1)S(1)} %copy.57), channel_id=1, source_target_pairs={{0,8},{8,16},{16,24},{24,32},{32,40},{40,48},{48,56},{56,64},{64,7... | collective-permute-start | bytes 393224 | tf_op jit(solution)/shard_map/ppermute | solution.py:18
  13.1 12.8 %copy-start.2 = (bf16[256,256]{1,0:T(8,128)(2,1)S(1)}, bf16[256,256]{1,0:T(8,128)(2,1)}, u32[]{:S(2)}) copy-start(bf16[256,256]{1,0:T(8,128)(2,1)} %param.11) | copy-start | bytes 393220
  18.8 12.9 %collective-permute-start.5 = (f32[2,128,128]{2,1,0:T(8,128)S(1)}, f32[2,128,128]{2,1,0:T(8,128)S(1)}, u32[]{:S(2)}, u32[]{:S(2)}) collective-permute-start(f32[2,128,128]{2,1,0:T(8,128)S(1)} %get-tuple-element.101), channel_id=1, source_target_pairs={{0,8},{8,16},{16,24},{24,32},{32,40},{40,48},{48,56},{56,64},{64,7... | collective-permute-start | bytes 393224 | tf_op jit(solution)/shard_map/ppermute | solution.py:18
  22.3 12.1 %collective-permute-start = (f32[2,128,128]{2,1,0:T(8,128)S(1)}, f32[2,128,128]{2,1,0:T(8,128)S(1)}, u32[]{:S(2)}, u32[]{:S(2)}) collective-permute-start(f32[2,128,128]{2,1,0:T(8,128)S(1)} %get-tuple-element.100), channel_id=1, source_target_pairs={{0,8},{8,16},{16,24},{24,32},{32,40},{40,48},{48,56},{56,64},{64,7... | collective-permute-start | bytes 393224 | tf_op jit(solution)/shard_map/ppermute | solution.py:18
  31.9 11.3 %collective-permute-start.6 = (f32[2,128,128]{2,1,0:T(8,128)S(1)}, f32[2,128,128]{2,1,0:T(8,128)S(1)}, u32[]{:S(2)}, u32[]{:S(2)}) collective-permute-start(f32[2,128,128]{2,1,0:T(8,128)S(1)} %fusion.55), channel_id=1, source_target_pairs={{0,16},{8,24},{16,32},{24,40},{32,48},{40,56},{48,64},{56,72},{64,... | collective-permute-start | bytes 393224 | tf_op jit(solution)/shard_map/ppermute | solution.py:18
  34.8 13.7 %collective-permute-start.1 = (f32[2,128,128]{2,1,0:T(8,128)S(1)}, f32[2,128,128]{2,1,0:T(8,128)S(1)}, u32[]{:S(2)}, u32[]{:S(2)}) collective-permute-start(f32[2,128,128]{2,1,0:T(8,128)S(1)} %convolution_select_fusion.5), channel_id=1, source_target_pairs={{0,16},{8,24},{16,32},{24,40},{32,48},{40,56},{48,64},{56,72},{64,... | collective-permute-start | bytes 393224 | tf_op jit(solution)/shard_map/ppermute | solution.py:18
  37.9 14.5 %collective-permute-start.21 = (bf16[256,256]{0,1:T(8,128)(2,1)S(1)}, bf16[256,256]{0,1:T(8,128)(2,1)S(1)}, u32[]{:S(2)}, u32[]{:S(2)}) collective-permute-start(bf16[256,256]{0,1:T(8,128)(2,1)S(1)} %collective-permute-done.20), channel_id=1, source_target_pairs={{0,8},{8,16},{16,24},{24,32},{32,40},{40,48},{48,56},{56,64},{64,7... | collective-permute-start | bytes 393224 | tf_op jit(solution)/shard_map/ppermute | solution.py:18
  43.5 12.9 %collective-permute-start.7 = (f32[2,128,128]{2,1,0:T(8,128)S(1)}, f32[2,128,128]{2,1,0:T(8,128)S(1)}, u32[]{:S(2)}, u32[]{:S(2)}) collective-permute-start(f32[2,128,128]{2,1,0:T(8,128)S(1)} %fusion.54), channel_id=1, source_target_pairs={{0,32},{8,40},{16,48},{24,56},{32,64},{40,72},{48,80},{56,88},{64,... | collective-permute-start | bytes 393224 | tf_op jit(solution)/shard_map/ppermute | solution.py:18
  48.7 17.3 %collective-permute-start.2 = (f32[2,128,128]{2,1,0:T(8,128)S(1)}, f32[2,128,128]{2,1,0:T(8,128)S(1)}, u32[]{:S(2)}, u32[]{:S(2)}) collective-permute-start(f32[2,128,128]{2,1,0:T(8,128)S(1)} %convolution_select_fusion.4), channel_id=1, source_target_pairs={{0,32},{8,40},{16,48},{24,56},{32,64},{40,72},{48,80},{56,88},{64,... | collective-permute-start | bytes 393224 | tf_op jit(solution)/shard_map/ppermute | solution.py:18
  52.4 23.4 %collective-permute-start.22 = (bf16[256,256]{0,1:T(8,128)(2,1)S(1)}, bf16[256,256]{0,1:T(8,128)(2,1)S(1)}, u32[]{:S(2)}, u32[]{:S(2)}) collective-permute-start(bf16[256,256]{0,1:T(8,128)(2,1)S(1)} %collective-permute-done.21), channel_id=1, source_target_pairs={{0,8},{8,16},{16,24},{24,32},{32,40},{40,48},{48,56},{56,64},{64,7... | collective-permute-start | bytes 393224 | tf_op jit(solution)/shard_map/ppermute | solution.py:18
  56.7 27.3 %collective-permute-start.8 = (f32[2,128,128]{2,1,0:T(8,128)S(1)}, f32[2,128,128]{2,1,0:T(8,128)S(1)}, u32[]{:S(2)}, u32[]{:S(2)}) collective-permute-start(f32[2,128,128]{2,1,0:T(8,128)S(1)} %fusion.53), channel_id=1, source_target_pairs={{0,64},{8,72},{16,80},{24,88},{32,96},{40,104},{48,112},{56,120},{... | collective-permute-start | bytes 393224 | tf_op jit(solution)/shard_map/ppermute | solution.py:18
  66.3 23.0 %collective-permute-start.3 = (f32[2,128,128]{2,1,0:T(8,128)S(1)}, f32[2,128,128]{2,1,0:T(8,128)S(1)}, u32[]{:S(2)}, u32[]{:S(2)}) collective-permute-start(f32[2,128,128]{2,1,0:T(8,128)S(1)} %convolution_select_fusion.3), channel_id=1, source_target_pairs={{0,64},{8,72},{16,80},{24,88},{32,96},{40,104},{48,112},{56,120},{... | collective-permute-start | bytes 393224 | tf_op jit(solution)/shard_map/ppermute | solution.py:18
  75.9 26.4 %collective-permute-start.23 = (bf16[256,256]{0,1:T(8,128)(2,1)S(1)}, bf16[256,256]{0,1:T(8,128)(2,1)S(1)}, u32[]{:S(2)}, u32[]{:S(2)}) collective-permute-start(bf16[256,256]{0,1:T(8,128)(2,1)S(1)} %collective-permute-done.22), channel_id=1, source_target_pairs={{0,8},{8,16},{16,24},{24,32},{32,40},{40,48},{48,56},{56,64},{64,7... | collective-permute-start | bytes 393224 | tf_op jit(solution)/shard_map/ppermute | solution.py:18
  84.2 20.0 %collective-permute-start.9 = (f32[2,128,128]{2,1,0:T(8,128)S(1)}, f32[2,128,128]{2,1,0:T(8,128)S(1)}, u32[]{:S(2)}, u32[]{:S(2)}) collective-permute-start(f32[2,128,128]{2,1,0:T(8,128)S(1)} %fusion.52), channel_id=1, source_target_pairs={{0,128},{8,136},{16,144},{24,152},{32,160},{40,168},{48,176},{56,1... | collective-permute-start | bytes 393224 | tf_op jit(solution)/shard_map/ppermute | solution.py:18
  89.5 22.4 %collective-permute-start.4 = (f32[2,128,128]{2,1,0:T(8,128)S(1)}, f32[2,128,128]{2,1,0:T(8,128)S(1)}, u32[]{:S(2)}, u32[]{:S(2)}) collective-permute-start(f32[2,128,128]{2,1,0:T(8,128)S(1)} %convolution_select_fusion.2), channel_id=1, source_target_pairs={{0,128},{8,136},{16,144},{24,152},{32,160},{40,168},{48,176},{56,1... | collective-permute-start | bytes 393224 | tf_op jit(solution)/shard_map/ppermute | solution.py:18
  102.2 7.8 %collective-permute-start.24 = (bf16[256,256]{0,1:T(8,128)(2,1)S(1)}, bf16[256,256]{0,1:T(8,128)(2,1)S(1)}, u32[]{:S(2)}, u32[]{:S(2)}) collective-permute-start(bf16[256,256]{0,1:T(8,128)(2,1)S(1)} %collective-permute-done.23), channel_id=1, source_target_pairs={{0,8},{8,16},{16,24},{24,32},{32,40},{40,48},{48,56},{56,64},{64,7... | collective-permute-start | bytes 393224 | tf_op jit(solution)/shard_map/ppermute | solution.py:18
  104.4 7.8 %collective-permute-start.10 = (f32[2,128,128]{2,1,0:T(8,128)S(1)}, f32[2,128,128]{2,1,0:T(8,128)S(1)}, u32[]{:S(2)}, u32[]{:S(2)}) collective-permute-start(f32[2,128,128]{2,1,0:T(8,128)S(1)} %fusion.51), channel_id=1, source_target_pairs={{0,256},{8,264},{16,272},{24,280},{32,288},{40,296},{48,304},{56,3... | collective-permute-start | bytes 393224 | tf_op jit(solution)/shard_map/ppermute | solution.py:18
  110.0 7.8 %collective-permute-start.25 = (bf16[256,256]{0,1:T(8,128)(2,1)S(1)}, bf16[256,256]{0,1:T(8,128)(2,1)S(1)}, u32[]{:S(2)}, u32[]{:S(2)}) collective-permute-start(bf16[256,256]{0,1:T(8,128)(2,1)S(1)} %collective-permute-done.24), channel_id=1, source_target_pairs={{0,8},{8,16},{16,24},{24,32},{32,40},{40,48},{48,56},{56,64},{64,7... | collective-permute-start | bytes 393224 | tf_op jit(solution)/shard_map/ppermute | solution.py:18
  112.5 7.8 %collective-permute-start.11 = (f32[2,128,128]{2,1,0:T(8,128)S(1)}, f32[2,128,128]{2,1,0:T(8,128)S(1)}, u32[]{:S(2)}, u32[]{:S(2)}) collective-permute-start(f32[2,128,128]{2,1,0:T(8,128)S(1)} %fusion.50), channel_id=1, source_target_pairs={{0,8},{8,16},{16,24},{24,32},{32,40},{40,48},{48,56},{56,64},{64,7... | collective-permute-start | bytes 393224 | tf_op jit(solution)/shard_map/ppermute | solution.py:18
  117.9 9.1 %collective-permute-start.26 = (bf16[256,256]{0,1:T(8,128)(2,1)S(1)}, bf16[256,256]{0,1:T(8,128)(2,1)S(1)}, u32[]{:S(2)}, u32[]{:S(2)}) collective-permute-start(bf16[256,256]{0,1:T(8,128)(2,1)S(1)} %collective-permute-done.25), channel_id=1, source_target_pairs={{0,8},{8,16},{16,24},{24,32},{32,40},{40,48},{48,56},{56,64},{64,7... | collective-permute-start | bytes 393224 | tf_op jit(solution)/shard_map/ppermute | solution.py:18
  125.0 7.9 %collective-permute-start.12 = (bf16[256,256]{0,1:T(8,128)(2,1)S(1)}, bf16[256,256]{0,1:T(8,128)(2,1)S(1)}, u32[]{:S(2)}, u32[]{:S(2)}) collective-permute-start(bf16[256,256]{0,1:T(8,128)(2,1)S(1)} %bitcast.193), channel_id=1, source_target_pairs={{0,8},{8,16},{16,24},{24,32},{32,40},{40,48},{48,56},{56,64},{64,7... | collective-permute-start | bytes 393224 | tf_op jit(solution)/shard_map/ppermute | solution.py:18
  126.9 10.0 %collective-permute-start.27 = (bf16[256,256]{0,1:T(8,128)(2,1)S(1)}, bf16[256,256]{0,1:T(8,128)(2,1)S(1)}, u32[]{:S(2)}, u32[]{:S(2)}) collective-permute-start(bf16[256,256]{0,1:T(8,128)(2,1)S(1)} %collective-permute-done.26), channel_id=1, source_target_pairs={{0,8},{8,16},{16,24},{24,32},{32,40},{40,48},{48,56},{56,64},{64,7... | collective-permute-start | bytes 393224 | tf_op jit(solution)/shard_map/ppermute | solution.py:18
  132.8 8.6 %collective-permute-start.13 = (bf16[256,256]{0,1:T(8,128)(2,1)S(1)}, bf16[256,256]{0,1:T(8,128)(2,1)S(1)}, u32[]{:S(2)}, u32[]{:S(2)}) collective-permute-start(bf16[256,256]{0,1:T(8,128)(2,1)S(1)} %collective-permute-done.12), channel_id=1, source_target_pairs={{0,8},{8,16},{16,24},{24,32},{32,40},{40,48},{48,56},{56,64},{64,7... | collective-permute-start | bytes 393224 | tf_op jit(solution)/shard_map/ppermute | solution.py:18
  141.4 8.2 %collective-permute-start.14 = (bf16[256,256]{0,1:T(8,128)(2,1)S(1)}, bf16[256,256]{0,1:T(8,128)(2,1)S(1)}, u32[]{:S(2)}, u32[]{:S(2)}) collective-permute-start(bf16[256,256]{0,1:T(8,128)(2,1)S(1)} %collective-permute-done.13), channel_id=1, source_target_pairs={{0,8},{8,16},{16,24},{24,32},{32,40},{40,48},{48,56},{56,64},{64,7... | collective-permute-start | bytes 393224 | tf_op jit(solution)/shard_map/ppermute | solution.py:18
  149.6 9.3 %collective-permute-start.15 = (bf16[256,256]{0,1:T(8,128)(2,1)S(1)}, bf16[256,256]{0,1:T(8,128)(2,1)S(1)}, u32[]{:S(2)}, u32[]{:S(2)}) collective-permute-start(bf16[256,256]{0,1:T(8,128)(2,1)S(1)} %collective-permute-done.14), channel_id=1, source_target_pairs={{0,8},{8,16},{16,24},{24,32},{32,40},{40,48},{48,56},{56,64},{64,7... | collective-permute-start | bytes 393224 | tf_op jit(solution)/shard_map/ppermute | solution.py:18
  159.0 8.5 %collective-permute-start.16 = (bf16[256,256]{0,1:T(8,128)(2,1)S(1)}, bf16[256,256]{0,1:T(8,128)(2,1)S(1)}, u32[]{:S(2)}, u32[]{:S(2)}) collective-permute-start(bf16[256,256]{0,1:T(8,128)(2,1)S(1)} %collective-permute-done.15), channel_id=1, source_target_pairs={{0,8},{8,16},{16,24},{24,32},{32,40},{40,48},{48,56},{56,64},{64,7... | collective-permute-start | bytes 393224 | tf_op jit(solution)/shard_map/ppermute | solution.py:18
  167.5 7.8 %collective-permute-start.17 = (bf16[256,256]{0,1:T(8,128)(2,1)S(1)}, bf16[256,256]{0,1:T(8,128)(2,1)S(1)}, u32[]{:S(2)}, u32[]{:S(2)}) collective-permute-start(bf16[256,256]{0,1:T(8,128)(2,1)S(1)} %collective-permute-done.16), channel_id=1, source_target_pairs={{0,8},{8,16},{16,24},{24,32},{32,40},{40,48},{48,56},{56,64},{64,7... | collective-permute-start | bytes 393224 | tf_op jit(solution)/shard_map/ppermute | solution.py:18
  175.3 7.8 %collective-permute-start.18 = (bf16[256,256]{0,1:T(8,128)(2,1)S(1)}, bf16[256,256]{0,1:T(8,128)(2,1)S(1)}, u32[]{:S(2)}, u32[]{:S(2)}) collective-permute-start(bf16[256,256]{0,1:T(8,128)(2,1)S(1)} %collective-permute-done.17), channel_id=1, source_target_pairs={{0,8},{8,16},{16,24},{24,32},{32,40},{40,48},{48,56},{56,64},{64,7... | collective-permute-start | bytes 393224 | tf_op jit(solution)/shard_map/ppermute | solution.py:18
  183.1 7.8 %collective-permute-start.19 = (bf16[256,256]{0,1:T(8,128)(2,1)S(1)}, bf16[256,256]{0,1:T(8,128)(2,1)S(1)}, u32[]{:S(2)}, u32[]{:S(2)}) collective-permute-start(bf16[256,256]{0,1:T(8,128)(2,1)S(1)} %collective-permute-done.18), channel_id=1, source_target_pairs={{0,8},{8,16},{16,24},{24,32},{32,40},{40,48},{48,56},{56,64},{64,7... | collective-permute-start | bytes 393224 | tf_op jit(solution)/shard_map/ppermute | solution.py:18
  191.1 26.3 %copy-start.3 = (f32[256]{0:T(256)S(1)}, f32[256]{0:T(256)}, u32[]{:S(2)}) copy-start(f32[256]{0:T(256)} %param.17) | copy-start | bytes 3076

commit v2 on v1

--- a/solution.py
+++ b/solution.py
@@ -113,7 +113,7 @@
         if final:
             carried_prev = shifted(carried, "seq", distance)
         else:
-            transit_prev, carried_prev = shifted((transit, carried), "seq", distance)
+            transit_prev, carried_prev = shifted(jnp.stack((transit, carried)), "seq", distance)
         has_prev = position >= distance
         carried = jnp.where(has_prev, batched_dot(transit, carried_prev) + carried, carried)
         if not final:
@@ -166,7 +166,13 @@
     starts = jnp.arange(tok_rows // block_rows) * block_rows
     attended = lax.map(attend_block, starts).reshape(tok_rows, features)
     squares = jnp.sum(attended * attended, axis=1)
-    total_sq = lax.psum(squares, "head")
+    total_sq = squares
+    head_size_axis = lax.axis_size("head")
+    stride_bit = 1
+    while stride_bit < head_size_axis:
+        partner_pairs = [(i, i ^ stride_bit) for i in range(head_size_axis)]
+        total_sq = total_sq + lax.ppermute(total_sq, "head", partner_pairs)
+        stride_bit *= 2
     scale_rows = lax.rsqrt(total_sq / (features * lax.axis_size("head")) + 1e-06)
     normed_out = (attended * out_gain[None, :] * scale_rows[:, None]).astype(jnp.bfloat16)
     return (delta_out, normed_out)

time: 219 us -> 243 us (1.11)
  waiting for transfers between devices: 84.4 us -> 138 us
  blocking collectives: 25.6 us -> 0 us
  starting transfers between devices: 77 us -> 72.4 us
    ppermute x28 -> x23, waiting for transfers between devices: 84.4 us -> 136 us  [shifted(): return lax.ppermute(value, axis, pairs)]
    ppermute x28 -> x23, starting transfers between devices: 77 us -> 50.8 us  [shifted(): return lax.ppermute(value, axis, pairs)]
    psum x1 -> x0, blocking collectives: 25.6 us -> none  [on_device(): total_sq = lax.psum(squares, 'head')]
    ppermute x0 -> x3, starting transfers between devices: none -> 21.5 us  [on_device(): total_sq = total_sq + lax.ppermute(total_sq, 'head', partner_pairs)]
  transfers between devices with their start and end apart: 28 -> 26, of which waited for: 21 -> 19; matrix products, arithmetic and copies ran while one was open for 12% -> 6% of each run, Pallas kernels for 0% -> 0%
where the time goes in v2:
time: 243 us; the launch traced here: 241 us
  waiting for transfers between devices  138 us (57%)
  starting transfers between devices  72.4 us (30%)
  matrix products  19.8 us (8%)
  other arithmetic  4.74 us (2%)
  local copies, waits for them, and re-layouts  3.8 us (2%)
    ppermute x23, waiting for transfers between devices, shifted(): return lax.ppermute(value, axis, pairs)  136 us
    ppermute x23, starting transfers between devices, shifted(): return lax.ppermute(value, axis, pairs)  50.8 us
    ppermute x3, starting transfers between devices, on_device(): total_sq = total_sq + lax.ppermute(total_sq, 'head', partner_pairs)  21.5 us
  transfers between devices with their start and end apart: 26, of which 19 were waited for; matrix products, arithmetic and copies ran while one was open for 6% of the time, Pallas kernels for 0%

profile of v2, /device:TPU:25, one launch (start us, length us, event | category | flops | bytes accessed | tf_op | source)
XLA Modules:
  0.0 240.5 jit_solution(6535503912099472523)
XLA Ops:
  1.5 1.0 copy.41
  8.5 5.7 %while.30 = (s32[]{:T(128)}, f32[2,128,128]{2,1,0:T(8,128)S(1)}, f32[2,128,128]{2,1,0:T(8,128)S(1)}, f32[4,2,64,128]{3,2,1,0:T(8,128)S(1)}, f32[4,2,64,128]{3,2,...) while((s32[]{:T(128)}, f32[2,128,128]{2,1,0:T(8,128)S(1)}, ...), condition=%wide.region_2.3_spmd.clone, body=%wide.region_1.0_spmd.clone.sunk | while | flops 151126016 | bytes 1837159 | solution.py:74
  14.2 3.7 %collective-permute-start = (f32[2,2,128,128]{3,2,1,0:T(8,128)S(1)}, f32[2,2,128,128]{3,2,1,0:T(8,128)S(1)}, u32[]{:S(2)}, u32[]{:S(2)}) collective-permute-start(f32[2,2,128,128]{3,2,1,0:T(8,128)S(1)} %pad_maximum_fusion), channel_id=1, source_target_pairs={{0,8},{8,16},{16,24},{24,32},{32,40},{40,48},{48,56},{56,64},{64,7... | collective-permute-start | bytes 786440 | tf_op jit(solution)/shard_map/ppermute | solution.py:18
  17.9 13.8 %collective-permute-done = f32[2,2,128,128]{3,2,1,0:T(8,128)S(1)} collective-permute-done((f32[2,2,128,128]{3,2,1,0:T(8,128)S(1)}, f32[2,2,128,128]{3,2,1,0:T(8,128)S(1)}, u32[]{:S(2)}, u32[]{:S(2)}) %collective-permute-start) | collective-permute-done | bytes 262176 | tf_op jit(solution)/shard_map/ppermute | solution.py:18
  32.3 2.1 collective-permute-start.1
  34.4 1.9 collective-permute-start.15
  36.4 13.0 %collective-permute-done.1 = f32[2,2,128,128]{3,2,1,0:T(8,128)S(1)} collective-permute-done((f32[2,2,128,128]{3,2,1,0:T(8,128)S(1)}, f32[2,2,128,128]{3,2,1,0:T(8,128)S(1)}, u32[]{:S(2)}, u32[]{:S(2)}) %collective-permute-start.1) | collective-permute-done | bytes 262176 | tf_op jit(solution)/shard_map/ppermute | solution.py:18
  49.9 1.9 collective-permute-start.2
  51.9 1.9 collective-permute-start.16
  53.9 22.4 %collective-permute-done.16 = bf16[256,256]{0,1:T(8,128)(2,1)S(1)} collective-permute-done((bf16[256,256]{0,1:T(8,128)(2,1)S(1)}, bf16[256,256]{0,1:T(8,128)(2,1)S(1)}, u32[]{:S(2)}, u32[]{:S(2)}) %collective-permute-start.16) | collective-permute-done | bytes 131104 | tf_op jit(solution)/shard_map/ppermute | solution.py:18
  76.3 1.9 collective-permute-start.17
  78.8 7.9 %collective-permute-start.3 = (f32[2,2,128,128]{3,2,1,0:T(8,128)S(1)}, f32[2,2,128,128]{3,2,1,0:T(8,128)S(1)}, u32[]{:S(2)}, u32[]{:S(2)}) collective-permute-start(f32[2,2,128,128]{3,2,1,0:T(8,128)S(1)} %pad_maximum_fusion.3), channel_id=1, source_target_pairs={{0,64},{8,72},{16,80},{24,88},{32,96},{40,104},{48,112},{56,120},{... | collective-permute-start | bytes 786440 | tf_op jit(solution)/shard_map/ppermute | solution.py:18
  86.8 1.9 collective-permute-start.18
  88.7 24.8 %collective-permute-done.18 = bf16[256,256]{0,1:T(8,128)(2,1)S(1)} collective-permute-done((bf16[256,256]{0,1:T(8,128)(2,1)S(1)}, bf16[256,256]{0,1:T(8,128)(2,1)S(1)}, u32[]{:S(2)}, u32[]{:S(2)}) %collective-permute-start.18) | collective-permute-done | bytes 131104 | tf_op jit(solution)/shard_map/ppermute | solution.py:18
  113.6 1.9 collective-permute-start.19
  116.1 1.3 collective-permute-start.4
  117.6 4.6 %collective-permute-done.19 = bf16[256,256]{0,1:T(8,128)(2,1)S(1)} collective-permute-done((bf16[256,256]{0,1:T(8,128)(2,1)S(1)}, bf16[256,256]{0,1:T(8,128)(2,1)S(1)}, u32[]{:S(2)}, u32[]{:S(2)}) %collective-permute-start.19) | collective-permute-done | bytes 131104 | tf_op jit(solution)/shard_map/ppermute | solution.py:18
  122.1 1.9 collective-permute-start.20
  124.0 4.6 %collective-permute-done.4 = f32[2,2,128,128]{3,2,1,0:T(8,128)S(1)} collective-permute-done((f32[2,2,128,128]{3,2,1,0:T(8,128)S(1)}, f32[2,2,128,128]{3,2,1,0:T(8,128)S(1)}, u32[]{:S(2)}, u32[]{:S(2)}) %collective-permute-start.4) | collective-permute-done | bytes 262176 | tf_op jit(solution)/shard_map/ppermute | solution.py:18
  128.9 1.3 collective-permute-start.5
  130.4 6.4 %collective-permute-done.5 = f32[2,128,128]{2,1,0:T(8,128)S(1)} collective-permute-done((f32[2,128,128]{2,1,0:T(8,128)S(1)}, f32[2,128,128]{2,1,0:T(8,128)S(1)}, u32[]{:S(2)}, u32[]{:S(2)}) %collective-permute-start.5) | collective-permute-done | bytes 131104 | tf_op jit(solution)/shard_map/ppermute | solution.py:18
  137.1 1.9 collective-permute-start.6
  139.6 1.9 collective-permute-start.21
  141.5 3.4 %collective-permute-done.6 = f32[2,128,128]{2,1,0:T(8,128)S(1)} collective-permute-done((f32[2,128,128]{2,1,0:T(8,128)S(1)}, f32[2,128,128]{2,1,0:T(8,128)S(1)}, u32[]{:S(2)}, u32[]{:S(2)}) %collective-permute-start.6) | collective-permute-done | bytes 131104 | tf_op jit(solution)/shard_map/ppermute | solution.py:18
  144.9 4.5 %while.29 = (s32[]{:T(128)}, f32[2,128,128]{2,1,0:T(8,128)S(1)}, bf16[4,2,64,128]{3,2,0,1:T(8,128)(2,1)S(1)}, f32[4,2,64,128]{3,2,1,0:T(8,128)S(1)}, f32[4,2,64,...) while((s32[]{:T(128)}, f32[2,128,128]{2,1,0:T(8,128)S(1)}, ...), condition=%wide.region_5.6_spmd, body=%wide.region_4.5_spmd.sunk | while | flops 88145920 | bytes 1247341 | solution.py:88
  149.5 1.9 collective-permute-start.7
  151.5 1.9 collective-permute-start.22
  153.4 3.9 %collective-permute-done.7 = bf16[256,256]{0,1:T(8,128)(2,1)S(1)} collective-permute-done((bf16[256,256]{0,1:T(8,128)(2,1)S(1)}, bf16[256,256]{0,1:T(8,128)(2,1)S(1)}, u32[]{:S(2)}, u32[]{:S(2)}) %collective-permute-start.7) | collective-permute-done | bytes 131104 | tf_op jit(solution)/shard_map/ppermute | solution.py:18
  157.4 2.1 collective-permute-start.8
  159.5 1.3 fusion.46
  160.8 4.4 %collective-permute-done.8 = bf16[256,256]{0,1:T(8,128)(2,1)S(1)} collective-permute-done((bf16[256,256]{0,1:T(8,128)(2,1)S(1)}, bf16[256,256]{0,1:T(8,128)(2,1)S(1)}, u32[]{:S(2)}, u32[]{:S(2)}) %collective-permute-start.8) | collective-permute-done | bytes 131104 | tf_op jit(solution)/shard_map/ppermute | solution.py:18
  165.2 1.9 collective-permute-start.9
  167.1 5.9 %collective-permute-done.9 = bf16[256,256]{0,1:T(8,128)(2,1)S(1)} collective-permute-done((bf16[256,256]{0,1:T(8,128)(2,1)S(1)}, bf16[256,256]{0,1:T(8,128)(2,1)S(1)}, u32[]{:S(2)}, u32[]{:S(2)}) %collective-permute-start.9) | collective-permute-done | bytes 131104 | tf_op jit(solution)/shard_map/ppermute | solution.py:18
  173.0 1.9 collective-permute-start.10
  174.9 5.9 %collective-permute-done.10 = bf16[256,256]{0,1:T(8,128)(2,1)S(1)} collective-permute-done((bf16[256,256]{0,1:T(8,128)(2,1)S(1)}, bf16[256,256]{0,1:T(8,128)(2,1)S(1)}, u32[]{:S(2)}, u32[]{:S(2)}) %collective-permute-start.10) | collective-permute-done | bytes 131104 | tf_op jit(solution)/shard_map/ppermute | solution.py:18
  180.8 1.9 collective-permute-start.11
  182.8 6.6 %collective-permute-done.11 = bf16[256,256]{0,1:T(8,128)(2,1)S(1)} collective-permute-done((bf16[256,256]{0,1:T(8,128)(2,1)S(1)}, bf16[256,256]{0,1:T(8,128)(2,1)S(1)}, u32[]{:S(2)}, u32[]{:S(2)}) %collective-permute-start.11) | collective-permute-done | bytes 131104 | tf_op jit(solution)/shard_map/ppermute | solution.py:18
  189.4 1.9 collective-permute-start.12
  191.3 7.1 %collective-permute-done.12 = bf16[256,256]{0,1:T(8,128)(2,1)S(1)} collective-permute-done((bf16[256,256]{0,1:T(8,128)(2,1)S(1)}, bf16[256,256]{0,1:T(8,128)(2,1)S(1)}, u32[]{:S(2)}, u32[]{:S(2)}) %collective-permute-start.12) | collective-permute-done | bytes 131104 | tf_op jit(solution)/shard_map/ppermute | solution.py:18
  198.4 1.9 collective-permute-start.13
  201.2 5.4 %collective-permute-done.13 = bf16[256,256]{0,1:T(8,128)(2,1)S(1)} collective-permute-done((bf16[256,256]{0,1:T(8,128)(2,1)S(1)}, bf16[256,256]{0,1:T(8,128)(2,1)S(1)}, u32[]{:S(2)}, u32[]{:S(2)}) %collective-permute-start.13) | collective-permute-done | bytes 131104 | tf_op jit(solution)/shard_map/ppermute | solution.py:18
  206.5 1.9 collective-permute-start.14
  208.4 2.3 fusion.85
  210.8 3.5 %collective-permute-done.14 = bf16[256,256]{0,1:T(8,128)(2,1)S(1)} collective-permute-done((bf16[256,256]{0,1:T(8,128)(2,1)S(1)}, bf16[256,256]{0,1:T(8,128)(2,1)S(1)}, u32[]{:S(2)}, u32[]{:S(2)}) %collective-permute-start.14) | collective-permute-done | bytes 131104 | tf_op jit(solution)/shard_map/ppermute | solution.py:18
  215.0 13.8 %collective-permute-start.23 = (f32[256]{0:T(256)S(1)}, f32[256]{0:T(256)S(1)}, u32[]{:S(2)}, u32[]{:S(2)}) collective-permute-start(f32[256]{0:T(256)S(1)} %get-tuple-element.200), channel_id=1, source_target_pairs={{0,1},{1,0},{2,3},{3,2},{4,5},{5,4},{6,7},{7,6},{8,9},{9,8},{10,11... | collective-permute-start | bytes 3080 | tf_op jit(solution)/shard_map/ppermute | solution.py:174
  229.6 3.1 %collective-permute-start.24 = (f32[256]{0:T(256)S(1)}, f32[256]{0:T(256)S(1)}, u32[]{:S(2)}, u32[]{:S(2)}) collective-permute-start(f32[256]{0:T(256)S(1)} %add.136), channel_id=1, source_target_pairs={{0,2},{1,3},{2,0},{3,1},{4,6},{5,7},{6,4},{7,5},{8,10},{9,11},{10,... | collective-permute-start | bytes 3080 | tf_op jit(solution)/shard_map/ppermute | solution.py:174
  232.7 1.2 collective-permute-done.24
  233.9 4.7 %collective-permute-start.25 = (f32[256]{0:T(256)S(1)}, f32[256]{0:T(256)S(1)}, u32[]{:S(2)}, u32[]{:S(2)}) collective-permute-start(f32[256]{0:T(256)S(1)} %add.137), channel_id=1, source_target_pairs={{0,4},{1,5},{2,6},{3,7},{4,0},{5,1},{6,2},{7,3},{8,12},{9,13},{10,... | collective-permute-start | bytes 3080 | tf_op jit(solution)/shard_map/ppermute | solution.py:174
  (142 shorter events, 24.8 us)
Async XLA Ops:
  0.6 199.7 %copy-start = (bf16[256,256]{1,0:T(8,128)(2,1)S(1)}, bf16[256,256]{1,0:T(8,128)(2,1)}, u32[]{:S(2)}) copy-start(bf16[256,256]{1,0:T(8,128)(2,1)} %param.15) | copy-start | bytes 393220
  0.6 2.1 copy-start.1
  14.2 20.1 %copy-start.2 = (bf16[256,256]{1,0:T(8,128)(2,1)S(1)}, bf16[256,256]{1,0:T(8,128)(2,1)}, u32[]{:S(2)}) copy-start(bf16[256,256]{1,0:T(8,128)(2,1)} %param.16) | copy-start | bytes 393220
  14.2 17.5 %collective-permute-start = (f32[2,2,128,128]{3,2,1,0:T(8,128)S(1)}, f32[2,2,128,128]{3,2,1,0:T(8,128)S(1)}, u32[]{:S(2)}, u32[]{:S(2)}) collective-permute-start(f32[2,2,128,128]{3,2,1,0:T(8,128)S(1)} %pad_maximum_fusion), channel_id=1, source_target_pairs={{0,8},{8,16},{16,24},{24,32},{32,40},{40,48},{48,56},{56,64},{64,7... | collective-permute-start | bytes 786440 | tf_op jit(solution)/shard_map/ppermute | solution.py:18
  32.2 21.6 %copy-start.3 = (bf16[256,256]{1,0:T(8,128)(2,1)S(1)}, bf16[256,256]{1,0:T(8,128)(2,1)}, u32[]{:S(2)}) copy-start(bf16[256,256]{1,0:T(8,128)(2,1)} %param.11) | copy-start | bytes 393220
  32.3 17.1 %collective-permute-start.1 = (f32[2,2,128,128]{3,2,1,0:T(8,128)S(1)}, f32[2,2,128,128]{3,2,1,0:T(8,128)S(1)}, u32[]{:S(2)}, u32[]{:S(2)}) collective-permute-start(f32[2,2,128,128]{3,2,1,0:T(8,128)S(1)} %pad_maximum_fusion.1), channel_id=1, source_target_pairs={{0,16},{8,24},{16,32},{24,40},{32,48},{40,56},{48,64},{56,72},{64,... | collective-permute-start | bytes 786440 | tf_op jit(solution)/shard_map/ppermute | solution.py:18
  34.4 17.4 %collective-permute-start.15 = (bf16[256,256]{0,1:T(8,128)(2,1)S(1)}, bf16[256,256]{0,1:T(8,128)(2,1)S(1)}, u32[]{:S(2)}, u32[]{:S(2)}) collective-permute-start(bf16[256,256]{0,1:T(8,128)(2,1)S(1)} %copy.57), channel_id=1, source_target_pairs={{0,8},{8,16},{16,24},{24,32},{32,40},{40,48},{48,56},{56,64},{64,7... | collective-permute-start | bytes 393224 | tf_op jit(solution)/shard_map/ppermute | solution.py:18
  49.9 28.3 %collective-permute-start.2 = (f32[2,2,128,128]{3,2,1,0:T(8,128)S(1)}, f32[2,2,128,128]{3,2,1,0:T(8,128)S(1)}, u32[]{:S(2)}, u32[]{:S(2)}) collective-permute-start(f32[2,2,128,128]{3,2,1,0:T(8,128)S(1)} %pad_maximum_fusion.2), channel_id=1, source_target_pairs={{0,32},{8,40},{16,48},{24,56},{32,64},{40,72},{48,80},{56,88},{64,... | collective-permute-start | bytes 786440 | tf_op jit(solution)/shard_map/ppermute | solution.py:18
  51.9 24.5 %collective-permute-start.16 = (bf16[256,256]{0,1:T(8,128)(2,1)S(1)}, bf16[256,256]{0,1:T(8,128)(2,1)S(1)}, u32[]{:S(2)}, u32[]{:S(2)}) collective-permute-start(bf16[256,256]{0,1:T(8,128)(2,1)S(1)} %collective-permute-done.15), channel_id=1, source_target_pairs={{0,8},{8,16},{16,24},{24,32},{32,40},{40,48},{48,56},{56,64},{64,7... | collective-permute-start | bytes 393224 | tf_op jit(solution)/shard_map/ppermute | solution.py:18
  76.3 10.5 %collective-permute-start.17 = (bf16[256,256]{0,1:T(8,128)(2,1)S(1)}, bf16[256,256]{0,1:T(8,128)(2,1)S(1)}, u32[]{:S(2)}, u32[]{:S(2)}) collective-permute-start(bf16[256,256]{0,1:T(8,128)(2,1)S(1)} %collective-permute-done.16), channel_id=1, source_target_pairs={{0,8},{8,16},{16,24},{24,32},{32,40},{40,48},{48,56},{56,64},{64,7... | collective-permute-start | bytes 393224 | tf_op jit(solution)/shard_map/ppermute | solution.py:18
  78.8 36.7 %collective-permute-start.3 = (f32[2,2,128,128]{3,2,1,0:T(8,128)S(1)}, f32[2,2,128,128]{3,2,1,0:T(8,128)S(1)}, u32[]{:S(2)}, u32[]{:S(2)}) collective-permute-start(f32[2,2,128,128]{3,2,1,0:T(8,128)S(1)} %pad_maximum_fusion.3), channel_id=1, source_target_pairs={{0,64},{8,72},{16,80},{24,88},{32,96},{40,104},{48,112},{56,120},{... | collective-permute-start | bytes 786440 | tf_op jit(solution)/shard_map/ppermute | solution.py:18
  86.8 26.8 %collective-permute-start.18 = (bf16[256,256]{0,1:T(8,128)(2,1)S(1)}, bf16[256,256]{0,1:T(8,128)(2,1)S(1)}, u32[]{:S(2)}, u32[]{:S(2)}) collective-permute-start(bf16[256,256]{0,1:T(8,128)(2,1)S(1)} %collective-permute-done.17), channel_id=1, source_target_pairs={{0,8},{8,16},{16,24},{24,32},{32,40},{40,48},{48,56},{56,64},{64,7... | collective-permute-start | bytes 393224 | tf_op jit(solution)/shard_map/ppermute | solution.py:18
  113.6 8.6 %collective-permute-start.19 = (bf16[256,256]{0,1:T(8,128)(2,1)S(1)}, bf16[256,256]{0,1:T(8,128)(2,1)S(1)}, u32[]{:S(2)}, u32[]{:S(2)}) collective-permute-start(bf16[256,256]{0,1:T(8,128)(2,1)S(1)} %collective-permute-done.18), channel_id=1, source_target_pairs={{0,8},{8,16},{16,24},{24,32},{32,40},{40,48},{48,56},{56,64},{64,7... | collective-permute-start | bytes 393224 | tf_op jit(solution)/shard_map/ppermute | solution.py:18
  116.1 12.5 %collective-permute-start.4 = (f32[2,2,128,128]{3,2,1,0:T(8,128)S(1)}, f32[2,2,128,128]{3,2,1,0:T(8,128)S(1)}, u32[]{:S(2)}, u32[]{:S(2)}) collective-permute-start(f32[2,2,128,128]{3,2,1,0:T(8,128)S(1)} %pad_maximum_fusion.4), channel_id=1, source_target_pairs={{0,128},{8,136},{16,144},{24,152},{32,160},{40,168},{48,176},{56,1... | collective-permute-start | bytes 786440 | tf_op jit(solution)/shard_map/ppermute | solution.py:18
  122.1 17.5 %collective-permute-start.20 = (bf16[256,256]{0,1:T(8,128)(2,1)S(1)}, bf16[256,256]{0,1:T(8,128)(2,1)S(1)}, u32[]{:S(2)}, u32[]{:S(2)}) collective-permute-start(bf16[256,256]{0,1:T(8,128)(2,1)S(1)} %collective-permute-done.19), channel_id=1, source_target_pairs={{0,8},{8,16},{16,24},{24,32},{32,40},{40,48},{48,56},{56,64},{64,7... | collective-permute-start | bytes 393224 | tf_op jit(solution)/shard_map/ppermute | solution.py:18
  128.9 8.0 %collective-permute-start.5 = (f32[2,128,128]{2,1,0:T(8,128)S(1)}, f32[2,128,128]{2,1,0:T(8,128)S(1)}, u32[]{:S(2)}, u32[]{:S(2)}) collective-permute-start(f32[2,128,128]{2,1,0:T(8,128)S(1)} %fusion.51), channel_id=1, source_target_pairs={{0,256},{8,264},{16,272},{24,280},{32,288},{40,296},{48,304},{56,3... | collective-permute-start | bytes 393224 | tf_op jit(solution)/shard_map/ppermute | solution.py:18
  137.1 7.8 %collective-permute-start.6 = (f32[2,128,128]{2,1,0:T(8,128)S(1)}, f32[2,128,128]{2,1,0:T(8,128)S(1)}, u32[]{:S(2)}, u32[]{:S(2)}) collective-permute-start(f32[2,128,128]{2,1,0:T(8,128)S(1)} %fusion.50), channel_id=1, source_target_pairs={{0,8},{8,16},{16,24},{24,32},{32,40},{40,48},{48,56},{56,64},{64,7... | collective-permute-start | bytes 393224 | tf_op jit(solution)/shard_map/ppermute | solution.py:18
  139.6 11.9 %collective-permute-start.21 = (bf16[256,256]{0,1:T(8,128)(2,1)S(1)}, bf16[256,256]{0,1:T(8,128)(2,1)S(1)}, u32[]{:S(2)}, u32[]{:S(2)}) collective-permute-start(bf16[256,256]{0,1:T(8,128)(2,1)S(1)} %collective-permute-done.20), channel_id=1, source_target_pairs={{0,8},{8,16},{16,24},{24,32},{32,40},{40,48},{48,56},{56,64},{64,7... | collective-permute-start | bytes 393224 | tf_op jit(solution)/shard_map/ppermute | solution.py:18
  149.5 7.8 %collective-permute-start.7 = (bf16[256,256]{0,1:T(8,128)(2,1)S(1)}, bf16[256,256]{0,1:T(8,128)(2,1)S(1)}, u32[]{:S(2)}, u32[]{:S(2)}) collective-permute-start(bf16[256,256]{0,1:T(8,128)(2,1)S(1)} %bitcast.233), channel_id=1, source_target_pairs={{0,8},{8,16},{16,24},{24,32},{32,40},{40,48},{48,56},{56,64},{64,7... | collective-permute-start | bytes 393224 | tf_op jit(solution)/shard_map/ppermute | solution.py:18
  151.5 9.2 %collective-permute-start.22 = (bf16[256,256]{0,1:T(8,128)(2,1)S(1)}, bf16[256,256]{0,1:T(8,128)(2,1)S(1)}, u32[]{:S(2)}, u32[]{:S(2)}) collective-permute-start(bf16[256,256]{0,1:T(8,128)(2,1)S(1)} %collective-permute-done.21), channel_id=1, source_target_pairs={{0,8},{8,16},{16,24},{24,32},{32,40},{40,48},{48,56},{56,64},{64,7... | collective-permute-start | bytes 393224 | tf_op jit(solution)/shard_map/ppermute | solution.py:18
  157.4 7.8 %collective-permute-start.8 = (bf16[256,256]{0,1:T(8,128)(2,1)S(1)}, bf16[256,256]{0,1:T(8,128)(2,1)S(1)}, u32[]{:S(2)}, u32[]{:S(2)}) collective-permute-start(bf16[256,256]{0,1:T(8,128)(2,1)S(1)} %collective-permute-done.7), channel_id=1, source_target_pairs={{0,8},{8,16},{16,24},{24,32},{32,40},{40,48},{48,56},{56,64},{64,7... | collective-permute-start | bytes 393224 | tf_op jit(solution)/shard_map/ppermute | solution.py:18
  165.2 7.8 %collective-permute-start.9 = (bf16[256,256]{0,1:T(8,128)(2,1)S(1)}, bf16[256,256]{0,1:T(8,128)(2,1)S(1)}, u32[]{:S(2)}, u32[]{:S(2)}) collective-permute-start(bf16[256,256]{0,1:T(8,128)(2,1)S(1)} %collective-permute-done.8), channel_id=1, source_target_pairs={{0,8},{8,16},{16,24},{24,32},{32,40},{40,48},{48,56},{56,64},{64,7... | collective-permute-start | bytes 393224 | tf_op jit(solution)/shard_map/ppermute | solution.py:18
  173.0 7.8 %collective-permute-start.10 = (bf16[256,256]{0,1:T(8,128)(2,1)S(1)}, bf16[256,256]{0,1:T(8,128)(2,1)S(1)}, u32[]{:S(2)}, u32[]{:S(2)}) collective-permute-start(bf16[256,256]{0,1:T(8,128)(2,1)S(1)} %collective-permute-done.9), channel_id=1, source_target_pairs={{0,8},{8,16},{16,24},{24,32},{32,40},{40,48},{48,56},{56,64},{64,7... | collective-permute-start | bytes 393224 | tf_op jit(solution)/shard_map/ppermute | solution.py:18
  180.8 8.6 %collective-permute-start.11 = (bf16[256,256]{0,1:T(8,128)(2,1)S(1)}, bf16[256,256]{0,1:T(8,128)(2,1)S(1)}, u32[]{:S(2)}, u32[]{:S(2)}) collective-permute-start(bf16[256,256]{0,1:T(8,128)(2,1)S(1)} %collective-permute-done.10), channel_id=1, source_target_pairs={{0,8},{8,16},{16,24},{24,32},{32,40},{40,48},{48,56},{56,64},{64,7... | collective-permute-start | bytes 393224 | tf_op jit(solution)/shard_map/ppermute | solution.py:18
  189.4 9.0 %collective-permute-start.12 = (bf16[256,256]{0,1:T(8,128)(2,1)S(1)}, bf16[256,256]{0,1:T(8,128)(2,1)S(1)}, u32[]{:S(2)}, u32[]{:S(2)}) collective-permute-start(bf16[256,256]{0,1:T(8,128)(2,1)S(1)} %collective-permute-done.11), channel_id=1, source_target_pairs={{0,8},{8,16},{16,24},{24,32},{32,40},{40,48},{48,56},{56,64},{64,7... | collective-permute-start | bytes 393224 | tf_op jit(solution)/shard_map/ppermute | solution.py:18
  198.4 8.1 %collective-permute-start.13 = (bf16[256,256]{0,1:T(8,128)(2,1)S(1)}, bf16[256,256]{0,1:T(8,128)(2,1)S(1)}, u32[]{:S(2)}, u32[]{:S(2)}) collective-permute-start(bf16[256,256]{0,1:T(8,128)(2,1)S(1)} %collective-permute-done.12), channel_id=1, source_target_pairs={{0,8},{8,16},{16,24},{24,32},{32,40},{40,48},{48,56},{56,64},{64,7... | collective-permute-start | bytes 393224 | tf_op jit(solution)/shard_map/ppermute | solution.py:18
  206.5 7.8 %collective-permute-start.14 = (bf16[256,256]{0,1:T(8,128)(2,1)S(1)}, bf16[256,256]{0,1:T(8,128)(2,1)S(1)}, u32[]{:S(2)}, u32[]{:S(2)}) collective-permute-start(bf16[256,256]{0,1:T(8,128)(2,1)S(1)} %collective-permute-done.13), channel_id=1, source_target_pairs={{0,8},{8,16},{16,24},{24,32},{32,40},{40,48},{48,56},{56,64},{64,7... | collective-permute-start | bytes 393224 | tf_op jit(solution)/shard_map/ppermute | solution.py:18
  214.5 25.2 %copy-start.4 = (f32[256]{0:T(256)S(1)}, f32[256]{0:T(256)}, u32[]{:S(2)}) copy-start(f32[256]{0:T(256)} %param.17) | copy-start | bytes 3076
  215.0 14.6 %collective-permute-start.23 = (f32[256]{0:T(256)S(1)}, f32[256]{0:T(256)S(1)}, u32[]{:S(2)}, u32[]{:S(2)}) collective-permute-start(f32[256]{0:T(256)S(1)} %get-tuple-element.200), channel_id=1, source_target_pairs={{0,1},{1,0},{2,3},{3,2},{4,5},{5,4},{6,7},{7,6},{8,9},{9,8},{10,11... | collective-permute-start | bytes 3080 | tf_op jit(solution)/shard_map/ppermute | solution.py:174
  229.6 4.3 %collective-permute-start.24 = (f32[256]{0:T(256)S(1)}, f32[256]{0:T(256)S(1)}, u32[]{:S(2)}, u32[]{:S(2)}) collective-permute-start(f32[256]{0:T(256)S(1)} %add.136), channel_id=1, source_target_pairs={{0,2},{1,3},{2,0},{3,1},{4,6},{5,7},{6,4},{7,5},{8,10},{9,11},{10,... | collective-permute-start | bytes 3080 | tf_op jit(solution)/shard_map/ppermute | solution.py:174
  233.9 5.8 %collective-permute-start.25 = (f32[256]{0:T(256)S(1)}, f32[256]{0:T(256)S(1)}, u32[]{:S(2)}, u32[]{:S(2)}) collective-permute-start(f32[256]{0:T(256)S(1)} %add.137), channel_id=1, source_target_pairs={{0,4},{1,5},{2,6},{3,7},{4,0},{5,1},{6,2},{7,3},{8,12},{9,13},{10,... | collective-permute-start | bytes 3080 | tf_op jit(solution)/shard_map/ppermute | solution.py:174

commit v3 on v1

--- a/solution.py
+++ b/solution.py
@@ -107,19 +107,45 @@
     transit, carried = jax.vmap(local_pair)(k_unit, writes, updates)
     position = lax.axis_index("seq")
     seq_size = lax.axis_size("seq")
+    group = min(4, seq_size)
+    rank = position % group
+
+    def moved(value, by, sources):
+        pairs = [(i, i + by) for i in sources if 0 <= i + by < seq_size]
+        return lax.ppermute(value, "seq", pairs)
+
     distance = 1
+    while distance < group:
+        inside = [i for i in range(seq_size) if i % group + distance < group]
+        transit_prev = moved(transit, distance, inside)
+        carried_prev = moved(carried, distance, inside)
+        has_prev = rank >= distance
+        carried_in = jnp.where(has_prev, batched_dot(transit, carried_prev) + carried, carried)
+        transit = jnp.where(has_prev, batched_dot(transit, transit_prev), transit)
+        carried = carried_in
+        distance *= 2
+    ends = [i for i in range(seq_size) if i % group == group - 1]
+    end_transit, end_carried = transit, carried
+    distance = group
     while distance < seq_size:
         final = 2 * distance >= seq_size
-        if final:
-            carried_prev = shifted(carried, "seq", distance)
-        else:
-            transit_prev, carried_prev = shifted((transit, carried), "seq", distance)
-        has_prev = position >= distance
-        carried = jnp.where(has_prev, batched_dot(transit, carried_prev) + carried, carried)
+        carried_prev = moved(end_carried, distance, ends)
+        has_prev = (rank == group - 1) & (position >= distance)
+        carried_next = jnp.where(
+            has_prev, batched_dot(end_transit, carried_prev) + end_carried, end_carried
+        )
         if not final:
-            transit = jnp.where(has_prev, batched_dot(transit, transit_prev), transit)
+            transit_prev = moved(end_transit, distance, ends)
+            end_transit = jnp.where(has_prev, batched_dot(end_transit, transit_prev), end_transit)
+        end_carried = carried_next
         distance *= 2
-    incoming = shifted(carried, "seq", 1)
+    group_in = jnp.zeros_like(carried)
+    for hop in range(1, group):
+        group_in = group_in + moved(end_carried, hop, ends)
+    leaving = jnp.where(
+        rank == group - 1, end_carried, batched_dot(transit, group_in) + carried
+    )
+    incoming = shifted(leaving, "seq", 1)
     results = jax.vmap(run_blocks)(incoming, q_unit, k_unit, writes, updates, query_key)
     delta_out = (
         results.reshape(heads_here, tok_rows, head_size)

time: 219 us -> 212 us (0.968)
  starting transfers between devices: 77 us -> 63.3 us
  blocking collectives: 25.6 us -> 30.1 us
  waiting for transfers between devices: 84.4 us -> 81.3 us
  matrix products: 19.8 us -> 22.5 us
    ppermute x28 -> x17, starting transfers between devices: 77 us -> 41.2 us  [shifted(): return lax.ppermute(value, axis, pairs)]
    ppermute x0 -> x14, starting transfers between devices: none -> 22.2 us  [moved(): return lax.ppermute(value, 'seq', pairs)]
    ppermute x28 -> x17, waiting for transfers between devices: 84.4 us -> 70.6 us  [shifted(): return lax.ppermute(value, axis, pairs)]
    ppermute x0 -> x14, waiting for transfers between devices: none -> 10.7 us  [moved(): return lax.ppermute(value, 'seq', pairs)]
    psum x1, blocking collectives: 25.6 us -> 30.1 us  [on_device(): total_sq = lax.psum(squares, 'head')]
    dot_general x1, matrix products: 0.52 us -> 2.94 us  [attend_block(): jnp.einsum('hqk,khd->qhd', weights, near_values, preferred_element_type=j...]
  transfers between devices with their start and end apart: 28 -> 31, of which waited for: 21 -> 14; matrix products, arithmetic and copies ran while one was open for 12% -> 14% of each run, Pallas kernels for 0% -> 0%
where the time goes in v3:
time: 212 us; the launch traced here: 211 us
  waiting for transfers between devices  81.3 us (38%)
  starting transfers between devices  63.3 us (30%)
  blocking collectives  30.1 us (14%)
  matrix products  22.5 us (11%)
  other arithmetic  6.6 us (3%)
  local copies, waits for them, and re-layouts  4.72 us (2%)
    ppermute x17, waiting for transfers between devices, shifted(): return lax.ppermute(value, axis, pairs)  70.6 us
    ppermute x17, starting transfers between devices, shifted(): return lax.ppermute(value, axis, pairs)  41.2 us
    psum x1, blocking collectives, on_device(): total_sq = lax.psum(squares, 'head')  30.1 us
    ppermute x14, starting transfers between devices, moved(): return lax.ppermute(value, 'seq', pairs)  22.2 us
    ppermute x14, waiting for transfers between devices, moved(): return lax.ppermute(value, 'seq', pairs)  10.7 us
    sub x1, other arithmetic, attend_block(): exps = jnp.exp(jnp.where(allowed[None], scores - row_top, -1e+30))  4.3 us
  transfers between devices with their start and end apart: 31, of which 14 were waited for; matrix products, arithmetic and copies ran while one was open for 14% of the time, Pallas kernels for 0%

profile of v3, /device:TPU:25, one launch (start us, length us, event | category | flops | bytes accessed | tf_op | source)
XLA Modules:
  0.0 210.7 jit_solution(11813537045578096434)
XLA Ops:
  0.7 1.1 copy.57
  1.7 3.5 %collective-permute-start.23 = (bf16[256,256]{0,1:T(8,128)(2,1)S(1)}, bf16[256,256]{0,1:T(8,128)(2,1)S(1)}, u32[]{:S(2)}, u32[]{:S(2)}) collective-permute-start(bf16[256,256]{0,1:T(8,128)(2,1)S(1)} %copy.57), channel_id=1, source_target_pairs={{0,8},{8,16},{16,24},{24,32},{32,40},{40,48},{48,56},{56,64},{64,7... | collective-permute-start | bytes 393224 | tf_op jit(solution)/shard_map/ppermute | solution.py:18
  5.3 0.8 mul.79
  6.1 1.0 copy.41
  13.1 5.7 %while.30 = (s32[]{:T(128)}, f32[2,128,128]{2,1,0:T(8,128)S(1)}, f32[2,128,128]{2,1,0:T(8,128)S(1)}, f32[4,2,64,128]{3,2,1,0:T(8,128)S(1)}, f32[4,2,64,128]{3,2,...) while((s32[]{:T(128)}, f32[2,128,128]{2,1,0:T(8,128)S(1)}, ...), condition=%wide.region_2.3_spmd.clone, body=%wide.region_1.0_spmd.clone.sunk | while | flops 151126016 | bytes 1837159 | solution.py:74
  18.8 3.5 %collective-permute-start.5 = (f32[2,128,128]{2,1,0:T(8,128)S(1)}, f32[2,128,128]{2,1,0:T(8,128)S(1)}, u32[]{:S(2)}, u32[]{:S(2)}) collective-permute-start(f32[2,128,128]{2,1,0:T(8,128)S(1)} %get-tuple-element.101), channel_id=1, source_target_pairs={{0,8},{8,16},{16,24},{32,40},{40,48},{48,56},{64,72},{72,80},{80,8... | collective-permute-start | bytes 393224 | tf_op jit(solution)/shard_map/ppermute | solution.py:115
  22.3 3.5 %collective-permute-start = (f32[2,128,128]{2,1,0:T(8,128)S(1)}, f32[2,128,128]{2,1,0:T(8,128)S(1)}, u32[]{:S(2)}, u32[]{:S(2)}) collective-permute-start(f32[2,128,128]{2,1,0:T(8,128)S(1)} %get-tuple-element.100), channel_id=1, source_target_pairs={{0,8},{8,16},{16,24},{32,40},{40,48},{48,56},{64,72},{72,80},{80,8... | collective-permute-start | bytes 393224 | tf_op jit(solution)/shard_map/ppermute | solution.py:115
  26.4 4.5 %collective-permute-start.6 = (f32[2,128,128]{2,1,0:T(8,128)S(1)}, f32[2,128,128]{2,1,0:T(8,128)S(1)}, u32[]{:S(2)}, u32[]{:S(2)}) collective-permute-start(f32[2,128,128]{2,1,0:T(8,128)S(1)} %fusion.56), channel_id=1, source_target_pairs={{0,16},{8,24},{32,48},{40,56},{64,80},{72,88},{96,112},{104,120},{... | collective-permute-start | bytes 393224 | tf_op jit(solution)/shard_map/ppermute | solution.py:115
  31.2 3.3 %collective-permute-start.1 = (f32[2,128,128]{2,1,0:T(8,128)S(1)}, f32[2,128,128]{2,1,0:T(8,128)S(1)}, u32[]{:S(2)}, u32[]{:S(2)}) collective-permute-start(f32[2,128,128]{2,1,0:T(8,128)S(1)} %convolution_select_fusion.5), channel_id=1, source_target_pairs={{0,16},{8,24},{32,48},{40,56},{64,80},{72,88},{96,112},{104,120},{... | collective-permute-start | bytes 393224 | tf_op jit(solution)/shard_map/ppermute | solution.py:115
  34.5 3.5 %collective-permute-start.24 = (bf16[256,256]{0,1:T(8,128)(2,1)S(1)}, bf16[256,256]{0,1:T(8,128)(2,1)S(1)}, u32[]{:S(2)}, u32[]{:S(2)}) collective-permute-start(bf16[256,256]{0,1:T(8,128)(2,1)S(1)} %collective-permute-done.23), channel_id=1, source_target_pairs={{0,8},{8,16},{16,24},{24,32},{32,40},{40,48},{48,56},{56,64},{64,7... | collective-permute-start | bytes 393224 | tf_op jit(solution)/shard_map/ppermute | solution.py:18
  39.9 2.3 %collective-permute-done.24 = bf16[256,256]{0,1:T(8,128)(2,1)S(1)} collective-permute-done((bf16[256,256]{0,1:T(8,128)(2,1)S(1)}, bf16[256,256]{0,1:T(8,128)(2,1)S(1)}, u32[]{:S(2)}, u32[]{:S(2)}) %collective-permute-start.24) | collective-permute-done | bytes 131104 | tf_op jit(solution)/shard_map/ppermute | solution.py:18
  42.3 5.0 %collective-permute-start.25 = (bf16[256,256]{0,1:T(8,128)(2,1)S(1)}, bf16[256,256]{0,1:T(8,128)(2,1)S(1)}, u32[]{:S(2)}, u32[]{:S(2)}) collective-permute-start(bf16[256,256]{0,1:T(8,128)(2,1)S(1)} %collective-permute-done.24), channel_id=1, source_target_pairs={{0,8},{8,16},{16,24},{24,32},{32,40},{40,48},{48,56},{56,64},{64,7... | collective-permute-start | bytes 393224 | tf_op jit(solution)/shard_map/ppermute | solution.py:18
  49.2 8.6 %collective-permute-done.25 = bf16[256,256]{0,1:T(8,128)(2,1)S(1)} collective-permute-done((bf16[256,256]{0,1:T(8,128)(2,1)S(1)}, bf16[256,256]{0,1:T(8,128)(2,1)S(1)}, u32[]{:S(2)}, u32[]{:S(2)}) %collective-permute-start.25) | collective-permute-done | bytes 131104 | tf_op jit(solution)/shard_map/ppermute | solution.py:18
  57.8 1.9 collective-permute-start.26
  61.6 10.8 %collective-permute-done.26 = bf16[256,256]{0,1:T(8,128)(2,1)S(1)} collective-permute-done((bf16[256,256]{0,1:T(8,128)(2,1)S(1)}, bf16[256,256]{0,1:T(8,128)(2,1)S(1)}, u32[]{:S(2)}, u32[]{:S(2)}) %collective-permute-start.26) | collective-permute-done | bytes 131104 | tf_op jit(solution)/shard_map/ppermute | solution.py:18
  72.5 1.9 collective-permute-start.27
  77.3 1.3 collective-permute-start.11
  78.8 7.2 %collective-permute-done.27 = bf16[256,256]{0,1:T(8,128)(2,1)S(1)} collective-permute-done((bf16[256,256]{0,1:T(8,128)(2,1)S(1)}, bf16[256,256]{0,1:T(8,128)(2,1)S(1)}, u32[]{:S(2)}, u32[]{:S(2)}) %collective-permute-start.27) | collective-permute-done | bytes 131104 | tf_op jit(solution)/shard_map/ppermute | solution.py:18
  85.9 1.9 collective-permute-start.28
  87.9 10.7 %collective-permute-done.11 = f32[2,128,128]{2,1,0:T(8,128)S(1)} collective-permute-done((f32[2,128,128]{2,1,0:T(8,128)S(1)}, f32[2,128,128]{2,1,0:T(8,128)S(1)}, u32[]{:S(2)}, u32[]{:S(2)}) %collective-permute-start.11) | collective-permute-done | bytes 131104 | tf_op jit(solution)/shard_map/ppermute | solution.py:115
  98.8 1.9 collective-permute-start.14
  101.3 4.1 %collective-permute-start.29 = (bf16[256,256]{0,1:T(8,128)(2,1)S(1)}, bf16[256,256]{0,1:T(8,128)(2,1)S(1)}, u32[]{:S(2)}, u32[]{:S(2)}) collective-permute-start(bf16[256,256]{0,1:T(8,128)(2,1)S(1)} %collective-permute-done.28), channel_id=1, source_target_pairs={{0,8},{8,16},{16,24},{24,32},{32,40},{40,48},{48,56},{56,64},{64,7... | collective-permute-start | bytes 393224 | tf_op jit(solution)/shard_map/ppermute | solution.py:18
  105.4 3.0 %collective-permute-done.14 = f32[2,128,128]{2,1,0:T(8,128)S(1)} collective-permute-done((f32[2,128,128]{2,1,0:T(8,128)S(1)}, f32[2,128,128]{2,1,0:T(8,128)S(1)}, u32[]{:S(2)}, u32[]{:S(2)}) %collective-permute-start.14) | collective-permute-done | bytes 131104 | tf_op jit(solution)/shard_map/ppermute | solution.py:18
  108.4 4.5 %while.29 = (s32[]{:T(128)}, f32[2,128,128]{2,1,0:T(8,128)S(1)}, bf16[4,2,64,128]{3,2,0,1:T(8,128)(2,1)S(1)}, f32[4,2,64,128]{3,2,1,0:T(8,128)S(1)}, f32[4,2,64,...) while((s32[]{:T(128)}, f32[2,128,128]{2,1,0:T(8,128)S(1)}, ...), condition=%wide.region_5.6_spmd, body=%wide.region_4.5_spmd.sunk | while | flops 88145920 | bytes 1247341 | solution.py:88
  113.0 2.1 collective-permute-start.15
  115.2 2.0 collective-permute-start.30
  117.1 3.7 %collective-permute-done.15 = bf16[256,256]{0,1:T(8,128)(2,1)S(1)} collective-permute-done((bf16[256,256]{0,1:T(8,128)(2,1)S(1)}, bf16[256,256]{0,1:T(8,128)(2,1)S(1)}, u32[]{:S(2)}, u32[]{:S(2)}) %collective-permute-start.15) | collective-permute-done | bytes 131104 | tf_op jit(solution)/shard_map/ppermute | solution.py:18
  120.9 1.9 collective-permute-start.16
  122.8 1.3 fusion.46
  124.1 4.6 %collective-permute-done.16 = bf16[256,256]{0,1:T(8,128)(2,1)S(1)} collective-permute-done((bf16[256,256]{0,1:T(8,128)(2,1)S(1)}, bf16[256,256]{0,1:T(8,128)(2,1)S(1)}, u32[]{:S(2)}, u32[]{:S(2)}) %collective-permute-start.16) | collective-permute-done | bytes 131104 | tf_op jit(solution)/shard_map/ppermute | solution.py:18
  128.7 1.9 collective-permute-start.17
  130.6 5.9 %collective-permute-done.17 = bf16[256,256]{0,1:T(8,128)(2,1)S(1)} collective-permute-done((bf16[256,256]{0,1:T(8,128)(2,1)S(1)}, bf16[256,256]{0,1:T(8,128)(2,1)S(1)}, u32[]{:S(2)}, u32[]{:S(2)}) %collective-permute-start.17) | collective-permute-done | bytes 131104 | tf_op jit(solution)/shard_map/ppermute | solution.py:18
  136.5 1.9 collective-permute-start.18
  138.4 5.9 %collective-permute-done.18 = bf16[256,256]{0,1:T(8,128)(2,1)S(1)} collective-permute-done((bf16[256,256]{0,1:T(8,128)(2,1)S(1)}, bf16[256,256]{0,1:T(8,128)(2,1)S(1)}, u32[]{:S(2)}, u32[]{:S(2)}) %collective-permute-start.18) | collective-permute-done | bytes 131104 | tf_op jit(solution)/shard_map/ppermute | solution.py:18
  144.3 1.9 collective-permute-start.19
  146.2 5.9 %collective-permute-done.19 = bf16[256,256]{0,1:T(8,128)(2,1)S(1)} collective-permute-done((bf16[256,256]{0,1:T(8,128)(2,1)S(1)}, bf16[256,256]{0,1:T(8,128)(2,1)S(1)}, u32[]{:S(2)}, u32[]{:S(2)}) %collective-permute-start.19) | collective-permute-done | bytes 131104 | tf_op jit(solution)/shard_map/ppermute | solution.py:18
  152.1 1.9 collective-permute-start.20
  154.1 5.9 %collective-permute-done.20 = bf16[256,256]{0,1:T(8,128)(2,1)S(1)} collective-permute-done((bf16[256,256]{0,1:T(8,128)(2,1)S(1)}, bf16[256,256]{0,1:T(8,128)(2,1)S(1)}, u32[]{:S(2)}, u32[]{:S(2)}) %collective-permute-start.20) | collective-permute-done | bytes 131104 | tf_op jit(solution)/shard_map/ppermute | solution.py:18
  159.9 1.9 collective-permute-start.21
  161.8 0.8 fusion.39
  162.7 5.1 %collective-permute-done.21 = bf16[256,256]{0,1:T(8,128)(2,1)S(1)} collective-permute-done((bf16[256,256]{0,1:T(8,128)(2,1)S(1)}, bf16[256,256]{0,1:T(8,128)(2,1)S(1)}, u32[]{:S(2)}, u32[]{:S(2)}) %collective-permute-start.21) | collective-permute-done | bytes 131104 | tf_op jit(solution)/shard_map/ppermute | solution.py:18
  167.7 1.9 collective-permute-start.22
  169.6 4.3 %fusion.88 = (f32[2,256]{1,0:T(2,128)S(1)}, f32[2,256,2304]{1,2,0:T(8,128)}) fusion(f32[2,256,2304]{1,2,0:T(8,128)S(1)} %fusion.39, pred[256,2304]{0,1:T(8,128)(4,1)S(1)} %fusion.46), kind=kOutput, calls=%fused_computation.143 | output fusion | flops 4720895 | bytes 10029056 | tf_op jit(solution)/shard_map/while/body/eval_jaxpr/sub | solution.py:185
  173.9 0.8 copy.63
  174.7 1.8 collective-permute-done.22
  176.7 2.9 %fusion.57 = (f32[256]{0:T(256)S(1)}, f32[2,128,256]{2,1,0:T(8,128)S(1)}) fusion(bf16[2304,2,128]{0,2,1:T(8,128)(2,1)S(1)} %bitcast.201, f32[2,256,2304]{1,2,0:T(8,128)} %get-tuple-element.199, f32[2,256]{1,0:T(2,128)S(1)} %get-tuple-element.198), kind=kOutput, calls=%fused_computation.82 | convolution fusion | flops 304480000 | bytes 6163456 | tf_op jit(solution)/shard_map/while/body/eval_jaxpr/hqk,khd->qhd/dot_general | solution.py:187
  179.7 30.1 %psum.7 = f32[256]{0:T(256)S(1)} all-reduce(f32[256]{0:T(256)S(1)} %get-tuple-element.200), channel_id=1, replica_groups=mesh['seq'=64,'head'=8] {'head'}, use_global_device_ids=true, to_apply=%region_9.10 | all-reduce | flops 256 | bytes 2048 | tf_op jit(solution)/shard_map/psum | solution.py:195
  209.9 0.8 multiply_convert_fusion
  (145 shorter events, 26.2 us)
Async XLA Ops:
  0.6 161.2 %copy-start = (bf16[256,256]{1,0:T(8,128)(2,1)S(1)}, bf16[256,256]{1,0:T(8,128)(2,1)}, u32[]{:S(2)}) copy-start(bf16[256,256]{1,0:T(8,128)(2,1)} %param.15) | copy-start | bytes 393220
  0.6 6.7 %copy-start.1 = (bf16[256,256]{1,0:T(8,128)(2,1)S(1)}, bf16[256,256]{1,0:T(8,128)(2,1)}, u32[]{:S(2)}) copy-start(bf16[256,256]{1,0:T(8,128)(2,1)} %param.13) | copy-start | bytes 393220
  1.7 32.7 %collective-permute-start.23 = (bf16[256,256]{0,1:T(8,128)(2,1)S(1)}, bf16[256,256]{0,1:T(8,128)(2,1)S(1)}, u32[]{:S(2)}, u32[]{:S(2)}) collective-permute-start(bf16[256,256]{0,1:T(8,128)(2,1)S(1)} %copy.57), channel_id=1, source_target_pairs={{0,8},{8,16},{16,24},{24,32},{32,40},{40,48},{48,56},{56,64},{64,7... | collective-permute-start | bytes 393224 | tf_op jit(solution)/shard_map/ppermute | solution.py:18
  13.1 12.8 %copy-start.2 = (bf16[256,256]{1,0:T(8,128)(2,1)S(1)}, bf16[256,256]{1,0:T(8,128)(2,1)}, u32[]{:S(2)}) copy-start(bf16[256,256]{1,0:T(8,128)(2,1)} %param.11) | copy-start | bytes 393220
  18.8 7.3 %collective-permute-start.5 = (f32[2,128,128]{2,1,0:T(8,128)S(1)}, f32[2,128,128]{2,1,0:T(8,128)S(1)}, u32[]{:S(2)}, u32[]{:S(2)}) collective-permute-start(f32[2,128,128]{2,1,0:T(8,128)S(1)} %get-tuple-element.101), channel_id=1, source_target_pairs={{0,8},{8,16},{16,24},{32,40},{40,48},{48,56},{64,72},{72,80},{80,8... | collective-permute-start | bytes 393224 | tf_op jit(solution)/shard_map/ppermute | solution.py:115
  22.3 8.5 %collective-permute-start = (f32[2,128,128]{2,1,0:T(8,128)S(1)}, f32[2,128,128]{2,1,0:T(8,128)S(1)}, u32[]{:S(2)}, u32[]{:S(2)}) collective-permute-start(f32[2,128,128]{2,1,0:T(8,128)S(1)} %get-tuple-element.100), channel_id=1, source_target_pairs={{0,8},{8,16},{16,24},{32,40},{40,48},{48,56},{64,72},{72,80},{80,8... | collective-permute-start | bytes 393224 | tf_op jit(solution)/shard_map/ppermute | solution.py:115
  26.4 11.6 %collective-permute-start.6 = (f32[2,128,128]{2,1,0:T(8,128)S(1)}, f32[2,128,128]{2,1,0:T(8,128)S(1)}, u32[]{:S(2)}, u32[]{:S(2)}) collective-permute-start(f32[2,128,128]{2,1,0:T(8,128)S(1)} %fusion.56), channel_id=1, source_target_pairs={{0,16},{8,24},{32,48},{40,56},{64,80},{72,88},{96,112},{104,120},{... | collective-permute-start | bytes 393224 | tf_op jit(solution)/shard_map/ppermute | solution.py:115
  31.2 7.8 %collective-permute-start.1 = (f32[2,128,128]{2,1,0:T(8,128)S(1)}, f32[2,128,128]{2,1,0:T(8,128)S(1)}, u32[]{:S(2)}, u32[]{:S(2)}) collective-permute-start(f32[2,128,128]{2,1,0:T(8,128)S(1)} %convolution_select_fusion.5), channel_id=1, source_target_pairs={{0,16},{8,24},{32,48},{40,56},{64,80},{72,88},{96,112},{104,120},{... | collective-permute-start | bytes 393224 | tf_op jit(solution)/shard_map/ppermute | solution.py:115
  34.5 7.8 %collective-permute-start.24 = (bf16[256,256]{0,1:T(8,128)(2,1)S(1)}, bf16[256,256]{0,1:T(8,128)(2,1)S(1)}, u32[]{:S(2)}, u32[]{:S(2)}) collective-permute-start(bf16[256,256]{0,1:T(8,128)(2,1)S(1)} %collective-permute-done.23), channel_id=1, source_target_pairs={{0,8},{8,16},{16,24},{24,32},{32,40},{40,48},{48,56},{56,64},{64,7... | collective-permute-start | bytes 393224 | tf_op jit(solution)/shard_map/ppermute | solution.py:18
  38.3 9.0 %collective-permute-start.7 = (f32[2,128,128]{2,1,0:T(8,128)S(1)}, f32[2,128,128]{2,1,0:T(8,128)S(1)}, u32[]{:S(2)}, u32[]{:S(2)}) collective-permute-start(f32[2,128,128]{2,1,0:T(8,128)S(1)} %fusion.55), channel_id=1, source_target_pairs={{24,56},{56,88},{88,120},{120,152},{152,184},{184,216},{216,248},{... | collective-permute-start | bytes 393224 | tf_op jit(solution)/shard_map/ppermute | solution.py:115
  39.3 9.0 %collective-permute-start.2 = (f32[2,128,128]{2,1,0:T(8,128)S(1)}, f32[2,128,128]{2,1,0:T(8,128)S(1)}, u32[]{:S(2)}, u32[]{:S(2)}) collective-permute-start(f32[2,128,128]{2,1,0:T(8,128)S(1)} %convolution_select_fusion.4), channel_id=1, source_target_pairs={{24,56},{56,88},{88,120},{120,152},{152,184},{184,216},{216,248},{... | collective-permute-start | bytes 393224 | tf_op jit(solution)/shard_map/ppermute | solution.py:115
  42.3 15.5 %collective-permute-start.25 = (bf16[256,256]{0,1:T(8,128)(2,1)S(1)}, bf16[256,256]{0,1:T(8,128)(2,1)S(1)}, u32[]{:S(2)}, u32[]{:S(2)}) collective-permute-start(bf16[256,256]{0,1:T(8,128)(2,1)S(1)} %collective-permute-done.24), channel_id=1, source_target_pairs={{0,8},{8,16},{16,24},{24,32},{32,40},{40,48},{48,56},{56,64},{64,7... | collective-permute-start | bytes 393224 | tf_op jit(solution)/shard_map/ppermute | solution.py:18
  47.5 12.2 %collective-permute-start.8 = (f32[2,128,128]{2,1,0:T(8,128)S(1)}, f32[2,128,128]{2,1,0:T(8,128)S(1)}, u32[]{:S(2)}, u32[]{:S(2)}) collective-permute-start(f32[2,128,128]{2,1,0:T(8,128)S(1)} %fusion.54), channel_id=1, source_target_pairs={{24,88},{56,120},{88,152},{120,184},{152,216},{184,248},{216,280},... | collective-permute-start | bytes 393224 | tf_op jit(solution)/shard_map/ppermute | solution.py:115
  48.5 12.2 %collective-permute-start.3 = (f32[2,128,128]{2,1,0:T(8,128)S(1)}, f32[2,128,128]{2,1,0:T(8,128)S(1)}, u32[]{:S(2)}, u32[]{:S(2)}) collective-permute-start(f32[2,128,128]{2,1,0:T(8,128)S(1)} %convolution_select_fusion.3), channel_id=1, source_target_pairs={{24,88},{56,120},{88,152},{120,184},{152,216},{184,248},{216,280},... | collective-permute-start | bytes 393224 | tf_op jit(solution)/shard_map/ppermute | solution.py:115
  57.8 14.7 %collective-permute-start.26 = (bf16[256,256]{0,1:T(8,128)(2,1)S(1)}, bf16[256,256]{0,1:T(8,128)(2,1)S(1)}, u32[]{:S(2)}, u32[]{:S(2)}) collective-permute-start(bf16[256,256]{0,1:T(8,128)(2,1)S(1)} %collective-permute-done.25), channel_id=1, source_target_pairs={{0,8},{8,16},{16,24},{24,32},{32,40},{40,48},{48,56},{56,64},{64,7... | collective-permute-start | bytes 393224 | tf_op jit(solution)/shard_map/ppermute | solution.py:18
  60.0 14.4 %collective-permute-start.9 = (f32[2,128,128]{2,1,0:T(8,128)S(1)}, f32[2,128,128]{2,1,0:T(8,128)S(1)}, u32[]{:S(2)}, u32[]{:S(2)}) collective-permute-start(f32[2,128,128]{2,1,0:T(8,128)S(1)} %fusion.53), channel_id=1, source_target_pairs={{24,152},{56,184},{88,216},{120,248},{152,280},{184,312},{216,344}... | collective-permute-start | bytes 393224 | tf_op jit(solution)/shard_map/ppermute | solution.py:115
  61.0 14.4 %collective-permute-start.4 = (f32[2,128,128]{2,1,0:T(8,128)S(1)}, f32[2,128,128]{2,1,0:T(8,128)S(1)}, u32[]{:S(2)}, u32[]{:S(2)}) collective-permute-start(f32[2,128,128]{2,1,0:T(8,128)S(1)} %convolution_select_fusion.2), channel_id=1, source_target_pairs={{24,152},{56,184},{88,216},{120,248},{152,280},{184,312},{216,344}... | collective-permute-start | bytes 393224 | tf_op jit(solution)/shard_map/ppermute | solution.py:115
  72.5 13.5 %collective-permute-start.27 = (bf16[256,256]{0,1:T(8,128)(2,1)S(1)}, bf16[256,256]{0,1:T(8,128)(2,1)S(1)}, u32[]{:S(2)}, u32[]{:S(2)}) collective-permute-start(bf16[256,256]{0,1:T(8,128)(2,1)S(1)} %collective-permute-done.26), channel_id=1, source_target_pairs={{0,8},{8,16},{16,24},{24,32},{32,40},{40,48},{48,56},{56,64},{64,7... | collective-permute-start | bytes 393224 | tf_op jit(solution)/shard_map/ppermute | solution.py:18
  74.7 1.0 collective-permute-start.10
  75.9 11.9 %collective-permute-start.13 = (f32[2,128,128]{2,1,0:T(8,128)S(1)}, f32[2,128,128]{2,1,0:T(8,128)S(1)}, u32[]{:S(2)}, u32[]{:S(2)}) collective-permute-start(f32[2,128,128]{2,1,0:T(8,128)S(1)} %fusion.51), channel_id=1, source_target_pairs={{24,48},{56,80},{88,112},{120,144},{152,176},{184,208},{216,240},{... | collective-permute-start | bytes 393224 | tf_op jit(solution)/shard_map/ppermute | solution.py:115
  76.6 11.3 %collective-permute-start.12 = (f32[2,128,128]{2,1,0:T(8,128)S(1)}, f32[2,128,128]{2,1,0:T(8,128)S(1)}, u32[]{:S(2)}, u32[]{:S(2)}) collective-permute-start(f32[2,128,128]{2,1,0:T(8,128)S(1)} %fusion.51), channel_id=1, source_target_pairs={{24,40},{56,72},{88,104},{120,136},{152,168},{184,200},{216,232},{... | collective-permute-start | bytes 393224 | tf_op jit(solution)/shard_map/ppermute | solution.py:115
  77.3 21.3 %collective-permute-start.11 = (f32[2,128,128]{2,1,0:T(8,128)S(1)}, f32[2,128,128]{2,1,0:T(8,128)S(1)}, u32[]{:S(2)}, u32[]{:S(2)}) collective-permute-start(f32[2,128,128]{2,1,0:T(8,128)S(1)} %fusion.51), channel_id=1, source_target_pairs={{24,32},{56,64},{88,96},{120,128},{152,160},{184,192},{216,224},{2... | collective-permute-start | bytes 393224 | tf_op jit(solution)/shard_map/ppermute | solution.py:115
  85.9 15.4 %collective-permute-start.28 = (bf16[256,256]{0,1:T(8,128)(2,1)S(1)}, bf16[256,256]{0,1:T(8,128)(2,1)S(1)}, u32[]{:S(2)}, u32[]{:S(2)}) collective-permute-start(bf16[256,256]{0,1:T(8,128)(2,1)S(1)} %collective-permute-done.27), channel_id=1, source_target_pairs={{0,8},{8,16},{16,24},{24,32},{32,40},{40,48},{48,56},{56,64},{64,7... | collective-permute-start | bytes 393224 | tf_op jit(solution)/shard_map/ppermute | solution.py:18
  98.8 9.6 %collective-permute-start.14 = (f32[2,128,128]{2,1,0:T(8,128)S(1)}, f32[2,128,128]{2,1,0:T(8,128)S(1)}, u32[]{:S(2)}, u32[]{:S(2)}) collective-permute-start(f32[2,128,128]{2,1,0:T(8,128)S(1)} %fusion.50), channel_id=1, source_target_pairs={{0,8},{8,16},{16,24},{24,32},{32,40},{40,48},{48,56},{56,64},{64,7... | collective-permute-start | bytes 393224 | tf_op jit(solution)/shard_map/ppermute | solution.py:18
  101.3 13.9 %collective-permute-start.29 = (bf16[256,256]{0,1:T(8,128)(2,1)S(1)}, bf16[256,256]{0,1:T(8,128)(2,1)S(1)}, u32[]{:S(2)}, u32[]{:S(2)}) collective-permute-start(bf16[256,256]{0,1:T(8,128)(2,1)S(1)} %collective-permute-done.28), channel_id=1, source_target_pairs={{0,8},{8,16},{16,24},{24,32},{32,40},{40,48},{48,56},{56,64},{64,7... | collective-permute-start | bytes 393224 | tf_op jit(solution)/shard_map/ppermute | solution.py:18
  113.0 7.8 %collective-permute-start.15 = (bf16[256,256]{0,1:T(8,128)(2,1)S(1)}, bf16[256,256]{0,1:T(8,128)(2,1)S(1)}, u32[]{:S(2)}, u32[]{:S(2)}) collective-permute-start(bf16[256,256]{0,1:T(8,128)(2,1)S(1)} %bitcast.194), channel_id=1, source_target_pairs={{0,8},{8,16},{16,24},{24,32},{32,40},{40,48},{48,56},{56,64},{64,7... | collective-permute-start | bytes 393224 | tf_op jit(solution)/shard_map/ppermute | solution.py:18
  115.2 8.9 %collective-permute-start.30 = (bf16[256,256]{0,1:T(8,128)(2,1)S(1)}, bf16[256,256]{0,1:T(8,128)(2,1)S(1)}, u32[]{:S(2)}, u32[]{:S(2)}) collective-permute-start(bf16[256,256]{0,1:T(8,128)(2,1)S(1)} %collective-permute-done.29), channel_id=1, source_target_pairs={{0,8},{8,16},{16,24},{24,32},{32,40},{40,48},{48,56},{56,64},{64,7... | collective-permute-start | bytes 393224 | tf_op jit(solution)/shard_map/ppermute | solution.py:18
  120.9 7.8 %collective-permute-start.16 = (bf16[256,256]{0,1:T(8,128)(2,1)S(1)}, bf16[256,256]{0,1:T(8,128)(2,1)S(1)}, u32[]{:S(2)}, u32[]{:S(2)}) collective-permute-start(bf16[256,256]{0,1:T(8,128)(2,1)S(1)} %collective-permute-done.15), channel_id=1, source_target_pairs={{0,8},{8,16},{16,24},{24,32},{32,40},{40,48},{48,56},{56,64},{64,7... | collective-permute-start | bytes 393224 | tf_op jit(solution)/shard_map/ppermute | solution.py:18
  128.7 7.8 %collective-permute-start.17 = (bf16[256,256]{0,1:T(8,128)(2,1)S(1)}, bf16[256,256]{0,1:T(8,128)(2,1)S(1)}, u32[]{:S(2)}, u32[]{:S(2)}) collective-permute-start(bf16[256,256]{0,1:T(8,128)(2,1)S(1)} %collective-permute-done.16), channel_id=1, source_target_pairs={{0,8},{8,16},{16,24},{24,32},{32,40},{40,48},{48,56},{56,64},{64,7... | collective-permute-start | bytes 393224 | tf_op jit(solution)/shard_map/ppermute | solution.py:18
  136.5 7.8 %collective-permute-start.18 = (bf16[256,256]{0,1:T(8,128)(2,1)S(1)}, bf16[256,256]{0,1:T(8,128)(2,1)S(1)}, u32[]{:S(2)}, u32[]{:S(2)}) collective-permute-start(bf16[256,256]{0,1:T(8,128)(2,1)S(1)} %collective-permute-done.17), channel_id=1, source_target_pairs={{0,8},{8,16},{16,24},{24,32},{32,40},{40,48},{48,56},{56,64},{64,7... | collective-permute-start | bytes 393224 | tf_op jit(solution)/shard_map/ppermute | solution.py:18
  144.3 7.8 %collective-permute-start.19 = (bf16[256,256]{0,1:T(8,128)(2,1)S(1)}, bf16[256,256]{0,1:T(8,128)(2,1)S(1)}, u32[]{:S(2)}, u32[]{:S(2)}) collective-permute-start(bf16[256,256]{0,1:T(8,128)(2,1)S(1)} %collective-permute-done.18), channel_id=1, source_target_pairs={{0,8},{8,16},{16,24},{24,32},{32,40},{40,48},{48,56},{56,64},{64,7... | collective-permute-start | bytes 393224 | tf_op jit(solution)/shard_map/ppermute | solution.py:18
  152.1 7.8 %collective-permute-start.20 = (bf16[256,256]{0,1:T(8,128)(2,1)S(1)}, bf16[256,256]{0,1:T(8,128)(2,1)S(1)}, u32[]{:S(2)}, u32[]{:S(2)}) collective-permute-start(bf16[256,256]{0,1:T(8,128)(2,1)S(1)} %collective-permute-done.19), channel_id=1, source_target_pairs={{0,8},{8,16},{16,24},{24,32},{32,40},{40,48},{48,56},{56,64},{64,7... | collective-permute-start | bytes 393224 | tf_op jit(solution)/shard_map/ppermute | solution.py:18
  159.9 7.8 %collective-permute-start.21 = (bf16[256,256]{0,1:T(8,128)(2,1)S(1)}, bf16[256,256]{0,1:T(8,128)(2,1)S(1)}, u32[]{:S(2)}, u32[]{:S(2)}) collective-permute-start(bf16[256,256]{0,1:T(8,128)(2,1)S(1)} %collective-permute-done.20), channel_id=1, source_target_pairs={{0,8},{8,16},{16,24},{24,32},{32,40},{40,48},{48,56},{56,64},{64,7... | collective-permute-start | bytes 393224 | tf_op jit(solution)/shard_map/ppermute | solution.py:18
  167.7 8.8 %collective-permute-start.22 = (bf16[256,256]{0,1:T(8,128)(2,1)S(1)}, bf16[256,256]{0,1:T(8,128)(2,1)S(1)}, u32[]{:S(2)}, u32[]{:S(2)}) collective-permute-start(bf16[256,256]{0,1:T(8,128)(2,1)S(1)} %collective-permute-done.21), channel_id=1, source_target_pairs={{0,8},{8,16},{16,24},{24,32},{32,40},{40,48},{48,56},{56,64},{64,7... | collective-permute-start | bytes 393224 | tf_op jit(solution)/shard_map/ppermute | solution.py:18
  176.7 33.2 %copy-start.3 = (f32[256]{0:T(256)S(1)}, f32[256]{0:T(256)}, u32[]{:S(2)}) copy-start(f32[256]{0:T(256)} %param.17) | copy-start | bytes 3076

commit v4 on v3

--- a/solution.py
+++ b/solution.py
@@ -161,7 +161,8 @@
             pieces = [shifted(pieces[0], "seq", 1)] + pieces
         return jnp.concatenate(pieces, axis=0)
 
-    rows_all = (window_rows(k_attn), window_rows(delta_out))
+    rows_all = window_rows(jnp.stack((k_attn, delta_out), axis=1))
+    rows_all = (rows_all[:, 0], rows_all[:, 1])
     block_rows = min(512, tok_rows)
     first_row = lax.axis_index("seq") * tok_rows
     score_scale = 1.0 / math.sqrt(head_size)

time: 212 us -> 222 us (1.047)
  waiting for transfers between devices: 81.3 us -> 124 us
  starting transfers between devices: 63.3 us -> 38.5 us
  blocking collectives: 30.1 us -> 27 us
  matrix products: 22.5 us -> 20.1 us
    ppermute x14, waiting for transfers between devices: 10.7 us -> 54.2 us  [moved(): return lax.ppermute(value, 'seq', pairs)]
    ppermute x17 -> x9, starting transfers between devices: 41.2 us -> 17.4 us  [shifted(): return lax.ppermute(value, axis, pairs)]
    psum x1, blocking collectives: 30.1 us -> 27 us  [on_device(): total_sq = lax.psum(squares, 'head')]
    dot_general x1, matrix products: 2.94 us -> 0.52 us  [attend_block(): jnp.einsum('hqk,khd->qhd', weights, near_values, preferred_element_type=j...]
    ppermute x17 -> x9, waiting for transfers between devices: 70.6 us -> 70.1 us  [shifted(): return lax.ppermute(value, axis, pairs)]
  transfers between devices with their start and end apart: 31 -> 23, of which waited for: 14 -> 11; matrix products, arithmetic and copies ran while one was open for 14% -> 3% of each run, Pallas kernels for 0% -> 0%
where the time goes in v4:
time: 222 us; the launch traced here: 221 us
  waiting for transfers between devices  124 us (56%)
  starting transfers between devices  38.5 us (17%)
  blocking collectives  27 us (12%)
  matrix products  20.1 us (9%)
  local copies, waits for them, and re-layouts  4.79 us (2%)
  other arithmetic  4.7 us (2%)
    ppermute x9, waiting for transfers between devices, shifted(): return lax.ppermute(value, axis, pairs)  70.1 us
    ppermute x14, waiting for transfers between devices, moved(): return lax.ppermute(value, 'seq', pairs)  54.2 us
    psum x1, blocking collectives, on_device(): total_sq = lax.psum(squares, 'head')  27 us
    ppermute x14, starting transfers between devices, moved(): return lax.ppermute(value, 'seq', pairs)  21.1 us
    ppermute x9, starting transfers between devices, shifted(): return lax.ppermute(value, axis, pairs)  17.4 us
  transfers between devices with their start and end apart: 23, of which 11 were waited for; matrix products, arithmetic and copies ran while one was open for 3% of the time, Pallas kernels for 0%

profile of v4, /device:TPU:25, one launch (start us, length us, event | category | flops | bytes accessed | tf_op | source)
XLA Modules:
  0.0 221.3 jit_solution(11387626029644994202)
XLA Ops:
  0.7 0.8 mul.79
  1.5 1.0 copy.39
  2.7 1.0 copy.41
  3.9 0.6 fusion.49
  9.4 5.7 %while.30 = (s32[]{:T(128)}, f32[2,128,128]{2,1,0:T(8,128)S(1)}, f32[2,128,128]{2,1,0:T(8,128)S(1)}, f32[4,2,64,128]{3,2,1,0:T(8,128)S(1)}, f32[4,2,64,128]{3,2,...) while((s32[]{:T(128)}, f32[2,128,128]{2,1,0:T(8,128)S(1)}, ...), condition=%wide.region_2.3_spmd.clone, body=%wide.region_1.0_spmd.clone.sunk | while | flops 151126016 | bytes 1837159 | solution.py:74
  15.1 3.5 %collective-permute-start.5 = (f32[2,128,128]{2,1,0:T(8,128)S(1)}, f32[2,128,128]{2,1,0:T(8,128)S(1)}, u32[]{:S(2)}, u32[]{:S(2)}) collective-permute-start(f32[2,128,128]{2,1,0:T(8,128)S(1)} %get-tuple-element.101), channel_id=1, source_target_pairs={{0,8},{8,16},{16,24},{32,40},{40,48},{48,56},{64,72},{72,80},{80,8... | collective-permute-start | bytes 393224 | tf_op jit(solution)/shard_map/ppermute | solution.py:115
  18.6 3.5 %collective-permute-start = (f32[2,128,128]{2,1,0:T(8,128)S(1)}, f32[2,128,128]{2,1,0:T(8,128)S(1)}, u32[]{:S(2)}, u32[]{:S(2)}) collective-permute-start(f32[2,128,128]{2,1,0:T(8,128)S(1)} %get-tuple-element.100), channel_id=1, source_target_pairs={{0,8},{8,16},{16,24},{32,40},{40,48},{48,56},{64,72},{72,80},{80,8... | collective-permute-start | bytes 393224 | tf_op jit(solution)/shard_map/ppermute | solution.py:115
  22.7 3.8 %collective-permute-start.6 = (f32[2,128,128]{2,1,0:T(8,128)S(1)}, f32[2,128,128]{2,1,0:T(8,128)S(1)}, u32[]{:S(2)}, u32[]{:S(2)}) collective-permute-start(f32[2,128,128]{2,1,0:T(8,128)S(1)} %fusion.56), channel_id=1, source_target_pairs={{0,16},{8,24},{32,48},{40,56},{64,80},{72,88},{96,112},{104,120},{... | collective-permute-start | bytes 393224 | tf_op jit(solution)/shard_map/ppermute | solution.py:115
  26.8 2.7 %collective-permute-start.1 = (f32[2,128,128]{2,1,0:T(8,128)S(1)}, f32[2,128,128]{2,1,0:T(8,128)S(1)}, u32[]{:S(2)}, u32[]{:S(2)}) collective-permute-start(f32[2,128,128]{2,1,0:T(8,128)S(1)} %convolution_select_fusion.5), channel_id=1, source_target_pairs={{0,16},{8,24},{32,48},{40,56},{64,80},{72,88},{96,112},{104,120},{... | collective-permute-start | bytes 393224 | tf_op jit(solution)/shard_map/ppermute | solution.py:115
  29.8 0.8 collective-permute-start.7
  30.6 1.6 collective-permute-done.1
  32.5 0.7 collective-permute-start.2
  33.4 0.7 collective-permute-start.8
  34.4 0.7 collective-permute-start.3
  35.4 0.7 collective-permute-start.9
  36.3 0.7 collective-permute-start.4
  37.3 0.7 collective-permute-start.10
  38.6 0.7 collective-permute-start.13
  39.2 0.7 collective-permute-start.12
  39.9 1.3 collective-permute-start.11
  41.5 52.6 %collective-permute-done.11 = f32[2,128,128]{2,1,0:T(8,128)S(1)} collective-permute-done((f32[2,128,128]{2,1,0:T(8,128)S(1)}, f32[2,128,128]{2,1,0:T(8,128)S(1)}, u32[]{:S(2)}, u32[]{:S(2)}) %collective-permute-start.11) | collective-permute-done | bytes 131104 | tf_op jit(solution)/shard_map/ppermute | solution.py:115
  94.4 1.9 collective-permute-start.14
  96.4 0.5 fusion.48
  96.9 5.4 %collective-permute-done.14 = f32[2,128,128]{2,1,0:T(8,128)S(1)} collective-permute-done((f32[2,128,128]{2,1,0:T(8,128)S(1)}, f32[2,128,128]{2,1,0:T(8,128)S(1)}, u32[]{:S(2)}, u32[]{:S(2)}) %collective-permute-start.14) | collective-permute-done | bytes 131104 | tf_op jit(solution)/shard_map/ppermute | solution.py:18
  102.3 4.5 %while.29 = (s32[]{:T(128)}, f32[2,128,128]{2,1,0:T(8,128)S(1)}, bf16[4,2,64,128]{3,2,0,1:T(8,128)(2,1)S(1)}, f32[4,2,64,128]{3,2,1,0:T(8,128)S(1)}, f32[4,2,64,...) while((s32[]{:T(128)}, f32[2,128,128]{2,1,0:T(8,128)S(1)}, ...), condition=%wide.region_5.6_spmd, body=%wide.region_4.5_spmd.sunk | while | flops 88145920 | bytes 1247341 | solution.py:88
  106.9 1.9 collective-permute-start.15
  108.8 7.3 %collective-permute-done.15 = bf16[256,2,256]{0,2,1:T(8,128)(2,1)S(1)} collective-permute-done((bf16[256,2,256]{0,2,1:T(8,128)(2,1)S(1)}, bf16[256,2,256]{0,2,1:T(8,128)(2,1)S(1)}, u32[]{:S(2)}, u32[]{:S(2)}) %collective-permute-start.15) | collective-permute-done | bytes 262176 | tf_op jit(solution)/shard_map/ppermute | solution.py:18
  116.1 1.9 collective-permute-start.16
  118.1 8.3 %collective-permute-done.16 = bf16[256,2,256]{0,2,1:T(8,128)(2,1)S(1)} collective-permute-done((bf16[256,2,256]{0,2,1:T(8,128)(2,1)S(1)}, bf16[256,2,256]{0,2,1:T(8,128)(2,1)S(1)}, u32[]{:S(2)}, u32[]{:S(2)}) %collective-permute-start.16) | collective-permute-done | bytes 262176 | tf_op jit(solution)/shard_map/ppermute | solution.py:18
  126.3 1.9 collective-permute-start.17
  128.3 9.4 %collective-permute-done.17 = bf16[256,2,256]{0,2,1:T(8,128)(2,1)S(1)} collective-permute-done((bf16[256,2,256]{0,2,1:T(8,128)(2,1)S(1)}, bf16[256,2,256]{0,2,1:T(8,128)(2,1)S(1)}, u32[]{:S(2)}, u32[]{:S(2)}) %collective-permute-start.17) | collective-permute-done | bytes 262176 | tf_op jit(solution)/shard_map/ppermute | solution.py:18
  137.6 1.9 collective-permute-start.18
  139.5 10.0 %collective-permute-done.18 = bf16[256,2,256]{0,2,1:T(8,128)(2,1)S(1)} collective-permute-done((bf16[256,2,256]{0,2,1:T(8,128)(2,1)S(1)}, bf16[256,2,256]{0,2,1:T(8,128)(2,1)S(1)}, u32[]{:S(2)}, u32[]{:S(2)}) %collective-permute-start.18) | collective-permute-done | bytes 262176 | tf_op jit(solution)/shard_map/ppermute | solution.py:18
  149.6 1.9 collective-permute-start.19
  151.5 9.2 %collective-permute-done.19 = bf16[256,2,256]{0,2,1:T(8,128)(2,1)S(1)} collective-permute-done((bf16[256,2,256]{0,2,1:T(8,128)(2,1)S(1)}, bf16[256,2,256]{0,2,1:T(8,128)(2,1)S(1)}, u32[]{:S(2)}, u32[]{:S(2)}) %collective-permute-start.19) | collective-permute-done | bytes 262176 | tf_op jit(solution)/shard_map/ppermute | solution.py:18
  160.6 2.1 collective-permute-start.20
  162.7 8.1 %collective-permute-done.20 = bf16[256,2,256]{0,2,1:T(8,128)(2,1)S(1)} collective-permute-done((bf16[256,2,256]{0,2,1:T(8,128)(2,1)S(1)}, bf16[256,2,256]{0,2,1:T(8,128)(2,1)S(1)}, u32[]{:S(2)}, u32[]{:S(2)}) %collective-permute-start.20) | collective-permute-done | bytes 262176 | tf_op jit(solution)/shard_map/ppermute | solution.py:18
  170.8 1.9 collective-permute-start.21
  172.7 7.3 %collective-permute-done.21 = bf16[256,2,256]{0,2,1:T(8,128)(2,1)S(1)} collective-permute-done((bf16[256,2,256]{0,2,1:T(8,128)(2,1)S(1)}, bf16[256,2,256]{0,2,1:T(8,128)(2,1)S(1)}, u32[]{:S(2)}, u32[]{:S(2)}) %collective-permute-start.21) | collective-permute-done | bytes 262176 | tf_op jit(solution)/shard_map/ppermute | solution.py:18
  180.0 1.9 collective-permute-start.22
  181.9 1.3 fusion.46
  183.2 0.8 copy.61
  184.0 5.3 %collective-permute-done.22 = bf16[256,2,256]{0,2,1:T(8,128)(2,1)S(1)} collective-permute-done((bf16[256,2,256]{0,2,1:T(8,128)(2,1)S(1)}, bf16[256,2,256]{0,2,1:T(8,128)(2,1)S(1)}, u32[]{:S(2)}, u32[]{:S(2)}) %collective-permute-start.22) | collective-permute-done | bytes 262176 | tf_op jit(solution)/shard_map/ppermute | solution.py:18
  189.6 0.8 fusion.39
  190.5 2.4 %fusion.89 = (f32[2,256]{1,0:T(2,128)S(1)}, f32[2,256,2304]{1,2,0:T(8,128)S(1)}) fusion(f32[2,256,2304]{1,2,0:T(8,128)S(1)} %fusion.39, pred[256,2304]{0,1:T(8,128)(4,1)S(1)} %fusion.46), kind=kOutput, calls=%fused_computation.136 | output fusion | flops 4720895 | bytes 10029056 | tf_op jit(solution)/shard_map/while/body/eval_jaxpr/sub | solution.py:186
  192.8 0.5 fusion.57
  193.4 27.0 %psum.7 = f32[256]{0:T(256)S(1)} all-reduce(f32[256]{0:T(256)S(1)} %get-tuple-element.202), channel_id=1, replica_groups=mesh['seq'=64,'head'=8] {'head'}, use_global_device_ids=true, to_apply=%region_9.10 | all-reduce | flops 256 | bytes 2048 | tf_op jit(solution)/shard_map/psum | solution.py:196
  220.5 0.8 multiply_convert_fusion
  (122 shorter events, 19.3 us)
Async XLA Ops:
  0.6 189.0 %copy-start = (bf16[256,256]{1,0:T(8,128)(2,1)S(1)}, bf16[256,256]{1,0:T(8,128)(2,1)}, u32[]{:S(2)}) copy-start(bf16[256,256]{1,0:T(8,128)(2,1)} %param.15) | copy-start | bytes 393220
  9.4 12.8 %copy-start.1 = (bf16[256,256]{1,0:T(8,128)(2,1)S(1)}, bf16[256,256]{1,0:T(8,128)(2,1)}, u32[]{:S(2)}) copy-start(bf16[256,256]{1,0:T(8,128)(2,1)} %param.11) | copy-start | bytes 393220
  15.1 7.3 %collective-permute-start.5 = (f32[2,128,128]{2,1,0:T(8,128)S(1)}, f32[2,128,128]{2,1,0:T(8,128)S(1)}, u32[]{:S(2)}, u32[]{:S(2)}) collective-permute-start(f32[2,128,128]{2,1,0:T(8,128)S(1)} %get-tuple-element.101), channel_id=1, source_target_pairs={{0,8},{8,16},{16,24},{32,40},{40,48},{48,56},{64,72},{72,80},{80,8... | collective-permute-start | bytes 393224 | tf_op jit(solution)/shard_map/ppermute | solution.py:115
  18.6 7.9 %collective-permute-start = (f32[2,128,128]{2,1,0:T(8,128)S(1)}, f32[2,128,128]{2,1,0:T(8,128)S(1)}, u32[]{:S(2)}, u32[]{:S(2)}) collective-permute-start(f32[2,128,128]{2,1,0:T(8,128)S(1)} %get-tuple-element.100), channel_id=1, source_target_pairs={{0,8},{8,16},{16,24},{32,40},{40,48},{48,56},{64,72},{72,80},{80,8... | collective-permute-start | bytes 393224 | tf_op jit(solution)/shard_map/ppermute | solution.py:115
  22.7 6.8 %collective-permute-start.6 = (f32[2,128,128]{2,1,0:T(8,128)S(1)}, f32[2,128,128]{2,1,0:T(8,128)S(1)}, u32[]{:S(2)}, u32[]{:S(2)}) collective-permute-start(f32[2,128,128]{2,1,0:T(8,128)S(1)} %fusion.56), channel_id=1, source_target_pairs={{0,16},{8,24},{32,48},{40,56},{64,80},{72,88},{96,112},{104,120},{... | collective-permute-start | bytes 393224 | tf_op jit(solution)/shard_map/ppermute | solution.py:115
  26.8 5.4 %collective-permute-start.1 = (f32[2,128,128]{2,1,0:T(8,128)S(1)}, f32[2,128,128]{2,1,0:T(8,128)S(1)}, u32[]{:S(2)}, u32[]{:S(2)}) collective-permute-start(f32[2,128,128]{2,1,0:T(8,128)S(1)} %convolution_select_fusion.5), channel_id=1, source_target_pairs={{0,16},{8,24},{32,48},{40,56},{64,80},{72,88},{96,112},{104,120},{... | collective-permute-start | bytes 393224 | tf_op jit(solution)/shard_map/ppermute | solution.py:115
  29.8 11.6 %copy-start.2 = (bf16[256,256]{1,0:T(8,128)(2,1)S(1)}, bf16[256,256]{1,0:T(8,128)(2,1)}, u32[]{:S(2)}) copy-start(bf16[256,256]{1,0:T(8,128)(2,1)} %param.16) | copy-start | bytes 393220
  29.8 3.3 %collective-permute-start.7 = (f32[2,128,128]{2,1,0:T(8,128)S(1)}, f32[2,128,128]{2,1,0:T(8,128)S(1)}, u32[]{:S(2)}, u32[]{:S(2)}) collective-permute-start(f32[2,128,128]{2,1,0:T(8,128)S(1)} %fusion.55), channel_id=1, source_target_pairs={{24,56},{56,88},{88,120},{120,152},{152,184},{184,216},{216,248},{... | collective-permute-start | bytes 393224 | tf_op jit(solution)/shard_map/ppermute | solution.py:115
  32.5 1.6 collective-permute-start.2
  33.4 1.6 collective-permute-start.8
  34.4 1.6 collective-permute-start.3
  35.4 1.6 collective-permute-start.9
  36.3 1.6 collective-permute-start.4
  37.3 1.0 collective-permute-start.10
  38.6 3.0 %collective-permute-start.13 = (f32[2,128,128]{2,1,0:T(8,128)S(1)}, f32[2,128,128]{2,1,0:T(8,128)S(1)}, u32[]{:S(2)}, u32[]{:S(2)}) collective-permute-start(f32[2,128,128]{2,1,0:T(8,128)S(1)} %fusion.51), channel_id=1, source_target_pairs={{24,48},{56,80},{88,112},{120,144},{152,176},{184,208},{216,240},{... | collective-permute-start | bytes 393224 | tf_op jit(solution)/shard_map/ppermute | solution.py:115
  39.2 2.3 %collective-permute-start.12 = (f32[2,128,128]{2,1,0:T(8,128)S(1)}, f32[2,128,128]{2,1,0:T(8,128)S(1)}, u32[]{:S(2)}, u32[]{:S(2)}) collective-permute-start(f32[2,128,128]{2,1,0:T(8,128)S(1)} %fusion.51), channel_id=1, source_target_pairs={{24,40},{56,72},{88,104},{120,136},{152,168},{184,200},{216,232},{... | collective-permute-start | bytes 393224 | tf_op jit(solution)/shard_map/ppermute | solution.py:115
  39.9 54.3 %collective-permute-start.11 = (f32[2,128,128]{2,1,0:T(8,128)S(1)}, f32[2,128,128]{2,1,0:T(8,128)S(1)}, u32[]{:S(2)}, u32[]{:S(2)}) collective-permute-start(f32[2,128,128]{2,1,0:T(8,128)S(1)} %fusion.51), channel_id=1, source_target_pairs={{24,32},{56,64},{88,96},{120,128},{152,160},{184,192},{216,224},{2... | collective-permute-start | bytes 393224 | tf_op jit(solution)/shard_map/ppermute | solution.py:115
  94.4 7.8 %collective-permute-start.14 = (f32[2,128,128]{2,1,0:T(8,128)S(1)}, f32[2,128,128]{2,1,0:T(8,128)S(1)}, u32[]{:S(2)}, u32[]{:S(2)}) collective-permute-start(f32[2,128,128]{2,1,0:T(8,128)S(1)} %fusion.50), channel_id=1, source_target_pairs={{0,8},{8,16},{16,24},{24,32},{32,40},{40,48},{48,56},{56,64},{64,7... | collective-permute-start | bytes 393224 | tf_op jit(solution)/shard_map/ppermute | solution.py:18
  106.9 9.2 %collective-permute-start.15 = (bf16[256,2,256]{0,2,1:T(8,128)(2,1)S(1)}, bf16[256,2,256]{0,2,1:T(8,128)(2,1)S(1)}, u32[]{:S(2)}, u32[]{:S(2)}) collective-permute-start(bf16[256,2,256]{0,2,1:T(8,128)(2,1)S(1)} %pad_maximum_fusion), channel_id=1, source_target_pairs={{0,8},{8,16},{16,24},{24,32},{32,40},{40,48},{48,56},{56,64},{64,7... | collective-permute-start | bytes 786440 | tf_op jit(solution)/shard_map/ppermute | solution.py:18
  116.1 10.2 %collective-permute-start.16 = (bf16[256,2,256]{0,2,1:T(8,128)(2,1)S(1)}, bf16[256,2,256]{0,2,1:T(8,128)(2,1)S(1)}, u32[]{:S(2)}, u32[]{:S(2)}) collective-permute-start(bf16[256,2,256]{0,2,1:T(8,128)(2,1)S(1)} %collective-permute-done.15), channel_id=1, source_target_pairs={{0,8},{8,16},{16,24},{24,32},{32,40},{40,48},{48,56},{56,64},{64,7... | collective-permute-start | bytes 786440 | tf_op jit(solution)/shard_map/ppermute | solution.py:18
  126.3 11.3 %collective-permute-start.17 = (bf16[256,2,256]{0,2,1:T(8,128)(2,1)S(1)}, bf16[256,2,256]{0,2,1:T(8,128)(2,1)S(1)}, u32[]{:S(2)}, u32[]{:S(2)}) collective-permute-start(bf16[256,2,256]{0,2,1:T(8,128)(2,1)S(1)} %collective-permute-done.16), channel_id=1, source_target_pairs={{0,8},{8,16},{16,24},{24,32},{32,40},{40,48},{48,56},{56,64},{64,7... | collective-permute-start | bytes 786440 | tf_op jit(solution)/shard_map/ppermute | solution.py:18
  137.6 12.0 %collective-permute-start.18 = (bf16[256,2,256]{0,2,1:T(8,128)(2,1)S(1)}, bf16[256,2,256]{0,2,1:T(8,128)(2,1)S(1)}, u32[]{:S(2)}, u32[]{:S(2)}) collective-permute-start(bf16[256,2,256]{0,2,1:T(8,128)(2,1)S(1)} %collective-permute-done.17), channel_id=1, source_target_pairs={{0,8},{8,16},{16,24},{24,32},{32,40},{40,48},{48,56},{56,64},{64,7... | collective-permute-start | bytes 786440 | tf_op jit(solution)/shard_map/ppermute | solution.py:18
  149.6 11.1 %collective-permute-start.19 = (bf16[256,2,256]{0,2,1:T(8,128)(2,1)S(1)}, bf16[256,2,256]{0,2,1:T(8,128)(2,1)S(1)}, u32[]{:S(2)}, u32[]{:S(2)}) collective-permute-start(bf16[256,2,256]{0,2,1:T(8,128)(2,1)S(1)} %collective-permute-done.18), channel_id=1, source_target_pairs={{0,8},{8,16},{16,24},{24,32},{32,40},{40,48},{48,56},{56,64},{64,7... | collective-permute-start | bytes 786440 | tf_op jit(solution)/shard_map/ppermute | solution.py:18
  160.6 10.2 %collective-permute-start.20 = (bf16[256,2,256]{0,2,1:T(8,128)(2,1)S(1)}, bf16[256,2,256]{0,2,1:T(8,128)(2,1)S(1)}, u32[]{:S(2)}, u32[]{:S(2)}) collective-permute-start(bf16[256,2,256]{0,2,1:T(8,128)(2,1)S(1)} %collective-permute-done.19), channel_id=1, source_target_pairs={{0,8},{8,16},{16,24},{24,32},{32,40},{40,48},{48,56},{56,64},{64,7... | collective-permute-start | bytes 786440 | tf_op jit(solution)/shard_map/ppermute | solution.py:18
  170.8 9.2 %collective-permute-start.21 = (bf16[256,2,256]{0,2,1:T(8,128)(2,1)S(1)}, bf16[256,2,256]{0,2,1:T(8,128)(2,1)S(1)}, u32[]{:S(2)}, u32[]{:S(2)}) collective-permute-start(bf16[256,2,256]{0,2,1:T(8,128)(2,1)S(1)} %collective-permute-done.20), channel_id=1, source_target_pairs={{0,8},{8,16},{16,24},{24,32},{32,40},{40,48},{48,56},{56,64},{64,7... | collective-permute-start | bytes 786440 | tf_op jit(solution)/shard_map/ppermute | solution.py:18
  180.0 9.2 %collective-permute-start.22 = (bf16[256,2,256]{0,2,1:T(8,128)(2,1)S(1)}, bf16[256,2,256]{0,2,1:T(8,128)(2,1)S(1)}, u32[]{:S(2)}, u32[]{:S(2)}) collective-permute-start(bf16[256,2,256]{0,2,1:T(8,128)(2,1)S(1)} %collective-permute-done.21), channel_id=1, source_target_pairs={{0,8},{8,16},{16,24},{24,32},{32,40},{40,48},{48,56},{56,64},{64,7... | collective-permute-start | bytes 786440 | tf_op jit(solution)/shard_map/ppermute | solution.py:18
  192.8 27.7 %copy-start.3 = (f32[256]{0:T(256)S(1)}, f32[256]{0:T(256)}, u32[]{:S(2)}) copy-start(f32[256]{0:T(256)} %param.17) | copy-start | bytes 3076

commit v5 on v3

--- a/solution.py
+++ b/solution.py
@@ -114,12 +114,19 @@
         pairs = [(i, i + by) for i in sources if 0 <= i + by < seq_size]
         return lax.ppermute(value, "seq", pairs)
 
+    identity = jnp.broadcast_to(jnp.eye(head_size, dtype=jnp.float32), transit.shape)
+    before_transit = identity
+    before_carried = jnp.zeros_like(carried)
     distance = 1
     while distance < group:
         inside = [i for i in range(seq_size) if i % group + distance < group]
         transit_prev = moved(transit, distance, inside)
         carried_prev = moved(carried, distance, inside)
         has_prev = rank >= distance
+        before_carried = jnp.where(
+            has_prev, batched_dot(before_transit, carried_prev) + before_carried, before_carried
+        )
+        before_transit = jnp.where(has_prev, batched_dot(before_transit, transit_prev), before_transit)
         carried_in = jnp.where(has_prev, batched_dot(transit, carried_prev) + carried, carried)
         transit = jnp.where(has_prev, batched_dot(transit, transit_prev), transit)
         carried = carried_in
@@ -140,12 +147,9 @@
         end_carried = carried_next
         distance *= 2
     group_in = jnp.zeros_like(carried)
-    for hop in range(1, group):
+    for hop in range(1, group + 1):
         group_in = group_in + moved(end_carried, hop, ends)
-    leaving = jnp.where(
-        rank == group - 1, end_carried, batched_dot(transit, group_in) + carried
-    )
-    incoming = shifted(leaving, "seq", 1)
+    incoming = batched_dot(before_transit, group_in) + before_carried
     results = jax.vmap(run_blocks)(incoming, q_unit, k_unit, writes, updates, query_key)
     delta_out = (
         results.reshape(heads_here, tok_rows, head_size)

time: 212 us -> 210 us (level)
  waiting for transfers between devices: 81.3 us -> 89.1 us
  starting transfers between devices: 63.3 us -> 59.4 us
  blocking collectives: 30.1 us -> 26.7 us
    ppermute x17 -> x16, waiting for transfers between devices: 70.6 us -> 78 us  [shifted(): return lax.ppermute(value, axis, pairs)]
    ppermute x17 -> x16, starting transfers between devices: 41.2 us -> 37.3 us  [shifted(): return lax.ppermute(value, axis, pairs)]
    psum x1, blocking collectives: 30.1 us -> 26.7 us  [on_device(): total_sq = lax.psum(squares, 'head')]
    dot_general x1, matrix products: 2.94 us -> 0.52 us  [attend_block(): jnp.einsum('hqk,khd->qhd', weights, near_values, preferred_element_type=j...]
    dot_general x12 -> x16, matrix products: 3.24 us -> 4.34 us  [batched_dot(): return jnp.einsum('hij,hjk->hik', left, right, precision=highest)]
    ppermute x14 -> x15, waiting for transfers between devices: 10.7 us -> 11.1 us  [moved(): return lax.ppermute(value, 'seq', pairs)]
    ppermute x14 -> x15, starting transfers between devices: 22.2 us -> 22.1 us  [moved(): return lax.ppermute(value, 'seq', pairs)]
  transfers between devices with their start and end apart: 31 -> 31, of which waited for: 14 -> 14; matrix products, arithmetic and copies ran while one was open for 14% -> 13% of each run, Pallas kernels for 0% -> 0%
where the time goes in v5:
time: 210 us; the launch traced here: 208 us
  waiting for transfers between devices  89.1 us (42%)
  starting transfers between devices  59.4 us (28%)
  blocking collectives  26.7 us (13%)
  matrix products  21.2 us (10%)
  local copies, waits for them, and re-layouts  4.72 us (2%)
  other arithmetic  4.65 us (2%)
    ppermute x16, waiting for transfers between devices, shifted(): return lax.ppermute(value, axis, pairs)  78 us
    ppermute x16, starting transfers between devices, shifted(): return lax.ppermute(value, axis, pairs)  37.3 us
    psum x1, blocking collectives, on_device(): total_sq = lax.psum(squares, 'head')  26.7 us
    ppermute x15, starting transfers between devices, moved(): return lax.ppermute(value, 'seq', pairs)  22.1 us
    ppermute x15, waiting for transfers between devices, moved(): return lax.ppermute(value, 'seq', pairs)  11.1 us
    dot_general x16, matrix products, batched_dot(): return jnp.einsum('hij,hjk->hik', left, right, precision=highest)  4.34 us
  transfers between devices with their start and end apart: 31, of which 14 were waited for; matrix products, arithmetic and copies ran while one was open for 13% of the time, Pallas kernels for 0%

profile of v5, /device:TPU:25, one launch (start us, length us, event | category | flops | bytes accessed | tf_op | source)
XLA Modules:
  0.0 207.9 jit_solution(5686565318102226490)
XLA Ops:
  0.7 1.1 copy.57
  1.7 3.5 %collective-permute-start.23 = (bf16[256,256]{0,1:T(8,128)(2,1)S(1)}, bf16[256,256]{0,1:T(8,128)(2,1)S(1)}, u32[]{:S(2)}, u32[]{:S(2)}) collective-permute-start(bf16[256,256]{0,1:T(8,128)(2,1)S(1)} %copy.57), channel_id=1, source_target_pairs={{0,8},{8,16},{16,24},{24,32},{32,40},{40,48},{48,56},{56,64},{64,7... | collective-permute-start | bytes 393224 | tf_op jit(solution)/shard_map/ppermute | solution.py:18
  5.3 0.8 mul.79
  6.1 1.0 copy.41
  13.1 5.7 %while.30 = (s32[]{:T(128)}, f32[2,128,128]{2,1,0:T(8,128)S(1)}, f32[2,128,128]{2,1,0:T(8,128)S(1)}, f32[4,2,64,128]{3,2,1,0:T(8,128)S(1)}, f32[4,2,64,128]{3,2,...) while((s32[]{:T(128)}, f32[2,128,128]{2,1,0:T(8,128)S(1)}, ...), condition=%wide.region_2.3_spmd.clone, body=%wide.region_1.0_spmd.clone.sunk | while | flops 151126016 | bytes 1837159 | solution.py:74
  18.8 3.6 %collective-permute-start.5 = (f32[2,128,128]{2,1,0:T(8,128)S(1)}, f32[2,128,128]{2,1,0:T(8,128)S(1)}, u32[]{:S(2)}, u32[]{:S(2)}) collective-permute-start(f32[2,128,128]{2,1,0:T(8,128)S(1)} %get-tuple-element.101), channel_id=1, source_target_pairs={{0,8},{8,16},{16,24},{32,40},{40,48},{48,56},{64,72},{72,80},{80,8... | collective-permute-start | bytes 393224 | tf_op jit(solution)/shard_map/ppermute | solution.py:115
  22.3 3.5 %collective-permute-start = (f32[2,128,128]{2,1,0:T(8,128)S(1)}, f32[2,128,128]{2,1,0:T(8,128)S(1)}, u32[]{:S(2)}, u32[]{:S(2)}) collective-permute-start(f32[2,128,128]{2,1,0:T(8,128)S(1)} %get-tuple-element.100), channel_id=1, source_target_pairs={{0,8},{8,16},{16,24},{32,40},{40,48},{48,56},{64,72},{72,80},{80,8... | collective-permute-start | bytes 393224 | tf_op jit(solution)/shard_map/ppermute | solution.py:115
  27.1 4.5 %collective-permute-start.6 = (f32[2,128,128]{2,1,0:T(8,128)S(1)}, f32[2,128,128]{2,1,0:T(8,128)S(1)}, u32[]{:S(2)}, u32[]{:S(2)}) collective-permute-start(f32[2,128,128]{2,1,0:T(8,128)S(1)} %fusion.56), channel_id=1, source_target_pairs={{0,16},{8,24},{32,48},{40,56},{64,80},{72,88},{96,112},{104,120},{... | collective-permute-start | bytes 393224 | tf_op jit(solution)/shard_map/ppermute | solution.py:115
  31.9 2.5 %collective-permute-start.1 = (f32[2,128,128]{2,1,0:T(8,128)S(1)}, f32[2,128,128]{2,1,0:T(8,128)S(1)}, u32[]{:S(2)}, u32[]{:S(2)}) collective-permute-start(f32[2,128,128]{2,1,0:T(8,128)S(1)} %convolution_select_fusion.6), channel_id=1, source_target_pairs={{0,16},{8,24},{32,48},{40,56},{64,80},{72,88},{96,112},{104,120},{... | collective-permute-start | bytes 393224 | tf_op jit(solution)/shard_map/ppermute | solution.py:115
  34.7 3.5 %collective-permute-start.24 = (bf16[256,256]{0,1:T(8,128)(2,1)S(1)}, bf16[256,256]{0,1:T(8,128)(2,1)S(1)}, u32[]{:S(2)}, u32[]{:S(2)}) collective-permute-start(bf16[256,256]{0,1:T(8,128)(2,1)S(1)} %collective-permute-done.23), channel_id=1, source_target_pairs={{0,8},{8,16},{16,24},{24,32},{32,40},{40,48},{48,56},{56,64},{64,7... | collective-permute-start | bytes 393224 | tf_op jit(solution)/shard_map/ppermute | solution.py:18
  38.9 0.7 collective-permute-start.7
  40.5 2.1 collective-permute-done.24
  42.6 5.2 %collective-permute-start.25 = (bf16[256,256]{0,1:T(8,128)(2,1)S(1)}, bf16[256,256]{0,1:T(8,128)(2,1)S(1)}, u32[]{:S(2)}, u32[]{:S(2)}) collective-permute-start(bf16[256,256]{0,1:T(8,128)(2,1)S(1)} %collective-permute-done.24), channel_id=1, source_target_pairs={{0,8},{8,16},{16,24},{24,32},{32,40},{40,48},{48,56},{56,64},{64,7... | collective-permute-start | bytes 393224 | tf_op jit(solution)/shard_map/ppermute | solution.py:18
  48.3 0.7 collective-permute-start.8
  50.0 10.5 %collective-permute-done.25 = bf16[256,256]{0,1:T(8,128)(2,1)S(1)} collective-permute-done((bf16[256,256]{0,1:T(8,128)(2,1)S(1)}, bf16[256,256]{0,1:T(8,128)(2,1)S(1)}, u32[]{:S(2)}, u32[]{:S(2)}) %collective-permute-start.25) | collective-permute-done | bytes 131104 | tf_op jit(solution)/shard_map/ppermute | solution.py:18
  60.4 1.9 collective-permute-start.26
  64.3 9.0 %collective-permute-done.26 = bf16[256,256]{0,1:T(8,128)(2,1)S(1)} collective-permute-done((bf16[256,256]{0,1:T(8,128)(2,1)S(1)}, bf16[256,256]{0,1:T(8,128)(2,1)S(1)}, u32[]{:S(2)}, u32[]{:S(2)}) %collective-permute-start.26) | collective-permute-done | bytes 131104 | tf_op jit(solution)/shard_map/ppermute | solution.py:18
  73.2 1.9 collective-permute-start.27
  76.1 10.9 %collective-permute-done.27 = bf16[256,256]{0,1:T(8,128)(2,1)S(1)} collective-permute-done((bf16[256,256]{0,1:T(8,128)(2,1)S(1)}, bf16[256,256]{0,1:T(8,128)(2,1)S(1)}, u32[]{:S(2)}, u32[]{:S(2)}) %collective-permute-start.27) | collective-permute-done | bytes 131104 | tf_op jit(solution)/shard_map/ppermute | solution.py:18
  87.0 1.9 collective-permute-start.28
  91.6 1.3 collective-permute-start.11
  93.1 2.0 collective-permute-done.28
  95.1 2.1 %collective-permute-start.29 = (bf16[256,256]{0,1:T(8,128)(2,1)S(1)}, bf16[256,256]{0,1:T(8,128)(2,1)S(1)}, u32[]{:S(2)}, u32[]{:S(2)}) collective-permute-start(bf16[256,256]{0,1:T(8,128)(2,1)S(1)} %collective-permute-done.28), channel_id=1, source_target_pairs={{0,8},{8,16},{16,24},{24,32},{32,40},{40,48},{48,56},{56,64},{64,7... | collective-permute-start | bytes 393224 | tf_op jit(solution)/shard_map/ppermute | solution.py:18
  97.3 11.0 %collective-permute-done.11 = f32[2,128,128]{2,1,0:T(8,128)S(1)} collective-permute-done((f32[2,128,128]{2,1,0:T(8,128)S(1)}, f32[2,128,128]{2,1,0:T(8,128)S(1)}, u32[]{:S(2)}, u32[]{:S(2)}) %collective-permute-start.11) | collective-permute-done | bytes 131104 | tf_op jit(solution)/shard_map/ppermute | solution.py:115
  108.6 4.5 %while.29 = (s32[]{:T(128)}, f32[2,128,128]{2,1,0:T(8,128)S(1)}, bf16[4,2,64,128]{3,2,0,1:T(8,128)(2,1)S(1)}, f32[4,2,64,128]{3,2,1,0:T(8,128)S(1)}, f32[4,2,64,...) while((s32[]{:T(128)}, f32[2,128,128]{2,1,0:T(8,128)S(1)}, ...), condition=%wide.region_5.6_spmd, body=%wide.region_4.5_spmd.sunk | while | flops 88145920 | bytes 1247341 | solution.py:88
  113.2 1.9 collective-permute-start.15
  115.2 1.9 collective-permute-start.30
  117.1 3.9 %collective-permute-done.15 = bf16[256,256]{0,1:T(8,128)(2,1)S(1)} collective-permute-done((bf16[256,256]{0,1:T(8,128)(2,1)S(1)}, bf16[256,256]{0,1:T(8,128)(2,1)S(1)}, u32[]{:S(2)}, u32[]{:S(2)}) %collective-permute-start.15) | collective-permute-done | bytes 131104 | tf_op jit(solution)/shard_map/ppermute | solution.py:18
  121.0 1.9 collective-permute-start.16
  122.9 1.3 fusion.46
  124.2 0.8 copy.63
  125.0 5.5 %collective-permute-done.16 = bf16[256,256]{0,1:T(8,128)(2,1)S(1)} collective-permute-done((bf16[256,256]{0,1:T(8,128)(2,1)S(1)}, bf16[256,256]{0,1:T(8,128)(2,1)S(1)}, u32[]{:S(2)}, u32[]{:S(2)}) %collective-permute-start.16) | collective-permute-done | bytes 131104 | tf_op jit(solution)/shard_map/ppermute | solution.py:18
  130.4 1.9 collective-permute-start.17
  132.4 7.4 %collective-permute-done.17 = bf16[256,256]{0,1:T(8,128)(2,1)S(1)} collective-permute-done((bf16[256,256]{0,1:T(8,128)(2,1)S(1)}, bf16[256,256]{0,1:T(8,128)(2,1)S(1)}, u32[]{:S(2)}, u32[]{:S(2)}) %collective-permute-start.17) | collective-permute-done | bytes 131104 | tf_op jit(solution)/shard_map/ppermute | solution.py:18
  139.8 1.9 collective-permute-start.18
  141.8 6.5 %collective-permute-done.18 = bf16[256,256]{0,1:T(8,128)(2,1)S(1)} collective-permute-done((bf16[256,256]{0,1:T(8,128)(2,1)S(1)}, bf16[256,256]{0,1:T(8,128)(2,1)S(1)}, u32[]{:S(2)}, u32[]{:S(2)}) %collective-permute-start.18) | collective-permute-done | bytes 131104 | tf_op jit(solution)/shard_map/ppermute | solution.py:18
  148.3 1.9 collective-permute-start.19
  150.2 5.9 %collective-permute-done.19 = bf16[256,256]{0,1:T(8,128)(2,1)S(1)} collective-permute-done((bf16[256,256]{0,1:T(8,128)(2,1)S(1)}, bf16[256,256]{0,1:T(8,128)(2,1)S(1)}, u32[]{:S(2)}, u32[]{:S(2)}) %collective-permute-start.19) | collective-permute-done | bytes 131104 | tf_op jit(solution)/shard_map/ppermute | solution.py:18
  156.1 1.9 collective-permute-start.20
  158.1 5.9 %collective-permute-done.20 = bf16[256,256]{0,1:T(8,128)(2,1)S(1)} collective-permute-done((bf16[256,256]{0,1:T(8,128)(2,1)S(1)}, bf16[256,256]{0,1:T(8,128)(2,1)S(1)}, u32[]{:S(2)}, u32[]{:S(2)}) %collective-permute-start.20) | collective-permute-done | bytes 131104 | tf_op jit(solution)/shard_map/ppermute | solution.py:18
  163.9 1.9 collective-permute-start.21
  165.8 0.8 fusion.39
  166.7 5.1 %collective-permute-done.21 = bf16[256,256]{0,1:T(8,128)(2,1)S(1)} collective-permute-done((bf16[256,256]{0,1:T(8,128)(2,1)S(1)}, bf16[256,256]{0,1:T(8,128)(2,1)S(1)}, u32[]{:S(2)}, u32[]{:S(2)}) %collective-permute-start.21) | collective-permute-done | bytes 131104 | tf_op jit(solution)/shard_map/ppermute | solution.py:18
  171.7 1.9 collective-permute-start.22
  173.6 2.4 %fusion.91 = (f32[2,256]{1,0:T(2,128)S(1)}, f32[2,256,2304]{1,2,0:T(8,128)S(1)}) fusion(f32[2,256,2304]{1,2,0:T(8,128)S(1)} %fusion.39, pred[256,2304]{0,1:T(8,128)(4,1)S(1)} %fusion.46), kind=kOutput, calls=%fused_computation.150 | output fusion | flops 4720895 | bytes 10029056 | tf_op jit(solution)/shard_map/while/body/eval_jaxpr/sub | solution.py:189
  176.0 3.5 %collective-permute-done.22 = bf16[256,256]{0,1:T(8,128)(2,1)S(1)} collective-permute-done((bf16[256,256]{0,1:T(8,128)(2,1)S(1)}, bf16[256,256]{0,1:T(8,128)(2,1)S(1)}, u32[]{:S(2)}, u32[]{:S(2)}) %collective-permute-start.22) | collective-permute-done | bytes 131104 | tf_op jit(solution)/shard_map/ppermute | solution.py:18
  180.2 26.7 %psum.7 = f32[256]{0:T(256)S(1)} all-reduce(f32[256]{0:T(256)S(1)} %get-tuple-element.200), channel_id=1, replica_groups=mesh['seq'=64,'head'=8] {'head'}, use_global_device_ids=true, to_apply=%region_9.10 | all-reduce | flops 256 | bytes 2048 | tf_op jit(solution)/shard_map/psum | solution.py:199
  207.1 0.8 multiply_convert_fusion
  (149 shorter events, 27.2 us)
Async XLA Ops:
  0.6 165.2 %copy-start = (bf16[256,256]{1,0:T(8,128)(2,1)S(1)}, bf16[256,256]{1,0:T(8,128)(2,1)}, u32[]{:S(2)}) copy-start(bf16[256,256]{1,0:T(8,128)(2,1)} %param.15) | copy-start | bytes 393220
  0.6 6.7 %copy-start.1 = (bf16[256,256]{1,0:T(8,128)(2,1)S(1)}, bf16[256,256]{1,0:T(8,128)(2,1)}, u32[]{:S(2)}) copy-start(bf16[256,256]{1,0:T(8,128)(2,1)} %param.13) | copy-start | bytes 393220
  1.7 33.0 %collective-permute-start.23 = (bf16[256,256]{0,1:T(8,128)(2,1)S(1)}, bf16[256,256]{0,1:T(8,128)(2,1)S(1)}, u32[]{:S(2)}, u32[]{:S(2)}) collective-permute-start(bf16[256,256]{0,1:T(8,128)(2,1)S(1)} %copy.57), channel_id=1, source_target_pairs={{0,8},{8,16},{16,24},{24,32},{32,40},{40,48},{48,56},{56,64},{64,7... | collective-permute-start | bytes 393224 | tf_op jit(solution)/shard_map/ppermute | solution.py:18
  13.1 12.9 %copy-start.2 = (bf16[256,256]{1,0:T(8,128)(2,1)S(1)}, bf16[256,256]{1,0:T(8,128)(2,1)}, u32[]{:S(2)}) copy-start(bf16[256,256]{1,0:T(8,128)(2,1)} %param.11) | copy-start | bytes 393220
  18.8 8.1 %collective-permute-start.5 = (f32[2,128,128]{2,1,0:T(8,128)S(1)}, f32[2,128,128]{2,1,0:T(8,128)S(1)}, u32[]{:S(2)}, u32[]{:S(2)}) collective-permute-start(f32[2,128,128]{2,1,0:T(8,128)S(1)} %get-tuple-element.101), channel_id=1, source_target_pairs={{0,8},{8,16},{16,24},{32,40},{40,48},{48,56},{64,72},{72,80},{80,8... | collective-permute-start | bytes 393224 | tf_op jit(solution)/shard_map/ppermute | solution.py:115
  22.3 9.3 %collective-permute-start = (f32[2,128,128]{2,1,0:T(8,128)S(1)}, f32[2,128,128]{2,1,0:T(8,128)S(1)}, u32[]{:S(2)}, u32[]{:S(2)}) collective-permute-start(f32[2,128,128]{2,1,0:T(8,128)S(1)} %get-tuple-element.100), channel_id=1, source_target_pairs={{0,8},{8,16},{16,24},{32,40},{40,48},{48,56},{64,72},{72,80},{80,8... | collective-permute-start | bytes 393224 | tf_op jit(solution)/shard_map/ppermute | solution.py:115
  27.1 11.4 %collective-permute-start.6 = (f32[2,128,128]{2,1,0:T(8,128)S(1)}, f32[2,128,128]{2,1,0:T(8,128)S(1)}, u32[]{:S(2)}, u32[]{:S(2)}) collective-permute-start(f32[2,128,128]{2,1,0:T(8,128)S(1)} %fusion.56), channel_id=1, source_target_pairs={{0,16},{8,24},{32,48},{40,56},{64,80},{72,88},{96,112},{104,120},{... | collective-permute-start | bytes 393224 | tf_op jit(solution)/shard_map/ppermute | solution.py:115
  31.9 7.6 %collective-permute-start.1 = (f32[2,128,128]{2,1,0:T(8,128)S(1)}, f32[2,128,128]{2,1,0:T(8,128)S(1)}, u32[]{:S(2)}, u32[]{:S(2)}) collective-permute-start(f32[2,128,128]{2,1,0:T(8,128)S(1)} %convolution_select_fusion.6), channel_id=1, source_target_pairs={{0,16},{8,24},{32,48},{40,56},{64,80},{72,88},{96,112},{104,120},{... | collective-permute-start | bytes 393224 | tf_op jit(solution)/shard_map/ppermute | solution.py:115
  34.7 7.8 %collective-permute-start.24 = (bf16[256,256]{0,1:T(8,128)(2,1)S(1)}, bf16[256,256]{0,1:T(8,128)(2,1)S(1)}, u32[]{:S(2)}, u32[]{:S(2)}) collective-permute-start(bf16[256,256]{0,1:T(8,128)(2,1)S(1)} %collective-permute-done.23), channel_id=1, source_target_pairs={{0,8},{8,16},{16,24},{24,32},{32,40},{40,48},{48,56},{56,64},{64,7... | collective-permute-start | bytes 393224 | tf_op jit(solution)/shard_map/ppermute | solution.py:18
  38.9 9.2 %collective-permute-start.7 = (f32[2,128,128]{2,1,0:T(8,128)S(1)}, f32[2,128,128]{2,1,0:T(8,128)S(1)}, u32[]{:S(2)}, u32[]{:S(2)}) collective-permute-start(f32[2,128,128]{2,1,0:T(8,128)S(1)} %fusion.55), channel_id=1, source_target_pairs={{24,56},{56,88},{88,120},{120,152},{152,184},{184,216},{216,248},{... | collective-permute-start | bytes 393224 | tf_op jit(solution)/shard_map/ppermute | solution.py:115
  39.8 9.2 %collective-permute-start.2 = (f32[2,128,128]{2,1,0:T(8,128)S(1)}, f32[2,128,128]{2,1,0:T(8,128)S(1)}, u32[]{:S(2)}, u32[]{:S(2)}) collective-permute-start(f32[2,128,128]{2,1,0:T(8,128)S(1)} %convolution_select_fusion.4), channel_id=1, source_target_pairs={{24,56},{56,88},{88,120},{120,152},{152,184},{184,216},{216,248},{... | collective-permute-start | bytes 393224 | tf_op jit(solution)/shard_map/ppermute | solution.py:115
  42.6 17.9 %collective-permute-start.25 = (bf16[256,256]{0,1:T(8,128)(2,1)S(1)}, bf16[256,256]{0,1:T(8,128)(2,1)S(1)}, u32[]{:S(2)}, u32[]{:S(2)}) collective-permute-start(bf16[256,256]{0,1:T(8,128)(2,1)S(1)} %collective-permute-done.24), channel_id=1, source_target_pairs={{0,8},{8,16},{16,24},{24,32},{32,40},{40,48},{48,56},{56,64},{64,7... | collective-permute-start | bytes 393224 | tf_op jit(solution)/shard_map/ppermute | solution.py:18
  48.3 14.0 %collective-permute-start.8 = (f32[2,128,128]{2,1,0:T(8,128)S(1)}, f32[2,128,128]{2,1,0:T(8,128)S(1)}, u32[]{:S(2)}, u32[]{:S(2)}) collective-permute-start(f32[2,128,128]{2,1,0:T(8,128)S(1)} %fusion.54), channel_id=1, source_target_pairs={{24,88},{56,120},{88,152},{120,184},{152,216},{184,248},{216,280},... | collective-permute-start | bytes 393224 | tf_op jit(solution)/shard_map/ppermute | solution.py:115
  49.3 14.0 %collective-permute-start.3 = (f32[2,128,128]{2,1,0:T(8,128)S(1)}, f32[2,128,128]{2,1,0:T(8,128)S(1)}, u32[]{:S(2)}, u32[]{:S(2)}) collective-permute-start(f32[2,128,128]{2,1,0:T(8,128)S(1)} %convolution_select_fusion.3), channel_id=1, source_target_pairs={{24,88},{56,120},{88,152},{120,184},{152,216},{184,248},{216,280},... | collective-permute-start | bytes 393224 | tf_op jit(solution)/shard_map/ppermute | solution.py:115
  60.4 12.8 %collective-permute-start.26 = (bf16[256,256]{0,1:T(8,128)(2,1)S(1)}, bf16[256,256]{0,1:T(8,128)(2,1)S(1)}, u32[]{:S(2)}, u32[]{:S(2)}) collective-permute-start(bf16[256,256]{0,1:T(8,128)(2,1)S(1)} %collective-permute-done.25), channel_id=1, source_target_pairs={{0,8},{8,16},{16,24},{24,32},{32,40},{40,48},{48,56},{56,64},{64,7... | collective-permute-start | bytes 393224 | tf_op jit(solution)/shard_map/ppermute | solution.py:18
  62.6 12.5 %collective-permute-start.9 = (f32[2,128,128]{2,1,0:T(8,128)S(1)}, f32[2,128,128]{2,1,0:T(8,128)S(1)}, u32[]{:S(2)}, u32[]{:S(2)}) collective-permute-start(f32[2,128,128]{2,1,0:T(8,128)S(1)} %fusion.53), channel_id=1, source_target_pairs={{24,152},{56,184},{88,216},{120,248},{152,280},{184,312},{216,344}... | collective-permute-start | bytes 393224 | tf_op jit(solution)/shard_map/ppermute | solution.py:115
  63.6 25.3 %collective-permute-start.4 = (f32[2,128,128]{2,1,0:T(8,128)S(1)}, f32[2,128,128]{2,1,0:T(8,128)S(1)}, u32[]{:S(2)}, u32[]{:S(2)}) collective-permute-start(f32[2,128,128]{2,1,0:T(8,128)S(1)} %convolution_select_fusion.2), channel_id=1, source_target_pairs={{24,152},{56,184},{88,216},{120,248},{152,280},{184,312},{216,344}... | collective-permute-start | bytes 393224 | tf_op jit(solution)/shard_map/ppermute | solution.py:115
  73.2 13.8 %collective-permute-start.27 = (bf16[256,256]{0,1:T(8,128)(2,1)S(1)}, bf16[256,256]{0,1:T(8,128)(2,1)S(1)}, u32[]{:S(2)}, u32[]{:S(2)}) collective-permute-start(bf16[256,256]{0,1:T(8,128)(2,1)S(1)} %collective-permute-done.26), channel_id=1, source_target_pairs={{0,8},{8,16},{16,24},{24,32},{32,40},{40,48},{48,56},{56,64},{64,7... | collective-permute-start | bytes 393224 | tf_op jit(solution)/shard_map/ppermute | solution.py:18
  75.4 13.8 %collective-permute-start.10 = (f32[2,128,128]{2,1,0:T(8,128)S(1)}, f32[2,128,128]{2,1,0:T(8,128)S(1)}, u32[]{:S(2)}, u32[]{:S(2)}) collective-permute-start(f32[2,128,128]{2,1,0:T(8,128)S(1)} %fusion.52), channel_id=1, source_target_pairs={{24,280},{56,312},{88,344},{120,376},{152,408},{184,440},{216,472}... | collective-permute-start | bytes 393224 | tf_op jit(solution)/shard_map/ppermute | solution.py:115
  87.0 8.1 %collective-permute-start.28 = (bf16[256,256]{0,1:T(8,128)(2,1)S(1)}, bf16[256,256]{0,1:T(8,128)(2,1)S(1)}, u32[]{:S(2)}, u32[]{:S(2)}) collective-permute-start(bf16[256,256]{0,1:T(8,128)(2,1)S(1)} %collective-permute-done.27), channel_id=1, source_target_pairs={{0,8},{8,16},{16,24},{24,32},{32,40},{40,48},{48,56},{56,64},{64,7... | collective-permute-start | bytes 393224 | tf_op jit(solution)/shard_map/ppermute | solution.py:18
  89.5 7.7 %collective-permute-start.14 = (f32[2,128,128]{2,1,0:T(8,128)S(1)}, f32[2,128,128]{2,1,0:T(8,128)S(1)}, u32[]{:S(2)}, u32[]{:S(2)}) collective-permute-start(f32[2,128,128]{2,1,0:T(8,128)S(1)} %fusion.51), channel_id=1, source_target_pairs={{24,56},{56,88},{88,120},{120,152},{152,184},{184,216},{216,248},{... | collective-permute-start | bytes 393224 | tf_op jit(solution)/shard_map/ppermute | solution.py:115
  90.2 7.0 %collective-permute-start.13 = (f32[2,128,128]{2,1,0:T(8,128)S(1)}, f32[2,128,128]{2,1,0:T(8,128)S(1)}, u32[]{:S(2)}, u32[]{:S(2)}) collective-permute-start(f32[2,128,128]{2,1,0:T(8,128)S(1)} %fusion.51), channel_id=1, source_target_pairs={{24,48},{56,80},{88,112},{120,144},{152,176},{184,208},{216,240},{... | collective-permute-start | bytes 393224 | tf_op jit(solution)/shard_map/ppermute | solution.py:115
  90.9 6.4 %collective-permute-start.12 = (f32[2,128,128]{2,1,0:T(8,128)S(1)}, f32[2,128,128]{2,1,0:T(8,128)S(1)}, u32[]{:S(2)}, u32[]{:S(2)}) collective-permute-start(f32[2,128,128]{2,1,0:T(8,128)S(1)} %fusion.51), channel_id=1, source_target_pairs={{24,40},{56,72},{88,104},{120,136},{152,168},{184,200},{216,232},{... | collective-permute-start | bytes 393224 | tf_op jit(solution)/shard_map/ppermute | solution.py:115
  91.6 16.7 %collective-permute-start.11 = (f32[2,128,128]{2,1,0:T(8,128)S(1)}, f32[2,128,128]{2,1,0:T(8,128)S(1)}, u32[]{:S(2)}, u32[]{:S(2)}) collective-permute-start(f32[2,128,128]{2,1,0:T(8,128)S(1)} %fusion.51), channel_id=1, source_target_pairs={{24,32},{56,64},{88,96},{120,128},{152,160},{184,192},{216,224},{2... | collective-permute-start | bytes 393224 | tf_op jit(solution)/shard_map/ppermute | solution.py:115
  95.1 20.0 %collective-permute-start.29 = (bf16[256,256]{0,1:T(8,128)(2,1)S(1)}, bf16[256,256]{0,1:T(8,128)(2,1)S(1)}, u32[]{:S(2)}, u32[]{:S(2)}) collective-permute-start(bf16[256,256]{0,1:T(8,128)(2,1)S(1)} %collective-permute-done.28), channel_id=1, source_target_pairs={{0,8},{8,16},{16,24},{24,32},{32,40},{40,48},{48,56},{56,64},{64,7... | collective-permute-start | bytes 393224 | tf_op jit(solution)/shard_map/ppermute | solution.py:18
  113.2 7.8 %collective-permute-start.15 = (bf16[256,256]{0,1:T(8,128)(2,1)S(1)}, bf16[256,256]{0,1:T(8,128)(2,1)S(1)}, u32[]{:S(2)}, u32[]{:S(2)}) collective-permute-start(bf16[256,256]{0,1:T(8,128)(2,1)S(1)} %bitcast.200), channel_id=1, source_target_pairs={{0,8},{8,16},{16,24},{24,32},{32,40},{40,48},{48,56},{56,64},{64,7... | collective-permute-start | bytes 393224 | tf_op jit(solution)/shard_map/ppermute | solution.py:18
  115.2 9.8 %collective-permute-start.30 = (bf16[256,256]{0,1:T(8,128)(2,1)S(1)}, bf16[256,256]{0,1:T(8,128)(2,1)S(1)}, u32[]{:S(2)}, u32[]{:S(2)}) collective-permute-start(bf16[256,256]{0,1:T(8,128)(2,1)S(1)} %collective-permute-done.29), channel_id=1, source_target_pairs={{0,8},{8,16},{16,24},{24,32},{32,40},{40,48},{48,56},{56,64},{64,7... | collective-permute-start | bytes 393224 | tf_op jit(solution)/shard_map/ppermute | solution.py:18
  121.0 9.4 %collective-permute-start.16 = (bf16[256,256]{0,1:T(8,128)(2,1)S(1)}, bf16[256,256]{0,1:T(8,128)(2,1)S(1)}, u32[]{:S(2)}, u32[]{:S(2)}) collective-permute-start(bf16[256,256]{0,1:T(8,128)(2,1)S(1)} %collective-permute-done.15), channel_id=1, source_target_pairs={{0,8},{8,16},{16,24},{24,32},{32,40},{40,48},{48,56},{56,64},{64,7... | collective-permute-start | bytes 393224 | tf_op jit(solution)/shard_map/ppermute | solution.py:18
  130.4 9.3 %collective-permute-start.17 = (bf16[256,256]{0,1:T(8,128)(2,1)S(1)}, bf16[256,256]{0,1:T(8,128)(2,1)S(1)}, u32[]{:S(2)}, u32[]{:S(2)}) collective-permute-start(bf16[256,256]{0,1:T(8,128)(2,1)S(1)} %collective-permute-done.16), channel_id=1, source_target_pairs={{0,8},{8,16},{16,24},{24,32},{32,40},{40,48},{48,56},{56,64},{64,7... | collective-permute-start | bytes 393224 | tf_op jit(solution)/shard_map/ppermute | solution.py:18
  139.8 8.5 %collective-permute-start.18 = (bf16[256,256]{0,1:T(8,128)(2,1)S(1)}, bf16[256,256]{0,1:T(8,128)(2,1)S(1)}, u32[]{:S(2)}, u32[]{:S(2)}) collective-permute-start(bf16[256,256]{0,1:T(8,128)(2,1)S(1)} %collective-permute-done.17), channel_id=1, source_target_pairs={{0,8},{8,16},{16,24},{24,32},{32,40},{40,48},{48,56},{56,64},{64,7... | collective-permute-start | bytes 393224 | tf_op jit(solution)/shard_map/ppermute | solution.py:18
  148.3 7.8 %collective-permute-start.19 = (bf16[256,256]{0,1:T(8,128)(2,1)S(1)}, bf16[256,256]{0,1:T(8,128)(2,1)S(1)}, u32[]{:S(2)}, u32[]{:S(2)}) collective-permute-start(bf16[256,256]{0,1:T(8,128)(2,1)S(1)} %collective-permute-done.18), channel_id=1, source_target_pairs={{0,8},{8,16},{16,24},{24,32},{32,40},{40,48},{48,56},{56,64},{64,7... | collective-permute-start | bytes 393224 | tf_op jit(solution)/shard_map/ppermute | solution.py:18
  156.1 7.8 %collective-permute-start.20 = (bf16[256,256]{0,1:T(8,128)(2,1)S(1)}, bf16[256,256]{0,1:T(8,128)(2,1)S(1)}, u32[]{:S(2)}, u32[]{:S(2)}) collective-permute-start(bf16[256,256]{0,1:T(8,128)(2,1)S(1)} %collective-permute-done.19), channel_id=1, source_target_pairs={{0,8},{8,16},{16,24},{24,32},{32,40},{40,48},{48,56},{56,64},{64,7... | collective-permute-start | bytes 393224 | tf_op jit(solution)/shard_map/ppermute | solution.py:18
  163.9 7.8 %collective-permute-start.21 = (bf16[256,256]{0,1:T(8,128)(2,1)S(1)}, bf16[256,256]{0,1:T(8,128)(2,1)S(1)}, u32[]{:S(2)}, u32[]{:S(2)}) collective-permute-start(bf16[256,256]{0,1:T(8,128)(2,1)S(1)} %collective-permute-done.20), channel_id=1, source_target_pairs={{0,8},{8,16},{16,24},{24,32},{32,40},{40,48},{48,56},{56,64},{64,7... | collective-permute-start | bytes 393224 | tf_op jit(solution)/shard_map/ppermute | solution.py:18
  171.7 7.8 %collective-permute-start.22 = (bf16[256,256]{0,1:T(8,128)(2,1)S(1)}, bf16[256,256]{0,1:T(8,128)(2,1)S(1)}, u32[]{:S(2)}, u32[]{:S(2)}) collective-permute-start(bf16[256,256]{0,1:T(8,128)(2,1)S(1)} %collective-permute-done.21), channel_id=1, source_target_pairs={{0,8},{8,16},{16,24},{24,32},{32,40},{40,48},{48,56},{56,64},{64,7... | collective-permute-start | bytes 393224 | tf_op jit(solution)/shard_map/ppermute | solution.py:18
  179.7 27.4 %copy-start.3 = (f32[256]{0:T(256)S(1)}, f32[256]{0:T(256)}, u32[]{:S(2)}) copy-start(f32[256]{0:T(256)} %param.17) | copy-start | bytes 3076

commit v6 on v5

--- a/solution.py
+++ b/solution.py
@@ -159,13 +159,20 @@
     )
     shard_reach = WINDOW // tok_rows
 
-    def window_rows(own):
-        pieces = [own]
-        for _ in range(shard_reach):
-            pieces = [shifted(pieces[0], "seq", 1)] + pieces
-        return jnp.concatenate(pieces, axis=0)
-
-    rows_all = (window_rows(k_attn), window_rows(delta_out))
+    def window_rows(own, lanes):
+        lane_length = -(-shard_reach // lanes)
+        pieces = []
+        for lane in range(lanes):
+            first = lane * lane_length + 1
+            last = min(shard_reach, (lane + 1) * lane_length)
+            piece = shifted(own, "seq", first)
+            pieces.append(piece)
+            for _ in range(first, last):
+                piece = shifted(piece, "seq", 1)
+                pieces.append(piece)
+        return jnp.concatenate(pieces[::-1] + [own], axis=0)
+
+    rows_all = (window_rows(k_attn, 1), window_rows(delta_out, 2))
     block_rows = min(512, tok_rows)
     first_row = lax.axis_index("seq") * tok_rows
     score_scale = 1.0 / math.sqrt(head_size)

time: 210 us -> 190 us (0.905)
  waiting for transfers between devices: 89.1 us -> 69.4 us
  blocking collectives: 26.7 us -> 22.8 us
  starting transfers between devices: 59.4 us -> 63 us
    ppermute x16, waiting for transfers between devices: 78 us -> 58.4 us  [shifted(): return lax.ppermute(value, axis, pairs)]
    psum x1, blocking collectives: 26.7 us -> 22.8 us  [on_device(): total_sq = lax.psum(squares, 'head')]
    ppermute x16, starting transfers between devices: 37.3 us -> 40.9 us  [shifted(): return lax.ppermute(value, axis, pairs)]
  transfers between devices with their start and end apart: 31 -> 31, of which waited for: 14 -> 12; matrix products, arithmetic and copies ran while one was open for 13% -> 15% of each run, Pallas kernels for 0% -> 0%
where the time goes in v6:
time: 190 us; the launch traced here: 188 us
  waiting for transfers between devices  69.4 us (37%)
  starting transfers between devices  63 us (33%)
  blocking collectives  22.8 us (12%)
  matrix products  21.2 us (11%)
  local copies, waits for them, and re-layouts  4.72 us (2%)
  other arithmetic  4.65 us (2%)
    ppermute x16, waiting for transfers between devices, shifted(): return lax.ppermute(value, axis, pairs)  58.4 us
    ppermute x16, starting transfers between devices, shifted(): return lax.ppermute(value, axis, pairs)  40.9 us
    psum x1, blocking collectives, on_device(): total_sq = lax.psum(squares, 'head')  22.8 us
    ppermute x15, starting transfers between devices, moved(): return lax.ppermute(value, 'seq', pairs)  22.1 us
    ppermute x15, waiting for transfers between devices, moved(): return lax.ppermute(value, 'seq', pairs)  11.1 us
    dot_general x16, matrix products, batched_dot(): return jnp.einsum('hij,hjk->hik', left, right, precision=highest)  4.34 us
  transfers between devices with their start and end apart: 31, of which 12 were waited for; matrix products, arithmetic and copies ran while one was open for 15% of the time, Pallas kernels for 0%

profile of v6, /device:TPU:25, one launch (start us, length us, event | category | flops | bytes accessed | tf_op | source)
XLA Modules:
  0.0 187.9 jit_solution(5672970409313380071)
XLA Ops:
  0.7 1.1 copy.57
  1.7 3.5 %collective-permute-start.23 = (bf16[256,256]{0,1:T(8,128)(2,1)S(1)}, bf16[256,256]{0,1:T(8,128)(2,1)S(1)}, u32[]{:S(2)}, u32[]{:S(2)}) collective-permute-start(bf16[256,256]{0,1:T(8,128)(2,1)S(1)} %copy.57), channel_id=1, source_target_pairs={{0,8},{8,16},{16,24},{24,32},{32,40},{40,48},{48,56},{56,64},{64,7... | collective-permute-start | bytes 393224 | tf_op jit(solution)/shard_map/ppermute | solution.py:18
  5.3 0.8 mul.79
  6.1 1.0 copy.41
  13.1 5.7 %while.30 = (s32[]{:T(128)}, f32[2,128,128]{2,1,0:T(8,128)S(1)}, f32[2,128,128]{2,1,0:T(8,128)S(1)}, f32[4,2,64,128]{3,2,1,0:T(8,128)S(1)}, f32[4,2,64,128]{3,2,...) while((s32[]{:T(128)}, f32[2,128,128]{2,1,0:T(8,128)S(1)}, ...), condition=%wide.region_2.3_spmd.clone, body=%wide.region_1.0_spmd.clone.sunk | while | flops 151126016 | bytes 1837159 | solution.py:74
  18.8 3.6 %collective-permute-start.5 = (f32[2,128,128]{2,1,0:T(8,128)S(1)}, f32[2,128,128]{2,1,0:T(8,128)S(1)}, u32[]{:S(2)}, u32[]{:S(2)}) collective-permute-start(f32[2,128,128]{2,1,0:T(8,128)S(1)} %get-tuple-element.101), channel_id=1, source_target_pairs={{0,8},{8,16},{16,24},{32,40},{40,48},{48,56},{64,72},{72,80},{80,8... | collective-permute-start | bytes 393224 | tf_op jit(solution)/shard_map/ppermute | solution.py:115
  22.3 3.5 %collective-permute-start = (f32[2,128,128]{2,1,0:T(8,128)S(1)}, f32[2,128,128]{2,1,0:T(8,128)S(1)}, u32[]{:S(2)}, u32[]{:S(2)}) collective-permute-start(f32[2,128,128]{2,1,0:T(8,128)S(1)} %get-tuple-element.100), channel_id=1, source_target_pairs={{0,8},{8,16},{16,24},{32,40},{40,48},{48,56},{64,72},{72,80},{80,8... | collective-permute-start | bytes 393224 | tf_op jit(solution)/shard_map/ppermute | solution.py:115
  27.2 4.5 %collective-permute-start.6 = (f32[2,128,128]{2,1,0:T(8,128)S(1)}, f32[2,128,128]{2,1,0:T(8,128)S(1)}, u32[]{:S(2)}, u32[]{:S(2)}) collective-permute-start(f32[2,128,128]{2,1,0:T(8,128)S(1)} %fusion.56), channel_id=1, source_target_pairs={{0,16},{8,24},{32,48},{40,56},{64,80},{72,88},{96,112},{104,120},{... | collective-permute-start | bytes 393224 | tf_op jit(solution)/shard_map/ppermute | solution.py:115
  31.9 2.5 %collective-permute-start.1 = (f32[2,128,128]{2,1,0:T(8,128)S(1)}, f32[2,128,128]{2,1,0:T(8,128)S(1)}, u32[]{:S(2)}, u32[]{:S(2)}) collective-permute-start(f32[2,128,128]{2,1,0:T(8,128)S(1)} %convolution_select_fusion.6), channel_id=1, source_target_pairs={{0,16},{8,24},{32,48},{40,56},{64,80},{72,88},{96,112},{104,120},{... | collective-permute-start | bytes 393224 | tf_op jit(solution)/shard_map/ppermute | solution.py:115
  34.7 3.5 %collective-permute-start.24 = (bf16[256,256]{0,1:T(8,128)(2,1)S(1)}, bf16[256,256]{0,1:T(8,128)(2,1)S(1)}, u32[]{:S(2)}, u32[]{:S(2)}) collective-permute-start(bf16[256,256]{0,1:T(8,128)(2,1)S(1)} %collective-permute-done.23), channel_id=1, source_target_pairs={{0,8},{8,16},{16,24},{24,32},{32,40},{40,48},{48,56},{56,64},{64,7... | collective-permute-start | bytes 393224 | tf_op jit(solution)/shard_map/ppermute | solution.py:18
  38.9 0.7 collective-permute-start.7
  40.5 2.1 %collective-permute-done.24 = bf16[256,256]{0,1:T(8,128)(2,1)S(1)} collective-permute-done((bf16[256,256]{0,1:T(8,128)(2,1)S(1)}, bf16[256,256]{0,1:T(8,128)(2,1)S(1)}, u32[]{:S(2)}, u32[]{:S(2)}) %collective-permute-start.24) | collective-permute-done | bytes 131104 | tf_op jit(solution)/shard_map/ppermute | solution.py:18
  42.6 5.2 %collective-permute-start.25 = (bf16[256,256]{0,1:T(8,128)(2,1)S(1)}, bf16[256,256]{0,1:T(8,128)(2,1)S(1)}, u32[]{:S(2)}, u32[]{:S(2)}) collective-permute-start(bf16[256,256]{0,1:T(8,128)(2,1)S(1)} %collective-permute-done.24), channel_id=1, source_target_pairs={{0,8},{8,16},{16,24},{24,32},{32,40},{40,48},{48,56},{56,64},{64,7... | collective-permute-start | bytes 393224 | tf_op jit(solution)/shard_map/ppermute | solution.py:18
  48.3 0.7 collective-permute-start.8
  49.3 0.7 collective-permute-start.3
  50.0 10.5 %collective-permute-done.25 = bf16[256,256]{0,1:T(8,128)(2,1)S(1)} collective-permute-done((bf16[256,256]{0,1:T(8,128)(2,1)S(1)}, bf16[256,256]{0,1:T(8,128)(2,1)S(1)}, u32[]{:S(2)}, u32[]{:S(2)}) %collective-permute-start.25) | collective-permute-done | bytes 131104 | tf_op jit(solution)/shard_map/ppermute | solution.py:18
  60.4 1.9 %collective-permute-start.26 = (bf16[256,256]{0,1:T(8,128)(2,1)S(1)}, bf16[256,256]{0,1:T(8,128)(2,1)S(1)}, u32[]{:S(2)}, u32[]{:S(2)}) collective-permute-start(bf16[256,256]{0,1:T(8,128)(2,1)S(1)} %collective-permute-done.25), channel_id=1, source_target_pairs={{0,8},{8,16},{16,24},{24,32},{32,40},{40,48},{48,56},{56,64},{64,7... | collective-permute-start | bytes 393224 | tf_op jit(solution)/shard_map/ppermute | solution.py:18
  62.6 0.7 collective-permute-start.9
  64.3 9.0 %collective-permute-done.26 = bf16[256,256]{0,1:T(8,128)(2,1)S(1)} collective-permute-done((bf16[256,256]{0,1:T(8,128)(2,1)S(1)}, bf16[256,256]{0,1:T(8,128)(2,1)S(1)}, u32[]{:S(2)}, u32[]{:S(2)}) %collective-permute-start.26) | collective-permute-done | bytes 131104 | tf_op jit(solution)/shard_map/ppermute | solution.py:18
  73.2 1.9 %collective-permute-start.27 = (bf16[256,256]{0,1:T(8,128)(2,1)S(1)}, bf16[256,256]{0,1:T(8,128)(2,1)S(1)}, u32[]{:S(2)}, u32[]{:S(2)}) collective-permute-start(bf16[256,256]{0,1:T(8,128)(2,1)S(1)} %collective-permute-done.26), channel_id=1, source_target_pairs={{0,8},{8,16},{16,24},{24,32},{32,40},{40,48},{48,56},{56,64},{64,7... | collective-permute-start | bytes 393224 | tf_op jit(solution)/shard_map/ppermute | solution.py:18
  76.1 10.9 %collective-permute-done.27 = bf16[256,256]{0,1:T(8,128)(2,1)S(1)} collective-permute-done((bf16[256,256]{0,1:T(8,128)(2,1)S(1)}, bf16[256,256]{0,1:T(8,128)(2,1)S(1)}, u32[]{:S(2)}, u32[]{:S(2)}) %collective-permute-start.27) | collective-permute-done | bytes 131104 | tf_op jit(solution)/shard_map/ppermute | solution.py:18
  87.0 1.9 %collective-permute-start.28 = (bf16[256,256]{0,1:T(8,128)(2,1)S(1)}, bf16[256,256]{0,1:T(8,128)(2,1)S(1)}, u32[]{:S(2)}, u32[]{:S(2)}) collective-permute-start(bf16[256,256]{0,1:T(8,128)(2,1)S(1)} %collective-permute-done.27), channel_id=1, source_target_pairs={{0,8},{8,16},{16,24},{24,32},{32,40},{40,48},{48,56},{56,64},{64,7... | collective-permute-start | bytes 393224 | tf_op jit(solution)/shard_map/ppermute | solution.py:18
  91.6 1.3 collective-permute-start.11
  93.1 2.0 %collective-permute-done.28 = bf16[256,256]{0,1:T(8,128)(2,1)S(1)} collective-permute-done((bf16[256,256]{0,1:T(8,128)(2,1)S(1)}, bf16[256,256]{0,1:T(8,128)(2,1)S(1)}, u32[]{:S(2)}, u32[]{:S(2)}) %collective-permute-start.28) | collective-permute-done | bytes 131104 | tf_op jit(solution)/shard_map/ppermute | solution.py:18
  95.1 2.1 %collective-permute-start.29 = (bf16[256,256]{0,1:T(8,128)(2,1)S(1)}, bf16[256,256]{0,1:T(8,128)(2,1)S(1)}, u32[]{:S(2)}, u32[]{:S(2)}) collective-permute-start(bf16[256,256]{0,1:T(8,128)(2,1)S(1)} %collective-permute-done.28), channel_id=1, source_target_pairs={{0,8},{8,16},{16,24},{24,32},{32,40},{40,48},{48,56},{56,64},{64,7... | collective-permute-start | bytes 393224 | tf_op jit(solution)/shard_map/ppermute | solution.py:18
  97.3 11.0 %collective-permute-done.11 = f32[2,128,128]{2,1,0:T(8,128)S(1)} collective-permute-done((f32[2,128,128]{2,1,0:T(8,128)S(1)}, f32[2,128,128]{2,1,0:T(8,128)S(1)}, u32[]{:S(2)}, u32[]{:S(2)}) %collective-permute-start.11) | collective-permute-done | bytes 131104 | tf_op jit(solution)/shard_map/ppermute | solution.py:115
  108.6 4.5 %while.29 = (s32[]{:T(128)}, f32[2,128,128]{2,1,0:T(8,128)S(1)}, bf16[4,2,64,128]{3,2,0,1:T(8,128)(2,1)S(1)}, f32[4,2,64,128]{3,2,1,0:T(8,128)S(1)}, f32[4,2,64,...) while((s32[]{:T(128)}, f32[2,128,128]{2,1,0:T(8,128)S(1)}, ...), condition=%wide.region_5.6_spmd, body=%wide.region_4.5_spmd.sunk | while | flops 88145920 | bytes 1247341 | solution.py:88
  113.2 1.9 %collective-permute-start.19 = (bf16[256,256]{0,1:T(8,128)(2,1)S(1)}, bf16[256,256]{0,1:T(8,128)(2,1)S(1)}, u32[]{:S(2)}, u32[]{:S(2)}) collective-permute-start(bf16[256,256]{0,1:T(8,128)(2,1)S(1)} %bitcast.200), channel_id=1, source_target_pairs={{0,8},{8,16},{16,24},{24,32},{32,40},{40,48},{48,56},{56,64},{64,7... | collective-permute-start | bytes 393224 | tf_op jit(solution)/shard_map/ppermute | solution.py:18
  115.1 1.9 %collective-permute-start.15 = (bf16[256,256]{0,1:T(8,128)(2,1)S(1)}, bf16[256,256]{0,1:T(8,128)(2,1)S(1)}, u32[]{:S(2)}, u32[]{:S(2)}) collective-permute-start(bf16[256,256]{0,1:T(8,128)(2,1)S(1)} %bitcast.201), channel_id=1, source_target_pairs={{0,40},{8,48},{16,56},{24,64},{32,72},{40,80},{48,88},{56,96},{64,... | collective-permute-start | bytes 393224 | tf_op jit(solution)/shard_map/ppermute | solution.py:18
  117.1 2.4 %collective-permute-start.30 = (bf16[256,256]{0,1:T(8,128)(2,1)S(1)}, bf16[256,256]{0,1:T(8,128)(2,1)S(1)}, u32[]{:S(2)}, u32[]{:S(2)}) collective-permute-start(bf16[256,256]{0,1:T(8,128)(2,1)S(1)} %collective-permute-done.29), channel_id=1, source_target_pairs={{0,8},{8,16},{16,24},{24,32},{32,40},{40,48},{48,56},{56,64},{64,7... | collective-permute-start | bytes 393224 | tf_op jit(solution)/shard_map/ppermute | solution.py:18
  119.5 1.3 fusion.46
  120.8 0.8 copy.63
  121.5 5.0 %collective-permute-start.20 = (bf16[256,256]{0,1:T(8,128)(2,1)S(1)}, bf16[256,256]{0,1:T(8,128)(2,1)S(1)}, u32[]{:S(2)}, u32[]{:S(2)}) collective-permute-start(bf16[256,256]{0,1:T(8,128)(2,1)S(1)} %collective-permute-done.19), channel_id=1, source_target_pairs={{0,8},{8,16},{16,24},{24,32},{32,40},{40,48},{48,56},{56,64},{64,7... | collective-permute-start | bytes 393224 | tf_op jit(solution)/shard_map/ppermute | solution.py:18
  126.5 3.9 %collective-permute-done.15 = bf16[256,256]{0,1:T(8,128)(2,1)S(1)} collective-permute-done((bf16[256,256]{0,1:T(8,128)(2,1)S(1)}, bf16[256,256]{0,1:T(8,128)(2,1)S(1)}, u32[]{:S(2)}, u32[]{:S(2)}) %collective-permute-start.15) | collective-permute-done | bytes 131104 | tf_op jit(solution)/shard_map/ppermute | solution.py:18
  130.4 1.9 %collective-permute-start.16 = (bf16[256,256]{0,1:T(8,128)(2,1)S(1)}, bf16[256,256]{0,1:T(8,128)(2,1)S(1)}, u32[]{:S(2)}, u32[]{:S(2)}) collective-permute-start(bf16[256,256]{0,1:T(8,128)(2,1)S(1)} %collective-permute-done.15), channel_id=1, source_target_pairs={{0,8},{8,16},{16,24},{24,32},{32,40},{40,48},{48,56},{56,64},{64,7... | collective-permute-start | bytes 393224 | tf_op jit(solution)/shard_map/ppermute | solution.py:18
  132.3 1.1 collective-permute-done.30
  133.6 9.8 %collective-permute-done.16 = bf16[256,256]{0,1:T(8,128)(2,1)S(1)} collective-permute-done((bf16[256,256]{0,1:T(8,128)(2,1)S(1)}, bf16[256,256]{0,1:T(8,128)(2,1)S(1)}, u32[]{:S(2)}, u32[]{:S(2)}) %collective-permute-start.16) | collective-permute-done | bytes 131104 | tf_op jit(solution)/shard_map/ppermute | solution.py:18
  143.4 1.9 %collective-permute-start.17 = (bf16[256,256]{0,1:T(8,128)(2,1)S(1)}, bf16[256,256]{0,1:T(8,128)(2,1)S(1)}, u32[]{:S(2)}, u32[]{:S(2)}) collective-permute-start(bf16[256,256]{0,1:T(8,128)(2,1)S(1)} %collective-permute-done.16), channel_id=1, source_target_pairs={{0,8},{8,16},{16,24},{24,32},{32,40},{40,48},{48,56},{56,64},{64,7... | collective-permute-start | bytes 393224 | tf_op jit(solution)/shard_map/ppermute | solution.py:18
  145.3 0.8 fusion.39
  146.1 1.9 %collective-permute-start.21 = (bf16[256,256]{0,1:T(8,128)(2,1)S(1)}, bf16[256,256]{0,1:T(8,128)(2,1)S(1)}, u32[]{:S(2)}, u32[]{:S(2)}) collective-permute-start(bf16[256,256]{0,1:T(8,128)(2,1)S(1)} %collective-permute-done.20), channel_id=1, source_target_pairs={{0,8},{8,16},{16,24},{24,32},{32,40},{40,48},{48,56},{56,64},{64,7... | collective-permute-start | bytes 393224 | tf_op jit(solution)/shard_map/ppermute | solution.py:18
  148.0 3.4 %collective-permute-done.17 = bf16[256,256]{0,1:T(8,128)(2,1)S(1)} collective-permute-done((bf16[256,256]{0,1:T(8,128)(2,1)S(1)}, bf16[256,256]{0,1:T(8,128)(2,1)S(1)}, u32[]{:S(2)}, u32[]{:S(2)}) %collective-permute-start.17) | collective-permute-done | bytes 131104 | tf_op jit(solution)/shard_map/ppermute | solution.py:18
  151.5 1.9 %collective-permute-start.18 = (bf16[256,256]{0,1:T(8,128)(2,1)S(1)}, bf16[256,256]{0,1:T(8,128)(2,1)S(1)}, u32[]{:S(2)}, u32[]{:S(2)}) collective-permute-start(bf16[256,256]{0,1:T(8,128)(2,1)S(1)} %collective-permute-done.17), channel_id=1, source_target_pairs={{0,8},{8,16},{16,24},{24,32},{32,40},{40,48},{48,56},{56,64},{64,7... | collective-permute-start | bytes 393224 | tf_op jit(solution)/shard_map/ppermute | solution.py:18
  153.4 2.4 %fusion.91 = (f32[2,256]{1,0:T(2,128)S(1)}, f32[2,256,2304]{1,2,0:T(8,128)S(1)}) fusion(f32[2,256,2304]{1,2,0:T(8,128)S(1)} %fusion.39, pred[256,2304]{0,1:T(8,128)(4,1)S(1)} %fusion.46), kind=kOutput, calls=%fused_computation.150 | output fusion | flops 4720895 | bytes 10029056 | tf_op jit(solution)/shard_map/while/body/eval_jaxpr/sub | solution.py:196
  155.8 1.9 %collective-permute-start.22 = (bf16[256,256]{0,1:T(8,128)(2,1)S(1)}, bf16[256,256]{0,1:T(8,128)(2,1)S(1)}, u32[]{:S(2)}, u32[]{:S(2)}) collective-permute-start(bf16[256,256]{0,1:T(8,128)(2,1)S(1)} %collective-permute-done.21), channel_id=1, source_target_pairs={{0,8},{8,16},{16,24},{24,32},{32,40},{40,48},{48,56},{56,64},{64,7... | collective-permute-start | bytes 393224 | tf_op jit(solution)/shard_map/ppermute | solution.py:18
  157.7 3.3 %collective-permute-done.18 = bf16[256,256]{0,1:T(8,128)(2,1)S(1)} collective-permute-done((bf16[256,256]{0,1:T(8,128)(2,1)S(1)}, bf16[256,256]{0,1:T(8,128)(2,1)S(1)}, u32[]{:S(2)}, u32[]{:S(2)}) %collective-permute-start.18) | collective-permute-done | bytes 131104 | tf_op jit(solution)/shard_map/ppermute | solution.py:18
  161.0 2.6 %collective-permute-done.22 = bf16[256,256]{0,1:T(8,128)(2,1)S(1)} collective-permute-done((bf16[256,256]{0,1:T(8,128)(2,1)S(1)}, bf16[256,256]{0,1:T(8,128)(2,1)S(1)}, u32[]{:S(2)}, u32[]{:S(2)}) %collective-permute-start.22) | collective-permute-done | bytes 131104 | tf_op jit(solution)/shard_map/ppermute | solution.py:18
  164.2 22.8 %psum.7 = f32[256]{0:T(256)S(1)} all-reduce(f32[256]{0:T(256)S(1)} %get-tuple-element.200), channel_id=1, replica_groups=mesh['seq'=64,'head'=8] {'head'}, use_global_device_ids=true, to_apply=%region_9.10 | all-reduce | flops 256 | bytes 2048 | tf_op jit(solution)/shard_map/psum | solution.py:206
  187.2 0.8 multiply_convert_fusion
  (149 shorter events, 25.9 us)
Async XLA Ops:
  0.6 144.6 %copy-start = (bf16[256,256]{1,0:T(8,128)(2,1)S(1)}, bf16[256,256]{1,0:T(8,128)(2,1)}, u32[]{:S(2)}) copy-start(bf16[256,256]{1,0:T(8,128)(2,1)} %param.15) | copy-start | bytes 393220
  0.6 6.7 %copy-start.1 = (bf16[256,256]{1,0:T(8,128)(2,1)S(1)}, bf16[256,256]{1,0:T(8,128)(2,1)}, u32[]{:S(2)}) copy-start(bf16[256,256]{1,0:T(8,128)(2,1)} %param.13) | copy-start | bytes 393220
  1.7 33.0 %collective-permute-start.23 = (bf16[256,256]{0,1:T(8,128)(2,1)S(1)}, bf16[256,256]{0,1:T(8,128)(2,1)S(1)}, u32[]{:S(2)}, u32[]{:S(2)}) collective-permute-start(bf16[256,256]{0,1:T(8,128)(2,1)S(1)} %copy.57), channel_id=1, source_target_pairs={{0,8},{8,16},{16,24},{24,32},{32,40},{40,48},{48,56},{56,64},{64,7... | collective-permute-start | bytes 393224 | tf_op jit(solution)/shard_map/ppermute | solution.py:18
  13.1 12.8 %copy-start.2 = (bf16[256,256]{1,0:T(8,128)(2,1)S(1)}, bf16[256,256]{1,0:T(8,128)(2,1)}, u32[]{:S(2)}) copy-start(bf16[256,256]{1,0:T(8,128)(2,1)} %param.11) | copy-start | bytes 393220
  18.8 8.1 %collective-permute-start.5 = (f32[2,128,128]{2,1,0:T(8,128)S(1)}, f32[2,128,128]{2,1,0:T(8,128)S(1)}, u32[]{:S(2)}, u32[]{:S(2)}) collective-permute-start(f32[2,128,128]{2,1,0:T(8,128)S(1)} %get-tuple-element.101), channel_id=1, source_target_pairs={{0,8},{8,16},{16,24},{32,40},{40,48},{48,56},{64,72},{72,80},{80,8... | collective-permute-start | bytes 393224 | tf_op jit(solution)/shard_map/ppermute | solution.py:115
  22.3 9.3 %collective-permute-start = (f32[2,128,128]{2,1,0:T(8,128)S(1)}, f32[2,128,128]{2,1,0:T(8,128)S(1)}, u32[]{:S(2)}, u32[]{:S(2)}) collective-permute-start(f32[2,128,128]{2,1,0:T(8,128)S(1)} %get-tuple-element.100), channel_id=1, source_target_pairs={{0,8},{8,16},{16,24},{32,40},{40,48},{48,56},{64,72},{72,80},{80,8... | collective-permute-start | bytes 393224 | tf_op jit(solution)/shard_map/ppermute | solution.py:115
  27.2 11.4 %collective-permute-start.6 = (f32[2,128,128]{2,1,0:T(8,128)S(1)}, f32[2,128,128]{2,1,0:T(8,128)S(1)}, u32[]{:S(2)}, u32[]{:S(2)}) collective-permute-start(f32[2,128,128]{2,1,0:T(8,128)S(1)} %fusion.56), channel_id=1, source_target_pairs={{0,16},{8,24},{32,48},{40,56},{64,80},{72,88},{96,112},{104,120},{... | collective-permute-start | bytes 393224 | tf_op jit(solution)/shard_map/ppermute | solution.py:115
  31.9 7.6 %collective-permute-start.1 = (f32[2,128,128]{2,1,0:T(8,128)S(1)}, f32[2,128,128]{2,1,0:T(8,128)S(1)}, u32[]{:S(2)}, u32[]{:S(2)}) collective-permute-start(f32[2,128,128]{2,1,0:T(8,128)S(1)} %convolution_select_fusion.6), channel_id=1, source_target_pairs={{0,16},{8,24},{32,48},{40,56},{64,80},{72,88},{96,112},{104,120},{... | collective-permute-start | bytes 393224 | tf_op jit(solution)/shard_map/ppermute | solution.py:115
  34.7 7.8 %collective-permute-start.24 = (bf16[256,256]{0,1:T(8,128)(2,1)S(1)}, bf16[256,256]{0,1:T(8,128)(2,1)S(1)}, u32[]{:S(2)}, u32[]{:S(2)}) collective-permute-start(bf16[256,256]{0,1:T(8,128)(2,1)S(1)} %collective-permute-done.23), channel_id=1, source_target_pairs={{0,8},{8,16},{16,24},{24,32},{32,40},{40,48},{48,56},{56,64},{64,7... | collective-permute-start | bytes 393224 | tf_op jit(solution)/shard_map/ppermute | solution.py:18
  38.9 9.2 %collective-permute-start.7 = (f32[2,128,128]{2,1,0:T(8,128)S(1)}, f32[2,128,128]{2,1,0:T(8,128)S(1)}, u32[]{:S(2)}, u32[]{:S(2)}) collective-permute-start(f32[2,128,128]{2,1,0:T(8,128)S(1)} %fusion.55), channel_id=1, source_target_pairs={{24,56},{56,88},{88,120},{120,152},{152,184},{184,216},{216,248},{... | collective-permute-start | bytes 393224 | tf_op jit(solution)/shard_map/ppermute | solution.py:115
  39.8 9.2 %collective-permute-start.2 = (f32[2,128,128]{2,1,0:T(8,128)S(1)}, f32[2,128,128]{2,1,0:T(8,128)S(1)}, u32[]{:S(2)}, u32[]{:S(2)}) collective-permute-start(f32[2,128,128]{2,1,0:T(8,128)S(1)} %convolution_select_fusion.4), channel_id=1, source_target_pairs={{24,56},{56,88},{88,120},{120,152},{152,184},{184,216},{216,248},{... | collective-permute-start | bytes 393224 | tf_op jit(solution)/shard_map/ppermute | solution.py:115
  42.6 17.9 %collective-permute-start.25 = (bf16[256,256]{0,1:T(8,128)(2,1)S(1)}, bf16[256,256]{0,1:T(8,128)(2,1)S(1)}, u32[]{:S(2)}, u32[]{:S(2)}) collective-permute-start(bf16[256,256]{0,1:T(8,128)(2,1)S(1)} %collective-permute-done.24), channel_id=1, source_target_pairs={{0,8},{8,16},{16,24},{24,32},{32,40},{40,48},{48,56},{56,64},{64,7... | collective-permute-start | bytes 393224 | tf_op jit(solution)/shard_map/ppermute | solution.py:18
  48.3 14.0 %collective-permute-start.8 = (f32[2,128,128]{2,1,0:T(8,128)S(1)}, f32[2,128,128]{2,1,0:T(8,128)S(1)}, u32[]{:S(2)}, u32[]{:S(2)}) collective-permute-start(f32[2,128,128]{2,1,0:T(8,128)S(1)} %fusion.54), channel_id=1, source_target_pairs={{24,88},{56,120},{88,152},{120,184},{152,216},{184,248},{216,280},... | collective-permute-start | bytes 393224 | tf_op jit(solution)/shard_map/ppermute | solution.py:115
  49.3 14.0 %collective-permute-start.3 = (f32[2,128,128]{2,1,0:T(8,128)S(1)}, f32[2,128,128]{2,1,0:T(8,128)S(1)}, u32[]{:S(2)}, u32[]{:S(2)}) collective-permute-start(f32[2,128,128]{2,1,0:T(8,128)S(1)} %convolution_select_fusion.3), channel_id=1, source_target_pairs={{24,88},{56,120},{88,152},{120,184},{152,216},{184,248},{216,280},... | collective-permute-start | bytes 393224 | tf_op jit(solution)/shard_map/ppermute | solution.py:115
  60.4 12.8 %collective-permute-start.26 = (bf16[256,256]{0,1:T(8,128)(2,1)S(1)}, bf16[256,256]{0,1:T(8,128)(2,1)S(1)}, u32[]{:S(2)}, u32[]{:S(2)}) collective-permute-start(bf16[256,256]{0,1:T(8,128)(2,1)S(1)} %collective-permute-done.25), channel_id=1, source_target_pairs={{0,8},{8,16},{16,24},{24,32},{32,40},{40,48},{48,56},{56,64},{64,7... | collective-permute-start | bytes 393224 | tf_op jit(solution)/shard_map/ppermute | solution.py:18
  62.6 12.5 %collective-permute-start.9 = (f32[2,128,128]{2,1,0:T(8,128)S(1)}, f32[2,128,128]{2,1,0:T(8,128)S(1)}, u32[]{:S(2)}, u32[]{:S(2)}) collective-permute-start(f32[2,128,128]{2,1,0:T(8,128)S(1)} %fusion.53), channel_id=1, source_target_pairs={{24,152},{56,184},{88,216},{120,248},{152,280},{184,312},{216,344}... | collective-permute-start | bytes 393224 | tf_op jit(solution)/shard_map/ppermute | solution.py:115
  63.6 25.3 %collective-permute-start.4 = (f32[2,128,128]{2,1,0:T(8,128)S(1)}, f32[2,128,128]{2,1,0:T(8,128)S(1)}, u32[]{:S(2)}, u32[]{:S(2)}) collective-permute-start(f32[2,128,128]{2,1,0:T(8,128)S(1)} %convolution_select_fusion.2), channel_id=1, source_target_pairs={{24,152},{56,184},{88,216},{120,248},{152,280},{184,312},{216,344}... | collective-permute-start | bytes 393224 | tf_op jit(solution)/shard_map/ppermute | solution.py:115
  73.2 13.8 %collective-permute-start.27 = (bf16[256,256]{0,1:T(8,128)(2,1)S(1)}, bf16[256,256]{0,1:T(8,128)(2,1)S(1)}, u32[]{:S(2)}, u32[]{:S(2)}) collective-permute-start(bf16[256,256]{0,1:T(8,128)(2,1)S(1)} %collective-permute-done.26), channel_id=1, source_target_pairs={{0,8},{8,16},{16,24},{24,32},{32,40},{40,48},{48,56},{56,64},{64,7... | collective-permute-start | bytes 393224 | tf_op jit(solution)/shard_map/ppermute | solution.py:18
  75.4 13.8 %collective-permute-start.10 = (f32[2,128,128]{2,1,0:T(8,128)S(1)}, f32[2,128,128]{2,1,0:T(8,128)S(1)}, u32[]{:S(2)}, u32[]{:S(2)}) collective-permute-start(f32[2,128,128]{2,1,0:T(8,128)S(1)} %fusion.52), channel_id=1, source_target_pairs={{24,280},{56,312},{88,344},{120,376},{152,408},{184,440},{216,472}... | collective-permute-start | bytes 393224 | tf_op jit(solution)/shard_map/ppermute | solution.py:115
  87.0 8.1 %collective-permute-start.28 = (bf16[256,256]{0,1:T(8,128)(2,1)S(1)}, bf16[256,256]{0,1:T(8,128)(2,1)S(1)}, u32[]{:S(2)}, u32[]{:S(2)}) collective-permute-start(bf16[256,256]{0,1:T(8,128)(2,1)S(1)} %collective-permute-done.27), channel_id=1, source_target_pairs={{0,8},{8,16},{16,24},{24,32},{32,40},{40,48},{48,56},{56,64},{64,7... | collective-permute-start | bytes 393224 | tf_op jit(solution)/shard_map/ppermute | solution.py:18
  89.5 7.7 %collective-permute-start.14 = (f32[2,128,128]{2,1,0:T(8,128)S(1)}, f32[2,128,128]{2,1,0:T(8,128)S(1)}, u32[]{:S(2)}, u32[]{:S(2)}) collective-permute-start(f32[2,128,128]{2,1,0:T(8,128)S(1)} %fusion.51), channel_id=1, source_target_pairs={{24,56},{56,88},{88,120},{120,152},{152,184},{184,216},{216,248},{... | collective-permute-start | bytes 393224 | tf_op jit(solution)/shard_map/ppermute | solution.py:115
  90.2 7.0 %collective-permute-start.13 = (f32[2,128,128]{2,1,0:T(8,128)S(1)}, f32[2,128,128]{2,1,0:T(8,128)S(1)}, u32[]{:S(2)}, u32[]{:S(2)}) collective-permute-start(f32[2,128,128]{2,1,0:T(8,128)S(1)} %fusion.51), channel_id=1, source_target_pairs={{24,48},{56,80},{88,112},{120,144},{152,176},{184,208},{216,240},{... | collective-permute-start | bytes 393224 | tf_op jit(solution)/shard_map/ppermute | solution.py:115
  90.9 6.4 %collective-permute-start.12 = (f32[2,128,128]{2,1,0:T(8,128)S(1)}, f32[2,128,128]{2,1,0:T(8,128)S(1)}, u32[]{:S(2)}, u32[]{:S(2)}) collective-permute-start(f32[2,128,128]{2,1,0:T(8,128)S(1)} %fusion.51), channel_id=1, source_target_pairs={{24,40},{56,72},{88,104},{120,136},{152,168},{184,200},{216,232},{... | collective-permute-start | bytes 393224 | tf_op jit(solution)/shard_map/ppermute | solution.py:115
  91.6 16.7 %collective-permute-start.11 = (f32[2,128,128]{2,1,0:T(8,128)S(1)}, f32[2,128,128]{2,1,0:T(8,128)S(1)}, u32[]{:S(2)}, u32[]{:S(2)}) collective-permute-start(f32[2,128,128]{2,1,0:T(8,128)S(1)} %fusion.51), channel_id=1, source_target_pairs={{24,32},{56,64},{88,96},{120,128},{152,160},{184,192},{216,224},{2... | collective-permute-start | bytes 393224 | tf_op jit(solution)/shard_map/ppermute | solution.py:115
  95.1 21.9 %collective-permute-start.29 = (bf16[256,256]{0,1:T(8,128)(2,1)S(1)}, bf16[256,256]{0,1:T(8,128)(2,1)S(1)}, u32[]{:S(2)}, u32[]{:S(2)}) collective-permute-start(bf16[256,256]{0,1:T(8,128)(2,1)S(1)} %collective-permute-done.28), channel_id=1, source_target_pairs={{0,8},{8,16},{16,24},{24,32},{32,40},{40,48},{48,56},{56,64},{64,7... | collective-permute-start | bytes 393224 | tf_op jit(solution)/shard_map/ppermute | solution.py:18
  113.2 8.3 %collective-permute-start.19 = (bf16[256,256]{0,1:T(8,128)(2,1)S(1)}, bf16[256,256]{0,1:T(8,128)(2,1)S(1)}, u32[]{:S(2)}, u32[]{:S(2)}) collective-permute-start(bf16[256,256]{0,1:T(8,128)(2,1)S(1)} %bitcast.200), channel_id=1, source_target_pairs={{0,8},{8,16},{16,24},{24,32},{32,40},{40,48},{48,56},{56,64},{64,7... | collective-permute-start | bytes 393224 | tf_op jit(solution)/shard_map/ppermute | solution.py:18
  115.1 15.3 %collective-permute-start.15 = (bf16[256,256]{0,1:T(8,128)(2,1)S(1)}, bf16[256,256]{0,1:T(8,128)(2,1)S(1)}, u32[]{:S(2)}, u32[]{:S(2)}) collective-permute-start(bf16[256,256]{0,1:T(8,128)(2,1)S(1)} %bitcast.201), channel_id=1, source_target_pairs={{0,40},{8,48},{16,56},{24,64},{32,72},{40,80},{48,88},{56,96},{64,... | collective-permute-start | bytes 393224 | tf_op jit(solution)/shard_map/ppermute | solution.py:18
  117.1 16.3 %collective-permute-start.30 = (bf16[256,256]{0,1:T(8,128)(2,1)S(1)}, bf16[256,256]{0,1:T(8,128)(2,1)S(1)}, u32[]{:S(2)}, u32[]{:S(2)}) collective-permute-start(bf16[256,256]{0,1:T(8,128)(2,1)S(1)} %collective-permute-done.29), channel_id=1, source_target_pairs={{0,8},{8,16},{16,24},{24,32},{32,40},{40,48},{48,56},{56,64},{64,7... | collective-permute-start | bytes 393224 | tf_op jit(solution)/shard_map/ppermute | solution.py:18
  121.5 24.6 %collective-permute-start.20 = (bf16[256,256]{0,1:T(8,128)(2,1)S(1)}, bf16[256,256]{0,1:T(8,128)(2,1)S(1)}, u32[]{:S(2)}, u32[]{:S(2)}) collective-permute-start(bf16[256,256]{0,1:T(8,128)(2,1)S(1)} %collective-permute-done.19), channel_id=1, source_target_pairs={{0,8},{8,16},{16,24},{24,32},{32,40},{40,48},{48,56},{56,64},{64,7... | collective-permute-start | bytes 393224 | tf_op jit(solution)/shard_map/ppermute | solution.py:18
  130.4 12.9 %collective-permute-start.16 = (bf16[256,256]{0,1:T(8,128)(2,1)S(1)}, bf16[256,256]{0,1:T(8,128)(2,1)S(1)}, u32[]{:S(2)}, u32[]{:S(2)}) collective-permute-start(bf16[256,256]{0,1:T(8,128)(2,1)S(1)} %collective-permute-done.15), channel_id=1, source_target_pairs={{0,8},{8,16},{16,24},{24,32},{32,40},{40,48},{48,56},{56,64},{64,7... | collective-permute-start | bytes 393224 | tf_op jit(solution)/shard_map/ppermute | solution.py:18
  143.4 8.1 %collective-permute-start.17 = (bf16[256,256]{0,1:T(8,128)(2,1)S(1)}, bf16[256,256]{0,1:T(8,128)(2,1)S(1)}, u32[]{:S(2)}, u32[]{:S(2)}) collective-permute-start(bf16[256,256]{0,1:T(8,128)(2,1)S(1)} %collective-permute-done.16), channel_id=1, source_target_pairs={{0,8},{8,16},{16,24},{24,32},{32,40},{40,48},{48,56},{56,64},{64,7... | collective-permute-start | bytes 393224 | tf_op jit(solution)/shard_map/ppermute | solution.py:18
  146.1 9.6 %collective-permute-start.21 = (bf16[256,256]{0,1:T(8,128)(2,1)S(1)}, bf16[256,256]{0,1:T(8,128)(2,1)S(1)}, u32[]{:S(2)}, u32[]{:S(2)}) collective-permute-start(bf16[256,256]{0,1:T(8,128)(2,1)S(1)} %collective-permute-done.20), channel_id=1, source_target_pairs={{0,8},{8,16},{16,24},{24,32},{32,40},{40,48},{48,56},{56,64},{64,7... | collective-permute-start | bytes 393224 | tf_op jit(solution)/shard_map/ppermute | solution.py:18
  151.5 9.5 %collective-permute-start.18 = (bf16[256,256]{0,1:T(8,128)(2,1)S(1)}, bf16[256,256]{0,1:T(8,128)(2,1)S(1)}, u32[]{:S(2)}, u32[]{:S(2)}) collective-permute-start(bf16[256,256]{0,1:T(8,128)(2,1)S(1)} %collective-permute-done.17), channel_id=1, source_target_pairs={{0,8},{8,16},{16,24},{24,32},{32,40},{40,48},{48,56},{56,64},{64,7... | collective-permute-start | bytes 393224 | tf_op jit(solution)/shard_map/ppermute | solution.py:18
  155.8 7.8 %collective-permute-start.22 = (bf16[256,256]{0,1:T(8,128)(2,1)S(1)}, bf16[256,256]{0,1:T(8,128)(2,1)S(1)}, u32[]{:S(2)}, u32[]{:S(2)}) collective-permute-start(bf16[256,256]{0,1:T(8,128)(2,1)S(1)} %collective-permute-done.21), channel_id=1, source_target_pairs={{0,8},{8,16},{16,24},{24,32},{32,40},{40,48},{48,56},{56,64},{64,7... | collective-permute-start | bytes 393224 | tf_op jit(solution)/shard_map/ppermute | solution.py:18
  163.7 23.5 %copy-start.3 = (f32[256]{0:T(256)S(1)}, f32[256]{0:T(256)}, u32[]{:S(2)}) copy-start(f32[256]{0:T(256)} %param.17) | copy-start | bytes 3076

commit v7 on v6

--- a/solution.py
+++ b/solution.py
@@ -59,20 +59,18 @@
 def local_pair(k_unit, writes, updates):
     head_size = k_unit.shape[-1]
     identity = jnp.eye(head_size, dtype=jnp.float32)
-
-    def stride(carry, inputs_now):
-        transit, carried = carry
-        k_block, w_block, u_block = inputs_now
-        stepped = identity - jnp.dot(k_block.T, w_block, precision=highest)
-        transit = jnp.dot(stepped, transit, precision=highest)
-        carried = jnp.dot(stepped, carried, precision=highest) + jnp.dot(
-            k_block.T, u_block, precision=highest
-        )
-        return ((transit, carried), None)
-
-    start_pair = (identity, jnp.zeros((head_size, head_size), jnp.float32))
-    (transit, carried), _ = lax.scan(stride, start_pair, (k_unit, writes, updates))
-    return (transit, carried)
+    key_cols = jnp.swapaxes(k_unit, -1, -2)
+    transit = identity - jnp.einsum("nij,njk->nik", key_cols, writes, precision=highest)
+    carried = jnp.einsum("nij,njk->nik", key_cols, updates, precision=highest)
+    while transit.shape[0] > 1:
+        if transit.shape[0] % 2:
+            transit = jnp.concatenate([identity[None], transit], axis=0)
+            carried = jnp.concatenate([jnp.zeros_like(carried[:1]), carried], axis=0)
+        early_t, late_t = transit[0::2], transit[1::2]
+        early_c, late_c = carried[0::2], carried[1::2]
+        transit = jnp.einsum("nij,njk->nik", late_t, early_t, precision=highest)
+        carried = jnp.einsum("nij,njk->nik", late_t, early_c, precision=highest) + late_c
+    return (transit[0], carried[0])
 
 
 def advance(carried, inputs_now):

time: 190 us -> 192 us (1.011)
  waiting for transfers between devices: 69.4 us -> 79.3 us
  starting transfers between devices: 63 us -> 59 us
    ppermute x16, waiting for transfers between devices: 58.4 us -> 68.9 us  [shifted(): return lax.ppermute(value, axis, pairs)]
    ppermute x16, starting transfers between devices: 40.9 us -> 37 us  [shifted(): return lax.ppermute(value, axis, pairs)]
    dot_general x16 -> x6, matrix products: 5.32 us -> 3.33 us  [the longest x1 1.01 us: local_pair(): jnp.einsum('nij,njk->nik', key_cols, writes, precision=highest)]
  transfers between devices with their start and end apart: 31 -> 31, of which waited for: 12 -> 11; matrix products, arithmetic and copies ran while one was open for 15% -> 14% of each run, Pallas kernels for 0% -> 0%
where the time goes in v7:
time: 192 us
  waiting for transfers between devices  79.3 us (41%)
  starting transfers between devices  59 us (31%)
  blocking collectives  22.7 us (12%)
  matrix products  19.3 us (10%)
  local copies, waits for them, and re-layouts  4.63 us (2%)
  other arithmetic  4.6 us (2%)
    ppermute x16, waiting for transfers between devices, shifted(): return lax.ppermute(value, axis, pairs)  68.9 us
    ppermute x16, starting transfers between devices, shifted(): return lax.ppermute(value, axis, pairs)  37 us
    psum x1, blocking collectives, on_device(): total_sq = lax.psum(squares, 'head')  22.7 us
    ppermute x15, starting transfers between devices, moved(): return lax.ppermute(value, 'seq', pairs)  22.1 us
    ppermute x15, waiting for transfers between devices, moved(): return lax.ppermute(value, 'seq', pairs)  10.4 us
    dot_general x16, matrix products, batched_dot(): return jnp.einsum('hij,hjk->hik', left, right, precision=highest)  4.33 us
  transfers between devices with their start and end apart: 31, of which 11 were waited for; matrix products, arithmetic and copies ran while one was open for 14% of the time, Pallas kernels for 0%

profile of v7, /device:TPU:25, one launch (start us, length us, event | category | flops | bytes accessed | tf_op | source)
XLA Modules:
  0.0 191.5 jit_solution(1486634712594144819)
XLA Ops:
  0.6 1.0 copy.57
  1.7 3.5 %collective-permute-start.23 = (bf16[256,256]{0,1:T(8,128)(2,1)S(1)}, bf16[256,256]{0,1:T(8,128)(2,1)S(1)}, u32[]{:S(2)}, u32[]{:S(2)}) collective-permute-start(bf16[256,256]{0,1:T(8,128)(2,1)S(1)} %copy.57), channel_id=1, source_target_pairs={{0,8},{8,16},{16,24},{24,32},{32,40},{40,48},{48,56},{56,64},{64,7... | collective-permute-start | bytes 393224 | tf_op jit(solution)/shard_map/ppermute | solution.py:18
  5.3 0.8 mul.79
  6.1 1.0 copy.42
  12.3 1.0 convolution_subtract_fusion.1
  14.0 3.5 %collective-permute-start = (f32[2,128,128]{2,1,0:T(8,128)S(1)}, f32[2,128,128]{2,1,0:T(8,128)S(1)}, u32[]{:S(2)}, u32[]{:S(2)}) collective-permute-start(f32[2,128,128]{2,1,0:T(8,128)S(1)} %fusion.67), channel_id=1, source_target_pairs={{0,8},{8,16},{16,24},{32,40},{40,48},{48,56},{64,72},{72,80},{80,8... | collective-permute-start | bytes 393224 | tf_op jit(solution)/shard_map/ppermute | solution.py:113
  18.3 1.0 fusion.90
  20.0 3.5 %collective-permute-start.5 = (f32[2,128,128]{2,1,0:T(8,128)S(1)}, f32[2,128,128]{2,1,0:T(8,128)S(1)}, u32[]{:S(2)}, u32[]{:S(2)}) collective-permute-start(f32[2,128,128]{2,1,0:T(8,128)S(1)} %fusion.40), channel_id=1, source_target_pairs={{0,8},{8,16},{16,24},{32,40},{40,48},{48,56},{64,72},{72,80},{80,8... | collective-permute-start | bytes 393224 | tf_op jit(solution)/shard_map/ppermute | solution.py:113
  24.8 4.5 %collective-permute-start.1 = (f32[2,128,128]{2,1,0:T(8,128)S(1)}, f32[2,128,128]{2,1,0:T(8,128)S(1)}, u32[]{:S(2)}, u32[]{:S(2)}) collective-permute-start(f32[2,128,128]{2,1,0:T(8,128)S(1)} %convolution_select_fusion.6), channel_id=1, source_target_pairs={{0,16},{8,24},{32,48},{40,56},{64,80},{72,88},{96,112},{104,120},{... | collective-permute-start | bytes 393224 | tf_op jit(solution)/shard_map/ppermute | solution.py:113
  29.6 2.5 %collective-permute-start.6 = (f32[2,128,128]{2,1,0:T(8,128)S(1)}, f32[2,128,128]{2,1,0:T(8,128)S(1)}, u32[]{:S(2)}, u32[]{:S(2)}) collective-permute-start(f32[2,128,128]{2,1,0:T(8,128)S(1)} %fusion.38), channel_id=1, source_target_pairs={{0,16},{8,24},{32,48},{40,56},{64,80},{72,88},{96,112},{104,120},{... | collective-permute-start | bytes 393224 | tf_op jit(solution)/shard_map/ppermute | solution.py:113
  32.4 1.9 %collective-permute-start.24 = (bf16[256,256]{0,1:T(8,128)(2,1)S(1)}, bf16[256,256]{0,1:T(8,128)(2,1)S(1)}, u32[]{:S(2)}, u32[]{:S(2)}) collective-permute-start(bf16[256,256]{0,1:T(8,128)(2,1)S(1)} %collective-permute-done.23), channel_id=1, source_target_pairs={{0,8},{8,16},{16,24},{24,32},{32,40},{40,48},{48,56},{56,64},{64,7... | collective-permute-start | bytes 393224 | tf_op jit(solution)/shard_map/ppermute | solution.py:18
  34.9 0.7 collective-permute-start.2
  35.8 0.7 collective-permute-start.7
  36.5 3.7 %collective-permute-done.24 = bf16[256,256]{0,1:T(8,128)(2,1)S(1)} collective-permute-done((bf16[256,256]{0,1:T(8,128)(2,1)S(1)}, bf16[256,256]{0,1:T(8,128)(2,1)S(1)}, u32[]{:S(2)}, u32[]{:S(2)}) %collective-permute-start.24) | collective-permute-done | bytes 131104 | tf_op jit(solution)/shard_map/ppermute | solution.py:18
  40.2 4.6 %collective-permute-start.25 = (bf16[256,256]{0,1:T(8,128)(2,1)S(1)}, bf16[256,256]{0,1:T(8,128)(2,1)S(1)}, u32[]{:S(2)}, u32[]{:S(2)}) collective-permute-start(bf16[256,256]{0,1:T(8,128)(2,1)S(1)} %collective-permute-done.24), channel_id=1, source_target_pairs={{0,8},{8,16},{16,24},{24,32},{32,40},{40,48},{48,56},{56,64},{64,7... | collective-permute-start | bytes 393224 | tf_op jit(solution)/shard_map/ppermute | solution.py:18
  45.3 0.7 collective-permute-start.8
  47.0 10.5 %collective-permute-done.25 = bf16[256,256]{0,1:T(8,128)(2,1)S(1)} collective-permute-done((bf16[256,256]{0,1:T(8,128)(2,1)S(1)}, bf16[256,256]{0,1:T(8,128)(2,1)S(1)}, u32[]{:S(2)}, u32[]{:S(2)}) %collective-permute-start.25) | collective-permute-done | bytes 131104 | tf_op jit(solution)/shard_map/ppermute | solution.py:18
  57.5 2.1 %collective-permute-start.26 = (bf16[256,256]{0,1:T(8,128)(2,1)S(1)}, bf16[256,256]{0,1:T(8,128)(2,1)S(1)}, u32[]{:S(2)}, u32[]{:S(2)}) collective-permute-start(bf16[256,256]{0,1:T(8,128)(2,1)S(1)} %collective-permute-done.25), channel_id=1, source_target_pairs={{0,8},{8,16},{16,24},{24,32},{32,40},{40,48},{48,56},{56,64},{64,7... | collective-permute-start | bytes 393224 | tf_op jit(solution)/shard_map/ppermute | solution.py:18
  60.9 0.7 collective-permute-start.4
  61.6 14.0 %collective-permute-done.26 = bf16[256,256]{0,1:T(8,128)(2,1)S(1)} collective-permute-done((bf16[256,256]{0,1:T(8,128)(2,1)S(1)}, bf16[256,256]{0,1:T(8,128)(2,1)S(1)}, u32[]{:S(2)}, u32[]{:S(2)}) %collective-permute-start.26) | collective-permute-done | bytes 131104 | tf_op jit(solution)/shard_map/ppermute | solution.py:18
  75.6 1.9 collective-permute-start.27
  78.4 10.2 %collective-permute-done.27 = bf16[256,256]{0,1:T(8,128)(2,1)S(1)} collective-permute-done((bf16[256,256]{0,1:T(8,128)(2,1)S(1)}, bf16[256,256]{0,1:T(8,128)(2,1)S(1)}, u32[]{:S(2)}, u32[]{:S(2)}) %collective-permute-start.27) | collective-permute-done | bytes 131104 | tf_op jit(solution)/shard_map/ppermute | solution.py:18
  88.6 1.9 collective-permute-start.28
  93.1 1.3 collective-permute-start.11
  94.7 1.7 collective-permute-done.28
  96.4 3.8 %collective-permute-start.29 = (bf16[256,256]{0,1:T(8,128)(2,1)S(1)}, bf16[256,256]{0,1:T(8,128)(2,1)S(1)}, u32[]{:S(2)}, u32[]{:S(2)}) collective-permute-start(bf16[256,256]{0,1:T(8,128)(2,1)S(1)} %collective-permute-done.28), channel_id=1, source_target_pairs={{0,8},{8,16},{16,24},{24,32},{32,40},{40,48},{48,56},{56,64},{64,7... | collective-permute-start | bytes 393224 | tf_op jit(solution)/shard_map/ppermute | solution.py:18
  100.2 10.3 %collective-permute-done.11 = f32[2,128,128]{2,1,0:T(8,128)S(1)} collective-permute-done((f32[2,128,128]{2,1,0:T(8,128)S(1)}, f32[2,128,128]{2,1,0:T(8,128)S(1)}, u32[]{:S(2)}, u32[]{:S(2)}) %collective-permute-start.11) | collective-permute-done | bytes 131104 | tf_op jit(solution)/shard_map/ppermute | solution.py:113
  110.9 4.5 %while.3 = (s32[]{:T(128)}, f32[2,128,128]{2,1,0:T(8,128)S(1)}, bf16[4,2,64,128]{3,2,0,1:T(8,128)(2,1)S(1)}, f32[4,2,64,128]{3,2,0,1:T(8,128)S(1)}, f32[4,2,64,1...) while((s32[]{:T(128)}, f32[2,128,128]{2,1,0:T(8,128)S(1)}, ...), condition=%wide.region_3.4_spmd, body=%wide.region_2.3_spmd.sunk | while | flops 88145920 | bytes 1247341 | solution.py:86
  115.5 1.9 %collective-permute-start.19 = (bf16[256,256]{0,1:T(8,128)(2,1)S(1)}, bf16[256,256]{0,1:T(8,128)(2,1)S(1)}, u32[]{:S(2)}, u32[]{:S(2)}) collective-permute-start(bf16[256,256]{0,1:T(8,128)(2,1)S(1)} %bitcast.202), channel_id=1, source_target_pairs={{0,8},{8,16},{16,24},{24,32},{32,40},{40,48},{48,56},{56,64},{64,7... | collective-permute-start | bytes 393224 | tf_op jit(solution)/shard_map/ppermute | solution.py:18
  117.4 1.9 %collective-permute-start.15 = (bf16[256,256]{0,1:T(8,128)(2,1)S(1)}, bf16[256,256]{0,1:T(8,128)(2,1)S(1)}, u32[]{:S(2)}, u32[]{:S(2)}) collective-permute-start(bf16[256,256]{0,1:T(8,128)(2,1)S(1)} %bitcast.203), channel_id=1, source_target_pairs={{0,40},{8,48},{16,56},{24,64},{32,72},{40,80},{48,88},{56,96},{64,... | collective-permute-start | bytes 393224 | tf_op jit(solution)/shard_map/ppermute | solution.py:18
  119.4 1.9 %collective-permute-start.30 = (bf16[256,256]{0,1:T(8,128)(2,1)S(1)}, bf16[256,256]{0,1:T(8,128)(2,1)S(1)}, u32[]{:S(2)}, u32[]{:S(2)}) collective-permute-start(bf16[256,256]{0,1:T(8,128)(2,1)S(1)} %collective-permute-done.29), channel_id=1, source_target_pairs={{0,8},{8,16},{16,24},{24,32},{32,40},{40,48},{48,56},{56,64},{64,7... | collective-permute-start | bytes 393224 | tf_op jit(solution)/shard_map/ppermute | solution.py:18
  121.3 1.3 fusion.28
  122.6 0.8 copy.63
  123.3 1.9 collective-permute-start.20
  125.2 11.7 %collective-permute-done.15 = bf16[256,256]{0,1:T(8,128)(2,1)S(1)} collective-permute-done((bf16[256,256]{0,1:T(8,128)(2,1)S(1)}, bf16[256,256]{0,1:T(8,128)(2,1)S(1)}, u32[]{:S(2)}, u32[]{:S(2)}) %collective-permute-start.15) | collective-permute-done | bytes 131104 | tf_op jit(solution)/shard_map/ppermute | solution.py:18
  136.9 1.9 collective-permute-start.16
  139.0 8.0 %collective-permute-done.16 = bf16[256,256]{0,1:T(8,128)(2,1)S(1)} collective-permute-done((bf16[256,256]{0,1:T(8,128)(2,1)S(1)}, bf16[256,256]{0,1:T(8,128)(2,1)S(1)}, u32[]{:S(2)}, u32[]{:S(2)}) %collective-permute-start.16) | collective-permute-done | bytes 131104 | tf_op jit(solution)/shard_map/ppermute | solution.py:18
  147.0 1.9 collective-permute-start.17
  148.9 0.8 fusion.21
  149.8 1.9 %collective-permute-start.21 = (bf16[256,256]{0,1:T(8,128)(2,1)S(1)}, bf16[256,256]{0,1:T(8,128)(2,1)S(1)}, u32[]{:S(2)}, u32[]{:S(2)}) collective-permute-start(bf16[256,256]{0,1:T(8,128)(2,1)S(1)} %collective-permute-done.20), channel_id=1, source_target_pairs={{0,8},{8,16},{16,24},{24,32},{32,40},{40,48},{48,56},{56,64},{64,7... | collective-permute-start | bytes 393224 | tf_op jit(solution)/shard_map/ppermute | solution.py:18
  151.7 3.3 %collective-permute-done.17 = bf16[256,256]{0,1:T(8,128)(2,1)S(1)} collective-permute-done((bf16[256,256]{0,1:T(8,128)(2,1)S(1)}, bf16[256,256]{0,1:T(8,128)(2,1)S(1)}, u32[]{:S(2)}, u32[]{:S(2)}) %collective-permute-start.17) | collective-permute-done | bytes 131104 | tf_op jit(solution)/shard_map/ppermute | solution.py:18
  155.0 1.9 collective-permute-start.18
  157.0 2.4 %fusion.84 = (f32[2,256]{1,0:T(2,128)S(1)}, f32[2,256,2304]{1,2,0:T(8,128)S(1)}) fusion(f32[2,256,2304]{1,2,0:T(8,128)S(1)} %fusion.21, pred[256,2304]{0,1:T(8,128)(4,1)S(1)} %fusion.28), kind=kOutput, calls=%fused_computation.145 | output fusion | flops 4720895 | bytes 10029056 | tf_op jit(solution)/shard_map/while/body/eval_jaxpr/sub | solution.py:194
  159.3 1.9 %collective-permute-start.22 = (bf16[256,256]{0,1:T(8,128)(2,1)S(1)}, bf16[256,256]{0,1:T(8,128)(2,1)S(1)}, u32[]{:S(2)}, u32[]{:S(2)}) collective-permute-start(bf16[256,256]{0,1:T(8,128)(2,1)S(1)} %collective-permute-done.21), channel_id=1, source_target_pairs={{0,8},{8,16},{16,24},{24,32},{32,40},{40,48},{48,56},{56,64},{64,7... | collective-permute-start | bytes 393224 | tf_op jit(solution)/shard_map/ppermute | solution.py:18
  161.3 3.2 %collective-permute-done.18 = bf16[256,256]{0,1:T(8,128)(2,1)S(1)} collective-permute-done((bf16[256,256]{0,1:T(8,128)(2,1)S(1)}, bf16[256,256]{0,1:T(8,128)(2,1)S(1)}, u32[]{:S(2)}, u32[]{:S(2)}) %collective-permute-start.18) | collective-permute-done | bytes 131104 | tf_op jit(solution)/shard_map/ppermute | solution.py:18
  164.5 2.6 %collective-permute-done.22 = bf16[256,256]{0,1:T(8,128)(2,1)S(1)} collective-permute-done((bf16[256,256]{0,1:T(8,128)(2,1)S(1)}, bf16[256,256]{0,1:T(8,128)(2,1)S(1)}, u32[]{:S(2)}, u32[]{:S(2)}) %collective-permute-start.22) | collective-permute-done | bytes 131104 | tf_op jit(solution)/shard_map/ppermute | solution.py:18
  167.8 22.7 %psum.7 = f32[256]{0:T(256)S(1)} all-reduce(f32[256]{0:T(256)S(1)} %get-tuple-element.109), channel_id=1, replica_groups=mesh['seq'=64,'head'=8] {'head'}, use_global_device_ids=true, to_apply=%region_7.8 | all-reduce | flops 256 | bytes 2048 | tf_op jit(solution)/shard_map/psum | solution.py:204
  190.8 0.8 multiply_convert_fusion
  (126 shorter events, 21.8 us)
Async XLA Ops:
  0.6 148.3 %copy-start = (bf16[256,256]{1,0:T(8,128)(2,1)S(1)}, bf16[256,256]{1,0:T(8,128)(2,1)}, u32[]{:S(2)}) copy-start(bf16[256,256]{1,0:T(8,128)(2,1)} %param.13) | copy-start | bytes 393220
  1.7 30.7 %collective-permute-start.23 = (bf16[256,256]{0,1:T(8,128)(2,1)S(1)}, bf16[256,256]{0,1:T(8,128)(2,1)S(1)}, u32[]{:S(2)}, u32[]{:S(2)}) collective-permute-start(bf16[256,256]{0,1:T(8,128)(2,1)S(1)} %copy.57), channel_id=1, source_target_pairs={{0,8},{8,16},{16,24},{24,32},{32,40},{40,48},{48,56},{56,64},{64,7... | collective-permute-start | bytes 393224 | tf_op jit(solution)/shard_map/ppermute | solution.py:18
  12.3 5.3 %copy-start.1 = (bf16[256,256]{1,0:T(8,128)(2,1)S(1)}, bf16[256,256]{1,0:T(8,128)(2,1)}, u32[]{:S(2)}) copy-start(bf16[256,256]{1,0:T(8,128)(2,1)} %param.11) | copy-start | bytes 393220
  14.0 10.6 %collective-permute-start = (f32[2,128,128]{2,1,0:T(8,128)S(1)}, f32[2,128,128]{2,1,0:T(8,128)S(1)}, u32[]{:S(2)}, u32[]{:S(2)}) collective-permute-start(f32[2,128,128]{2,1,0:T(8,128)S(1)} %fusion.67), channel_id=1, source_target_pairs={{0,8},{8,16},{16,24},{32,40},{40,48},{48,56},{64,72},{72,80},{80,8... | collective-permute-start | bytes 393224 | tf_op jit(solution)/shard_map/ppermute | solution.py:113
  19.3 4.3 %copy-start.2 = (bf16[256,256]{1,0:T(8,128)(2,1)S(1)}, bf16[256,256]{1,0:T(8,128)(2,1)}, u32[]{:S(2)}) copy-start(bf16[256,256]{1,0:T(8,128)(2,1)} %param.9) | copy-start | bytes 393220
  20.0 9.3 %collective-permute-start.5 = (f32[2,128,128]{2,1,0:T(8,128)S(1)}, f32[2,128,128]{2,1,0:T(8,128)S(1)}, u32[]{:S(2)}, u32[]{:S(2)}) collective-permute-start(f32[2,128,128]{2,1,0:T(8,128)S(1)} %fusion.40), channel_id=1, source_target_pairs={{0,8},{8,16},{16,24},{32,40},{40,48},{48,56},{64,72},{72,80},{80,8... | collective-permute-start | bytes 393224 | tf_op jit(solution)/shard_map/ppermute | solution.py:113
  24.8 9.8 %collective-permute-start.1 = (f32[2,128,128]{2,1,0:T(8,128)S(1)}, f32[2,128,128]{2,1,0:T(8,128)S(1)}, u32[]{:S(2)}, u32[]{:S(2)}) collective-permute-start(f32[2,128,128]{2,1,0:T(8,128)S(1)} %convolution_select_fusion.6), channel_id=1, source_target_pairs={{0,16},{8,24},{32,48},{40,56},{64,80},{72,88},{96,112},{104,120},{... | collective-permute-start | bytes 393224 | tf_op jit(solution)/shard_map/ppermute | solution.py:113
  29.6 6.0 %collective-permute-start.6 = (f32[2,128,128]{2,1,0:T(8,128)S(1)}, f32[2,128,128]{2,1,0:T(8,128)S(1)}, u32[]{:S(2)}, u32[]{:S(2)}) collective-permute-start(f32[2,128,128]{2,1,0:T(8,128)S(1)} %fusion.38), channel_id=1, source_target_pairs={{0,16},{8,24},{32,48},{40,56},{64,80},{72,88},{96,112},{104,120},{... | collective-permute-start | bytes 393224 | tf_op jit(solution)/shard_map/ppermute | solution.py:113
  32.4 7.8 %collective-permute-start.24 = (bf16[256,256]{0,1:T(8,128)(2,1)S(1)}, bf16[256,256]{0,1:T(8,128)(2,1)S(1)}, u32[]{:S(2)}, u32[]{:S(2)}) collective-permute-start(bf16[256,256]{0,1:T(8,128)(2,1)S(1)} %collective-permute-done.23), channel_id=1, source_target_pairs={{0,8},{8,16},{16,24},{24,32},{32,40},{40,48},{48,56},{56,64},{64,7... | collective-permute-start | bytes 393224 | tf_op jit(solution)/shard_map/ppermute | solution.py:18
  34.9 11.1 %collective-permute-start.2 = (f32[2,128,128]{2,1,0:T(8,128)S(1)}, f32[2,128,128]{2,1,0:T(8,128)S(1)}, u32[]{:S(2)}, u32[]{:S(2)}) collective-permute-start(f32[2,128,128]{2,1,0:T(8,128)S(1)} %convolution_select_fusion.4), channel_id=1, source_target_pairs={{24,56},{56,88},{88,120},{120,152},{152,184},{184,216},{216,248},{... | collective-permute-start | bytes 393224 | tf_op jit(solution)/shard_map/ppermute | solution.py:113
  35.8 9.2 %collective-permute-start.7 = (f32[2,128,128]{2,1,0:T(8,128)S(1)}, f32[2,128,128]{2,1,0:T(8,128)S(1)}, u32[]{:S(2)}, u32[]{:S(2)}) collective-permute-start(f32[2,128,128]{2,1,0:T(8,128)S(1)} %fusion.37), channel_id=1, source_target_pairs={{24,56},{56,88},{88,120},{120,152},{152,184},{184,216},{216,248},{... | collective-permute-start | bytes 393224 | tf_op jit(solution)/shard_map/ppermute | solution.py:113
  40.2 17.3 %collective-permute-start.25 = (bf16[256,256]{0,1:T(8,128)(2,1)S(1)}, bf16[256,256]{0,1:T(8,128)(2,1)S(1)}, u32[]{:S(2)}, u32[]{:S(2)}) collective-permute-start(bf16[256,256]{0,1:T(8,128)(2,1)S(1)} %collective-permute-done.24), channel_id=1, source_target_pairs={{0,8},{8,16},{16,24},{24,32},{32,40},{40,48},{48,56},{56,64},{64,7... | collective-permute-start | bytes 393224 | tf_op jit(solution)/shard_map/ppermute | solution.py:18
  45.3 14.3 %collective-permute-start.8 = (f32[2,128,128]{2,1,0:T(8,128)S(1)}, f32[2,128,128]{2,1,0:T(8,128)S(1)}, u32[]{:S(2)}, u32[]{:S(2)}) collective-permute-start(f32[2,128,128]{2,1,0:T(8,128)S(1)} %fusion.36), channel_id=1, source_target_pairs={{24,88},{56,120},{88,152},{120,184},{152,216},{184,248},{216,280},... | collective-permute-start | bytes 393224 | tf_op jit(solution)/shard_map/ppermute | solution.py:113
  46.3 14.3 %collective-permute-start.3 = (f32[2,128,128]{2,1,0:T(8,128)S(1)}, f32[2,128,128]{2,1,0:T(8,128)S(1)}, u32[]{:S(2)}, u32[]{:S(2)}) collective-permute-start(f32[2,128,128]{2,1,0:T(8,128)S(1)} %convolution_select_fusion.3), channel_id=1, source_target_pairs={{24,88},{56,120},{88,152},{120,184},{152,216},{184,248},{216,280},... | collective-permute-start | bytes 393224 | tf_op jit(solution)/shard_map/ppermute | solution.py:113
  57.5 18.0 %collective-permute-start.26 = (bf16[256,256]{0,1:T(8,128)(2,1)S(1)}, bf16[256,256]{0,1:T(8,128)(2,1)S(1)}, u32[]{:S(2)}, u32[]{:S(2)}) collective-permute-start(bf16[256,256]{0,1:T(8,128)(2,1)S(1)} %collective-permute-done.25), channel_id=1, source_target_pairs={{0,8},{8,16},{16,24},{24,32},{32,40},{40,48},{48,56},{56,64},{64,7... | collective-permute-start | bytes 393224 | tf_op jit(solution)/shard_map/ppermute | solution.py:18
  59.9 17.6 %collective-permute-start.9 = (f32[2,128,128]{2,1,0:T(8,128)S(1)}, f32[2,128,128]{2,1,0:T(8,128)S(1)}, u32[]{:S(2)}, u32[]{:S(2)}) collective-permute-start(f32[2,128,128]{2,1,0:T(8,128)S(1)} %fusion.35), channel_id=1, source_target_pairs={{24,152},{56,184},{88,216},{120,248},{152,280},{184,312},{216,344}... | collective-permute-start | bytes 393224 | tf_op jit(solution)/shard_map/ppermute | solution.py:113
  60.9 29.6 %collective-permute-start.4 = (f32[2,128,128]{2,1,0:T(8,128)S(1)}, f32[2,128,128]{2,1,0:T(8,128)S(1)}, u32[]{:S(2)}, u32[]{:S(2)}) collective-permute-start(f32[2,128,128]{2,1,0:T(8,128)S(1)} %convolution_select_fusion.2), channel_id=1, source_target_pairs={{24,152},{56,184},{88,216},{120,248},{152,280},{184,312},{216,344}... | collective-permute-start | bytes 393224 | tf_op jit(solution)/shard_map/ppermute | solution.py:113
  75.6 13.0 %collective-permute-start.27 = (bf16[256,256]{0,1:T(8,128)(2,1)S(1)}, bf16[256,256]{0,1:T(8,128)(2,1)S(1)}, u32[]{:S(2)}, u32[]{:S(2)}) collective-permute-start(bf16[256,256]{0,1:T(8,128)(2,1)S(1)} %collective-permute-done.26), channel_id=1, source_target_pairs={{0,8},{8,16},{16,24},{24,32},{32,40},{40,48},{48,56},{56,64},{64,7... | collective-permute-start | bytes 393224 | tf_op jit(solution)/shard_map/ppermute | solution.py:18
  77.8 13.0 %collective-permute-start.10 = (f32[2,128,128]{2,1,0:T(8,128)S(1)}, f32[2,128,128]{2,1,0:T(8,128)S(1)}, u32[]{:S(2)}, u32[]{:S(2)}) collective-permute-start(f32[2,128,128]{2,1,0:T(8,128)S(1)} %fusion.34), channel_id=1, source_target_pairs={{24,280},{56,312},{88,344},{120,376},{152,408},{184,440},{216,472}... | collective-permute-start | bytes 393224 | tf_op jit(solution)/shard_map/ppermute | solution.py:113
  88.6 7.8 %collective-permute-start.28 = (bf16[256,256]{0,1:T(8,128)(2,1)S(1)}, bf16[256,256]{0,1:T(8,128)(2,1)S(1)}, u32[]{:S(2)}, u32[]{:S(2)}) collective-permute-start(bf16[256,256]{0,1:T(8,128)(2,1)S(1)} %collective-permute-done.27), channel_id=1, source_target_pairs={{0,8},{8,16},{16,24},{24,32},{32,40},{40,48},{48,56},{56,64},{64,7... | collective-permute-start | bytes 393224 | tf_op jit(solution)/shard_map/ppermute | solution.py:18
  91.1 9.1 %collective-permute-start.14 = (f32[2,128,128]{2,1,0:T(8,128)S(1)}, f32[2,128,128]{2,1,0:T(8,128)S(1)}, u32[]{:S(2)}, u32[]{:S(2)}) collective-permute-start(f32[2,128,128]{2,1,0:T(8,128)S(1)} %fusion.33), channel_id=1, source_target_pairs={{24,56},{56,88},{88,120},{120,152},{152,184},{184,216},{216,248},{... | collective-permute-start | bytes 393224 | tf_op jit(solution)/shard_map/ppermute | solution.py:113
  91.8 8.4 %collective-permute-start.13 = (f32[2,128,128]{2,1,0:T(8,128)S(1)}, f32[2,128,128]{2,1,0:T(8,128)S(1)}, u32[]{:S(2)}, u32[]{:S(2)}) collective-permute-start(f32[2,128,128]{2,1,0:T(8,128)S(1)} %fusion.33), channel_id=1, source_target_pairs={{24,48},{56,80},{88,112},{120,144},{152,176},{184,208},{216,240},{... | collective-permute-start | bytes 393224 | tf_op jit(solution)/shard_map/ppermute | solution.py:113
  92.4 7.8 %collective-permute-start.12 = (f32[2,128,128]{2,1,0:T(8,128)S(1)}, f32[2,128,128]{2,1,0:T(8,128)S(1)}, u32[]{:S(2)}, u32[]{:S(2)}) collective-permute-start(f32[2,128,128]{2,1,0:T(8,128)S(1)} %fusion.33), channel_id=1, source_target_pairs={{24,40},{56,72},{88,104},{120,136},{152,168},{184,200},{216,232},{... | collective-permute-start | bytes 393224 | tf_op jit(solution)/shard_map/ppermute | solution.py:113
  93.1 17.4 %collective-permute-start.11 = (f32[2,128,128]{2,1,0:T(8,128)S(1)}, f32[2,128,128]{2,1,0:T(8,128)S(1)}, u32[]{:S(2)}, u32[]{:S(2)}) collective-permute-start(f32[2,128,128]{2,1,0:T(8,128)S(1)} %fusion.33), channel_id=1, source_target_pairs={{24,32},{56,64},{88,96},{120,128},{152,160},{184,192},{216,224},{2... | collective-permute-start | bytes 393224 | tf_op jit(solution)/shard_map/ppermute | solution.py:113
  96.4 22.9 %collective-permute-start.29 = (bf16[256,256]{0,1:T(8,128)(2,1)S(1)}, bf16[256,256]{0,1:T(8,128)(2,1)S(1)}, u32[]{:S(2)}, u32[]{:S(2)}) collective-permute-start(bf16[256,256]{0,1:T(8,128)(2,1)S(1)} %collective-permute-done.28), channel_id=1, source_target_pairs={{0,8},{8,16},{16,24},{24,32},{32,40},{40,48},{48,56},{56,64},{64,7... | collective-permute-start | bytes 393224 | tf_op jit(solution)/shard_map/ppermute | solution.py:18
  115.5 7.8 %collective-permute-start.19 = (bf16[256,256]{0,1:T(8,128)(2,1)S(1)}, bf16[256,256]{0,1:T(8,128)(2,1)S(1)}, u32[]{:S(2)}, u32[]{:S(2)}) collective-permute-start(bf16[256,256]{0,1:T(8,128)(2,1)S(1)} %bitcast.202), channel_id=1, source_target_pairs={{0,8},{8,16},{16,24},{24,32},{32,40},{40,48},{48,56},{56,64},{64,7... | collective-permute-start | bytes 393224 | tf_op jit(solution)/shard_map/ppermute | solution.py:18
  117.4 19.5 %collective-permute-start.15 = (bf16[256,256]{0,1:T(8,128)(2,1)S(1)}, bf16[256,256]{0,1:T(8,128)(2,1)S(1)}, u32[]{:S(2)}, u32[]{:S(2)}) collective-permute-start(bf16[256,256]{0,1:T(8,128)(2,1)S(1)} %bitcast.203), channel_id=1, source_target_pairs={{0,40},{8,48},{16,56},{24,64},{32,72},{40,80},{48,88},{56,96},{64,... | collective-permute-start | bytes 393224 | tf_op jit(solution)/shard_map/ppermute | solution.py:18
  119.4 19.5 %collective-permute-start.30 = (bf16[256,256]{0,1:T(8,128)(2,1)S(1)}, bf16[256,256]{0,1:T(8,128)(2,1)S(1)}, u32[]{:S(2)}, u32[]{:S(2)}) collective-permute-start(bf16[256,256]{0,1:T(8,128)(2,1)S(1)} %collective-permute-done.29), channel_id=1, source_target_pairs={{0,8},{8,16},{16,24},{24,32},{32,40},{40,48},{48,56},{56,64},{64,7... | collective-permute-start | bytes 393224 | tf_op jit(solution)/shard_map/ppermute | solution.py:18
  123.3 26.4 %collective-permute-start.20 = (bf16[256,256]{0,1:T(8,128)(2,1)S(1)}, bf16[256,256]{0,1:T(8,128)(2,1)S(1)}, u32[]{:S(2)}, u32[]{:S(2)}) collective-permute-start(bf16[256,256]{0,1:T(8,128)(2,1)S(1)} %collective-permute-done.19), channel_id=1, source_target_pairs={{0,8},{8,16},{16,24},{24,32},{32,40},{40,48},{48,56},{56,64},{64,7... | collective-permute-start | bytes 393224 | tf_op jit(solution)/shard_map/ppermute | solution.py:18
  136.9 10.1 %collective-permute-start.16 = (bf16[256,256]{0,1:T(8,128)(2,1)S(1)}, bf16[256,256]{0,1:T(8,128)(2,1)S(1)}, u32[]{:S(2)}, u32[]{:S(2)}) collective-permute-start(bf16[256,256]{0,1:T(8,128)(2,1)S(1)} %collective-permute-done.15), channel_id=1, source_target_pairs={{0,8},{8,16},{16,24},{24,32},{32,40},{40,48},{48,56},{56,64},{64,7... | collective-permute-start | bytes 393224 | tf_op jit(solution)/shard_map/ppermute | solution.py:18
  147.0 8.1 %collective-permute-start.17 = (bf16[256,256]{0,1:T(8,128)(2,1)S(1)}, bf16[256,256]{0,1:T(8,128)(2,1)S(1)}, u32[]{:S(2)}, u32[]{:S(2)}) collective-permute-start(bf16[256,256]{0,1:T(8,128)(2,1)S(1)} %collective-permute-done.16), channel_id=1, source_target_pairs={{0,8},{8,16},{16,24},{24,32},{32,40},{40,48},{48,56},{56,64},{64,7... | collective-permute-start | bytes 393224 | tf_op jit(solution)/shard_map/ppermute | solution.py:18
  149.8 9.6 %collective-permute-start.21 = (bf16[256,256]{0,1:T(8,128)(2,1)S(1)}, bf16[256,256]{0,1:T(8,128)(2,1)S(1)}, u32[]{:S(2)}, u32[]{:S(2)}) collective-permute-start(bf16[256,256]{0,1:T(8,128)(2,1)S(1)} %collective-permute-done.20), channel_id=1, source_target_pairs={{0,8},{8,16},{16,24},{24,32},{32,40},{40,48},{48,56},{56,64},{64,7... | collective-permute-start | bytes 393224 | tf_op jit(solution)/shard_map/ppermute | solution.py:18
  155.0 9.4 %collective-permute-start.18 = (bf16[256,256]{0,1:T(8,128)(2,1)S(1)}, bf16[256,256]{0,1:T(8,128)(2,1)S(1)}, u32[]{:S(2)}, u32[]{:S(2)}) collective-permute-start(bf16[256,256]{0,1:T(8,128)(2,1)S(1)} %collective-permute-done.17), channel_id=1, source_target_pairs={{0,8},{8,16},{16,24},{24,32},{32,40},{40,48},{48,56},{56,64},{64,7... | collective-permute-start | bytes 393224 | tf_op jit(solution)/shard_map/ppermute | solution.py:18
  159.3 7.8 %collective-permute-start.22 = (bf16[256,256]{0,1:T(8,128)(2,1)S(1)}, bf16[256,256]{0,1:T(8,128)(2,1)S(1)}, u32[]{:S(2)}, u32[]{:S(2)}) collective-permute-start(bf16[256,256]{0,1:T(8,128)(2,1)S(1)} %collective-permute-done.21), channel_id=1, source_target_pairs={{0,8},{8,16},{16,24},{24,32},{32,40},{40,48},{48,56},{56,64},{64,7... | collective-permute-start | bytes 393224 | tf_op jit(solution)/shard_map/ppermute | solution.py:18
  167.2 23.5 %copy-start.3 = (f32[256]{0:T(256)S(1)}, f32[256]{0:T(256)}, u32[]{:S(2)}) copy-start(f32[256]{0:T(256)} %param.15) | copy-start | bytes 3076

commit v8 on v6

--- a/solution.py
+++ b/solution.py
@@ -172,7 +172,7 @@
                 pieces.append(piece)
         return jnp.concatenate(pieces[::-1] + [own], axis=0)
 
-    rows_all = (window_rows(k_attn, 1), window_rows(delta_out, 2))
+    rows_all = (window_rows(k_attn, 2), window_rows(delta_out, 2))
     block_rows = min(512, tok_rows)
     first_row = lax.axis_index("seq") * tok_rows
     score_scale = 1.0 / math.sqrt(head_size)

time: 190 us -> 195 us (1.026)
  waiting for transfers between devices: 69.4 us -> 61.9 us
  starting transfers between devices: 63 us -> 69.6 us
  other arithmetic: 4.65 us -> 7.34 us
  matrix products: 21.2 us -> 23.6 us
    ppermute x16, waiting for transfers between devices: 58.4 us -> 35.5 us  [shifted(): return lax.ppermute(value, axis, pairs)]
    ppermute x15, waiting for transfers between devices: 11.1 us -> 26.4 us  [moved(): return lax.ppermute(value, 'seq', pairs)]
    ppermute x16, starting transfers between devices: 40.9 us -> 49.3 us  [shifted(): return lax.ppermute(value, axis, pairs)]
    dot_general x1, matrix products: 0.52 us -> 2.93 us  [attend_block(): jnp.einsum('hqk,khd->qhd', weights, near_values, preferred_element_type=j...]
    sub x1, other arithmetic: 2.35 us -> 4.34 us  [attend_block(): exps = jnp.exp(jnp.where(allowed[None], scores - row_top, -1e+30))]
  transfers between devices with their start and end apart: 31 -> 31, of which waited for: 12 -> 8; matrix products, arithmetic and copies ran while one was open for 15% -> 13% of each run, Pallas kernels for 0% -> 0%
where the time goes in v8:
time: 195 us; the launch traced here: 194 us
  starting transfers between devices  69.6 us (36%)
  waiting for transfers between devices  61.9 us (32%)
  blocking collectives  24.3 us (12%)
  matrix products  23.6 us (12%)
  other arithmetic  7.34 us (4%)
  local copies, waits for them, and re-layouts  4.75 us (2%)
    ppermute x16, starting transfers between devices, shifted(): return lax.ppermute(value, axis, pairs)  49.3 us
    ppermute x16, waiting for transfers between devices, shifted(): return lax.ppermute(value, axis, pairs)  35.5 us
    ppermute x15, waiting for transfers between devices, moved(): return lax.ppermute(value, 'seq', pairs)  26.4 us
    psum x1, blocking collectives, on_device(): total_sq = lax.psum(squares, 'head')  24.3 us
    ppermute x15, starting transfers between devices, moved(): return lax.ppermute(value, 'seq', pairs)  20.3 us
    sub x1, other arithmetic, attend_block(): exps = jnp.exp(jnp.where(allowed[None], scores - row_top, -1e+30))  4.34 us
    dot_general x16, matrix products, batched_dot(): return jnp.einsum('hij,hjk->hik', left, right, precision=highest)  4.32 us
  transfers between devices with their start and end apart: 31, of which 8 were waited for; matrix products, arithmetic and copies ran while one was open for 13% of the time, Pallas kernels for 0%

profile of v8, /device:TPU:25, one launch (start us, length us, event | category | flops | bytes accessed | tf_op | source)
XLA Modules:
  0.0 193.6 jit_solution(501186555389898871)
XLA Ops:
  0.7 1.1 copy.58
  1.7 3.5 %collective-permute-start.27 = (bf16[256,256]{0,1:T(8,128)(2,1)S(1)}, bf16[256,256]{0,1:T(8,128)(2,1)S(1)}, u32[]{:S(2)}, u32[]{:S(2)}) collective-permute-start(bf16[256,256]{0,1:T(8,128)(2,1)S(1)} %copy.58), channel_id=1, source_target_pairs={{0,8},{8,16},{16,24},{24,32},{32,40},{40,48},{48,56},{56,64},{64,7... | collective-permute-start | bytes 393224 | tf_op jit(solution)/shard_map/ppermute | solution.py:18
  5.3 10.2 %collective-permute-start.23 = (bf16[256,256]{0,1:T(8,128)(2,1)S(1)}, bf16[256,256]{0,1:T(8,128)(2,1)S(1)}, u32[]{:S(2)}, u32[]{:S(2)}) collective-permute-start(bf16[256,256]{0,1:T(8,128)(2,1)S(1)} %copy.58), channel_id=1, source_target_pairs={{0,40},{8,48},{16,56},{24,64},{32,72},{40,80},{48,88},{56,96},{64,... | collective-permute-start | bytes 393224 | tf_op jit(solution)/shard_map/ppermute | solution.py:18
  15.5 0.8 mul.79
  16.3 1.0 copy.42
  23.3 5.7 %while.30 = (s32[]{:T(128)}, f32[2,128,128]{2,1,0:T(8,128)S(1)}, f32[2,128,128]{2,1,0:T(8,128)S(1)}, f32[4,2,64,128]{3,2,1,0:T(8,128)S(1)}, f32[4,2,64,128]{3,2,...) while((s32[]{:T(128)}, f32[2,128,128]{2,1,0:T(8,128)S(1)}, ...), condition=%wide.region_2.3_spmd.clone, body=%wide.region_1.0_spmd.clone.sunk | while | flops 151126016 | bytes 1837159 | solution.py:74
  29.0 3.5 %collective-permute-start.5 = (f32[2,128,128]{2,1,0:T(8,128)S(1)}, f32[2,128,128]{2,1,0:T(8,128)S(1)}, u32[]{:S(2)}, u32[]{:S(2)}) collective-permute-start(f32[2,128,128]{2,1,0:T(8,128)S(1)} %get-tuple-element.101), channel_id=1, source_target_pairs={{0,8},{8,16},{16,24},{32,40},{40,48},{48,56},{64,72},{72,80},{80,8... | collective-permute-start | bytes 393224 | tf_op jit(solution)/shard_map/ppermute | solution.py:115
  32.5 4.8 %collective-permute-start = (f32[2,128,128]{2,1,0:T(8,128)S(1)}, f32[2,128,128]{2,1,0:T(8,128)S(1)}, u32[]{:S(2)}, u32[]{:S(2)}) collective-permute-start(f32[2,128,128]{2,1,0:T(8,128)S(1)} %get-tuple-element.100), channel_id=1, source_target_pairs={{0,8},{8,16},{16,24},{32,40},{40,48},{48,56},{64,72},{72,80},{80,8... | collective-permute-start | bytes 393224 | tf_op jit(solution)/shard_map/ppermute | solution.py:115
  37.7 2.0 %fusion.46 = pred[256,2304]{0,1:T(8,128)(4,1)} fusion(s32[256]{0:T(256)S(1)} %iota_add_fusion, pred[2304]{0:T(1024)(128)(4,1)S(1)} %add_compare_fusion), kind=kLoop, calls=%fused_computation.52 | loop fusion | flops 2359296 | bytes 593152 | tf_op jit(solution)/shard_map/while/body/eval_jaxpr/and | solution.py:191
  40.5 2.4 %collective-permute-start.6 = (f32[2,128,128]{2,1,0:T(8,128)S(1)}, f32[2,128,128]{2,1,0:T(8,128)S(1)}, u32[]{:S(2)}, u32[]{:S(2)}) collective-permute-start(f32[2,128,128]{2,1,0:T(8,128)S(1)} %fusion.56), channel_id=1, source_target_pairs={{0,16},{8,24},{32,48},{40,56},{64,80},{72,88},{96,112},{104,120},{... | collective-permute-start | bytes 393224 | tf_op jit(solution)/shard_map/ppermute | solution.py:115
  43.2 1.3 collective-permute-start.1
  44.5 2.9 %collective-permute-start.28 = (bf16[256,256]{0,1:T(8,128)(2,1)S(1)}, bf16[256,256]{0,1:T(8,128)(2,1)S(1)}, u32[]{:S(2)}, u32[]{:S(2)}) collective-permute-start(bf16[256,256]{0,1:T(8,128)(2,1)S(1)} %collective-permute-done.27), channel_id=1, source_target_pairs={{0,8},{8,16},{16,24},{24,32},{32,40},{40,48},{48,56},{56,64},{64,7... | collective-permute-start | bytes 393224 | tf_op jit(solution)/shard_map/ppermute | solution.py:18
  47.7 1.9 collective-permute-start.24
  50.1 0.7 collective-permute-start.7
  51.1 0.7 collective-permute-start.2
  52.3 5.2 %collective-permute-start.29 = (bf16[256,256]{0,1:T(8,128)(2,1)S(1)}, bf16[256,256]{0,1:T(8,128)(2,1)S(1)}, u32[]{:S(2)}, u32[]{:S(2)}) collective-permute-start(bf16[256,256]{0,1:T(8,128)(2,1)S(1)} %collective-permute-done.28), channel_id=1, source_target_pairs={{0,8},{8,16},{16,24},{24,32},{32,40},{40,48},{48,56},{56,64},{64,7... | collective-permute-start | bytes 393224 | tf_op jit(solution)/shard_map/ppermute | solution.py:18
  57.6 3.8 %collective-permute-start.25 = (bf16[256,256]{0,1:T(8,128)(2,1)S(1)}, bf16[256,256]{0,1:T(8,128)(2,1)S(1)}, u32[]{:S(2)}, u32[]{:S(2)}) collective-permute-start(bf16[256,256]{0,1:T(8,128)(2,1)S(1)} %collective-permute-done.24), channel_id=1, source_target_pairs={{0,8},{8,16},{16,24},{24,32},{32,40},{40,48},{48,56},{56,64},{64,7... | collective-permute-start | bytes 393224 | tf_op jit(solution)/shard_map/ppermute | solution.py:18
  62.2 0.7 collective-permute-start.8
  63.2 0.7 collective-permute-start.3
  63.9 2.4 %collective-permute-done.29 = bf16[256,256]{0,1:T(8,128)(2,1)S(1)} collective-permute-done((bf16[256,256]{0,1:T(8,128)(2,1)S(1)}, bf16[256,256]{0,1:T(8,128)(2,1)S(1)}, u32[]{:S(2)}, u32[]{:S(2)}) %collective-permute-start.29) | collective-permute-done | bytes 131104 | tf_op jit(solution)/shard_map/ppermute | solution.py:18
  66.3 2.5 %collective-permute-start.30 = (bf16[256,256]{0,1:T(8,128)(2,1)S(1)}, bf16[256,256]{0,1:T(8,128)(2,1)S(1)}, u32[]{:S(2)}, u32[]{:S(2)}) collective-permute-start(bf16[256,256]{0,1:T(8,128)(2,1)S(1)} %collective-permute-done.29), channel_id=1, source_target_pairs={{0,8},{8,16},{16,24},{24,32},{32,40},{40,48},{48,56},{56,64},{64,7... | collective-permute-start | bytes 393224 | tf_op jit(solution)/shard_map/ppermute | solution.py:18
  68.8 1.9 collective-permute-start.26
  71.1 0.7 collective-permute-start.9
  72.0 0.7 collective-permute-start.4
  72.7 8.4 %collective-permute-done.26 = bf16[256,256]{0,1:T(8,128)(2,1)S(1)} collective-permute-done((bf16[256,256]{0,1:T(8,128)(2,1)S(1)}, bf16[256,256]{0,1:T(8,128)(2,1)S(1)}, u32[]{:S(2)}, u32[]{:S(2)}) %collective-permute-start.26) | collective-permute-done | bytes 131104 | tf_op jit(solution)/shard_map/ppermute | solution.py:18
  81.4 1.0 collective-permute-start.10
  84.4 0.7 collective-permute-start.12
  85.1 1.3 collective-permute-start.11
  86.4 26.4 %collective-permute-done.11 = f32[2,128,128]{2,1,0:T(8,128)S(1)} collective-permute-done((f32[2,128,128]{2,1,0:T(8,128)S(1)}, f32[2,128,128]{2,1,0:T(8,128)S(1)}, u32[]{:S(2)}, u32[]{:S(2)}) %collective-permute-start.11) | collective-permute-done | bytes 131104 | tf_op jit(solution)/shard_map/ppermute | solution.py:115
  113.1 4.5 %while.29 = (s32[]{:T(128)}, f32[2,128,128]{2,1,0:T(8,128)S(1)}, bf16[4,2,64,128]{3,2,0,1:T(8,128)(2,1)S(1)}, f32[4,2,64,128]{3,2,1,0:T(8,128)S(1)}, f32[4,2,64,...) while((s32[]{:T(128)}, f32[2,128,128]{2,1,0:T(8,128)S(1)}, ...), condition=%wide.region_5.6_spmd, body=%wide.region_4.5_spmd.sunk | while | flops 88145920 | bytes 1247341 | solution.py:88
  117.8 1.9 collective-permute-start.15
  119.8 1.9 collective-permute-start.19
  121.7 9.9 %collective-permute-done.15 = bf16[256,256]{0,1:T(8,128)(2,1)S(1)} collective-permute-done((bf16[256,256]{0,1:T(8,128)(2,1)S(1)}, bf16[256,256]{0,1:T(8,128)(2,1)S(1)}, u32[]{:S(2)}, u32[]{:S(2)}) %collective-permute-start.15) | collective-permute-done | bytes 131104 | tf_op jit(solution)/shard_map/ppermute | solution.py:18
  131.6 3.9 %collective-permute-start.16 = (bf16[256,256]{0,1:T(8,128)(2,1)S(1)}, bf16[256,256]{0,1:T(8,128)(2,1)S(1)}, u32[]{:S(2)}, u32[]{:S(2)}) collective-permute-start(bf16[256,256]{0,1:T(8,128)(2,1)S(1)} %collective-permute-done.15), channel_id=1, source_target_pairs={{0,8},{8,16},{16,24},{24,32},{32,40},{40,48},{48,56},{56,64},{64,7... | collective-permute-start | bytes 393224 | tf_op jit(solution)/shard_map/ppermute | solution.py:18
  135.5 1.9 collective-permute-start.20
  137.4 4.7 %collective-permute-done.16 = bf16[256,256]{0,1:T(8,128)(2,1)S(1)} collective-permute-done((bf16[256,256]{0,1:T(8,128)(2,1)S(1)}, bf16[256,256]{0,1:T(8,128)(2,1)S(1)}, u32[]{:S(2)}, u32[]{:S(2)}) %collective-permute-start.16) | collective-permute-done | bytes 131104 | tf_op jit(solution)/shard_map/ppermute | solution.py:18
  142.1 1.9 collective-permute-start.17
  144.0 0.8 fusion.39
  144.9 1.9 collective-permute-start.21
  146.8 3.1 %collective-permute-done.17 = bf16[256,256]{0,1:T(8,128)(2,1)S(1)} collective-permute-done((bf16[256,256]{0,1:T(8,128)(2,1)S(1)}, bf16[256,256]{0,1:T(8,128)(2,1)S(1)}, u32[]{:S(2)}, u32[]{:S(2)}) %collective-permute-start.17) | collective-permute-done | bytes 131104 | tf_op jit(solution)/shard_map/ppermute | solution.py:18
  149.9 1.9 collective-permute-start.18
  151.8 4.3 %fusion.91 = (f32[2,256]{1,0:T(2,128)S(1)}, f32[2,256,2304]{1,2,0:T(8,128)}) fusion(f32[2,256,2304]{1,2,0:T(8,128)S(1)} %fusion.39, pred[256,2304]{0,1:T(8,128)(4,1)S(1)} %copy-done.1), kind=kOutput, calls=%fused_computation.150 | output fusion | flops 4720895 | bytes 10029056 | tf_op jit(solution)/shard_map/while/body/eval_jaxpr/sub | solution.py:196
  156.2 0.8 copy.65
  156.9 1.9 collective-permute-start.22
  158.9 6.5 %collective-permute-done.22 = bf16[256,256]{0,1:T(8,128)(2,1)S(1)} collective-permute-done((bf16[256,256]{0,1:T(8,128)(2,1)S(1)}, bf16[256,256]{0,1:T(8,128)(2,1)S(1)}, u32[]{:S(2)}, u32[]{:S(2)}) %collective-permute-start.22) | collective-permute-done | bytes 131104 | tf_op jit(solution)/shard_map/ppermute | solution.py:18
  165.5 2.9 %fusion.57 = (f32[256]{0:T(256)S(1)}, f32[2,128,256]{2,1,0:T(8,128)S(1)}) fusion(bf16[2304,2,128]{0,2,1:T(8,128)(2,1)S(1)} %bitcast.208, f32[2,256,2304]{1,2,0:T(8,128)} %get-tuple-element.199, f32[2,256]{1,0:T(2,128)S(1)} %get-tuple-element.198), kind=kOutput, calls=%fused_computation.86 | convolution fusion | flops 304480000 | bytes 6163456 | tf_op jit(solution)/shard_map/while/body/eval_jaxpr/hqk,khd->qhd/dot_general | solution.py:198
  168.5 24.3 %psum.7 = f32[256]{0:T(256)S(1)} all-reduce(f32[256]{0:T(256)S(1)} %get-tuple-element.200), channel_id=1, replica_groups=mesh['seq'=64,'head'=8] {'head'}, use_global_device_ids=true, to_apply=%region_9.10 | all-reduce | flops 256 | bytes 2048 | tf_op jit(solution)/shard_map/psum | solution.py:206
  192.9 0.8 multiply_convert_fusion
  (161 shorter events, 23.2 us)
Async XLA Ops:
  0.6 143.4 %copy-start = (bf16[256,256]{1,0:T(8,128)(2,1)S(1)}, bf16[256,256]{1,0:T(8,128)(2,1)}, u32[]{:S(2)}) copy-start(bf16[256,256]{1,0:T(8,128)(2,1)} %param.15) | copy-start | bytes 393220
  0.6 16.9 %copy-start.2 = (bf16[256,256]{1,0:T(8,128)(2,1)S(1)}, bf16[256,256]{1,0:T(8,128)(2,1)}, u32[]{:S(2)}) copy-start(bf16[256,256]{1,0:T(8,128)(2,1)} %param.13) | copy-start | bytes 393220
  1.7 42.8 %collective-permute-start.27 = (bf16[256,256]{0,1:T(8,128)(2,1)S(1)}, bf16[256,256]{0,1:T(8,128)(2,1)S(1)}, u32[]{:S(2)}, u32[]{:S(2)}) collective-permute-start(bf16[256,256]{0,1:T(8,128)(2,1)S(1)} %copy.58), channel_id=1, source_target_pairs={{0,8},{8,16},{16,24},{24,32},{32,40},{40,48},{48,56},{56,64},{64,7... | collective-permute-start | bytes 393224 | tf_op jit(solution)/shard_map/ppermute | solution.py:18
  5.3 42.4 %collective-permute-start.23 = (bf16[256,256]{0,1:T(8,128)(2,1)S(1)}, bf16[256,256]{0,1:T(8,128)(2,1)S(1)}, u32[]{:S(2)}, u32[]{:S(2)}) collective-permute-start(bf16[256,256]{0,1:T(8,128)(2,1)S(1)} %copy.58), channel_id=1, source_target_pairs={{0,40},{8,48},{16,56},{24,64},{32,72},{40,80},{48,88},{56,96},{64,... | collective-permute-start | bytes 393224 | tf_op jit(solution)/shard_map/ppermute | solution.py:18
  23.3 14.1 %copy-start.3 = (bf16[256,256]{1,0:T(8,128)(2,1)S(1)}, bf16[256,256]{1,0:T(8,128)(2,1)}, u32[]{:S(2)}) copy-start(bf16[256,256]{1,0:T(8,128)(2,1)} %param.11) | copy-start | bytes 393220
  29.0 11.3 %collective-permute-start.5 = (f32[2,128,128]{2,1,0:T(8,128)S(1)}, f32[2,128,128]{2,1,0:T(8,128)S(1)}, u32[]{:S(2)}, u32[]{:S(2)}) collective-permute-start(f32[2,128,128]{2,1,0:T(8,128)S(1)} %get-tuple-element.101), channel_id=1, source_target_pairs={{0,8},{8,16},{16,24},{32,40},{40,48},{48,56},{64,72},{72,80},{80,8... | collective-permute-start | bytes 393224 | tf_op jit(solution)/shard_map/ppermute | solution.py:115
  32.5 10.4 %collective-permute-start = (f32[2,128,128]{2,1,0:T(8,128)S(1)}, f32[2,128,128]{2,1,0:T(8,128)S(1)}, u32[]{:S(2)}, u32[]{:S(2)}) collective-permute-start(f32[2,128,128]{2,1,0:T(8,128)S(1)} %get-tuple-element.100), channel_id=1, source_target_pairs={{0,8},{8,16},{16,24},{32,40},{40,48},{48,56},{64,72},{72,80},{80,8... | collective-permute-start | bytes 393224 | tf_op jit(solution)/shard_map/ppermute | solution.py:115
  40.5 9.3 %collective-permute-start.6 = (f32[2,128,128]{2,1,0:T(8,128)S(1)}, f32[2,128,128]{2,1,0:T(8,128)S(1)}, u32[]{:S(2)}, u32[]{:S(2)}) collective-permute-start(f32[2,128,128]{2,1,0:T(8,128)S(1)} %fusion.56), channel_id=1, source_target_pairs={{0,16},{8,24},{32,48},{40,56},{64,80},{72,88},{96,112},{104,120},{... | collective-permute-start | bytes 393224 | tf_op jit(solution)/shard_map/ppermute | solution.py:115
  43.2 7.6 %collective-permute-start.1 = (f32[2,128,128]{2,1,0:T(8,128)S(1)}, f32[2,128,128]{2,1,0:T(8,128)S(1)}, u32[]{:S(2)}, u32[]{:S(2)}) collective-permute-start(f32[2,128,128]{2,1,0:T(8,128)S(1)} %convolution_select_fusion.6), channel_id=1, source_target_pairs={{0,16},{8,24},{32,48},{40,56},{64,80},{72,88},{96,112},{104,120},{... | collective-permute-start | bytes 393224 | tf_op jit(solution)/shard_map/ppermute | solution.py:115
  44.5 7.8 %collective-permute-start.28 = (bf16[256,256]{0,1:T(8,128)(2,1)S(1)}, bf16[256,256]{0,1:T(8,128)(2,1)S(1)}, u32[]{:S(2)}, u32[]{:S(2)}) collective-permute-start(bf16[256,256]{0,1:T(8,128)(2,1)S(1)} %collective-permute-done.27), channel_id=1, source_target_pairs={{0,8},{8,16},{16,24},{24,32},{32,40},{40,48},{48,56},{56,64},{64,7... | collective-permute-start | bytes 393224 | tf_op jit(solution)/shard_map/ppermute | solution.py:18
  47.7 9.9 %collective-permute-start.24 = (bf16[256,256]{0,1:T(8,128)(2,1)S(1)}, bf16[256,256]{0,1:T(8,128)(2,1)S(1)}, u32[]{:S(2)}, u32[]{:S(2)}) collective-permute-start(bf16[256,256]{0,1:T(8,128)(2,1)S(1)} %collective-permute-done.23), channel_id=1, source_target_pairs={{0,8},{8,16},{16,24},{24,32},{32,40},{40,48},{48,56},{56,64},{64,7... | collective-permute-start | bytes 393224 | tf_op jit(solution)/shard_map/ppermute | solution.py:18
  50.1 11.8 %collective-permute-start.7 = (f32[2,128,128]{2,1,0:T(8,128)S(1)}, f32[2,128,128]{2,1,0:T(8,128)S(1)}, u32[]{:S(2)}, u32[]{:S(2)}) collective-permute-start(f32[2,128,128]{2,1,0:T(8,128)S(1)} %fusion.55), channel_id=1, source_target_pairs={{24,56},{56,88},{88,120},{120,152},{152,184},{184,216},{216,248},{... | collective-permute-start | bytes 393224 | tf_op jit(solution)/shard_map/ppermute | solution.py:115
  51.1 11.8 %collective-permute-start.2 = (f32[2,128,128]{2,1,0:T(8,128)S(1)}, f32[2,128,128]{2,1,0:T(8,128)S(1)}, u32[]{:S(2)}, u32[]{:S(2)}) collective-permute-start(f32[2,128,128]{2,1,0:T(8,128)S(1)} %convolution_select_fusion.4), channel_id=1, source_target_pairs={{24,56},{56,88},{88,120},{120,152},{152,184},{184,216},{216,248},{... | collective-permute-start | bytes 393224 | tf_op jit(solution)/shard_map/ppermute | solution.py:115
  52.3 18.7 %copy-start.5 = (bf16[256,256]{0,1:T(8,128)(2,1)}, bf16[256,256]{0,1:T(8,128)(2,1)S(1)}, u32[]{:S(2)}) copy-start(bf16[256,256]{0,1:T(8,128)(2,1)S(1)} %collective-permute-done.28) | copy-start | bytes 393220
  52.3 14.0 %collective-permute-start.29 = (bf16[256,256]{0,1:T(8,128)(2,1)S(1)}, bf16[256,256]{0,1:T(8,128)(2,1)S(1)}, u32[]{:S(2)}, u32[]{:S(2)}) collective-permute-start(bf16[256,256]{0,1:T(8,128)(2,1)S(1)} %collective-permute-done.28), channel_id=1, source_target_pairs={{0,8},{8,16},{16,24},{24,32},{32,40},{40,48},{48,56},{56,64},{64,7... | collective-permute-start | bytes 393224 | tf_op jit(solution)/shard_map/ppermute | solution.py:18
  57.6 11.2 %collective-permute-start.25 = (bf16[256,256]{0,1:T(8,128)(2,1)S(1)}, bf16[256,256]{0,1:T(8,128)(2,1)S(1)}, u32[]{:S(2)}, u32[]{:S(2)}) collective-permute-start(bf16[256,256]{0,1:T(8,128)(2,1)S(1)} %collective-permute-done.24), channel_id=1, source_target_pairs={{0,8},{8,16},{16,24},{24,32},{32,40},{40,48},{48,56},{56,64},{64,7... | collective-permute-start | bytes 393224 | tf_op jit(solution)/shard_map/ppermute | solution.py:18
  62.2 8.5 %collective-permute-start.8 = (f32[2,128,128]{2,1,0:T(8,128)S(1)}, f32[2,128,128]{2,1,0:T(8,128)S(1)}, u32[]{:S(2)}, u32[]{:S(2)}) collective-permute-start(f32[2,128,128]{2,1,0:T(8,128)S(1)} %fusion.54), channel_id=1, source_target_pairs={{24,88},{56,120},{88,152},{120,184},{152,216},{184,248},{216,280},... | collective-permute-start | bytes 393224 | tf_op jit(solution)/shard_map/ppermute | solution.py:115
  63.2 8.5 %collective-permute-start.3 = (f32[2,128,128]{2,1,0:T(8,128)S(1)}, f32[2,128,128]{2,1,0:T(8,128)S(1)}, u32[]{:S(2)}, u32[]{:S(2)}) collective-permute-start(f32[2,128,128]{2,1,0:T(8,128)S(1)} %convolution_select_fusion.3), channel_id=1, source_target_pairs={{24,88},{56,120},{88,152},{120,184},{152,216},{184,248},{216,280},... | collective-permute-start | bytes 393224 | tf_op jit(solution)/shard_map/ppermute | solution.py:115
  66.3 16.4 %copy-start.7 = (bf16[256,256]{0,1:T(8,128)(2,1)}, bf16[256,256]{0,1:T(8,128)(2,1)S(1)}, u32[]{:S(2)}) copy-start(bf16[256,256]{0,1:T(8,128)(2,1)S(1)} %collective-permute-done.29) | copy-start | bytes 393220
  66.3 20.1 %collective-permute-start.30 = (bf16[256,256]{0,1:T(8,128)(2,1)S(1)}, bf16[256,256]{0,1:T(8,128)(2,1)S(1)}, u32[]{:S(2)}, u32[]{:S(2)}) collective-permute-start(bf16[256,256]{0,1:T(8,128)(2,1)S(1)} %collective-permute-done.29), channel_id=1, source_target_pairs={{0,8},{8,16},{16,24},{24,32},{32,40},{40,48},{48,56},{56,64},{64,7... | collective-permute-start | bytes 393224 | tf_op jit(solution)/shard_map/ppermute | solution.py:18
  68.8 12.3 %collective-permute-start.26 = (bf16[256,256]{0,1:T(8,128)(2,1)S(1)}, bf16[256,256]{0,1:T(8,128)(2,1)S(1)}, u32[]{:S(2)}, u32[]{:S(2)}) collective-permute-start(bf16[256,256]{0,1:T(8,128)(2,1)S(1)} %collective-permute-done.25), channel_id=1, source_target_pairs={{0,8},{8,16},{16,24},{24,32},{32,40},{40,48},{48,56},{56,64},{64,7... | collective-permute-start | bytes 393224 | tf_op jit(solution)/shard_map/ppermute | solution.py:18
  71.1 10.1 %collective-permute-start.9 = (f32[2,128,128]{2,1,0:T(8,128)S(1)}, f32[2,128,128]{2,1,0:T(8,128)S(1)}, u32[]{:S(2)}, u32[]{:S(2)}) collective-permute-start(f32[2,128,128]{2,1,0:T(8,128)S(1)} %fusion.53), channel_id=1, source_target_pairs={{24,152},{56,184},{88,216},{120,248},{152,280},{184,312},{216,344}... | collective-permute-start | bytes 393224 | tf_op jit(solution)/shard_map/ppermute | solution.py:115
  72.0 10.4 %collective-permute-start.4 = (f32[2,128,128]{2,1,0:T(8,128)S(1)}, f32[2,128,128]{2,1,0:T(8,128)S(1)}, u32[]{:S(2)}, u32[]{:S(2)}) collective-permute-start(f32[2,128,128]{2,1,0:T(8,128)S(1)} %convolution_select_fusion.2), channel_id=1, source_target_pairs={{24,152},{56,184},{88,216},{120,248},{152,280},{184,312},{216,344}... | collective-permute-start | bytes 393224 | tf_op jit(solution)/shard_map/ppermute | solution.py:115
  81.4 31.7 %copy-start.4 = (bf16[4,2,64,128]{3,2,0,1:T(8,128)(2,1)S(1)}, bf16[4,2,64,128]{3,2,0,1:T(8,128)(2,1)}, u32[]{:S(2)}) copy-start(bf16[4,2,64,128]{3,2,0,1:T(8,128)(2,1)} %custom-call.3) | copy-start | bytes 393220
  81.4 1.3 collective-permute-start.10
  83.0 3.4 %collective-permute-start.14 = (f32[2,128,128]{2,1,0:T(8,128)S(1)}, f32[2,128,128]{2,1,0:T(8,128)S(1)}, u32[]{:S(2)}, u32[]{:S(2)}) collective-permute-start(f32[2,128,128]{2,1,0:T(8,128)S(1)} %fusion.51), channel_id=1, source_target_pairs={{24,56},{56,88},{88,120},{120,152},{152,184},{184,216},{216,248},{... | collective-permute-start | bytes 393224 | tf_op jit(solution)/shard_map/ppermute | solution.py:115
  83.7 2.7 %collective-permute-start.13 = (f32[2,128,128]{2,1,0:T(8,128)S(1)}, f32[2,128,128]{2,1,0:T(8,128)S(1)}, u32[]{:S(2)}, u32[]{:S(2)}) collective-permute-start(f32[2,128,128]{2,1,0:T(8,128)S(1)} %fusion.51), channel_id=1, source_target_pairs={{24,48},{56,80},{88,112},{120,144},{152,176},{184,208},{216,240},{... | collective-permute-start | bytes 393224 | tf_op jit(solution)/shard_map/ppermute | solution.py:115
  84.4 2.0 %collective-permute-start.12 = (f32[2,128,128]{2,1,0:T(8,128)S(1)}, f32[2,128,128]{2,1,0:T(8,128)S(1)}, u32[]{:S(2)}, u32[]{:S(2)}) collective-permute-start(f32[2,128,128]{2,1,0:T(8,128)S(1)} %fusion.51), channel_id=1, source_target_pairs={{24,40},{56,72},{88,104},{120,136},{152,168},{184,200},{216,232},{... | collective-permute-start | bytes 393224 | tf_op jit(solution)/shard_map/ppermute | solution.py:115
  85.1 27.8 %collective-permute-start.11 = (f32[2,128,128]{2,1,0:T(8,128)S(1)}, f32[2,128,128]{2,1,0:T(8,128)S(1)}, u32[]{:S(2)}, u32[]{:S(2)}) collective-permute-start(f32[2,128,128]{2,1,0:T(8,128)S(1)} %fusion.51), channel_id=1, source_target_pairs={{24,32},{56,64},{88,96},{120,128},{152,160},{184,192},{216,224},{2... | collective-permute-start | bytes 393224 | tf_op jit(solution)/shard_map/ppermute | solution.py:115
  113.1 6.6 %copy-start.8 = (bf16[256,256]{0,1:T(8,128)(2,1)S(1)}, bf16[256,256]{0,1:T(8,128)(2,1)}, u32[]{:S(2)}) copy-start(bf16[256,256]{0,1:T(8,128)(2,1)} %copy-done.7) | copy-start | bytes 393220
  113.1 6.6 %copy-start.6 = (bf16[256,256]{0,1:T(8,128)(2,1)S(1)}, bf16[256,256]{0,1:T(8,128)(2,1)}, u32[]{:S(2)}) copy-start(bf16[256,256]{0,1:T(8,128)(2,1)} %copy-done.5) | copy-start | bytes 393220
  117.8 13.8 %collective-permute-start.15 = (bf16[256,256]{0,1:T(8,128)(2,1)S(1)}, bf16[256,256]{0,1:T(8,128)(2,1)S(1)}, u32[]{:S(2)}, u32[]{:S(2)}) collective-permute-start(bf16[256,256]{0,1:T(8,128)(2,1)S(1)} %bitcast.200), channel_id=1, source_target_pairs={{0,40},{8,48},{16,56},{24,64},{32,72},{40,80},{48,88},{56,96},{64,... | collective-permute-start | bytes 393224 | tf_op jit(solution)/shard_map/ppermute | solution.py:18
  119.8 15.7 %collective-permute-start.19 = (bf16[256,256]{0,1:T(8,128)(2,1)S(1)}, bf16[256,256]{0,1:T(8,128)(2,1)S(1)}, u32[]{:S(2)}, u32[]{:S(2)}) collective-permute-start(bf16[256,256]{0,1:T(8,128)(2,1)S(1)} %bitcast.201), channel_id=1, source_target_pairs={{0,8},{8,16},{16,24},{24,32},{32,40},{40,48},{48,56},{56,64},{64,7... | collective-permute-start | bytes 393224 | tf_op jit(solution)/shard_map/ppermute | solution.py:18
  131.6 10.6 %collective-permute-start.16 = (bf16[256,256]{0,1:T(8,128)(2,1)S(1)}, bf16[256,256]{0,1:T(8,128)(2,1)S(1)}, u32[]{:S(2)}, u32[]{:S(2)}) collective-permute-start(bf16[256,256]{0,1:T(8,128)(2,1)S(1)} %collective-permute-done.15), channel_id=1, source_target_pairs={{0,8},{8,16},{16,24},{24,32},{32,40},{40,48},{48,56},{56,64},{64,7... | collective-permute-start | bytes 393224 | tf_op jit(solution)/shard_map/ppermute | solution.py:18
  135.5 9.4 %collective-permute-start.20 = (bf16[256,256]{0,1:T(8,128)(2,1)S(1)}, bf16[256,256]{0,1:T(8,128)(2,1)S(1)}, u32[]{:S(2)}, u32[]{:S(2)}) collective-permute-start(bf16[256,256]{0,1:T(8,128)(2,1)S(1)} %collective-permute-done.19), channel_id=1, source_target_pairs={{0,8},{8,16},{16,24},{24,32},{32,40},{40,48},{48,56},{56,64},{64,7... | collective-permute-start | bytes 393224 | tf_op jit(solution)/shard_map/ppermute | solution.py:18
  142.1 7.8 %collective-permute-start.17 = (bf16[256,256]{0,1:T(8,128)(2,1)S(1)}, bf16[256,256]{0,1:T(8,128)(2,1)S(1)}, u32[]{:S(2)}, u32[]{:S(2)}) collective-permute-start(bf16[256,256]{0,1:T(8,128)(2,1)S(1)} %collective-permute-done.16), channel_id=1, source_target_pairs={{0,8},{8,16},{16,24},{24,32},{32,40},{40,48},{48,56},{56,64},{64,7... | collective-permute-start | bytes 393224 | tf_op jit(solution)/shard_map/ppermute | solution.py:18
  144.0 7.8 %copy-start.1 = (pred[256,2304]{0,1:T(8,128)(4,1)S(1)}, pred[256,2304]{0,1:T(8,128)(4,1)}, u32[]{:S(2)}) copy-start(pred[256,2304]{0,1:T(8,128)(4,1)} %fusion.46) | copy-start | bytes 1769476
  144.9 12.1 %collective-permute-start.21 = (bf16[256,256]{0,1:T(8,128)(2,1)S(1)}, bf16[256,256]{0,1:T(8,128)(2,1)S(1)}, u32[]{:S(2)}, u32[]{:S(2)}) collective-permute-start(bf16[256,256]{0,1:T(8,128)(2,1)S(1)} %collective-permute-done.20), channel_id=1, source_target_pairs={{0,8},{8,16},{16,24},{24,32},{32,40},{40,48},{48,56},{56,64},{64,7... | collective-permute-start | bytes 393224 | tf_op jit(solution)/shard_map/ppermute | solution.py:18
  149.9 8.9 %collective-permute-start.18 = (bf16[256,256]{0,1:T(8,128)(2,1)S(1)}, bf16[256,256]{0,1:T(8,128)(2,1)S(1)}, u32[]{:S(2)}, u32[]{:S(2)}) collective-permute-start(bf16[256,256]{0,1:T(8,128)(2,1)S(1)} %collective-permute-done.17), channel_id=1, source_target_pairs={{0,8},{8,16},{16,24},{24,32},{32,40},{40,48},{48,56},{56,64},{64,7... | collective-permute-start | bytes 393224 | tf_op jit(solution)/shard_map/ppermute | solution.py:18
  156.9 8.5 %collective-permute-start.22 = (bf16[256,256]{0,1:T(8,128)(2,1)S(1)}, bf16[256,256]{0,1:T(8,128)(2,1)S(1)}, u32[]{:S(2)}, u32[]{:S(2)}) collective-permute-start(bf16[256,256]{0,1:T(8,128)(2,1)S(1)} %collective-permute-done.21), channel_id=1, source_target_pairs={{0,8},{8,16},{16,24},{24,32},{32,40},{40,48},{48,56},{56,64},{64,7... | collective-permute-start | bytes 393224 | tf_op jit(solution)/shard_map/ppermute | solution.py:18
  165.5 27.4 %copy-start.9 = (f32[256]{0:T(256)S(1)}, f32[256]{0:T(256)}, u32[]{:S(2)}) copy-start(f32[256]{0:T(256)} %param.17) | copy-start | bytes 3076

commit v9 on v6

--- a/solution.py
+++ b/solution.py
@@ -203,7 +203,12 @@
     starts = jnp.arange(tok_rows // block_rows) * block_rows
     attended = lax.map(attend_block, starts).reshape(tok_rows, features)
     squares = jnp.sum(attended * attended, axis=1)
-    total_sq = lax.psum(squares, "head")
+    head_count = lax.axis_size("head")
+    pair_sq = squares + lax.ppermute(squares, "head", [(i, i ^ 1) for i in range(head_count)])
+    total_sq = pair_sq
+    for offset in range(2, head_count, 2):
+        pairs = [(i, (i + offset) % head_count) for i in range(head_count)]
+        total_sq = total_sq + lax.ppermute(pair_sq, "head", pairs)
     scale_rows = lax.rsqrt(total_sq / (features * lax.axis_size("head")) + 1e-06)
     normed_out = (attended * out_gain[None, :] * scale_rows[:, None]).astype(jnp.bfloat16)
     return (delta_out, normed_out)

time: 190 us -> 195 us (1.026)
  the two profiles are of different devices: /device:TPU:25 before, /device:TPU:16 now
where the time goes in v9:
time: 195 us; the launch traced here: 194 us
  waiting for transfers between devices  87.7 us (45%)
  starting transfers between devices  73.8 us (38%)
  matrix products  21.3 us (11%)
  local copies, waits for them, and re-layouts  4.72 us (2%)
  other arithmetic  4.64 us (2%)
    ppermute x16, waiting for transfers between devices, shifted(): return lax.ppermute(value, axis, pairs)  74.8 us
    ppermute x16, starting transfers between devices, shifted(): return lax.ppermute(value, axis, pairs)  37.7 us
    ppermute x15, starting transfers between devices, moved(): return lax.ppermute(value, 'seq', pairs)  23.8 us
    ppermute x3, starting transfers between devices, on_device(): total_sq = total_sq + lax.ppermute(pair_sq, 'head', pairs)  10.4 us
    ppermute x15, waiting for transfers between devices, moved(): return lax.ppermute(value, 'seq', pairs)  8.76 us
    dot_general x16, matrix products, batched_dot(): return jnp.einsum('hij,hjk->hik', left, right, precision=highest)  4.34 us
  transfers between devices with their start and end apart: 35, of which 15 were waited for; matrix products, arithmetic and copies ran while one was open for 14% of the time, Pallas kernels for 0%

profile of v9, /device:TPU:16, one launch (start us, length us, event | category | flops | bytes accessed | tf_op | source)
XLA Modules:
  0.0 194.3 jit_solution(9384924245963004372)
XLA Ops:
  0.7 1.1 copy.57
  1.7 3.8 %collective-permute-start.23 = (bf16[256,256]{0,1:T(8,128)(2,1)S(1)}, bf16[256,256]{0,1:T(8,128)(2,1)S(1)}, u32[]{:S(2)}, u32[]{:S(2)}) collective-permute-start(bf16[256,256]{0,1:T(8,128)(2,1)S(1)} %copy.57), channel_id=1, source_target_pairs={{0,8},{8,16},{16,24},{24,32},{32,40},{40,48},{48,56},{56,64},{64,7... | collective-permute-start | bytes 393224 | tf_op jit(solution)/shard_map/ppermute | solution.py:18
  5.6 0.8 mul.79
  6.4 1.0 copy.41
  13.4 5.7 %while.30 = (s32[]{:T(128)}, f32[2,128,128]{2,1,0:T(8,128)S(1)}, f32[2,128,128]{2,1,0:T(8,128)S(1)}, f32[4,2,64,128]{3,2,1,0:T(8,128)S(1)}, f32[4,2,64,128]{3,2,...) while((s32[]{:T(128)}, f32[2,128,128]{2,1,0:T(8,128)S(1)}, ...), condition=%wide.region_2.3_spmd.clone, body=%wide.region_1.0_spmd.clone.sunk | while | flops 151126016 | bytes 1837159 | solution.py:74
  19.1 3.8 %collective-permute-start.5 = (f32[2,128,128]{2,1,0:T(8,128)S(1)}, f32[2,128,128]{2,1,0:T(8,128)S(1)}, u32[]{:S(2)}, u32[]{:S(2)}) collective-permute-start(f32[2,128,128]{2,1,0:T(8,128)S(1)} %get-tuple-element.101), channel_id=1, source_target_pairs={{0,8},{8,16},{16,24},{32,40},{40,48},{48,56},{64,72},{72,80},{80,8... | collective-permute-start | bytes 393224 | tf_op jit(solution)/shard_map/ppermute | solution.py:115
  22.9 3.8 %collective-permute-start = (f32[2,128,128]{2,1,0:T(8,128)S(1)}, f32[2,128,128]{2,1,0:T(8,128)S(1)}, u32[]{:S(2)}, u32[]{:S(2)}) collective-permute-start(f32[2,128,128]{2,1,0:T(8,128)S(1)} %get-tuple-element.100), channel_id=1, source_target_pairs={{0,8},{8,16},{16,24},{32,40},{40,48},{48,56},{64,72},{72,80},{80,8... | collective-permute-start | bytes 393224 | tf_op jit(solution)/shard_map/ppermute | solution.py:115
  28.0 5.0 %collective-permute-start.6 = (f32[2,128,128]{2,1,0:T(8,128)S(1)}, f32[2,128,128]{2,1,0:T(8,128)S(1)}, u32[]{:S(2)}, u32[]{:S(2)}) collective-permute-start(f32[2,128,128]{2,1,0:T(8,128)S(1)} %fusion.56), channel_id=1, source_target_pairs={{0,16},{8,24},{32,48},{40,56},{64,80},{72,88},{96,112},{104,120},{... | collective-permute-start | bytes 393224 | tf_op jit(solution)/shard_map/ppermute | solution.py:115
  33.3 3.1 %collective-permute-start.1 = (f32[2,128,128]{2,1,0:T(8,128)S(1)}, f32[2,128,128]{2,1,0:T(8,128)S(1)}, u32[]{:S(2)}, u32[]{:S(2)}) collective-permute-start(f32[2,128,128]{2,1,0:T(8,128)S(1)} %convolution_select_fusion.6), channel_id=1, source_target_pairs={{0,16},{8,24},{32,48},{40,56},{64,80},{72,88},{96,112},{104,120},{... | collective-permute-start | bytes 393224 | tf_op jit(solution)/shard_map/ppermute | solution.py:115
  36.7 2.8 %collective-permute-start.24 = (bf16[256,256]{0,1:T(8,128)(2,1)S(1)}, bf16[256,256]{0,1:T(8,128)(2,1)S(1)}, u32[]{:S(2)}, u32[]{:S(2)}) collective-permute-start(bf16[256,256]{0,1:T(8,128)(2,1)S(1)} %collective-permute-done.23), channel_id=1, source_target_pairs={{0,8},{8,16},{16,24},{24,32},{32,40},{40,48},{48,56},{56,64},{64,7... | collective-permute-start | bytes 393224 | tf_op jit(solution)/shard_map/ppermute | solution.py:18
  41.7 4.0 %collective-permute-done.24 = bf16[256,256]{0,1:T(8,128)(2,1)S(1)} collective-permute-done((bf16[256,256]{0,1:T(8,128)(2,1)S(1)}, bf16[256,256]{0,1:T(8,128)(2,1)S(1)}, u32[]{:S(2)}, u32[]{:S(2)}) %collective-permute-start.24) | collective-permute-done | bytes 131104 | tf_op jit(solution)/shard_map/ppermute | solution.py:18
  45.7 3.3 %collective-permute-start.25 = (bf16[256,256]{0,1:T(8,128)(2,1)S(1)}, bf16[256,256]{0,1:T(8,128)(2,1)S(1)}, u32[]{:S(2)}, u32[]{:S(2)}) collective-permute-start(bf16[256,256]{0,1:T(8,128)(2,1)S(1)} %collective-permute-done.24), channel_id=1, source_target_pairs={{0,8},{8,16},{16,24},{24,32},{32,40},{40,48},{48,56},{56,64},{64,7... | collective-permute-start | bytes 393224 | tf_op jit(solution)/shard_map/ppermute | solution.py:18
  51.2 14.4 %collective-permute-done.25 = bf16[256,256]{0,1:T(8,128)(2,1)S(1)} collective-permute-done((bf16[256,256]{0,1:T(8,128)(2,1)S(1)}, bf16[256,256]{0,1:T(8,128)(2,1)S(1)}, u32[]{:S(2)}, u32[]{:S(2)}) %collective-permute-start.25) | collective-permute-done | bytes 131104 | tf_op jit(solution)/shard_map/ppermute | solution.py:18
  65.6 1.9 collective-permute-start.26
  69.5 14.2 %collective-permute-done.26 = bf16[256,256]{0,1:T(8,128)(2,1)S(1)} collective-permute-done((bf16[256,256]{0,1:T(8,128)(2,1)S(1)}, bf16[256,256]{0,1:T(8,128)(2,1)S(1)}, u32[]{:S(2)}, u32[]{:S(2)}) %collective-permute-start.26) | collective-permute-done | bytes 131104 | tf_op jit(solution)/shard_map/ppermute | solution.py:18
  83.7 1.9 collective-permute-start.27
  86.6 8.4 %collective-permute-done.27 = bf16[256,256]{0,1:T(8,128)(2,1)S(1)} collective-permute-done((bf16[256,256]{0,1:T(8,128)(2,1)S(1)}, bf16[256,256]{0,1:T(8,128)(2,1)S(1)}, u32[]{:S(2)}, u32[]{:S(2)}) %collective-permute-start.27) | collective-permute-done | bytes 131104 | tf_op jit(solution)/shard_map/ppermute | solution.py:18
  95.0 1.9 collective-permute-start.28
  99.5 1.3 collective-permute-start.11
  101.1 4.2 %collective-permute-done.28 = bf16[256,256]{0,1:T(8,128)(2,1)S(1)} collective-permute-done((bf16[256,256]{0,1:T(8,128)(2,1)S(1)}, bf16[256,256]{0,1:T(8,128)(2,1)S(1)}, u32[]{:S(2)}, u32[]{:S(2)}) %collective-permute-start.28) | collective-permute-done | bytes 131104 | tf_op jit(solution)/shard_map/ppermute | solution.py:18
  105.3 2.1 %collective-permute-start.29 = (bf16[256,256]{0,1:T(8,128)(2,1)S(1)}, bf16[256,256]{0,1:T(8,128)(2,1)S(1)}, u32[]{:S(2)}, u32[]{:S(2)}) collective-permute-start(bf16[256,256]{0,1:T(8,128)(2,1)S(1)} %collective-permute-done.28), channel_id=1, source_target_pairs={{0,8},{8,16},{16,24},{24,32},{32,40},{40,48},{48,56},{56,64},{64,7... | collective-permute-start | bytes 393224 | tf_op jit(solution)/shard_map/ppermute | solution.py:18
  107.4 8.7 %collective-permute-done.11 = f32[2,128,128]{2,1,0:T(8,128)S(1)} collective-permute-done((f32[2,128,128]{2,1,0:T(8,128)S(1)}, f32[2,128,128]{2,1,0:T(8,128)S(1)}, u32[]{:S(2)}, u32[]{:S(2)}) %collective-permute-start.11) | collective-permute-done | bytes 131104 | tf_op jit(solution)/shard_map/ppermute | solution.py:115
  116.4 4.5 %while.29 = (s32[]{:T(128)}, f32[2,128,128]{2,1,0:T(8,128)S(1)}, bf16[4,2,64,128]{3,2,0,1:T(8,128)(2,1)S(1)}, f32[4,2,64,128]{3,2,1,0:T(8,128)S(1)}, f32[4,2,64,...) while((s32[]{:T(128)}, f32[2,128,128]{2,1,0:T(8,128)S(1)}, ...), condition=%wide.region_5.6_spmd, body=%wide.region_4.5_spmd.sunk | while | flops 88145920 | bytes 1247341 | solution.py:88
  121.1 2.0 %collective-permute-start.19 = (bf16[256,256]{0,1:T(8,128)(2,1)S(1)}, bf16[256,256]{0,1:T(8,128)(2,1)S(1)}, u32[]{:S(2)}, u32[]{:S(2)}) collective-permute-start(bf16[256,256]{0,1:T(8,128)(2,1)S(1)} %bitcast.200), channel_id=1, source_target_pairs={{0,8},{8,16},{16,24},{24,32},{32,40},{40,48},{48,56},{56,64},{64,7... | collective-permute-start | bytes 393224 | tf_op jit(solution)/shard_map/ppermute | solution.py:18
  123.0 3.4 %collective-permute-start.15 = (bf16[256,256]{0,1:T(8,128)(2,1)S(1)}, bf16[256,256]{0,1:T(8,128)(2,1)S(1)}, u32[]{:S(2)}, u32[]{:S(2)}) collective-permute-start(bf16[256,256]{0,1:T(8,128)(2,1)S(1)} %bitcast.201), channel_id=1, source_target_pairs={{0,40},{8,48},{16,56},{24,64},{32,72},{40,80},{48,88},{56,96},{64,... | collective-permute-start | bytes 393224 | tf_op jit(solution)/shard_map/ppermute | solution.py:18
  126.4 2.4 %collective-permute-start.30 = (bf16[256,256]{0,1:T(8,128)(2,1)S(1)}, bf16[256,256]{0,1:T(8,128)(2,1)S(1)}, u32[]{:S(2)}, u32[]{:S(2)}) collective-permute-start(bf16[256,256]{0,1:T(8,128)(2,1)S(1)} %collective-permute-done.29), channel_id=1, source_target_pairs={{0,8},{8,16},{16,24},{24,32},{32,40},{40,48},{48,56},{56,64},{64,7... | collective-permute-start | bytes 393224 | tf_op jit(solution)/shard_map/ppermute | solution.py:18
  128.9 1.3 fusion.46
  130.1 4.4 %collective-permute-done.19 = bf16[256,256]{0,1:T(8,128)(2,1)S(1)} collective-permute-done((bf16[256,256]{0,1:T(8,128)(2,1)S(1)}, bf16[256,256]{0,1:T(8,128)(2,1)S(1)}, u32[]{:S(2)}, u32[]{:S(2)}) %collective-permute-start.19) | collective-permute-done | bytes 131104 | tf_op jit(solution)/shard_map/ppermute | solution.py:18
  134.6 1.9 collective-permute-start.20
  136.5 6.9 %collective-permute-done.15 = bf16[256,256]{0,1:T(8,128)(2,1)S(1)} collective-permute-done((bf16[256,256]{0,1:T(8,128)(2,1)S(1)}, bf16[256,256]{0,1:T(8,128)(2,1)S(1)}, u32[]{:S(2)}, u32[]{:S(2)}) %collective-permute-start.15) | collective-permute-done | bytes 131104 | tf_op jit(solution)/shard_map/ppermute | solution.py:18
  143.4 1.9 collective-permute-start.16
  145.5 6.9 %collective-permute-done.16 = bf16[256,256]{0,1:T(8,128)(2,1)S(1)} collective-permute-done((bf16[256,256]{0,1:T(8,128)(2,1)S(1)}, bf16[256,256]{0,1:T(8,128)(2,1)S(1)}, u32[]{:S(2)}, u32[]{:S(2)}) %collective-permute-start.16) | collective-permute-done | bytes 131104 | tf_op jit(solution)/shard_map/ppermute | solution.py:18
  152.3 1.9 collective-permute-start.17
  154.2 0.8 fusion.39
  155.1 1.9 collective-permute-start.21
  157.0 5.2 %collective-permute-done.17 = bf16[256,256]{0,1:T(8,128)(2,1)S(1)} collective-permute-done((bf16[256,256]{0,1:T(8,128)(2,1)S(1)}, bf16[256,256]{0,1:T(8,128)(2,1)S(1)}, u32[]{:S(2)}, u32[]{:S(2)}) %collective-permute-start.17) | collective-permute-done | bytes 131104 | tf_op jit(solution)/shard_map/ppermute | solution.py:18
  162.2 1.9 collective-permute-start.18
  164.1 2.3 %fusion.91 = (f32[2,256]{1,0:T(2,128)S(1)}, f32[2,256,2304]{1,2,0:T(8,128)S(1)}) fusion(f32[2,256,2304]{1,2,0:T(8,128)S(1)} %fusion.39, pred[256,2304]{0,1:T(8,128)(4,1)S(1)} %fusion.46), kind=kOutput, calls=%fused_computation.150 | output fusion | flops 4720895 | bytes 10029056 | tf_op jit(solution)/shard_map/while/body/eval_jaxpr/sub | solution.py:196
  166.5 2.6 %collective-permute-start.22 = (bf16[256,256]{0,1:T(8,128)(2,1)S(1)}, bf16[256,256]{0,1:T(8,128)(2,1)S(1)}, u32[]{:S(2)}, u32[]{:S(2)}) collective-permute-start(bf16[256,256]{0,1:T(8,128)(2,1)S(1)} %collective-permute-done.21), channel_id=1, source_target_pairs={{0,8},{8,16},{16,24},{24,32},{32,40},{40,48},{48,56},{56,64},{64,7... | collective-permute-start | bytes 393224 | tf_op jit(solution)/shard_map/ppermute | solution.py:18
  169.1 2.0 %collective-permute-done.18 = bf16[256,256]{0,1:T(8,128)(2,1)S(1)} collective-permute-done((bf16[256,256]{0,1:T(8,128)(2,1)S(1)}, bf16[256,256]{0,1:T(8,128)(2,1)S(1)}, u32[]{:S(2)}, u32[]{:S(2)}) %collective-permute-start.18) | collective-permute-done | bytes 131104 | tf_op jit(solution)/shard_map/ppermute | solution.py:18
  171.3 4.2 %collective-permute-done.22 = bf16[256,256]{0,1:T(8,128)(2,1)S(1)} collective-permute-done((bf16[256,256]{0,1:T(8,128)(2,1)S(1)}, bf16[256,256]{0,1:T(8,128)(2,1)S(1)}, u32[]{:S(2)}, u32[]{:S(2)}) %collective-permute-start.22) | collective-permute-done | bytes 131104 | tf_op jit(solution)/shard_map/ppermute | solution.py:18
  176.2 1.9 collective-permute-start.31
  178.1 1.1 collective-permute-done.31
  179.2 4.7 %collective-permute-start.34 = (f32[256]{0:T(256)S(1)}, f32[256]{0:T(256)S(1)}, u32[]{:S(2)}, u32[]{:S(2)}) collective-permute-start(f32[256]{0:T(256)S(1)} %add.164), channel_id=1, source_target_pairs={{0,6},{1,7},{2,0},{3,1},{4,2},{5,3},{6,4},{7,5},{8,14},{9,15},{10,... | collective-permute-start | bytes 3080 | tf_op jit(solution)/shard_map/ppermute | solution.py:211
  183.9 3.0 %collective-permute-start.33 = (f32[256]{0:T(256)S(1)}, f32[256]{0:T(256)S(1)}, u32[]{:S(2)}, u32[]{:S(2)}) collective-permute-start(f32[256]{0:T(256)S(1)} %add.164), channel_id=1, source_target_pairs={{0,4},{1,5},{2,6},{3,7},{4,0},{5,1},{6,2},{7,3},{8,12},{9,13},{10,... | collective-permute-start | bytes 3080 | tf_op jit(solution)/shard_map/ppermute | solution.py:211
  186.9 2.8 %collective-permute-start.32 = (f32[256]{0:T(256)S(1)}, f32[256]{0:T(256)S(1)}, u32[]{:S(2)}, u32[]{:S(2)}) collective-permute-start(f32[256]{0:T(256)S(1)} %add.164), channel_id=1, source_target_pairs={{0,2},{1,3},{2,4},{3,5},{4,6},{5,7},{6,0},{7,1},{8,10},{9,11},{10,... | collective-permute-start | bytes 3080 | tf_op jit(solution)/shard_map/ppermute | solution.py:211
  190.8 2.7 %collective-permute-done.32 = f32[256]{0:T(256)S(1)} collective-permute-done((f32[256]{0:T(256)S(1)}, f32[256]{0:T(256)S(1)}, u32[]{:S(2)}, u32[]{:S(2)}) %collective-permute-start.32) | collective-permute-done | bytes 1056 | tf_op jit(solution)/shard_map/ppermute | solution.py:211
  193.5 0.8 multiply_convert_fusion
  (157 shorter events, 29.7 us)
Async XLA Ops:
  0.6 153.6 %copy-start = (bf16[256,256]{1,0:T(8,128)(2,1)S(1)}, bf16[256,256]{1,0:T(8,128)(2,1)}, u32[]{:S(2)}) copy-start(bf16[256,256]{1,0:T(8,128)(2,1)} %param.15) | copy-start | bytes 393220
  0.6 7.0 %copy-start.1 = (bf16[256,256]{1,0:T(8,128)(2,1)S(1)}, bf16[256,256]{1,0:T(8,128)(2,1)}, u32[]{:S(2)}) copy-start(bf16[256,256]{1,0:T(8,128)(2,1)} %param.13) | copy-start | bytes 393220
  1.7 35.0 %collective-permute-start.23 = (bf16[256,256]{0,1:T(8,128)(2,1)S(1)}, bf16[256,256]{0,1:T(8,128)(2,1)S(1)}, u32[]{:S(2)}, u32[]{:S(2)}) collective-permute-start(bf16[256,256]{0,1:T(8,128)(2,1)S(1)} %copy.57), channel_id=1, source_target_pairs={{0,8},{8,16},{16,24},{24,32},{32,40},{40,48},{48,56},{56,64},{64,7... | collective-permute-start | bytes 393224 | tf_op jit(solution)/shard_map/ppermute | solution.py:18
  13.4 13.4 %copy-start.2 = (bf16[256,256]{1,0:T(8,128)(2,1)S(1)}, bf16[256,256]{1,0:T(8,128)(2,1)}, u32[]{:S(2)}) copy-start(bf16[256,256]{1,0:T(8,128)(2,1)} %param.11) | copy-start | bytes 393220
  19.1 8.6 %collective-permute-start.5 = (f32[2,128,128]{2,1,0:T(8,128)S(1)}, f32[2,128,128]{2,1,0:T(8,128)S(1)}, u32[]{:S(2)}, u32[]{:S(2)}) collective-permute-start(f32[2,128,128]{2,1,0:T(8,128)S(1)} %get-tuple-element.101), channel_id=1, source_target_pairs={{0,8},{8,16},{16,24},{32,40},{40,48},{48,56},{64,72},{72,80},{80,8... | collective-permute-start | bytes 393224 | tf_op jit(solution)/shard_map/ppermute | solution.py:115
  22.9 10.1 %collective-permute-start = (f32[2,128,128]{2,1,0:T(8,128)S(1)}, f32[2,128,128]{2,1,0:T(8,128)S(1)}, u32[]{:S(2)}, u32[]{:S(2)}) collective-permute-start(f32[2,128,128]{2,1,0:T(8,128)S(1)} %get-tuple-element.100), channel_id=1, source_target_pairs={{0,8},{8,16},{16,24},{32,40},{40,48},{48,56},{64,72},{72,80},{80,8... | collective-permute-start | bytes 393224 | tf_op jit(solution)/shard_map/ppermute | solution.py:115
  28.0 11.8 %collective-permute-start.6 = (f32[2,128,128]{2,1,0:T(8,128)S(1)}, f32[2,128,128]{2,1,0:T(8,128)S(1)}, u32[]{:S(2)}, u32[]{:S(2)}) collective-permute-start(f32[2,128,128]{2,1,0:T(8,128)S(1)} %fusion.56), channel_id=1, source_target_pairs={{0,16},{8,24},{32,48},{40,56},{64,80},{72,88},{96,112},{104,120},{... | collective-permute-start | bytes 393224 | tf_op jit(solution)/shard_map/ppermute | solution.py:115
  33.3 7.5 %collective-permute-start.1 = (f32[2,128,128]{2,1,0:T(8,128)S(1)}, f32[2,128,128]{2,1,0:T(8,128)S(1)}, u32[]{:S(2)}, u32[]{:S(2)}) collective-permute-start(f32[2,128,128]{2,1,0:T(8,128)S(1)} %convolution_select_fusion.6), channel_id=1, source_target_pairs={{0,16},{8,24},{32,48},{40,56},{64,80},{72,88},{96,112},{104,120},{... | collective-permute-start | bytes 393224 | tf_op jit(solution)/shard_map/ppermute | solution.py:115
  36.7 9.0 %collective-permute-start.24 = (bf16[256,256]{0,1:T(8,128)(2,1)S(1)}, bf16[256,256]{0,1:T(8,128)(2,1)S(1)}, u32[]{:S(2)}, u32[]{:S(2)}) collective-permute-start(bf16[256,256]{0,1:T(8,128)(2,1)S(1)} %collective-permute-done.23), channel_id=1, source_target_pairs={{0,8},{8,16},{16,24},{24,32},{32,40},{40,48},{48,56},{56,64},{64,7... | collective-permute-start | bytes 393224 | tf_op jit(solution)/shard_map/ppermute | solution.py:18
  40.1 9.2 %collective-permute-start.7 = (f32[2,128,128]{2,1,0:T(8,128)S(1)}, f32[2,128,128]{2,1,0:T(8,128)S(1)}, u32[]{:S(2)}, u32[]{:S(2)}) collective-permute-start(f32[2,128,128]{2,1,0:T(8,128)S(1)} %fusion.55), channel_id=1, source_target_pairs={{24,56},{56,88},{88,120},{120,152},{152,184},{184,216},{216,248},{... | collective-permute-start | bytes 393224 | tf_op jit(solution)/shard_map/ppermute | solution.py:115
  41.1 9.2 %collective-permute-start.2 = (f32[2,128,128]{2,1,0:T(8,128)S(1)}, f32[2,128,128]{2,1,0:T(8,128)S(1)}, u32[]{:S(2)}, u32[]{:S(2)}) collective-permute-start(f32[2,128,128]{2,1,0:T(8,128)S(1)} %convolution_select_fusion.4), channel_id=1, source_target_pairs={{24,56},{56,88},{88,120},{120,152},{152,184},{184,216},{216,248},{... | collective-permute-start | bytes 393224 | tf_op jit(solution)/shard_map/ppermute | solution.py:115
  45.7 19.9 %collective-permute-start.25 = (bf16[256,256]{0,1:T(8,128)(2,1)S(1)}, bf16[256,256]{0,1:T(8,128)(2,1)S(1)}, u32[]{:S(2)}, u32[]{:S(2)}) collective-permute-start(bf16[256,256]{0,1:T(8,128)(2,1)S(1)} %collective-permute-done.24), channel_id=1, source_target_pairs={{0,8},{8,16},{16,24},{24,32},{32,40},{40,48},{48,56},{56,64},{64,7... | collective-permute-start | bytes 393224 | tf_op jit(solution)/shard_map/ppermute | solution.py:18
  49.6 18.0 %collective-permute-start.8 = (f32[2,128,128]{2,1,0:T(8,128)S(1)}, f32[2,128,128]{2,1,0:T(8,128)S(1)}, u32[]{:S(2)}, u32[]{:S(2)}) collective-permute-start(f32[2,128,128]{2,1,0:T(8,128)S(1)} %fusion.54), channel_id=1, source_target_pairs={{24,88},{56,120},{88,152},{120,184},{152,216},{184,248},{216,280},... | collective-permute-start | bytes 393224 | tf_op jit(solution)/shard_map/ppermute | solution.py:115
  50.5 18.0 %collective-permute-start.3 = (f32[2,128,128]{2,1,0:T(8,128)S(1)}, f32[2,128,128]{2,1,0:T(8,128)S(1)}, u32[]{:S(2)}, u32[]{:S(2)}) collective-permute-start(f32[2,128,128]{2,1,0:T(8,128)S(1)} %convolution_select_fusion.3), channel_id=1, source_target_pairs={{24,88},{56,120},{88,152},{120,184},{152,216},{184,248},{216,280},... | collective-permute-start | bytes 393224 | tf_op jit(solution)/shard_map/ppermute | solution.py:115
  65.6 18.1 %collective-permute-start.26 = (bf16[256,256]{0,1:T(8,128)(2,1)S(1)}, bf16[256,256]{0,1:T(8,128)(2,1)S(1)}, u32[]{:S(2)}, u32[]{:S(2)}) collective-permute-start(bf16[256,256]{0,1:T(8,128)(2,1)S(1)} %collective-permute-done.25), channel_id=1, source_target_pairs={{0,8},{8,16},{16,24},{24,32},{32,40},{40,48},{48,56},{56,64},{64,7... | collective-permute-start | bytes 393224 | tf_op jit(solution)/shard_map/ppermute | solution.py:18
  67.9 17.8 %collective-permute-start.9 = (f32[2,128,128]{2,1,0:T(8,128)S(1)}, f32[2,128,128]{2,1,0:T(8,128)S(1)}, u32[]{:S(2)}, u32[]{:S(2)}) collective-permute-start(f32[2,128,128]{2,1,0:T(8,128)S(1)} %fusion.53), channel_id=1, source_target_pairs={{24,152},{56,184},{88,216},{120,248},{152,280},{184,312},{216,344}... | collective-permute-start | bytes 393224 | tf_op jit(solution)/shard_map/ppermute | solution.py:115
  68.8 28.1 %collective-permute-start.4 = (f32[2,128,128]{2,1,0:T(8,128)S(1)}, f32[2,128,128]{2,1,0:T(8,128)S(1)}, u32[]{:S(2)}, u32[]{:S(2)}) collective-permute-start(f32[2,128,128]{2,1,0:T(8,128)S(1)} %convolution_select_fusion.2), channel_id=1, source_target_pairs={{24,152},{56,184},{88,216},{120,248},{152,280},{184,312},{216,344}... | collective-permute-start | bytes 393224 | tf_op jit(solution)/shard_map/ppermute | solution.py:115
  83.7 11.3 %collective-permute-start.27 = (bf16[256,256]{0,1:T(8,128)(2,1)S(1)}, bf16[256,256]{0,1:T(8,128)(2,1)S(1)}, u32[]{:S(2)}, u32[]{:S(2)}) collective-permute-start(bf16[256,256]{0,1:T(8,128)(2,1)S(1)} %collective-permute-done.26), channel_id=1, source_target_pairs={{0,8},{8,16},{16,24},{24,32},{32,40},{40,48},{48,56},{56,64},{64,7... | collective-permute-start | bytes 393224 | tf_op jit(solution)/shard_map/ppermute | solution.py:18
  85.9 11.3 %collective-permute-start.10 = (f32[2,128,128]{2,1,0:T(8,128)S(1)}, f32[2,128,128]{2,1,0:T(8,128)S(1)}, u32[]{:S(2)}, u32[]{:S(2)}) collective-permute-start(f32[2,128,128]{2,1,0:T(8,128)S(1)} %fusion.52), channel_id=1, source_target_pairs={{24,280},{56,312},{88,344},{120,376},{152,408},{184,440},{216,472}... | collective-permute-start | bytes 393224 | tf_op jit(solution)/shard_map/ppermute | solution.py:115
  95.0 10.3 %collective-permute-start.28 = (bf16[256,256]{0,1:T(8,128)(2,1)S(1)}, bf16[256,256]{0,1:T(8,128)(2,1)S(1)}, u32[]{:S(2)}, u32[]{:S(2)}) collective-permute-start(bf16[256,256]{0,1:T(8,128)(2,1)S(1)} %collective-permute-done.27), channel_id=1, source_target_pairs={{0,8},{8,16},{16,24},{24,32},{32,40},{40,48},{48,56},{56,64},{64,7... | collective-permute-start | bytes 393224 | tf_op jit(solution)/shard_map/ppermute | solution.py:18
  97.5 9.9 %collective-permute-start.14 = (f32[2,128,128]{2,1,0:T(8,128)S(1)}, f32[2,128,128]{2,1,0:T(8,128)S(1)}, u32[]{:S(2)}, u32[]{:S(2)}) collective-permute-start(f32[2,128,128]{2,1,0:T(8,128)S(1)} %fusion.51), channel_id=1, source_target_pairs={{24,56},{56,88},{88,120},{120,152},{152,184},{184,216},{216,248},{... | collective-permute-start | bytes 393224 | tf_op jit(solution)/shard_map/ppermute | solution.py:115
  98.2 9.2 %collective-permute-start.13 = (f32[2,128,128]{2,1,0:T(8,128)S(1)}, f32[2,128,128]{2,1,0:T(8,128)S(1)}, u32[]{:S(2)}, u32[]{:S(2)}) collective-permute-start(f32[2,128,128]{2,1,0:T(8,128)S(1)} %fusion.51), channel_id=1, source_target_pairs={{24,48},{56,80},{88,112},{120,144},{152,176},{184,208},{216,240},{... | collective-permute-start | bytes 393224 | tf_op jit(solution)/shard_map/ppermute | solution.py:115
  98.9 8.6 %collective-permute-start.12 = (f32[2,128,128]{2,1,0:T(8,128)S(1)}, f32[2,128,128]{2,1,0:T(8,128)S(1)}, u32[]{:S(2)}, u32[]{:S(2)}) collective-permute-start(f32[2,128,128]{2,1,0:T(8,128)S(1)} %fusion.51), channel_id=1, source_target_pairs={{24,40},{56,72},{88,104},{120,136},{152,168},{184,200},{216,232},{... | collective-permute-start | bytes 393224 | tf_op jit(solution)/shard_map/ppermute | solution.py:115
  99.5 16.6 %collective-permute-start.11 = (f32[2,128,128]{2,1,0:T(8,128)S(1)}, f32[2,128,128]{2,1,0:T(8,128)S(1)}, u32[]{:S(2)}, u32[]{:S(2)}) collective-permute-start(f32[2,128,128]{2,1,0:T(8,128)S(1)} %fusion.51), channel_id=1, source_target_pairs={{24,32},{56,64},{88,96},{120,128},{152,160},{184,192},{216,224},{2... | collective-permute-start | bytes 393224 | tf_op jit(solution)/shard_map/ppermute | solution.py:115
  105.3 21.1 %collective-permute-start.29 = (bf16[256,256]{0,1:T(8,128)(2,1)S(1)}, bf16[256,256]{0,1:T(8,128)(2,1)S(1)}, u32[]{:S(2)}, u32[]{:S(2)}) collective-permute-start(bf16[256,256]{0,1:T(8,128)(2,1)S(1)} %collective-permute-done.28), channel_id=1, source_target_pairs={{0,8},{8,16},{16,24},{24,32},{32,40},{40,48},{48,56},{56,64},{64,7... | collective-permute-start | bytes 393224 | tf_op jit(solution)/shard_map/ppermute | solution.py:18
  121.1 13.5 %collective-permute-start.19 = (bf16[256,256]{0,1:T(8,128)(2,1)S(1)}, bf16[256,256]{0,1:T(8,128)(2,1)S(1)}, u32[]{:S(2)}, u32[]{:S(2)}) collective-permute-start(bf16[256,256]{0,1:T(8,128)(2,1)S(1)} %bitcast.200), channel_id=1, source_target_pairs={{0,8},{8,16},{16,24},{24,32},{32,40},{40,48},{48,56},{56,64},{64,7... | collective-permute-start | bytes 393224 | tf_op jit(solution)/shard_map/ppermute | solution.py:18
  123.0 20.3 %collective-permute-start.15 = (bf16[256,256]{0,1:T(8,128)(2,1)S(1)}, bf16[256,256]{0,1:T(8,128)(2,1)S(1)}, u32[]{:S(2)}, u32[]{:S(2)}) collective-permute-start(bf16[256,256]{0,1:T(8,128)(2,1)S(1)} %bitcast.201), channel_id=1, source_target_pairs={{0,40},{8,48},{16,56},{24,64},{32,72},{40,80},{48,88},{56,96},{64,... | collective-permute-start | bytes 393224 | tf_op jit(solution)/shard_map/ppermute | solution.py:18
  126.4 18.8 %collective-permute-start.30 = (bf16[256,256]{0,1:T(8,128)(2,1)S(1)}, bf16[256,256]{0,1:T(8,128)(2,1)S(1)}, u32[]{:S(2)}, u32[]{:S(2)}) collective-permute-start(bf16[256,256]{0,1:T(8,128)(2,1)S(1)} %collective-permute-done.29), channel_id=1, source_target_pairs={{0,8},{8,16},{16,24},{24,32},{32,40},{40,48},{48,56},{56,64},{64,7... | collective-permute-start | bytes 393224 | tf_op jit(solution)/shard_map/ppermute | solution.py:18
  134.6 20.5 %collective-permute-start.20 = (bf16[256,256]{0,1:T(8,128)(2,1)S(1)}, bf16[256,256]{0,1:T(8,128)(2,1)S(1)}, u32[]{:S(2)}, u32[]{:S(2)}) collective-permute-start(bf16[256,256]{0,1:T(8,128)(2,1)S(1)} %collective-permute-done.19), channel_id=1, source_target_pairs={{0,8},{8,16},{16,24},{24,32},{32,40},{40,48},{48,56},{56,64},{64,7... | collective-permute-start | bytes 393224 | tf_op jit(solution)/shard_map/ppermute | solution.py:18
  143.4 9.0 %collective-permute-start.16 = (bf16[256,256]{0,1:T(8,128)(2,1)S(1)}, bf16[256,256]{0,1:T(8,128)(2,1)S(1)}, u32[]{:S(2)}, u32[]{:S(2)}) collective-permute-start(bf16[256,256]{0,1:T(8,128)(2,1)S(1)} %collective-permute-done.15), channel_id=1, source_target_pairs={{0,8},{8,16},{16,24},{24,32},{32,40},{40,48},{48,56},{56,64},{64,7... | collective-permute-start | bytes 393224 | tf_op jit(solution)/shard_map/ppermute | solution.py:18
  152.3 9.9 %collective-permute-start.17 = (bf16[256,256]{0,1:T(8,128)(2,1)S(1)}, bf16[256,256]{0,1:T(8,128)(2,1)S(1)}, u32[]{:S(2)}, u32[]{:S(2)}) collective-permute-start(bf16[256,256]{0,1:T(8,128)(2,1)S(1)} %collective-permute-done.16), channel_id=1, source_target_pairs={{0,8},{8,16},{16,24},{24,32},{32,40},{40,48},{48,56},{56,64},{64,7... | collective-permute-start | bytes 393224 | tf_op jit(solution)/shard_map/ppermute | solution.py:18
  155.1 11.4 %collective-permute-start.21 = (bf16[256,256]{0,1:T(8,128)(2,1)S(1)}, bf16[256,256]{0,1:T(8,128)(2,1)S(1)}, u32[]{:S(2)}, u32[]{:S(2)}) collective-permute-start(bf16[256,256]{0,1:T(8,128)(2,1)S(1)} %collective-permute-done.20), channel_id=1, source_target_pairs={{0,8},{8,16},{16,24},{24,32},{32,40},{40,48},{48,56},{56,64},{64,7... | collective-permute-start | bytes 393224 | tf_op jit(solution)/shard_map/ppermute | solution.py:18
  162.2 9.0 %collective-permute-start.18 = (bf16[256,256]{0,1:T(8,128)(2,1)S(1)}, bf16[256,256]{0,1:T(8,128)(2,1)S(1)}, u32[]{:S(2)}, u32[]{:S(2)}) collective-permute-start(bf16[256,256]{0,1:T(8,128)(2,1)S(1)} %collective-permute-done.17), channel_id=1, source_target_pairs={{0,8},{8,16},{16,24},{24,32},{32,40},{40,48},{48,56},{56,64},{64,7... | collective-permute-start | bytes 393224 | tf_op jit(solution)/shard_map/ppermute | solution.py:18
  166.5 9.0 %collective-permute-start.22 = (bf16[256,256]{0,1:T(8,128)(2,1)S(1)}, bf16[256,256]{0,1:T(8,128)(2,1)S(1)}, u32[]{:S(2)}, u32[]{:S(2)}) collective-permute-start(bf16[256,256]{0,1:T(8,128)(2,1)S(1)} %collective-permute-done.21), channel_id=1, source_target_pairs={{0,8},{8,16},{16,24},{24,32},{32,40},{40,48},{48,56},{56,64},{64,7... | collective-permute-start | bytes 393224 | tf_op jit(solution)/shard_map/ppermute | solution.py:18
  175.6 18.0 %copy-start.3 = (f32[256]{0:T(256)S(1)}, f32[256]{0:T(256)}, u32[]{:S(2)}) copy-start(f32[256]{0:T(256)} %param.17) | copy-start | bytes 3076
  176.2 3.0 %collective-permute-start.31 = (f32[256]{0:T(256)S(1)}, f32[256]{0:T(256)S(1)}, u32[]{:S(2)}, u32[]{:S(2)}) collective-permute-start(f32[256]{0:T(256)S(1)} %get-tuple-element.200), channel_id=1, source_target_pairs={{0,1},{1,0},{2,3},{3,2},{4,5},{5,4},{6,7},{7,6},{8,9},{9,8},{10,11... | collective-permute-start | bytes 3080 | tf_op jit(solution)/shard_map/ppermute | solution.py:207
  179.2 11.3 %collective-permute-start.34 = (f32[256]{0:T(256)S(1)}, f32[256]{0:T(256)S(1)}, u32[]{:S(2)}, u32[]{:S(2)}) collective-permute-start(f32[256]{0:T(256)S(1)} %add.164), channel_id=1, source_target_pairs={{0,6},{1,7},{2,0},{3,1},{4,2},{5,3},{6,4},{7,5},{8,14},{9,15},{10,... | collective-permute-start | bytes 3080 | tf_op jit(solution)/shard_map/ppermute | solution.py:211
  183.9 7.0 %collective-permute-start.33 = (f32[256]{0:T(256)S(1)}, f32[256]{0:T(256)S(1)}, u32[]{:S(2)}, u32[]{:S(2)}) collective-permute-start(f32[256]{0:T(256)S(1)} %add.164), channel_id=1, source_target_pairs={{0,4},{1,5},{2,6},{3,7},{4,0},{5,1},{6,2},{7,3},{8,12},{9,13},{10,... | collective-permute-start | bytes 3080 | tf_op jit(solution)/shard_map/ppermute | solution.py:211
  186.9 6.7 %collective-permute-start.32 = (f32[256]{0:T(256)S(1)}, f32[256]{0:T(256)S(1)}, u32[]{:S(2)}, u32[]{:S(2)}) collective-permute-start(f32[256]{0:T(256)S(1)} %add.164), channel_id=1, source_target_pairs={{0,2},{1,3},{2,4},{3,5},{4,6},{5,7},{6,0},{7,1},{8,10},{9,11},{10,... | collective-permute-start | bytes 3080 | tf_op jit(solution)/shard_map/ppermute | solution.py:211

commit v10 on v6

--- a/solution.py
+++ b/solution.py
@@ -75,6 +75,35 @@
     return (transit, carried)
 
 
+def local_affine(q_unit, k_unit, writes, updates, query_key):
+    n_blocks, _, head_size = k_unit.shape
+    identity = jnp.eye(head_size, dtype=jnp.float32)
+    key_cols = jnp.swapaxes(k_unit, -1, -2)
+    stepped = identity - jnp.einsum("nij,njk->nik", key_cols, writes, precision=highest)
+    written = jnp.einsum("nij,njk->nik", key_cols, updates, precision=highest)
+    transit_list = [identity]
+    carried_list = [jnp.zeros_like(identity)]
+    for block in range(n_blocks):
+        transit_list.append(jnp.dot(stepped[block], transit_list[-1], precision=highest))
+        carried_list.append(
+            jnp.dot(stepped[block], carried_list[-1], precision=highest) + written[block]
+        )
+    transit_before = jnp.stack(transit_list[:-1])
+    carried_before = jnp.stack(carried_list[:-1])
+    reading = q_unit - jnp.einsum("nij,njk->nik", query_key, writes, precision=highest)
+    slope = jnp.einsum("nij,njk->nik", reading, transit_before, precision=highest)
+    offset = jnp.einsum("nij,njk->nik", reading, carried_before, precision=highest) + jnp.einsum(
+        "nij,njk->nik", query_key, updates, precision=highest
+    )
+    rows = n_blocks * k_unit.shape[1]
+    return (
+        transit_list[-1],
+        carried_list[-1],
+        slope.reshape(rows, head_size),
+        offset.reshape(rows, head_size),
+    )
+
+
 def advance(carried, inputs_now):
     q_block, k_block, w_block, u_block, cross_block = inputs_now
     corrected = u_block - jnp.dot(w_block, carried, precision=highest)
@@ -104,7 +133,9 @@
     q_unit, k_unit, writes, updates, query_key = jax.vmap(prepare)(
         by_head(q_delta), by_head(k_delta), by_head(v_delta), write_rate.T
     )
-    transit, carried = jax.vmap(local_pair)(k_unit, writes, updates)
+    transit, carried, slope, offset = jax.vmap(local_affine)(
+        q_unit, k_unit, writes, updates, query_key
+    )
     position = lax.axis_index("seq")
     seq_size = lax.axis_size("seq")
     group = min(4, seq_size)
@@ -149,8 +180,9 @@
     group_in = jnp.zeros_like(carried)
     for hop in range(1, group + 1):
         group_in = group_in + moved(end_carried, hop, ends)
-    incoming = batched_dot(before_transit, group_in) + before_carried
-    results = jax.vmap(run_blocks)(incoming, q_unit, k_unit, writes, updates, query_key)
+    offset = offset + batched_dot(slope, before_carried)
+    slope = batched_dot(slope, before_transit)
+    results = batched_dot(slope, group_in) + offset
     delta_out = (
         results.reshape(heads_here, tok_rows, head_size)
         .transpose(1, 0, 2)

time: 190 us -> 190 us (level)
  the two profiles are of different devices: /device:TPU:25 before, /device:TPU:9 now
where the time goes in v10:
time: 190 us; the launch traced here: 189 us
  waiting for transfers between devices  75.3 us (40%)
  starting transfers between devices  61.6 us (32%)
  blocking collectives  22.1 us (12%)
  matrix products  18.5 us (10%)
  other arithmetic  5.42 us (3%)
  local copies, waits for them, and re-layouts  4.24 us (2%)
    ppermute x16, waiting for transfers between devices, shifted(): return lax.ppermute(value, axis, pairs)  66.3 us
    ppermute x16, starting transfers between devices, shifted(): return lax.ppermute(value, axis, pairs)  40.5 us
    psum x1, blocking collectives, on_device(): total_sq = lax.psum(squares, 'head')  22.1 us
    ppermute x15, starting transfers between devices, moved(): return lax.ppermute(value, 'seq', pairs)  21 us
    ppermute x15, waiting for transfers between devices, moved(): return lax.ppermute(value, 'seq', pairs)  9.06 us
    dot_general x18, matrix products, batched_dot(): return jnp.einsum('hij,hjk->hik', left, right, precision=highest)  5.25 us
  transfers between devices with their start and end apart: 31, of which 12 were waited for; matrix products, arithmetic and copies ran while one was open for 14% of the time, Pallas kernels for 0%

profile of v10, /device:TPU:9, one launch (start us, length us, event | category | flops | bytes accessed | tf_op | source)
XLA Modules:
  0.0 188.9 jit_solution(6009875652609351981)
XLA Ops:
  0.6 1.0 copy.90
  1.7 3.5 %collective-permute-start.23 = (bf16[256,256]{0,1:T(8,128)(2,1)S(1)}, bf16[256,256]{0,1:T(8,128)(2,1)S(1)}, u32[]{:S(2)}, u32[]{:S(2)}) collective-permute-start(bf16[256,256]{0,1:T(8,128)(2,1)S(1)} %copy.90), channel_id=1, source_target_pairs={{0,8},{8,16},{16,24},{24,32},{32,40},{40,48},{48,56},{56,64},{64,7... | collective-permute-start | bytes 393224 | tf_op jit(solution)/shard_map/ppermute | solution.py:18
  5.3 0.8 mul.82
  6.1 1.0 reshape.158
  12.8 1.0 convolution_subtract_fusion
  14.8 3.6 %collective-permute-start = (f32[2,128,128]{2,1,0:T(8,128)S(1)}, f32[2,128,128]{2,1,0:T(8,128)S(1)}, u32[]{:S(2)}, u32[]{:S(2)}) collective-permute-start(f32[2,128,128]{2,1,0:T(8,128)S(1)} %fusion.67), channel_id=1, source_target_pairs={{0,8},{8,16},{16,24},{32,40},{40,48},{48,56},{64,72},{72,80},{80,8... | collective-permute-start | bytes 393224 | tf_op jit(solution)/shard_map/ppermute | solution.py:146
  19.0 1.0 fusion.32
  21.1 3.7 %collective-permute-start.5 = (f32[2,128,128]{2,1,0:T(8,128)S(1)}, f32[2,128,128]{2,1,0:T(8,128)S(1)}, u32[]{:S(2)}, u32[]{:S(2)}) collective-permute-start(f32[2,128,128]{2,1,0:T(8,128)S(1)} %convolution_add_fusion.12), channel_id=1, source_target_pairs={{0,8},{8,16},{16,24},{32,40},{40,48},{48,56},{64,72},{72,80},{80,8... | collective-permute-start | bytes 393224 | tf_op jit(solution)/shard_map/ppermute | solution.py:146
  28.3 4.5 %collective-permute-start.1 = (f32[2,128,128]{2,1,0:T(8,128)S(1)}, f32[2,128,128]{2,1,0:T(8,128)S(1)}, u32[]{:S(2)}, u32[]{:S(2)}) collective-permute-start(f32[2,128,128]{2,1,0:T(8,128)S(1)} %convolution_select_fusion.6), channel_id=1, source_target_pairs={{0,16},{8,24},{32,48},{40,56},{64,80},{72,88},{96,112},{104,120},{... | collective-permute-start | bytes 393224 | tf_op jit(solution)/shard_map/ppermute | solution.py:146
  33.1 1.3 collective-permute-start.6
  34.7 1.9 %collective-permute-start.24 = (bf16[256,256]{0,1:T(8,128)(2,1)S(1)}, bf16[256,256]{0,1:T(8,128)(2,1)S(1)}, u32[]{:S(2)}, u32[]{:S(2)}) collective-permute-start(bf16[256,256]{0,1:T(8,128)(2,1)S(1)} %collective-permute-done.23), channel_id=1, source_target_pairs={{0,8},{8,16},{16,24},{24,32},{32,40},{40,48},{48,56},{56,64},{64,7... | collective-permute-start | bytes 393224 | tf_op jit(solution)/shard_map/ppermute | solution.py:18
  39.5 3.0 %collective-permute-done.24 = bf16[256,256]{0,1:T(8,128)(2,1)S(1)} collective-permute-done((bf16[256,256]{0,1:T(8,128)(2,1)S(1)}, bf16[256,256]{0,1:T(8,128)(2,1)S(1)}, u32[]{:S(2)}, u32[]{:S(2)}) %collective-permute-start.24) | collective-permute-done | bytes 131104 | tf_op jit(solution)/shard_map/ppermute | solution.py:18
  42.5 5.1 %collective-permute-start.25 = (bf16[256,256]{0,1:T(8,128)(2,1)S(1)}, bf16[256,256]{0,1:T(8,128)(2,1)S(1)}, u32[]{:S(2)}, u32[]{:S(2)}) collective-permute-start(bf16[256,256]{0,1:T(8,128)(2,1)S(1)} %collective-permute-done.24), channel_id=1, source_target_pairs={{0,8},{8,16},{16,24},{24,32},{32,40},{40,48},{48,56},{56,64},{64,7... | collective-permute-start | bytes 393224 | tf_op jit(solution)/shard_map/ppermute | solution.py:18
  48.1 0.7 collective-permute-start.8
  49.8 9.0 %collective-permute-done.25 = bf16[256,256]{0,1:T(8,128)(2,1)S(1)} collective-permute-done((bf16[256,256]{0,1:T(8,128)(2,1)S(1)}, bf16[256,256]{0,1:T(8,128)(2,1)S(1)}, u32[]{:S(2)}, u32[]{:S(2)}) %collective-permute-start.25) | collective-permute-done | bytes 131104 | tf_op jit(solution)/shard_map/ppermute | solution.py:18
  58.8 1.9 %collective-permute-start.26 = (bf16[256,256]{0,1:T(8,128)(2,1)S(1)}, bf16[256,256]{0,1:T(8,128)(2,1)S(1)}, u32[]{:S(2)}, u32[]{:S(2)}) collective-permute-start(bf16[256,256]{0,1:T(8,128)(2,1)S(1)} %collective-permute-done.25), channel_id=1, source_target_pairs={{0,8},{8,16},{16,24},{24,32},{32,40},{40,48},{48,56},{56,64},{64,7... | collective-permute-start | bytes 393224 | tf_op jit(solution)/shard_map/ppermute | solution.py:18
  62.7 16.9 %collective-permute-done.26 = bf16[256,256]{0,1:T(8,128)(2,1)S(1)} collective-permute-done((bf16[256,256]{0,1:T(8,128)(2,1)S(1)}, bf16[256,256]{0,1:T(8,128)(2,1)S(1)}, u32[]{:S(2)}, u32[]{:S(2)}) %collective-permute-start.26) | collective-permute-done | bytes 131104 | tf_op jit(solution)/shard_map/ppermute | solution.py:18
  79.6 1.9 %collective-permute-start.27 = (bf16[256,256]{0,1:T(8,128)(2,1)S(1)}, bf16[256,256]{0,1:T(8,128)(2,1)S(1)}, u32[]{:S(2)}, u32[]{:S(2)}) collective-permute-start(bf16[256,256]{0,1:T(8,128)(2,1)S(1)} %collective-permute-done.26), channel_id=1, source_target_pairs={{0,8},{8,16},{16,24},{24,32},{32,40},{40,48},{48,56},{56,64},{64,7... | collective-permute-start | bytes 393224 | tf_op jit(solution)/shard_map/ppermute | solution.py:18
  82.5 8.6 %collective-permute-done.27 = bf16[256,256]{0,1:T(8,128)(2,1)S(1)} collective-permute-done((bf16[256,256]{0,1:T(8,128)(2,1)S(1)}, bf16[256,256]{0,1:T(8,128)(2,1)S(1)}, u32[]{:S(2)}, u32[]{:S(2)}) %collective-permute-start.27) | collective-permute-done | bytes 131104 | tf_op jit(solution)/shard_map/ppermute | solution.py:18
  91.0 1.9 %collective-permute-start.28 = (bf16[256,256]{0,1:T(8,128)(2,1)S(1)}, bf16[256,256]{0,1:T(8,128)(2,1)S(1)}, u32[]{:S(2)}, u32[]{:S(2)}) collective-permute-start(bf16[256,256]{0,1:T(8,128)(2,1)S(1)} %collective-permute-done.27), channel_id=1, source_target_pairs={{0,8},{8,16},{16,24},{24,32},{32,40},{40,48},{48,56},{56,64},{64,7... | collective-permute-start | bytes 393224 | tf_op jit(solution)/shard_map/ppermute | solution.py:18
  93.5 0.7 collective-permute-start.14
  94.2 0.7 collective-permute-start.13
  94.9 0.7 collective-permute-start.12
  95.5 1.3 collective-permute-start.11
  97.2 2.5 %collective-permute-done.28 = bf16[256,256]{0,1:T(8,128)(2,1)S(1)} collective-permute-done((bf16[256,256]{0,1:T(8,128)(2,1)S(1)}, bf16[256,256]{0,1:T(8,128)(2,1)S(1)}, u32[]{:S(2)}, u32[]{:S(2)}) %collective-permute-start.28) | collective-permute-done | bytes 131104 | tf_op jit(solution)/shard_map/ppermute | solution.py:18
  99.8 1.9 %collective-permute-start.29 = (bf16[256,256]{0,1:T(8,128)(2,1)S(1)}, bf16[256,256]{0,1:T(8,128)(2,1)S(1)}, u32[]{:S(2)}, u32[]{:S(2)}) collective-permute-start(bf16[256,256]{0,1:T(8,128)(2,1)S(1)} %collective-permute-done.28), channel_id=1, source_target_pairs={{0,8},{8,16},{16,24},{24,32},{32,40},{40,48},{48,56},{56,64},{64,7... | collective-permute-start | bytes 393224 | tf_op jit(solution)/shard_map/ppermute | solution.py:18
  101.7 9.0 %collective-permute-done.11 = f32[2,128,128]{2,1,0:T(8,128)S(1)} collective-permute-done((f32[2,128,128]{2,1,0:T(8,128)S(1)}, f32[2,128,128]{2,1,0:T(8,128)S(1)}, u32[]{:S(2)}, u32[]{:S(2)}) %collective-permute-start.11) | collective-permute-done | bytes 131104 | tf_op jit(solution)/shard_map/ppermute | solution.py:146
  111.2 1.9 %collective-permute-start.19 = (bf16[256,256]{0,1:T(8,128)(2,1)S(1)}, bf16[256,256]{0,1:T(8,128)(2,1)S(1)}, u32[]{:S(2)}, u32[]{:S(2)}) collective-permute-start(bf16[256,256]{0,1:T(8,128)(2,1)S(1)} %bitcast.170), channel_id=1, source_target_pairs={{0,8},{8,16},{16,24},{24,32},{32,40},{40,48},{48,56},{56,64},{64,7... | collective-permute-start | bytes 393224 | tf_op jit(solution)/shard_map/ppermute | solution.py:18
  113.1 5.0 %collective-permute-start.15 = (bf16[256,256]{0,1:T(8,128)(2,1)S(1)}, bf16[256,256]{0,1:T(8,128)(2,1)S(1)}, u32[]{:S(2)}, u32[]{:S(2)}) collective-permute-start(bf16[256,256]{0,1:T(8,128)(2,1)S(1)} %bitcast.171), channel_id=1, source_target_pairs={{0,40},{8,48},{16,56},{24,64},{32,72},{40,80},{48,88},{56,96},{64,... | collective-permute-start | bytes 393224 | tf_op jit(solution)/shard_map/ppermute | solution.py:18
  118.1 1.9 %collective-permute-start.30 = (bf16[256,256]{0,1:T(8,128)(2,1)S(1)}, bf16[256,256]{0,1:T(8,128)(2,1)S(1)}, u32[]{:S(2)}, u32[]{:S(2)}) collective-permute-start(bf16[256,256]{0,1:T(8,128)(2,1)S(1)} %collective-permute-done.29), channel_id=1, source_target_pairs={{0,8},{8,16},{16,24},{24,32},{32,40},{40,48},{48,56},{56,64},{64,7... | collective-permute-start | bytes 393224 | tf_op jit(solution)/shard_map/ppermute | solution.py:18
  120.0 1.3 fusion.13
  121.3 0.8 copy.96
  122.0 2.9 %collective-permute-start.20 = (bf16[256,256]{0,1:T(8,128)(2,1)S(1)}, bf16[256,256]{0,1:T(8,128)(2,1)S(1)}, u32[]{:S(2)}, u32[]{:S(2)}) collective-permute-start(bf16[256,256]{0,1:T(8,128)(2,1)S(1)} %collective-permute-done.19), channel_id=1, source_target_pairs={{0,8},{8,16},{16,24},{24,32},{32,40},{40,48},{48,56},{56,64},{64,7... | collective-permute-start | bytes 393224 | tf_op jit(solution)/shard_map/ppermute | solution.py:18
  124.9 2.3 %collective-permute-done.15 = bf16[256,256]{0,1:T(8,128)(2,1)S(1)} collective-permute-done((bf16[256,256]{0,1:T(8,128)(2,1)S(1)}, bf16[256,256]{0,1:T(8,128)(2,1)S(1)}, u32[]{:S(2)}, u32[]{:S(2)}) %collective-permute-start.15) | collective-permute-done | bytes 131104 | tf_op jit(solution)/shard_map/ppermute | solution.py:18
  127.3 1.9 %collective-permute-start.16 = (bf16[256,256]{0,1:T(8,128)(2,1)S(1)}, bf16[256,256]{0,1:T(8,128)(2,1)S(1)}, u32[]{:S(2)}, u32[]{:S(2)}) collective-permute-start(bf16[256,256]{0,1:T(8,128)(2,1)S(1)} %collective-permute-done.15), channel_id=1, source_target_pairs={{0,8},{8,16},{16,24},{24,32},{32,40},{40,48},{48,56},{56,64},{64,7... | collective-permute-start | bytes 393224 | tf_op jit(solution)/shard_map/ppermute | solution.py:18
  129.2 6.2 %collective-permute-done.30 = bf16[256,256]{0,1:T(8,128)(2,1)S(1)} collective-permute-done((bf16[256,256]{0,1:T(8,128)(2,1)S(1)}, bf16[256,256]{0,1:T(8,128)(2,1)S(1)}, u32[]{:S(2)}, u32[]{:S(2)}) %collective-permute-start.30) | collective-permute-done | bytes 131104 | tf_op jit(solution)/shard_map/ppermute | solution.py:18
  135.5 8.1 %collective-permute-done.16 = bf16[256,256]{0,1:T(8,128)(2,1)S(1)} collective-permute-done((bf16[256,256]{0,1:T(8,128)(2,1)S(1)}, bf16[256,256]{0,1:T(8,128)(2,1)S(1)}, u32[]{:S(2)}, u32[]{:S(2)}) %collective-permute-start.16) | collective-permute-done | bytes 131104 | tf_op jit(solution)/shard_map/ppermute | solution.py:18
  143.6 1.9 %collective-permute-start.17 = (bf16[256,256]{0,1:T(8,128)(2,1)S(1)}, bf16[256,256]{0,1:T(8,128)(2,1)S(1)}, u32[]{:S(2)}, u32[]{:S(2)}) collective-permute-start(bf16[256,256]{0,1:T(8,128)(2,1)S(1)} %collective-permute-done.16), channel_id=1, source_target_pairs={{0,8},{8,16},{16,24},{24,32},{32,40},{40,48},{48,56},{56,64},{64,7... | collective-permute-start | bytes 393224 | tf_op jit(solution)/shard_map/ppermute | solution.py:18
  145.5 0.8 fusion.6
  146.4 2.6 %collective-permute-start.21 = (bf16[256,256]{0,1:T(8,128)(2,1)S(1)}, bf16[256,256]{0,1:T(8,128)(2,1)S(1)}, u32[]{:S(2)}, u32[]{:S(2)}) collective-permute-start(bf16[256,256]{0,1:T(8,128)(2,1)S(1)} %collective-permute-done.20), channel_id=1, source_target_pairs={{0,8},{8,16},{16,24},{24,32},{32,40},{40,48},{48,56},{56,64},{64,7... | collective-permute-start | bytes 393224 | tf_op jit(solution)/shard_map/ppermute | solution.py:18
  149.0 3.5 %collective-permute-done.17 = bf16[256,256]{0,1:T(8,128)(2,1)S(1)} collective-permute-done((bf16[256,256]{0,1:T(8,128)(2,1)S(1)}, bf16[256,256]{0,1:T(8,128)(2,1)S(1)}, u32[]{:S(2)}, u32[]{:S(2)}) %collective-permute-start.17) | collective-permute-done | bytes 131104 | tf_op jit(solution)/shard_map/ppermute | solution.py:18
  152.5 1.9 %collective-permute-start.18 = (bf16[256,256]{0,1:T(8,128)(2,1)S(1)}, bf16[256,256]{0,1:T(8,128)(2,1)S(1)}, u32[]{:S(2)}, u32[]{:S(2)}) collective-permute-start(bf16[256,256]{0,1:T(8,128)(2,1)S(1)} %collective-permute-done.17), channel_id=1, source_target_pairs={{0,8},{8,16},{16,24},{24,32},{32,40},{40,48},{48,56},{56,64},{64,7... | collective-permute-start | bytes 393224 | tf_op jit(solution)/shard_map/ppermute | solution.py:18
  154.4 2.4 %fusion.77 = (f32[2,256]{1,0:T(2,128)S(1)}, f32[2,256,2304]{1,2,0:T(8,128)S(1)}) fusion(f32[2,256,2304]{1,2,0:T(8,128)S(1)} %fusion.6, pred[256,2304]{0,1:T(8,128)(4,1)S(1)} %fusion.13), kind=kOutput, calls=%fused_computation.147 | output fusion | flops 4720895 | bytes 10029056 | tf_op jit(solution)/shard_map/while/body/eval_jaxpr/sub | solution.py:228
  156.7 2.3 %collective-permute-start.22 = (bf16[256,256]{0,1:T(8,128)(2,1)S(1)}, bf16[256,256]{0,1:T(8,128)(2,1)S(1)}, u32[]{:S(2)}, u32[]{:S(2)}) collective-permute-start(bf16[256,256]{0,1:T(8,128)(2,1)S(1)} %collective-permute-done.21), channel_id=1, source_target_pairs={{0,8},{8,16},{16,24},{24,32},{32,40},{40,48},{48,56},{56,64},{64,7... | collective-permute-start | bytes 393224 | tf_op jit(solution)/shard_map/ppermute | solution.py:18
  159.0 2.1 %collective-permute-done.18 = bf16[256,256]{0,1:T(8,128)(2,1)S(1)} collective-permute-done((bf16[256,256]{0,1:T(8,128)(2,1)S(1)}, bf16[256,256]{0,1:T(8,128)(2,1)S(1)}, u32[]{:S(2)}, u32[]{:S(2)}) %collective-permute-start.18) | collective-permute-done | bytes 131104 | tf_op jit(solution)/shard_map/ppermute | solution.py:18
  161.2 4.1 %collective-permute-done.22 = bf16[256,256]{0,1:T(8,128)(2,1)S(1)} collective-permute-done((bf16[256,256]{0,1:T(8,128)(2,1)S(1)}, bf16[256,256]{0,1:T(8,128)(2,1)S(1)}, u32[]{:S(2)}, u32[]{:S(2)}) %collective-permute-start.22) | collective-permute-done | bytes 131104 | tf_op jit(solution)/shard_map/ppermute | solution.py:18
  165.9 22.1 %psum.7 = f32[256]{0:T(256)S(1)} all-reduce(f32[256]{0:T(256)S(1)} %get-tuple-element.30), channel_id=1, replica_groups=mesh['seq'=64,'head'=8] {'head'}, use_global_device_ids=true, to_apply=%region_5.6 | all-reduce | flops 256 | bytes 2048 | tf_op jit(solution)/shard_map/psum | solution.py:238
  188.2 0.8 multiply_convert_fusion
  (115 shorter events, 21.4 us)
Async XLA Ops:
  0.6 144.9 %copy-start = (bf16[256,256]{1,0:T(8,128)(2,1)S(1)}, bf16[256,256]{1,0:T(8,128)(2,1)}, u32[]{:S(2)}) copy-start(bf16[256,256]{1,0:T(8,128)(2,1)} %param.11) | copy-start | bytes 393220
  1.7 33.0 %collective-permute-start.23 = (bf16[256,256]{0,1:T(8,128)(2,1)S(1)}, bf16[256,256]{0,1:T(8,128)(2,1)S(1)}, u32[]{:S(2)}, u32[]{:S(2)}) collective-permute-start(bf16[256,256]{0,1:T(8,128)(2,1)S(1)} %copy.90), channel_id=1, source_target_pairs={{0,8},{8,16},{16,24},{24,32},{32,40},{40,48},{48,56},{56,64},{64,7... | collective-permute-start | bytes 393224 | tf_op jit(solution)/shard_map/ppermute | solution.py:18
  12.8 5.6 %copy-start.2 = (bf16[256,256]{1,0:T(8,128)(2,1)S(1)}, bf16[256,256]{1,0:T(8,128)(2,1)}, u32[]{:S(2)}) copy-start(bf16[256,256]{1,0:T(8,128)(2,1)} %param.9) | copy-start | bytes 393220
  14.8 13.2 %collective-permute-start = (f32[2,128,128]{2,1,0:T(8,128)S(1)}, f32[2,128,128]{2,1,0:T(8,128)S(1)}, u32[]{:S(2)}, u32[]{:S(2)}) collective-permute-start(f32[2,128,128]{2,1,0:T(8,128)S(1)} %fusion.67), channel_id=1, source_target_pairs={{0,8},{8,16},{16,24},{32,40},{40,48},{48,56},{64,72},{72,80},{80,8... | collective-permute-start | bytes 393224 | tf_op jit(solution)/shard_map/ppermute | solution.py:146
  20.0 4.8 %copy-start.1 = (bf16[256,256]{1,0:T(8,128)(2,1)S(1)}, bf16[256,256]{1,0:T(8,128)(2,1)}, u32[]{:S(2)}) copy-start(bf16[256,256]{1,0:T(8,128)(2,1)} %param.7) | copy-start | bytes 393220
  21.1 11.6 %collective-permute-start.5 = (f32[2,128,128]{2,1,0:T(8,128)S(1)}, f32[2,128,128]{2,1,0:T(8,128)S(1)}, u32[]{:S(2)}, u32[]{:S(2)}) collective-permute-start(f32[2,128,128]{2,1,0:T(8,128)S(1)} %convolution_add_fusion.12), channel_id=1, source_target_pairs={{0,8},{8,16},{16,24},{32,40},{40,48},{48,56},{64,72},{72,80},{80,8... | collective-permute-start | bytes 393224 | tf_op jit(solution)/shard_map/ppermute | solution.py:146
  28.3 8.6 %collective-permute-start.1 = (f32[2,128,128]{2,1,0:T(8,128)S(1)}, f32[2,128,128]{2,1,0:T(8,128)S(1)}, u32[]{:S(2)}, u32[]{:S(2)}) collective-permute-start(f32[2,128,128]{2,1,0:T(8,128)S(1)} %convolution_select_fusion.6), channel_id=1, source_target_pairs={{0,16},{8,24},{32,48},{40,56},{64,80},{72,88},{96,112},{104,120},{... | collective-permute-start | bytes 393224 | tf_op jit(solution)/shard_map/ppermute | solution.py:146
  33.1 4.8 %collective-permute-start.6 = (f32[2,128,128]{2,1,0:T(8,128)S(1)}, f32[2,128,128]{2,1,0:T(8,128)S(1)}, u32[]{:S(2)}, u32[]{:S(2)}) collective-permute-start(f32[2,128,128]{2,1,0:T(8,128)S(1)} %fusion.23), channel_id=1, source_target_pairs={{0,16},{8,24},{32,48},{40,56},{64,80},{72,88},{96,112},{104,120},{... | collective-permute-start | bytes 393224 | tf_op jit(solution)/shard_map/ppermute | solution.py:146
  34.7 7.8 %collective-permute-start.24 = (bf16[256,256]{0,1:T(8,128)(2,1)S(1)}, bf16[256,256]{0,1:T(8,128)(2,1)S(1)}, u32[]{:S(2)}, u32[]{:S(2)}) collective-permute-start(bf16[256,256]{0,1:T(8,128)(2,1)S(1)} %collective-permute-done.23), channel_id=1, source_target_pairs={{0,8},{8,16},{16,24},{24,32},{32,40},{40,48},{48,56},{56,64},{64,7... | collective-permute-start | bytes 393224 | tf_op jit(solution)/shard_map/ppermute | solution.py:18
  37.1 11.7 %collective-permute-start.2 = (f32[2,128,128]{2,1,0:T(8,128)S(1)}, f32[2,128,128]{2,1,0:T(8,128)S(1)}, u32[]{:S(2)}, u32[]{:S(2)}) collective-permute-start(f32[2,128,128]{2,1,0:T(8,128)S(1)} %convolution_select_fusion.4), channel_id=1, source_target_pairs={{24,56},{56,88},{88,120},{120,152},{152,184},{184,216},{216,248},{... | collective-permute-start | bytes 393224 | tf_op jit(solution)/shard_map/ppermute | solution.py:146
  38.1 9.7 %collective-permute-start.7 = (f32[2,128,128]{2,1,0:T(8,128)S(1)}, f32[2,128,128]{2,1,0:T(8,128)S(1)}, u32[]{:S(2)}, u32[]{:S(2)}) collective-permute-start(f32[2,128,128]{2,1,0:T(8,128)S(1)} %fusion.22), channel_id=1, source_target_pairs={{24,56},{56,88},{88,120},{120,152},{152,184},{184,216},{216,248},{... | collective-permute-start | bytes 393224 | tf_op jit(solution)/shard_map/ppermute | solution.py:146
  42.5 16.3 %collective-permute-start.25 = (bf16[256,256]{0,1:T(8,128)(2,1)S(1)}, bf16[256,256]{0,1:T(8,128)(2,1)S(1)}, u32[]{:S(2)}, u32[]{:S(2)}) collective-permute-start(bf16[256,256]{0,1:T(8,128)(2,1)S(1)} %collective-permute-done.24), channel_id=1, source_target_pairs={{0,8},{8,16},{16,24},{24,32},{32,40},{40,48},{48,56},{56,64},{64,7... | collective-permute-start | bytes 393224 | tf_op jit(solution)/shard_map/ppermute | solution.py:18
  48.1 12.6 %collective-permute-start.8 = (f32[2,128,128]{2,1,0:T(8,128)S(1)}, f32[2,128,128]{2,1,0:T(8,128)S(1)}, u32[]{:S(2)}, u32[]{:S(2)}) collective-permute-start(f32[2,128,128]{2,1,0:T(8,128)S(1)} %fusion.21), channel_id=1, source_target_pairs={{24,88},{56,120},{88,152},{120,184},{152,216},{184,248},{216,280},... | collective-permute-start | bytes 393224 | tf_op jit(solution)/shard_map/ppermute | solution.py:146
  49.1 12.6 %collective-permute-start.3 = (f32[2,128,128]{2,1,0:T(8,128)S(1)}, f32[2,128,128]{2,1,0:T(8,128)S(1)}, u32[]{:S(2)}, u32[]{:S(2)}) collective-permute-start(f32[2,128,128]{2,1,0:T(8,128)S(1)} %convolution_select_fusion.3), channel_id=1, source_target_pairs={{24,88},{56,120},{88,152},{120,184},{152,216},{184,248},{216,280},... | collective-permute-start | bytes 393224 | tf_op jit(solution)/shard_map/ppermute | solution.py:146
  58.8 20.8 %collective-permute-start.26 = (bf16[256,256]{0,1:T(8,128)(2,1)S(1)}, bf16[256,256]{0,1:T(8,128)(2,1)S(1)}, u32[]{:S(2)}, u32[]{:S(2)}) collective-permute-start(bf16[256,256]{0,1:T(8,128)(2,1)S(1)} %collective-permute-done.25), channel_id=1, source_target_pairs={{0,8},{8,16},{16,24},{24,32},{32,40},{40,48},{48,56},{56,64},{64,7... | collective-permute-start | bytes 393224 | tf_op jit(solution)/shard_map/ppermute | solution.py:18
  61.0 20.5 %collective-permute-start.9 = (f32[2,128,128]{2,1,0:T(8,128)S(1)}, f32[2,128,128]{2,1,0:T(8,128)S(1)}, u32[]{:S(2)}, u32[]{:S(2)}) collective-permute-start(f32[2,128,128]{2,1,0:T(8,128)S(1)} %fusion.20), channel_id=1, source_target_pairs={{24,152},{56,184},{88,216},{120,248},{152,280},{184,312},{216,344}... | collective-permute-start | bytes 393224 | tf_op jit(solution)/shard_map/ppermute | solution.py:146
  62.0 30.9 %collective-permute-start.4 = (f32[2,128,128]{2,1,0:T(8,128)S(1)}, f32[2,128,128]{2,1,0:T(8,128)S(1)}, u32[]{:S(2)}, u32[]{:S(2)}) collective-permute-start(f32[2,128,128]{2,1,0:T(8,128)S(1)} %convolution_select_fusion.2), channel_id=1, source_target_pairs={{24,152},{56,184},{88,216},{120,248},{152,280},{184,312},{216,344}... | collective-permute-start | bytes 393224 | tf_op jit(solution)/shard_map/ppermute | solution.py:146
  79.6 11.4 %collective-permute-start.27 = (bf16[256,256]{0,1:T(8,128)(2,1)S(1)}, bf16[256,256]{0,1:T(8,128)(2,1)S(1)}, u32[]{:S(2)}, u32[]{:S(2)}) collective-permute-start(bf16[256,256]{0,1:T(8,128)(2,1)S(1)} %collective-permute-done.26), channel_id=1, source_target_pairs={{0,8},{8,16},{16,24},{24,32},{32,40},{40,48},{48,56},{56,64},{64,7... | collective-permute-start | bytes 393224 | tf_op jit(solution)/shard_map/ppermute | solution.py:18
  81.8 11.4 %collective-permute-start.10 = (f32[2,128,128]{2,1,0:T(8,128)S(1)}, f32[2,128,128]{2,1,0:T(8,128)S(1)}, u32[]{:S(2)}, u32[]{:S(2)}) collective-permute-start(f32[2,128,128]{2,1,0:T(8,128)S(1)} %fusion.19), channel_id=1, source_target_pairs={{24,280},{56,312},{88,344},{120,376},{152,408},{184,440},{216,472}... | collective-permute-start | bytes 393224 | tf_op jit(solution)/shard_map/ppermute | solution.py:146
  91.0 8.7 %collective-permute-start.28 = (bf16[256,256]{0,1:T(8,128)(2,1)S(1)}, bf16[256,256]{0,1:T(8,128)(2,1)S(1)}, u32[]{:S(2)}, u32[]{:S(2)}) collective-permute-start(bf16[256,256]{0,1:T(8,128)(2,1)S(1)} %collective-permute-done.27), channel_id=1, source_target_pairs={{0,8},{8,16},{16,24},{24,32},{32,40},{40,48},{48,56},{56,64},{64,7... | collective-permute-start | bytes 393224 | tf_op jit(solution)/shard_map/ppermute | solution.py:18
  93.5 8.2 %collective-permute-start.14 = (f32[2,128,128]{2,1,0:T(8,128)S(1)}, f32[2,128,128]{2,1,0:T(8,128)S(1)}, u32[]{:S(2)}, u32[]{:S(2)}) collective-permute-start(f32[2,128,128]{2,1,0:T(8,128)S(1)} %fusion.18), channel_id=1, source_target_pairs={{24,56},{56,88},{88,120},{120,152},{152,184},{184,216},{216,248},{... | collective-permute-start | bytes 393224 | tf_op jit(solution)/shard_map/ppermute | solution.py:146
  94.2 7.5 %collective-permute-start.13 = (f32[2,128,128]{2,1,0:T(8,128)S(1)}, f32[2,128,128]{2,1,0:T(8,128)S(1)}, u32[]{:S(2)}, u32[]{:S(2)}) collective-permute-start(f32[2,128,128]{2,1,0:T(8,128)S(1)} %fusion.18), channel_id=1, source_target_pairs={{24,48},{56,80},{88,112},{120,144},{152,176},{184,208},{216,240},{... | collective-permute-start | bytes 393224 | tf_op jit(solution)/shard_map/ppermute | solution.py:146
  94.9 6.8 %collective-permute-start.12 = (f32[2,128,128]{2,1,0:T(8,128)S(1)}, f32[2,128,128]{2,1,0:T(8,128)S(1)}, u32[]{:S(2)}, u32[]{:S(2)}) collective-permute-start(f32[2,128,128]{2,1,0:T(8,128)S(1)} %fusion.18), channel_id=1, source_target_pairs={{24,40},{56,72},{88,104},{120,136},{152,168},{184,200},{216,232},{... | collective-permute-start | bytes 393224 | tf_op jit(solution)/shard_map/ppermute | solution.py:146
  95.5 15.2 %collective-permute-start.11 = (f32[2,128,128]{2,1,0:T(8,128)S(1)}, f32[2,128,128]{2,1,0:T(8,128)S(1)}, u32[]{:S(2)}, u32[]{:S(2)}) collective-permute-start(f32[2,128,128]{2,1,0:T(8,128)S(1)} %fusion.18), channel_id=1, source_target_pairs={{24,32},{56,64},{88,96},{120,128},{152,160},{184,192},{216,224},{2... | collective-permute-start | bytes 393224 | tf_op jit(solution)/shard_map/ppermute | solution.py:146
  99.8 18.3 %collective-permute-start.29 = (bf16[256,256]{0,1:T(8,128)(2,1)S(1)}, bf16[256,256]{0,1:T(8,128)(2,1)S(1)}, u32[]{:S(2)}, u32[]{:S(2)}) collective-permute-start(bf16[256,256]{0,1:T(8,128)(2,1)S(1)} %collective-permute-done.28), channel_id=1, source_target_pairs={{0,8},{8,16},{16,24},{24,32},{32,40},{40,48},{48,56},{56,64},{64,7... | collective-permute-start | bytes 393224 | tf_op jit(solution)/shard_map/ppermute | solution.py:18
  111.2 10.9 %collective-permute-start.19 = (bf16[256,256]{0,1:T(8,128)(2,1)S(1)}, bf16[256,256]{0,1:T(8,128)(2,1)S(1)}, u32[]{:S(2)}, u32[]{:S(2)}) collective-permute-start(bf16[256,256]{0,1:T(8,128)(2,1)S(1)} %bitcast.170), channel_id=1, source_target_pairs={{0,8},{8,16},{16,24},{24,32},{32,40},{40,48},{48,56},{56,64},{64,7... | collective-permute-start | bytes 393224 | tf_op jit(solution)/shard_map/ppermute | solution.py:18
  113.1 14.2 %collective-permute-start.15 = (bf16[256,256]{0,1:T(8,128)(2,1)S(1)}, bf16[256,256]{0,1:T(8,128)(2,1)S(1)}, u32[]{:S(2)}, u32[]{:S(2)}) collective-permute-start(bf16[256,256]{0,1:T(8,128)(2,1)S(1)} %bitcast.171), channel_id=1, source_target_pairs={{0,40},{8,48},{16,56},{24,64},{32,72},{40,80},{48,88},{56,96},{64,... | collective-permute-start | bytes 393224 | tf_op jit(solution)/shard_map/ppermute | solution.py:18
  118.1 17.3 %collective-permute-start.30 = (bf16[256,256]{0,1:T(8,128)(2,1)S(1)}, bf16[256,256]{0,1:T(8,128)(2,1)S(1)}, u32[]{:S(2)}, u32[]{:S(2)}) collective-permute-start(bf16[256,256]{0,1:T(8,128)(2,1)S(1)} %collective-permute-done.29), channel_id=1, source_target_pairs={{0,8},{8,16},{16,24},{24,32},{32,40},{40,48},{48,56},{56,64},{64,7... | collective-permute-start | bytes 393224 | tf_op jit(solution)/shard_map/ppermute | solution.py:18
  122.0 24.3 %collective-permute-start.20 = (bf16[256,256]{0,1:T(8,128)(2,1)S(1)}, bf16[256,256]{0,1:T(8,128)(2,1)S(1)}, u32[]{:S(2)}, u32[]{:S(2)}) collective-permute-start(bf16[256,256]{0,1:T(8,128)(2,1)S(1)} %collective-permute-done.19), channel_id=1, source_target_pairs={{0,8},{8,16},{16,24},{24,32},{32,40},{40,48},{48,56},{56,64},{64,7... | collective-permute-start | bytes 393224 | tf_op jit(solution)/shard_map/ppermute | solution.py:18
  127.3 16.3 %collective-permute-start.16 = (bf16[256,256]{0,1:T(8,128)(2,1)S(1)}, bf16[256,256]{0,1:T(8,128)(2,1)S(1)}, u32[]{:S(2)}, u32[]{:S(2)}) collective-permute-start(bf16[256,256]{0,1:T(8,128)(2,1)S(1)} %collective-permute-done.15), channel_id=1, source_target_pairs={{0,8},{8,16},{16,24},{24,32},{32,40},{40,48},{48,56},{56,64},{64,7... | collective-permute-start | bytes 393224 | tf_op jit(solution)/shard_map/ppermute | solution.py:18
  143.6 8.9 %collective-permute-start.17 = (bf16[256,256]{0,1:T(8,128)(2,1)S(1)}, bf16[256,256]{0,1:T(8,128)(2,1)S(1)}, u32[]{:S(2)}, u32[]{:S(2)}) collective-permute-start(bf16[256,256]{0,1:T(8,128)(2,1)S(1)} %collective-permute-done.16), channel_id=1, source_target_pairs={{0,8},{8,16},{16,24},{24,32},{32,40},{40,48},{48,56},{56,64},{64,7... | collective-permute-start | bytes 393224 | tf_op jit(solution)/shard_map/ppermute | solution.py:18
  146.4 10.4 %collective-permute-start.21 = (bf16[256,256]{0,1:T(8,128)(2,1)S(1)}, bf16[256,256]{0,1:T(8,128)(2,1)S(1)}, u32[]{:S(2)}, u32[]{:S(2)}) collective-permute-start(bf16[256,256]{0,1:T(8,128)(2,1)S(1)} %collective-permute-done.20), channel_id=1, source_target_pairs={{0,8},{8,16},{16,24},{24,32},{32,40},{40,48},{48,56},{56,64},{64,7... | collective-permute-start | bytes 393224 | tf_op jit(solution)/shard_map/ppermute | solution.py:18
  152.5 8.7 %collective-permute-start.18 = (bf16[256,256]{0,1:T(8,128)(2,1)S(1)}, bf16[256,256]{0,1:T(8,128)(2,1)S(1)}, u32[]{:S(2)}, u32[]{:S(2)}) collective-permute-start(bf16[256,256]{0,1:T(8,128)(2,1)S(1)} %collective-permute-done.17), channel_id=1, source_target_pairs={{0,8},{8,16},{16,24},{24,32},{32,40},{40,48},{48,56},{56,64},{64,7... | collective-permute-start | bytes 393224 | tf_op jit(solution)/shard_map/ppermute | solution.py:18
  156.7 8.6 %collective-permute-start.22 = (bf16[256,256]{0,1:T(8,128)(2,1)S(1)}, bf16[256,256]{0,1:T(8,128)(2,1)S(1)}, u32[]{:S(2)}, u32[]{:S(2)}) collective-permute-start(bf16[256,256]{0,1:T(8,128)(2,1)S(1)} %collective-permute-done.21), channel_id=1, source_target_pairs={{0,8},{8,16},{16,24},{24,32},{32,40},{40,48},{48,56},{56,64},{64,7... | collective-permute-start | bytes 393224 | tf_op jit(solution)/shard_map/ppermute | solution.py:18
  165.4 22.8 %copy-start.3 = (f32[256]{0:T(256)S(1)}, f32[256]{0:T(256)}, u32[]{:S(2)}) copy-start(f32[256]{0:T(256)} %param.13) | copy-start | bytes 3076

commit v11 on v10

--- a/solution.py
+++ b/solution.py
@@ -162,6 +162,23 @@
         transit = jnp.where(has_prev, batched_dot(transit, transit_prev), transit)
         carried = carried_in
         distance *= 2
+    shard_reach = WINDOW // tok_rows
+
+    def window_rows(own, lanes):
+        lane_length = -(-shard_reach // lanes)
+        pieces = []
+        for lane in range(lanes):
+            first = lane * lane_length + 1
+            last = min(shard_reach, (lane + 1) * lane_length)
+            piece = shifted(own, "seq", first)
+            pieces.append(piece)
+            for _ in range(first, last):
+                piece = shifted(piece, "seq", 1)
+                pieces.append(piece)
+        return jnp.concatenate(pieces[::-1] + [own], axis=0)
+
+    key_rows = window_rows(k_attn, 1)
+    transit, carried, key_rows = lax.optimization_barrier((transit, carried, key_rows))
     ends = [i for i in range(seq_size) if i % group == group - 1]
     end_transit, end_carried = transit, carried
     distance = group
@@ -189,22 +206,7 @@
         .reshape(tok_rows, features)
         .astype(jnp.bfloat16)
     )
-    shard_reach = WINDOW // tok_rows
-
-    def window_rows(own, lanes):
-        lane_length = -(-shard_reach // lanes)
-        pieces = []
-        for lane in range(lanes):
-            first = lane * lane_length + 1
-            last = min(shard_reach, (lane + 1) * lane_length)
-            piece = shifted(own, "seq", first)
-            pieces.append(piece)
-            for _ in range(first, last):
-                piece = shifted(piece, "seq", 1)
-                pieces.append(piece)
-        return jnp.concatenate(pieces[::-1] + [own], axis=0)
-
-    rows_all = (window_rows(k_attn, 1), window_rows(delta_out, 2))
+    rows_all = (key_rows, window_rows(delta_out, 2))
     block_rows = min(512, tok_rows)
     first_row = lax.axis_index("seq") * tok_rows
     score_scale = 1.0 / math.sqrt(head_size)

time: 190 us -> 233 us (1.23)
  the two profiles are of different devices: /device:TPU:9 before, /device:TPU:25 now
where the time goes in v11:
time: 233 us; the launch traced here: 232 us
  waiting for transfers between devices  101 us (43%)
  starting transfers between devices  64.5 us (28%)
  blocking collectives  33 us (14%)
  matrix products  20.9 us (9%)
  other arithmetic  7.36 us (3%)
  local copies, waits for them, and re-layouts  3.21 us (1%)
    ppermute x16, waiting for transfers between devices, shifted(): return lax.ppermute(value, axis, pairs)  58.4 us
    ppermute x16, starting transfers between devices, shifted(): return lax.ppermute(value, axis, pairs)  43.4 us
    ppermute x15, waiting for transfers between devices, moved(): return lax.ppermute(value, 'seq', pairs)  42.7 us
    psum x1, blocking collectives, on_device(): total_sq = lax.psum(squares, 'head')  33 us
    ppermute x15, starting transfers between devices, moved(): return lax.ppermute(value, 'seq', pairs)  21 us
    dot_general x18, matrix products, batched_dot(): return jnp.einsum('hij,hjk->hik', left, right, precision=highest)  5.26 us
  transfers between devices with their start and end apart: 31, of which 13 were waited for; matrix products, arithmetic and copies ran while one was open for 12% of the time, Pallas kernels for 0%

profile of v11, /device:TPU:25, one launch (start us, length us, event | category | flops | bytes accessed | tf_op | source)
XLA Modules:
  0.0 231.8 jit_solution(15724249376127761217)
XLA Ops:
  0.6 3.7 %collective-permute-start.4 = (bf16[256,256]{1,0:T(8,128)(2,1)}, bf16[256,256]{1,0:T(8,128)(2,1)S(1)}, u32[]{:S(2)}, u32[]{:S(2)}) collective-permute-start(bf16[256,256]{1,0:T(8,128)(2,1)} %param.12), channel_id=1, source_target_pairs={{0,8},{8,16},{16,24},{24,32},{32,40},{40,48},{48,56},{56,64},{64,7... | collective-permute-start | bytes 393224 | tf_op jit(solution)/shard_map/ppermute | solution.py:18
  4.4 0.8 mul.82
  5.1 1.0 reshape.158
  11.9 1.0 convolution_subtract_fusion
  13.9 3.5 %collective-permute-start = (f32[2,128,128]{2,1,0:T(8,128)S(1)}, f32[2,128,128]{2,1,0:T(8,128)S(1)}, u32[]{:S(2)}, u32[]{:S(2)}) collective-permute-start(f32[2,128,128]{2,1,0:T(8,128)S(1)} %fusion.69), channel_id=1, source_target_pairs={{0,8},{8,16},{16,24},{32,40},{40,48},{48,56},{64,72},{72,80},{80,8... | collective-permute-start | bytes 393224 | tf_op jit(solution)/shard_map/ppermute | solution.py:146
  18.1 1.0 fusion.34
  20.2 3.7 %collective-permute-start.2 = (f32[2,128,128]{2,1,0:T(8,128)S(1)}, f32[2,128,128]{2,1,0:T(8,128)S(1)}, u32[]{:S(2)}, u32[]{:S(2)}) collective-permute-start(f32[2,128,128]{2,1,0:T(8,128)S(1)} %convolution_add_fusion.12), channel_id=1, source_target_pairs={{0,8},{8,16},{16,24},{32,40},{40,48},{48,56},{64,72},{72,80},{80,8... | collective-permute-start | bytes 393224 | tf_op jit(solution)/shard_map/ppermute | solution.py:146
  27.3 4.5 %collective-permute-start.1 = (f32[2,128,128]{2,1,0:T(8,128)S(1)}, f32[2,128,128]{2,1,0:T(8,128)S(1)}, u32[]{:S(2)}, u32[]{:S(2)}) collective-permute-start(f32[2,128,128]{2,1,0:T(8,128)S(1)} %convolution_select_fusion.6), channel_id=1, source_target_pairs={{0,16},{8,24},{32,48},{40,56},{64,80},{72,88},{96,112},{104,120},{... | collective-permute-start | bytes 393224 | tf_op jit(solution)/shard_map/ppermute | solution.py:146
  31.8 1.9 collective-permute-start.5
  34.0 1.3 collective-permute-start.3
  35.4 4.3 %collective-permute-done.5 = bf16[256,256]{1,0:T(8,128)(2,1)S(1)} collective-permute-done((bf16[256,256]{1,0:T(8,128)(2,1)S(1)}, bf16[256,256]{1,0:T(8,128)(2,1)S(1)}, u32[]{:S(2)}, u32[]{:S(2)}) %collective-permute-start.5) | collective-permute-done | bytes 131104 | tf_op jit(solution)/shard_map/ppermute | solution.py:18
  39.7 5.7 %collective-permute-start.6 = (bf16[256,256]{1,0:T(8,128)(2,1)S(1)}, bf16[256,256]{1,0:T(8,128)(2,1)S(1)}, u32[]{:S(2)}, u32[]{:S(2)}) collective-permute-start(bf16[256,256]{1,0:T(8,128)(2,1)S(1)} %collective-permute-done.5), channel_id=1, source_target_pairs={{0,8},{8,16},{16,24},{24,32},{32,40},{40,48},{48,56},{56,64},{64,7... | collective-permute-start | bytes 393224 | tf_op jit(solution)/shard_map/ppermute | solution.py:18
  45.6 1.8 collective-permute-done.6
  47.5 3.6 %collective-permute-start.7 = (bf16[256,256]{1,0:T(8,128)(2,1)S(1)}, bf16[256,256]{1,0:T(8,128)(2,1)S(1)}, u32[]{:S(2)}, u32[]{:S(2)}) collective-permute-start(bf16[256,256]{1,0:T(8,128)(2,1)S(1)} %collective-permute-done.6), channel_id=1, source_target_pairs={{0,8},{8,16},{16,24},{24,32},{32,40},{40,48},{48,56},{56,64},{64,7... | collective-permute-start | bytes 393224 | tf_op jit(solution)/shard_map/ppermute | solution.py:18
  51.3 4.8 %collective-permute-done.7 = bf16[256,256]{1,0:T(8,128)(2,1)S(1)} collective-permute-done((bf16[256,256]{1,0:T(8,128)(2,1)S(1)}, bf16[256,256]{1,0:T(8,128)(2,1)S(1)}, u32[]{:S(2)}, u32[]{:S(2)}) %collective-permute-start.7) | collective-permute-done | bytes 131104 | tf_op jit(solution)/shard_map/ppermute | solution.py:18
  56.1 1.9 collective-permute-start.8
  58.3 5.6 %collective-permute-done.8 = bf16[256,256]{1,0:T(8,128)(2,1)S(1)} collective-permute-done((bf16[256,256]{1,0:T(8,128)(2,1)S(1)}, bf16[256,256]{1,0:T(8,128)(2,1)S(1)}, u32[]{:S(2)}, u32[]{:S(2)}) %collective-permute-start.8) | collective-permute-done | bytes 131104 | tf_op jit(solution)/shard_map/ppermute | solution.py:18
  63.9 1.9 collective-permute-start.9
  66.3 5.5 %collective-permute-done.9 = bf16[256,256]{1,0:T(8,128)(2,1)S(1)} collective-permute-done((bf16[256,256]{1,0:T(8,128)(2,1)S(1)}, bf16[256,256]{1,0:T(8,128)(2,1)S(1)}, u32[]{:S(2)}, u32[]{:S(2)}) %collective-permute-start.9) | collective-permute-done | bytes 131104 | tf_op jit(solution)/shard_map/ppermute | solution.py:18
  71.7 1.9 collective-permute-start.10
  73.9 5.6 %collective-permute-done.10 = bf16[256,256]{1,0:T(8,128)(2,1)S(1)} collective-permute-done((bf16[256,256]{1,0:T(8,128)(2,1)S(1)}, bf16[256,256]{1,0:T(8,128)(2,1)S(1)}, u32[]{:S(2)}, u32[]{:S(2)}) %collective-permute-start.10) | collective-permute-done | bytes 131104 | tf_op jit(solution)/shard_map/ppermute | solution.py:18
  79.6 1.9 collective-permute-start.11
  81.8 6.2 %collective-permute-done.11 = bf16[256,256]{1,0:T(8,128)(2,1)S(1)} collective-permute-done((bf16[256,256]{1,0:T(8,128)(2,1)S(1)}, bf16[256,256]{1,0:T(8,128)(2,1)S(1)}, u32[]{:S(2)}, u32[]{:S(2)}) %collective-permute-start.11) | collective-permute-done | bytes 131104 | tf_op jit(solution)/shard_map/ppermute | solution.py:18
  88.1 0.7 collective-permute-start.15
  89.1 0.7 collective-permute-start.12
  90.0 0.7 collective-permute-start.16
  91.0 0.7 collective-permute-start.13
  97.2 1.3 collective-permute-start.19
  98.9 42.7 %collective-permute-done.19 = f32[2,128,128]{2,1,0:T(8,128)S(1)} collective-permute-done((f32[2,128,128]{2,1,0:T(8,128)S(1)}, f32[2,128,128]{2,1,0:T(8,128)S(1)}, u32[]{:S(2)}, u32[]{:S(2)}) %collective-permute-start.19) | collective-permute-done | bytes 131104 | tf_op jit(solution)/shard_map/ppermute | solution.py:146
  142.0 4.2 %collective-permute-start.23 = (bf16[256,256]{0,1:T(8,128)(2,1)S(1)}, bf16[256,256]{0,1:T(8,128)(2,1)S(1)}, u32[]{:S(2)}, u32[]{:S(2)}) collective-permute-start(bf16[256,256]{0,1:T(8,128)(2,1)S(1)} %bitcast.174), channel_id=1, source_target_pairs={{0,40},{8,48},{16,56},{24,64},{32,72},{40,80},{48,88},{56,96},{64,... | collective-permute-start | bytes 393224 | tf_op jit(solution)/shard_map/ppermute | solution.py:18
  146.2 1.9 collective-permute-start.27
  148.2 9.5 %collective-permute-done.23 = bf16[256,256]{0,1:T(8,128)(2,1)S(1)} collective-permute-done((bf16[256,256]{0,1:T(8,128)(2,1)S(1)}, bf16[256,256]{0,1:T(8,128)(2,1)S(1)}, u32[]{:S(2)}, u32[]{:S(2)}) %collective-permute-start.23) | collective-permute-done | bytes 131104 | tf_op jit(solution)/shard_map/ppermute | solution.py:18
  157.7 4.5 %collective-permute-start.24 = (bf16[256,256]{0,1:T(8,128)(2,1)S(1)}, bf16[256,256]{0,1:T(8,128)(2,1)S(1)}, u32[]{:S(2)}, u32[]{:S(2)}) collective-permute-start(bf16[256,256]{0,1:T(8,128)(2,1)S(1)} %collective-permute-done.23), channel_id=1, source_target_pairs={{0,8},{8,16},{16,24},{24,32},{32,40},{40,48},{48,56},{56,64},{64,7... | collective-permute-start | bytes 393224 | tf_op jit(solution)/shard_map/ppermute | solution.py:18
  162.2 1.3 fusion.13
  163.5 1.9 collective-permute-start.28
  165.5 2.4 %collective-permute-start.25 = (bf16[256,256]{0,1:T(8,128)(2,1)S(1)}, bf16[256,256]{0,1:T(8,128)(2,1)S(1)}, u32[]{:S(2)}, u32[]{:S(2)}) collective-permute-start(bf16[256,256]{0,1:T(8,128)(2,1)S(1)} %collective-permute-done.24), channel_id=1, source_target_pairs={{0,8},{8,16},{16,24},{24,32},{32,40},{40,48},{48,56},{56,64},{64,7... | collective-permute-start | bytes 393224 | tf_op jit(solution)/shard_map/ppermute | solution.py:18
  167.9 0.8 fusion.6
  168.7 4.1 %collective-permute-done.28 = bf16[256,256]{0,1:T(8,128)(2,1)S(1)} collective-permute-done((bf16[256,256]{0,1:T(8,128)(2,1)S(1)}, bf16[256,256]{0,1:T(8,128)(2,1)S(1)}, u32[]{:S(2)}, u32[]{:S(2)}) %collective-permute-start.28) | collective-permute-done | bytes 131104 | tf_op jit(solution)/shard_map/ppermute | solution.py:18
  172.8 1.9 collective-permute-start.29
  174.7 4.6 %collective-permute-done.25 = bf16[256,256]{0,1:T(8,128)(2,1)S(1)} collective-permute-done((bf16[256,256]{0,1:T(8,128)(2,1)S(1)}, bf16[256,256]{0,1:T(8,128)(2,1)S(1)}, u32[]{:S(2)}, u32[]{:S(2)}) %collective-permute-start.25) | collective-permute-done | bytes 131104 | tf_op jit(solution)/shard_map/ppermute | solution.py:18
  179.3 2.1 collective-permute-start.26
  181.5 4.3 %fusion.79 = (f32[2,256]{1,0:T(2,128)S(1)}, f32[2,256,2304]{1,2,0:T(8,128)}) fusion(f32[2,256,2304]{1,2,0:T(8,128)S(1)} %fusion.6, pred[256,2304]{0,1:T(8,128)(4,1)S(1)} %fusion.13), kind=kOutput, calls=%fused_computation.149 | output fusion | flops 4720895 | bytes 10029056 | tf_op jit(solution)/shard_map/while/body/eval_jaxpr/sub | solution.py:230
  185.8 0.8 copy.91
  186.5 1.9 collective-permute-start.30
  188.5 6.3 %collective-permute-done.30 = bf16[256,256]{0,1:T(8,128)(2,1)S(1)} collective-permute-done((bf16[256,256]{0,1:T(8,128)(2,1)S(1)}, bf16[256,256]{0,1:T(8,128)(2,1)S(1)}, u32[]{:S(2)}, u32[]{:S(2)}) %collective-permute-start.30) | collective-permute-done | bytes 131104 | tf_op jit(solution)/shard_map/ppermute | solution.py:18
  194.9 2.9 %fusion.33 = (f32[256]{0:T(256)S(1)}, f32[2,128,256]{2,1,0:T(8,128)S(1)}) fusion(bf16[2304,2,128]{0,2,1:T(8,128)(2,1)S(1)} %bitcast.188, f32[2,256,2304]{1,2,0:T(8,128)} %get-tuple-element.35, f32[2,256]{1,0:T(2,128)S(1)} %get-tuple-element.34), kind=kOutput, calls=%fused_computation.65 | convolution fusion | flops 304480000 | bytes 6163456 | tf_op jit(solution)/shard_map/while/body/eval_jaxpr/hqk,khd->qhd/dot_general | solution.py:232
  197.9 33.0 %psum.7 = f32[256]{0:T(256)S(1)} all-reduce(f32[256]{0:T(256)S(1)} %get-tuple-element.36), channel_id=1, replica_groups=mesh['seq'=64,'head'=8] {'head'}, use_global_device_ids=true, to_apply=%region_5.6 | all-reduce | flops 256 | bytes 2048 | tf_op jit(solution)/shard_map/psum | solution.py:240
  231.1 0.8 multiply_convert_fusion
  (116 shorter events, 21.0 us)
Async XLA Ops:
  0.6 167.3 %copy-start = (bf16[256,256]{1,0:T(8,128)(2,1)S(1)}, bf16[256,256]{1,0:T(8,128)(2,1)}, u32[]{:S(2)}) copy-start(bf16[256,256]{1,0:T(8,128)(2,1)} %param.11) | copy-start | bytes 393220
  0.6 31.2 %collective-permute-start.4 = (bf16[256,256]{1,0:T(8,128)(2,1)}, bf16[256,256]{1,0:T(8,128)(2,1)S(1)}, u32[]{:S(2)}, u32[]{:S(2)}) collective-permute-start(bf16[256,256]{1,0:T(8,128)(2,1)} %param.12), channel_id=1, source_target_pairs={{0,8},{8,16},{16,24},{24,32},{32,40},{40,48},{48,56},{56,64},{64,7... | collective-permute-start | bytes 393224 | tf_op jit(solution)/shard_map/ppermute | solution.py:18
  11.9 5.6 %copy-start.2 = (bf16[256,256]{1,0:T(8,128)(2,1)S(1)}, bf16[256,256]{1,0:T(8,128)(2,1)}, u32[]{:S(2)}) copy-start(bf16[256,256]{1,0:T(8,128)(2,1)} %param.9) | copy-start | bytes 393220
  13.9 13.1 %collective-permute-start = (f32[2,128,128]{2,1,0:T(8,128)S(1)}, f32[2,128,128]{2,1,0:T(8,128)S(1)}, u32[]{:S(2)}, u32[]{:S(2)}) collective-permute-start(f32[2,128,128]{2,1,0:T(8,128)S(1)} %fusion.69), channel_id=1, source_target_pairs={{0,8},{8,16},{16,24},{32,40},{40,48},{48,56},{64,72},{72,80},{80,8... | collective-permute-start | bytes 393224 | tf_op jit(solution)/shard_map/ppermute | solution.py:146
  19.1 4.9 %copy-start.1 = (bf16[256,256]{1,0:T(8,128)(2,1)S(1)}, bf16[256,256]{1,0:T(8,128)(2,1)}, u32[]{:S(2)}) copy-start(bf16[256,256]{1,0:T(8,128)(2,1)} %param.7) | copy-start | bytes 393220
  20.2 13.6 %collective-permute-start.2 = (f32[2,128,128]{2,1,0:T(8,128)S(1)}, f32[2,128,128]{2,1,0:T(8,128)S(1)}, u32[]{:S(2)}, u32[]{:S(2)}) collective-permute-start(f32[2,128,128]{2,1,0:T(8,128)S(1)} %convolution_add_fusion.12), channel_id=1, source_target_pairs={{0,8},{8,16},{16,24},{32,40},{40,48},{48,56},{64,72},{72,80},{80,8... | collective-permute-start | bytes 393224 | tf_op jit(solution)/shard_map/ppermute | solution.py:146
  27.3 54.1 %collective-permute-start.1 = (f32[2,128,128]{2,1,0:T(8,128)S(1)}, f32[2,128,128]{2,1,0:T(8,128)S(1)}, u32[]{:S(2)}, u32[]{:S(2)}) collective-permute-start(f32[2,128,128]{2,1,0:T(8,128)S(1)} %convolution_select_fusion.6), channel_id=1, source_target_pairs={{0,16},{8,24},{32,48},{40,56},{64,80},{72,88},{96,112},{104,120},{... | collective-permute-start | bytes 393224 | tf_op jit(solution)/shard_map/ppermute | solution.py:146
  31.8 7.8 %collective-permute-start.5 = (bf16[256,256]{1,0:T(8,128)(2,1)S(1)}, bf16[256,256]{1,0:T(8,128)(2,1)S(1)}, u32[]{:S(2)}, u32[]{:S(2)}) collective-permute-start(bf16[256,256]{1,0:T(8,128)(2,1)S(1)} %collective-permute-done.4), channel_id=1, source_target_pairs={{0,8},{8,16},{16,24},{24,32},{32,40},{40,48},{48,56},{56,64},{64,7... | collective-permute-start | bytes 393224 | tf_op jit(solution)/shard_map/ppermute | solution.py:18
  34.0 24.0 %collective-permute-start.3 = (f32[2,128,128]{2,1,0:T(8,128)S(1)}, f32[2,128,128]{2,1,0:T(8,128)S(1)}, u32[]{:S(2)}, u32[]{:S(2)}) collective-permute-start(f32[2,128,128]{2,1,0:T(8,128)S(1)} %fusion.25), channel_id=1, source_target_pairs={{0,16},{8,24},{32,48},{40,56},{64,80},{72,88},{96,112},{104,120},{... | collective-permute-start | bytes 393224 | tf_op jit(solution)/shard_map/ppermute | solution.py:146
  39.7 7.8 %collective-permute-start.6 = (bf16[256,256]{1,0:T(8,128)(2,1)S(1)}, bf16[256,256]{1,0:T(8,128)(2,1)S(1)}, u32[]{:S(2)}, u32[]{:S(2)}) collective-permute-start(bf16[256,256]{1,0:T(8,128)(2,1)S(1)} %collective-permute-done.5), channel_id=1, source_target_pairs={{0,8},{8,16},{16,24},{24,32},{32,40},{40,48},{48,56},{56,64},{64,7... | collective-permute-start | bytes 393224 | tf_op jit(solution)/shard_map/ppermute | solution.py:18
  47.5 8.7 %collective-permute-start.7 = (bf16[256,256]{1,0:T(8,128)(2,1)S(1)}, bf16[256,256]{1,0:T(8,128)(2,1)S(1)}, u32[]{:S(2)}, u32[]{:S(2)}) collective-permute-start(bf16[256,256]{1,0:T(8,128)(2,1)S(1)} %collective-permute-done.6), channel_id=1, source_target_pairs={{0,8},{8,16},{16,24},{24,32},{32,40},{40,48},{48,56},{56,64},{64,7... | collective-permute-start | bytes 393224 | tf_op jit(solution)/shard_map/ppermute | solution.py:18
  56.1 7.8 %collective-permute-start.8 = (bf16[256,256]{1,0:T(8,128)(2,1)S(1)}, bf16[256,256]{1,0:T(8,128)(2,1)S(1)}, u32[]{:S(2)}, u32[]{:S(2)}) collective-permute-start(bf16[256,256]{1,0:T(8,128)(2,1)S(1)} %collective-permute-done.7), channel_id=1, source_target_pairs={{0,8},{8,16},{16,24},{24,32},{32,40},{40,48},{48,56},{56,64},{64,7... | collective-permute-start | bytes 393224 | tf_op jit(solution)/shard_map/ppermute | solution.py:18
  63.9 7.8 %collective-permute-start.9 = (bf16[256,256]{1,0:T(8,128)(2,1)S(1)}, bf16[256,256]{1,0:T(8,128)(2,1)S(1)}, u32[]{:S(2)}, u32[]{:S(2)}) collective-permute-start(bf16[256,256]{1,0:T(8,128)(2,1)S(1)} %collective-permute-done.8), channel_id=1, source_target_pairs={{0,8},{8,16},{16,24},{24,32},{32,40},{40,48},{48,56},{56,64},{64,7... | collective-permute-start | bytes 393224 | tf_op jit(solution)/shard_map/ppermute | solution.py:18
  71.7 7.8 %collective-permute-start.10 = (bf16[256,256]{1,0:T(8,128)(2,1)S(1)}, bf16[256,256]{1,0:T(8,128)(2,1)S(1)}, u32[]{:S(2)}, u32[]{:S(2)}) collective-permute-start(bf16[256,256]{1,0:T(8,128)(2,1)S(1)} %collective-permute-done.9), channel_id=1, source_target_pairs={{0,8},{8,16},{16,24},{24,32},{32,40},{40,48},{48,56},{56,64},{64,7... | collective-permute-start | bytes 393224 | tf_op jit(solution)/shard_map/ppermute | solution.py:18
  73.9 14.2 %copy-start.3 = (bf16[256,256]{1,0:T(8,128)(2,1)S(1)}, bf16[256,256]{1,0:T(8,128)(2,1)}, u32[]{:S(2)}) copy-start(bf16[256,256]{1,0:T(8,128)(2,1)} %param.12) | copy-start | bytes 393220
  79.6 8.4 %collective-permute-start.11 = (bf16[256,256]{1,0:T(8,128)(2,1)S(1)}, bf16[256,256]{1,0:T(8,128)(2,1)S(1)}, u32[]{:S(2)}, u32[]{:S(2)}) collective-permute-start(bf16[256,256]{1,0:T(8,128)(2,1)S(1)} %collective-permute-done.10), channel_id=1, source_target_pairs={{0,8},{8,16},{16,24},{24,32},{32,40},{40,48},{48,56},{56,64},{64,7... | collective-permute-start | bytes 393224 | tf_op jit(solution)/shard_map/ppermute | solution.py:18
  88.1 1.6 collective-permute-start.15
  89.1 1.6 collective-permute-start.12
  90.0 1.6 collective-permute-start.16
  91.0 1.6 collective-permute-start.13
  92.0 1.6 collective-permute-start.17
  92.9 1.6 collective-permute-start.14
  93.9 1.0 collective-permute-start.18
  95.2 3.7 %collective-permute-start.22 = (f32[2,128,128]{2,1,0:T(8,128)S(1)}, f32[2,128,128]{2,1,0:T(8,128)S(1)}, u32[]{:S(2)}, u32[]{:S(2)}) collective-permute-start(f32[2,128,128]{2,1,0:T(8,128)S(1)} %fusion.20), channel_id=1, source_target_pairs={{24,56},{56,88},{88,120},{120,152},{152,184},{184,216},{216,248},{... | collective-permute-start | bytes 393224 | tf_op jit(solution)/shard_map/ppermute | solution.py:146
  95.8 3.0 %collective-permute-start.21 = (f32[2,128,128]{2,1,0:T(8,128)S(1)}, f32[2,128,128]{2,1,0:T(8,128)S(1)}, u32[]{:S(2)}, u32[]{:S(2)}) collective-permute-start(f32[2,128,128]{2,1,0:T(8,128)S(1)} %fusion.20), channel_id=1, source_target_pairs={{24,48},{56,80},{88,112},{120,144},{152,176},{184,208},{216,240},{... | collective-permute-start | bytes 393224 | tf_op jit(solution)/shard_map/ppermute | solution.py:146
  96.5 2.4 %collective-permute-start.20 = (f32[2,128,128]{2,1,0:T(8,128)S(1)}, f32[2,128,128]{2,1,0:T(8,128)S(1)}, u32[]{:S(2)}, u32[]{:S(2)}) collective-permute-start(f32[2,128,128]{2,1,0:T(8,128)S(1)} %fusion.20), channel_id=1, source_target_pairs={{24,40},{56,72},{88,104},{120,136},{152,168},{184,200},{216,232},{... | collective-permute-start | bytes 393224 | tf_op jit(solution)/shard_map/ppermute | solution.py:146
  97.2 44.4 %collective-permute-start.19 = (f32[2,128,128]{2,1,0:T(8,128)S(1)}, f32[2,128,128]{2,1,0:T(8,128)S(1)}, u32[]{:S(2)}, u32[]{:S(2)}) collective-permute-start(f32[2,128,128]{2,1,0:T(8,128)S(1)} %fusion.20), channel_id=1, source_target_pairs={{24,32},{56,64},{88,96},{120,128},{152,160},{184,192},{216,224},{2... | collective-permute-start | bytes 393224 | tf_op jit(solution)/shard_map/ppermute | solution.py:146
  142.0 15.6 %collective-permute-start.23 = (bf16[256,256]{0,1:T(8,128)(2,1)S(1)}, bf16[256,256]{0,1:T(8,128)(2,1)S(1)}, u32[]{:S(2)}, u32[]{:S(2)}) collective-permute-start(bf16[256,256]{0,1:T(8,128)(2,1)S(1)} %bitcast.174), channel_id=1, source_target_pairs={{0,40},{8,48},{16,56},{24,64},{32,72},{40,80},{48,88},{56,96},{64,... | collective-permute-start | bytes 393224 | tf_op jit(solution)/shard_map/ppermute | solution.py:18
  146.2 17.2 %collective-permute-start.27 = (bf16[256,256]{0,1:T(8,128)(2,1)S(1)}, bf16[256,256]{0,1:T(8,128)(2,1)S(1)}, u32[]{:S(2)}, u32[]{:S(2)}) collective-permute-start(bf16[256,256]{0,1:T(8,128)(2,1)S(1)} %bitcast.175), channel_id=1, source_target_pairs={{0,8},{8,16},{16,24},{24,32},{32,40},{40,48},{48,56},{56,64},{64,7... | collective-permute-start | bytes 393224 | tf_op jit(solution)/shard_map/ppermute | solution.py:18
  157.7 7.8 %collective-permute-start.24 = (bf16[256,256]{0,1:T(8,128)(2,1)S(1)}, bf16[256,256]{0,1:T(8,128)(2,1)S(1)}, u32[]{:S(2)}, u32[]{:S(2)}) collective-permute-start(bf16[256,256]{0,1:T(8,128)(2,1)S(1)} %collective-permute-done.23), channel_id=1, source_target_pairs={{0,8},{8,16},{16,24},{24,32},{32,40},{40,48},{48,56},{56,64},{64,7... | collective-permute-start | bytes 393224 | tf_op jit(solution)/shard_map/ppermute | solution.py:18
  163.5 9.3 %collective-permute-start.28 = (bf16[256,256]{0,1:T(8,128)(2,1)S(1)}, bf16[256,256]{0,1:T(8,128)(2,1)S(1)}, u32[]{:S(2)}, u32[]{:S(2)}) collective-permute-start(bf16[256,256]{0,1:T(8,128)(2,1)S(1)} %collective-permute-done.27), channel_id=1, source_target_pairs={{0,8},{8,16},{16,24},{24,32},{32,40},{40,48},{48,56},{56,64},{64,7... | collective-permute-start | bytes 393224 | tf_op jit(solution)/shard_map/ppermute | solution.py:18
  165.5 13.8 %collective-permute-start.25 = (bf16[256,256]{0,1:T(8,128)(2,1)S(1)}, bf16[256,256]{0,1:T(8,128)(2,1)S(1)}, u32[]{:S(2)}, u32[]{:S(2)}) collective-permute-start(bf16[256,256]{0,1:T(8,128)(2,1)S(1)} %collective-permute-done.24), channel_id=1, source_target_pairs={{0,8},{8,16},{16,24},{24,32},{32,40},{40,48},{48,56},{56,64},{64,7... | collective-permute-start | bytes 393224 | tf_op jit(solution)/shard_map/ppermute | solution.py:18
  172.8 13.7 %collective-permute-start.29 = (bf16[256,256]{0,1:T(8,128)(2,1)S(1)}, bf16[256,256]{0,1:T(8,128)(2,1)S(1)}, u32[]{:S(2)}, u32[]{:S(2)}) collective-permute-start(bf16[256,256]{0,1:T(8,128)(2,1)S(1)} %collective-permute-done.28), channel_id=1, source_target_pairs={{0,8},{8,16},{16,24},{24,32},{32,40},{40,48},{48,56},{56,64},{64,7... | collective-permute-start | bytes 393224 | tf_op jit(solution)/shard_map/ppermute | solution.py:18
  179.3 9.1 %collective-permute-start.26 = (bf16[256,256]{0,1:T(8,128)(2,1)S(1)}, bf16[256,256]{0,1:T(8,128)(2,1)S(1)}, u32[]{:S(2)}, u32[]{:S(2)}) collective-permute-start(bf16[256,256]{0,1:T(8,128)(2,1)S(1)} %collective-permute-done.25), channel_id=1, source_target_pairs={{0,8},{8,16},{16,24},{24,32},{32,40},{40,48},{48,56},{56,64},{64,7... | collective-permute-start | bytes 393224 | tf_op jit(solution)/shard_map/ppermute | solution.py:18
  186.5 8.3 %collective-permute-start.30 = (bf16[256,256]{0,1:T(8,128)(2,1)S(1)}, bf16[256,256]{0,1:T(8,128)(2,1)S(1)}, u32[]{:S(2)}, u32[]{:S(2)}) collective-permute-start(bf16[256,256]{0,1:T(8,128)(2,1)S(1)} %collective-permute-done.29), channel_id=1, source_target_pairs={{0,8},{8,16},{16,24},{24,32},{32,40},{40,48},{48,56},{56,64},{64,7... | collective-permute-start | bytes 393224 | tf_op jit(solution)/shard_map/ppermute | solution.py:18
  194.9 36.1 %copy-start.4 = (f32[256]{0:T(256)S(1)}, f32[256]{0:T(256)}, u32[]{:S(2)}) copy-start(f32[256]{0:T(256)} %param.13) | copy-start | bytes 3076

commit v12 on v10

--- a/solution.py
+++ b/solution.py
@@ -133,9 +133,27 @@
     q_unit, k_unit, writes, updates, query_key = jax.vmap(prepare)(
         by_head(q_delta), by_head(k_delta), by_head(v_delta), write_rate.T
     )
+    shard_reach = WINDOW // tok_rows
+
+    def window_rows(own, lanes, opened=()):
+        lane_length = -(-shard_reach // lanes)
+        pieces = []
+        for lane in range(lanes):
+            first = lane * lane_length + 1
+            last = min(shard_reach, (lane + 1) * lane_length)
+            piece = opened[lane] if lane < len(opened) else shifted(own, "seq", first)
+            pieces.append(piece)
+            for _ in range(first, last):
+                piece = shifted(piece, "seq", 1)
+                pieces.append(piece)
+        return jnp.concatenate(pieces[::-1] + [own], axis=0)
+
     transit, carried, slope, offset = jax.vmap(local_affine)(
         q_unit, k_unit, writes, updates, query_key
     )
+    key_near = shifted(k_attn, "seq", 1)
+    key_far = shifted(k_attn, "seq", -(-shard_reach // 2) + 1)
+    transit, carried, key_far = lax.optimization_barrier((transit, carried, key_far))
     position = lax.axis_index("seq")
     seq_size = lax.axis_size("seq")
     group = min(4, seq_size)
@@ -189,22 +207,7 @@
         .reshape(tok_rows, features)
         .astype(jnp.bfloat16)
     )
-    shard_reach = WINDOW // tok_rows
-
-    def window_rows(own, lanes):
-        lane_length = -(-shard_reach // lanes)
-        pieces = []
-        for lane in range(lanes):
-            first = lane * lane_length + 1
-            last = min(shard_reach, (lane + 1) * lane_length)
-            piece = shifted(own, "seq", first)
-            pieces.append(piece)
-            for _ in range(first, last):
-                piece = shifted(piece, "seq", 1)
-                pieces.append(piece)
-        return jnp.concatenate(pieces[::-1] + [own], axis=0)
-
-    rows_all = (window_rows(k_attn, 1), window_rows(delta_out, 2))
+    rows_all = (window_rows(k_attn, 2, (key_near, key_far)), window_rows(delta_out, 2))
     block_rows = min(512, tok_rows)
     first_row = lax.axis_index("seq") * tok_rows
     score_scale = 1.0 / math.sqrt(head_size)

time: 190 us -> 205 us (1.079)
  the two profiles are of different devices: /device:TPU:9 before, /device:TPU:25 now
where the time goes in v12:
time: 205 us; the launch traced here: 201 us
  starting transfers between devices  74.8 us (36%)
  waiting for transfers between devices  65.2 us (32%)
  blocking collectives  25.1 us (12%)
  matrix products  21 us (10%)
  other arithmetic  9.16 us (4%)
  local copies, waits for them, and re-layouts  4.24 us (2%)
    ppermute x16, starting transfers between devices, shifted(): return lax.ppermute(value, axis, pairs)  55.6 us
    ppermute x15, waiting for transfers between devices, moved(): return lax.ppermute(value, 'seq', pairs)  35.2 us
    ppermute x16, waiting for transfers between devices, shifted(): return lax.ppermute(value, axis, pairs)  30 us
    psum x1, blocking collectives, on_device(): total_sq = lax.psum(squares, 'head')  25.1 us
    ppermute x15, starting transfers between devices, moved(): return lax.ppermute(value, 'seq', pairs)  19.2 us
    dot_general x18, matrix products, batched_dot(): return jnp.einsum('hij,hjk->hik', left, right, precision=highest)  5.25 us
    sub x1, other arithmetic, attend_block(): exps = jnp.exp(jnp.where(allowed[None], scores - row_top, -1e+30))  4.29 us
  transfers between devices with their start and end apart: 31, of which 10 were waited for; matrix products, arithmetic and copies ran while one was open for 14% of the time, Pallas kernels for 0%

profile of v12, /device:TPU:25, one launch (start us, length us, event | category | flops | bytes accessed | tf_op | source)
XLA Modules:
  0.0 201.2 jit_solution(221426641096572955)
XLA Ops:
  0.6 1.0 copy.88
  1.7 3.5 %collective-permute-start.27 = (bf16[256,256]{0,1:T(8,128)(2,1)S(1)}, bf16[256,256]{0,1:T(8,128)(2,1)S(1)}, u32[]{:S(2)}, u32[]{:S(2)}) collective-permute-start(bf16[256,256]{0,1:T(8,128)(2,1)S(1)} %copy.88), channel_id=1, source_target_pairs={{0,8},{8,16},{16,24},{24,32},{32,40},{40,48},{48,56},{56,64},{64,7... | collective-permute-start | bytes 393224 | tf_op jit(solution)/shard_map/ppermute | solution.py:18
  5.2 10.2 %collective-permute-start = (bf16[256,256]{0,1:T(8,128)(2,1)S(1)}, bf16[256,256]{0,1:T(8,128)(2,1)S(1)}, u32[]{:S(2)}, u32[]{:S(2)}) collective-permute-start(bf16[256,256]{0,1:T(8,128)(2,1)S(1)} %copy.88), channel_id=1, source_target_pairs={{0,40},{8,48},{16,56},{24,64},{32,72},{40,80},{48,88},{56,96},{64,... | collective-permute-start | bytes 393224 | tf_op jit(solution)/shard_map/ppermute | solution.py:18
  15.5 1.1 fusion.30
  16.6 0.8 mul.82
  17.4 1.0 fusion.28
  18.4 1.0 reshape.158
  26.1 1.0 convolution_subtract_fusion
  28.6 1.0 fusion.32
  31.8 1.3 fusion.13
  33.4 3.7 %collective-permute-start.6 = (f32[2,128,128]{2,1,0:T(8,128)S(1)}, f32[2,128,128]{2,1,0:T(8,128)S(1)}, u32[]{:S(2)}, u32[]{:S(2)}) collective-permute-start(f32[2,128,128]{2,1,0:T(8,128)S(1)} %convolution_add_fusion.12), channel_id=1, source_target_pairs={{0,8},{8,16},{16,24},{32,40},{40,48},{48,56},{64,72},{72,80},{80,8... | collective-permute-start | bytes 393224 | tf_op jit(solution)/shard_map/ppermute | solution.py:164
  37.8 4.8 %collective-permute-start.24 = (bf16[256,256]{0,1:T(8,128)(2,1)S(1)}, bf16[256,256]{0,1:T(8,128)(2,1)S(1)}, u32[]{:S(2)}, u32[]{:S(2)}) collective-permute-start(bf16[256,256]{0,1:T(8,128)(2,1)S(1)} %collective-permute-done), channel_id=1, source_target_pairs={{0,8},{8,16},{16,24},{24,32},{32,40},{40,48},{48,56},{56,64},{64,7... | collective-permute-start | bytes 393224 | tf_op jit(solution)/shard_map/ppermute | solution.py:18
  42.5 2.6 %collective-permute-start.1 = (f32[2,128,128]{2,1,0:T(8,128)S(1)}, f32[2,128,128]{2,1,0:T(8,128)S(1)}, u32[]{:S(2)}, u32[]{:S(2)}) collective-permute-start(f32[2,128,128]{2,1,0:T(8,128)S(1)} %fusion.67), channel_id=1, source_target_pairs={{0,8},{8,16},{16,24},{32,40},{40,48},{48,56},{64,72},{72,80},{80,8... | collective-permute-start | bytes 393224 | tf_op jit(solution)/shard_map/ppermute | solution.py:164
  45.2 1.9 collective-permute-start.28
  47.4 3.1 %collective-permute-start.7 = (f32[2,128,128]{2,1,0:T(8,128)S(1)}, f32[2,128,128]{2,1,0:T(8,128)S(1)}, u32[]{:S(2)}, u32[]{:S(2)}) collective-permute-start(f32[2,128,128]{2,1,0:T(8,128)S(1)} %fusion.23), channel_id=1, source_target_pairs={{0,16},{8,24},{32,48},{40,56},{64,80},{72,88},{96,112},{104,120},{... | collective-permute-start | bytes 393224 | tf_op jit(solution)/shard_map/ppermute | solution.py:164
  50.8 1.7 collective-permute-start.2
  53.0 2.5 %collective-permute-start.29 = (bf16[256,256]{0,1:T(8,128)(2,1)S(1)}, bf16[256,256]{0,1:T(8,128)(2,1)S(1)}, u32[]{:S(2)}, u32[]{:S(2)}) collective-permute-start(bf16[256,256]{0,1:T(8,128)(2,1)S(1)} %collective-permute-done.28), channel_id=1, source_target_pairs={{0,8},{8,16},{16,24},{24,32},{32,40},{40,48},{48,56},{56,64},{64,7... | collective-permute-start | bytes 393224 | tf_op jit(solution)/shard_map/ppermute | solution.py:18
  55.8 1.9 collective-permute-start.25
  58.3 0.7 collective-permute-start.8
  59.2 0.7 collective-permute-start.3
  60.8 7.5 %collective-permute-start.30 = (bf16[256,256]{0,1:T(8,128)(2,1)S(1)}, bf16[256,256]{0,1:T(8,128)(2,1)S(1)}, u32[]{:S(2)}, u32[]{:S(2)}) collective-permute-start(bf16[256,256]{0,1:T(8,128)(2,1)S(1)} %collective-permute-done.29), channel_id=1, source_target_pairs={{0,8},{8,16},{16,24},{24,32},{32,40},{40,48},{48,56},{56,64},{64,7... | collective-permute-start | bytes 393224 | tf_op jit(solution)/shard_map/ppermute | solution.py:18
  68.6 4.1 %collective-permute-start.26 = (bf16[256,256]{0,1:T(8,128)(2,1)S(1)}, bf16[256,256]{0,1:T(8,128)(2,1)S(1)}, u32[]{:S(2)}, u32[]{:S(2)}) collective-permute-start(bf16[256,256]{0,1:T(8,128)(2,1)S(1)} %collective-permute-done.25), channel_id=1, source_target_pairs={{0,8},{8,16},{16,24},{24,32},{32,40},{40,48},{48,56},{56,64},{64,7... | collective-permute-start | bytes 393224 | tf_op jit(solution)/shard_map/ppermute | solution.py:18
  73.4 0.7 collective-permute-start.9
  74.4 0.7 collective-permute-start.4
  75.0 6.4 %collective-permute-done.26 = bf16[256,256]{0,1:T(8,128)(2,1)S(1)} collective-permute-done((bf16[256,256]{0,1:T(8,128)(2,1)S(1)}, bf16[256,256]{0,1:T(8,128)(2,1)S(1)}, u32[]{:S(2)}, u32[]{:S(2)}) %collective-permute-start.26) | collective-permute-done | bytes 131104 | tf_op jit(solution)/shard_map/ppermute | solution.py:18
  81.8 0.7 collective-permute-start.10
  82.7 0.7 collective-permute-start.5
  87.0 1.3 collective-permute-start.12
  88.4 35.2 %collective-permute-done.12 = f32[2,128,128]{2,1,0:T(8,128)S(1)} collective-permute-done((f32[2,128,128]{2,1,0:T(8,128)S(1)}, f32[2,128,128]{2,1,0:T(8,128)S(1)}, u32[]{:S(2)}, u32[]{:S(2)}) %collective-permute-start.12) | collective-permute-done | bytes 131104 | tf_op jit(solution)/shard_map/ppermute | solution.py:164
  124.0 3.4 %collective-permute-start.16 = (bf16[256,256]{0,1:T(8,128)(2,1)S(1)}, bf16[256,256]{0,1:T(8,128)(2,1)S(1)}, u32[]{:S(2)}, u32[]{:S(2)}) collective-permute-start(bf16[256,256]{0,1:T(8,128)(2,1)S(1)} %bitcast.170), channel_id=1, source_target_pairs={{0,40},{8,48},{16,56},{24,64},{32,72},{40,80},{48,88},{56,96},{64,... | collective-permute-start | bytes 393224 | tf_op jit(solution)/shard_map/ppermute | solution.py:18
  127.4 1.9 collective-permute-start.20
  129.3 8.1 %collective-permute-done.16 = bf16[256,256]{0,1:T(8,128)(2,1)S(1)} collective-permute-done((bf16[256,256]{0,1:T(8,128)(2,1)S(1)}, bf16[256,256]{0,1:T(8,128)(2,1)S(1)}, u32[]{:S(2)}, u32[]{:S(2)}) %collective-permute-start.16) | collective-permute-done | bytes 131104 | tf_op jit(solution)/shard_map/ppermute | solution.py:18
  137.4 3.8 %collective-permute-start.17 = (bf16[256,256]{0,1:T(8,128)(2,1)S(1)}, bf16[256,256]{0,1:T(8,128)(2,1)S(1)}, u32[]{:S(2)}, u32[]{:S(2)}) collective-permute-start(bf16[256,256]{0,1:T(8,128)(2,1)S(1)} %collective-permute-done.16), channel_id=1, source_target_pairs={{0,8},{8,16},{16,24},{24,32},{32,40},{40,48},{48,56},{56,64},{64,7... | collective-permute-start | bytes 393224 | tf_op jit(solution)/shard_map/ppermute | solution.py:18
  141.3 3.5 %collective-permute-done.20 = bf16[256,256]{0,1:T(8,128)(2,1)S(1)} collective-permute-done((bf16[256,256]{0,1:T(8,128)(2,1)S(1)}, bf16[256,256]{0,1:T(8,128)(2,1)S(1)}, u32[]{:S(2)}, u32[]{:S(2)}) %collective-permute-start.20) | collective-permute-done | bytes 131104 | tf_op jit(solution)/shard_map/ppermute | solution.py:18
  144.8 1.9 collective-permute-start.21
  146.7 2.7 %collective-permute-done.17 = bf16[256,256]{0,1:T(8,128)(2,1)S(1)} collective-permute-done((bf16[256,256]{0,1:T(8,128)(2,1)S(1)}, bf16[256,256]{0,1:T(8,128)(2,1)S(1)}, u32[]{:S(2)}, u32[]{:S(2)}) %collective-permute-start.17) | collective-permute-done | bytes 131104 | tf_op jit(solution)/shard_map/ppermute | solution.py:18
  149.4 1.9 collective-permute-start.18
  151.3 0.8 fusion.6
  152.6 1.9 collective-permute-start.22
  154.5 2.7 %collective-permute-done.18 = bf16[256,256]{0,1:T(8,128)(2,1)S(1)} collective-permute-done((bf16[256,256]{0,1:T(8,128)(2,1)S(1)}, bf16[256,256]{0,1:T(8,128)(2,1)S(1)}, u32[]{:S(2)}, u32[]{:S(2)}) %collective-permute-start.18) | collective-permute-done | bytes 131104 | tf_op jit(solution)/shard_map/ppermute | solution.py:18
  157.2 1.9 collective-permute-start.19
  159.1 4.3 %fusion.77 = (f32[2,256]{1,0:T(2,128)S(1)}, f32[2,256,2304]{1,2,0:T(8,128)}) fusion(f32[2,256,2304]{1,2,0:T(8,128)S(1)} %fusion.6, pred[256,2304]{0,1:T(8,128)(4,1)S(1)} %fusion.13), kind=kOutput, calls=%fused_computation.147 | output fusion | flops 4720895 | bytes 10029056 | tf_op jit(solution)/shard_map/while/body/eval_jaxpr/sub | solution.py:231
  163.4 0.8 copy.99
  164.2 2.5 %collective-permute-start.23 = (bf16[256,256]{0,1:T(8,128)(2,1)S(1)}, bf16[256,256]{0,1:T(8,128)(2,1)S(1)}, u32[]{:S(2)}, u32[]{:S(2)}) collective-permute-start(bf16[256,256]{0,1:T(8,128)(2,1)S(1)} %collective-permute-done.22), channel_id=1, source_target_pairs={{0,8},{8,16},{16,24},{24,32},{32,40},{40,48},{48,56},{56,64},{64,7... | collective-permute-start | bytes 393224 | tf_op jit(solution)/shard_map/ppermute | solution.py:18
  166.7 5.5 %collective-permute-done.23 = bf16[256,256]{0,1:T(8,128)(2,1)S(1)} collective-permute-done((bf16[256,256]{0,1:T(8,128)(2,1)S(1)}, bf16[256,256]{0,1:T(8,128)(2,1)S(1)}, u32[]{:S(2)}, u32[]{:S(2)}) %collective-permute-start.23) | collective-permute-done | bytes 131104 | tf_op jit(solution)/shard_map/ppermute | solution.py:18
  172.3 2.9 %fusion.31 = (f32[256]{0:T(256)S(1)}, f32[2,128,256]{2,1,0:T(8,128)S(1)}) fusion(bf16[2304,2,128]{0,2,1:T(8,128)(2,1)S(1)} %bitcast.184, f32[2,256,2304]{1,2,0:T(8,128)} %get-tuple-element.35, f32[2,256]{1,0:T(2,128)S(1)} %get-tuple-element.34), kind=kOutput, calls=%fused_computation.63 | convolution fusion | flops 304480000 | bytes 6163456 | tf_op jit(solution)/shard_map/while/body/eval_jaxpr/hqk,khd->qhd/dot_general | solution.py:233
  175.2 25.1 %psum.7 = f32[256]{0:T(256)S(1)} all-reduce(f32[256]{0:T(256)S(1)} %get-tuple-element.36), channel_id=1, replica_groups=mesh['seq'=64,'head'=8] {'head'}, use_global_device_ids=true, to_apply=%region_5.6 | all-reduce | flops 256 | bytes 2048 | tf_op jit(solution)/shard_map/psum | solution.py:241
  200.5 0.8 multiply_convert_fusion
  (113 shorter events, 20.5 us)
Async XLA Ops:
  0.6 150.7 %copy-start = (bf16[256,256]{1,0:T(8,128)(2,1)S(1)}, bf16[256,256]{1,0:T(8,128)(2,1)}, u32[]{:S(2)}) copy-start(bf16[256,256]{1,0:T(8,128)(2,1)} %param.11) | copy-start | bytes 393220
  1.7 43.5 %collective-permute-start.27 = (bf16[256,256]{0,1:T(8,128)(2,1)S(1)}, bf16[256,256]{0,1:T(8,128)(2,1)S(1)}, u32[]{:S(2)}, u32[]{:S(2)}) collective-permute-start(bf16[256,256]{0,1:T(8,128)(2,1)S(1)} %copy.88), channel_id=1, source_target_pairs={{0,8},{8,16},{16,24},{24,32},{32,40},{40,48},{48,56},{56,64},{64,7... | collective-permute-start | bytes 393224 | tf_op jit(solution)/shard_map/ppermute | solution.py:18
  5.2 28.1 %collective-permute-start = (bf16[256,256]{0,1:T(8,128)(2,1)S(1)}, bf16[256,256]{0,1:T(8,128)(2,1)S(1)}, u32[]{:S(2)}, u32[]{:S(2)}) collective-permute-start(bf16[256,256]{0,1:T(8,128)(2,1)S(1)} %copy.88), channel_id=1, source_target_pairs={{0,40},{8,48},{16,56},{24,64},{32,72},{40,80},{48,88},{56,96},{64,... | collective-permute-start | bytes 393224 | tf_op jit(solution)/shard_map/ppermute | solution.py:18
  26.1 1.8 copy-start.1
  33.4 13.7 %collective-permute-start.6 = (f32[2,128,128]{2,1,0:T(8,128)S(1)}, f32[2,128,128]{2,1,0:T(8,128)S(1)}, u32[]{:S(2)}, u32[]{:S(2)}) collective-permute-start(f32[2,128,128]{2,1,0:T(8,128)S(1)} %convolution_add_fusion.12), channel_id=1, source_target_pairs={{0,8},{8,16},{16,24},{32,40},{40,48},{48,56},{64,72},{72,80},{80,8... | collective-permute-start | bytes 393224 | tf_op jit(solution)/shard_map/ppermute | solution.py:164
  37.8 18.0 %collective-permute-start.24 = (bf16[256,256]{0,1:T(8,128)(2,1)S(1)}, bf16[256,256]{0,1:T(8,128)(2,1)S(1)}, u32[]{:S(2)}, u32[]{:S(2)}) collective-permute-start(bf16[256,256]{0,1:T(8,128)(2,1)S(1)} %collective-permute-done), channel_id=1, source_target_pairs={{0,8},{8,16},{16,24},{24,32},{32,40},{40,48},{48,56},{56,64},{64,7... | collective-permute-start | bytes 393224 | tf_op jit(solution)/shard_map/ppermute | solution.py:18
  42.5 8.0 %collective-permute-start.1 = (f32[2,128,128]{2,1,0:T(8,128)S(1)}, f32[2,128,128]{2,1,0:T(8,128)S(1)}, u32[]{:S(2)}, u32[]{:S(2)}) collective-permute-start(f32[2,128,128]{2,1,0:T(8,128)S(1)} %fusion.67), channel_id=1, source_target_pairs={{0,8},{8,16},{16,24},{32,40},{40,48},{48,56},{64,72},{72,80},{80,8... | collective-permute-start | bytes 393224 | tf_op jit(solution)/shard_map/ppermute | solution.py:164
  45.2 7.8 %collective-permute-start.28 = (bf16[256,256]{0,1:T(8,128)(2,1)S(1)}, bf16[256,256]{0,1:T(8,128)(2,1)S(1)}, u32[]{:S(2)}, u32[]{:S(2)}) collective-permute-start(bf16[256,256]{0,1:T(8,128)(2,1)S(1)} %collective-permute-done.27), channel_id=1, source_target_pairs={{0,8},{8,16},{16,24},{24,32},{32,40},{40,48},{48,56},{56,64},{64,7... | collective-permute-start | bytes 393224 | tf_op jit(solution)/shard_map/ppermute | solution.py:18
  47.4 10.6 %collective-permute-start.7 = (f32[2,128,128]{2,1,0:T(8,128)S(1)}, f32[2,128,128]{2,1,0:T(8,128)S(1)}, u32[]{:S(2)}, u32[]{:S(2)}) collective-permute-start(f32[2,128,128]{2,1,0:T(8,128)S(1)} %fusion.23), channel_id=1, source_target_pairs={{0,16},{8,24},{32,48},{40,56},{64,80},{72,88},{96,112},{104,120},{... | collective-permute-start | bytes 393224 | tf_op jit(solution)/shard_map/ppermute | solution.py:164
  50.8 8.2 %collective-permute-start.2 = (f32[2,128,128]{2,1,0:T(8,128)S(1)}, f32[2,128,128]{2,1,0:T(8,128)S(1)}, u32[]{:S(2)}, u32[]{:S(2)}) collective-permute-start(f32[2,128,128]{2,1,0:T(8,128)S(1)} %convolution_select_fusion.6), channel_id=1, source_target_pairs={{0,16},{8,24},{32,48},{40,56},{64,80},{72,88},{96,112},{104,120},{... | collective-permute-start | bytes 393224 | tf_op jit(solution)/shard_map/ppermute | solution.py:164
  53.0 7.8 %collective-permute-start.29 = (bf16[256,256]{0,1:T(8,128)(2,1)S(1)}, bf16[256,256]{0,1:T(8,128)(2,1)S(1)}, u32[]{:S(2)}, u32[]{:S(2)}) collective-permute-start(bf16[256,256]{0,1:T(8,128)(2,1)S(1)} %collective-permute-done.28), channel_id=1, source_target_pairs={{0,8},{8,16},{16,24},{24,32},{32,40},{40,48},{48,56},{56,64},{64,7... | collective-permute-start | bytes 393224 | tf_op jit(solution)/shard_map/ppermute | solution.py:18
  55.8 12.8 %collective-permute-start.25 = (bf16[256,256]{0,1:T(8,128)(2,1)S(1)}, bf16[256,256]{0,1:T(8,128)(2,1)S(1)}, u32[]{:S(2)}, u32[]{:S(2)}) collective-permute-start(bf16[256,256]{0,1:T(8,128)(2,1)S(1)} %collective-permute-done.24), channel_id=1, source_target_pairs={{0,8},{8,16},{16,24},{24,32},{32,40},{40,48},{48,56},{56,64},{64,7... | collective-permute-start | bytes 393224 | tf_op jit(solution)/shard_map/ppermute | solution.py:18
  58.3 14.8 %collective-permute-start.8 = (f32[2,128,128]{2,1,0:T(8,128)S(1)}, f32[2,128,128]{2,1,0:T(8,128)S(1)}, u32[]{:S(2)}, u32[]{:S(2)}) collective-permute-start(f32[2,128,128]{2,1,0:T(8,128)S(1)} %fusion.22), channel_id=1, source_target_pairs={{24,56},{56,88},{88,120},{120,152},{152,184},{184,216},{216,248},{... | collective-permute-start | bytes 393224 | tf_op jit(solution)/shard_map/ppermute | solution.py:164
  59.2 14.8 %collective-permute-start.3 = (f32[2,128,128]{2,1,0:T(8,128)S(1)}, f32[2,128,128]{2,1,0:T(8,128)S(1)}, u32[]{:S(2)}, u32[]{:S(2)}) collective-permute-start(f32[2,128,128]{2,1,0:T(8,128)S(1)} %convolution_select_fusion.4), channel_id=1, source_target_pairs={{24,56},{56,88},{88,120},{120,152},{152,184},{184,216},{216,248},{... | collective-permute-start | bytes 393224 | tf_op jit(solution)/shard_map/ppermute | solution.py:164
  60.8 27.5 %collective-permute-start.30 = (bf16[256,256]{0,1:T(8,128)(2,1)S(1)}, bf16[256,256]{0,1:T(8,128)(2,1)S(1)}, u32[]{:S(2)}, u32[]{:S(2)}) collective-permute-start(bf16[256,256]{0,1:T(8,128)(2,1)S(1)} %collective-permute-done.29), channel_id=1, source_target_pairs={{0,8},{8,16},{16,24},{24,32},{32,40},{40,48},{48,56},{56,64},{64,7... | collective-permute-start | bytes 393224 | tf_op jit(solution)/shard_map/ppermute | solution.py:18
  68.6 12.8 %collective-permute-start.26 = (bf16[256,256]{0,1:T(8,128)(2,1)S(1)}, bf16[256,256]{0,1:T(8,128)(2,1)S(1)}, u32[]{:S(2)}, u32[]{:S(2)}) collective-permute-start(bf16[256,256]{0,1:T(8,128)(2,1)S(1)} %collective-permute-done.25), channel_id=1, source_target_pairs={{0,8},{8,16},{16,24},{24,32},{32,40},{40,48},{48,56},{56,64},{64,7... | collective-permute-start | bytes 393224 | tf_op jit(solution)/shard_map/ppermute | solution.py:18
  73.4 8.1 %collective-permute-start.9 = (f32[2,128,128]{2,1,0:T(8,128)S(1)}, f32[2,128,128]{2,1,0:T(8,128)S(1)}, u32[]{:S(2)}, u32[]{:S(2)}) collective-permute-start(f32[2,128,128]{2,1,0:T(8,128)S(1)} %fusion.21), channel_id=1, source_target_pairs={{24,88},{56,120},{88,152},{120,184},{152,216},{184,248},{216,280},... | collective-permute-start | bytes 393224 | tf_op jit(solution)/shard_map/ppermute | solution.py:164
  74.4 8.1 %collective-permute-start.4 = (f32[2,128,128]{2,1,0:T(8,128)S(1)}, f32[2,128,128]{2,1,0:T(8,128)S(1)}, u32[]{:S(2)}, u32[]{:S(2)}) collective-permute-start(f32[2,128,128]{2,1,0:T(8,128)S(1)} %convolution_select_fusion.3), channel_id=1, source_target_pairs={{24,88},{56,120},{88,152},{120,184},{152,216},{184,248},{216,280},... | collective-permute-start | bytes 393224 | tf_op jit(solution)/shard_map/ppermute | solution.py:164
  81.8 1.6 collective-permute-start.10
  82.7 1.6 collective-permute-start.5
  83.7 1.0 collective-permute-start.11
  85.0 3.4 %collective-permute-start.15 = (f32[2,128,128]{2,1,0:T(8,128)S(1)}, f32[2,128,128]{2,1,0:T(8,128)S(1)}, u32[]{:S(2)}, u32[]{:S(2)}) collective-permute-start(f32[2,128,128]{2,1,0:T(8,128)S(1)} %fusion.18), channel_id=1, source_target_pairs={{24,56},{56,88},{88,120},{120,152},{152,184},{184,216},{216,248},{... | collective-permute-start | bytes 393224 | tf_op jit(solution)/shard_map/ppermute | solution.py:164
  85.6 2.7 %collective-permute-start.14 = (f32[2,128,128]{2,1,0:T(8,128)S(1)}, f32[2,128,128]{2,1,0:T(8,128)S(1)}, u32[]{:S(2)}, u32[]{:S(2)}) collective-permute-start(f32[2,128,128]{2,1,0:T(8,128)S(1)} %fusion.18), channel_id=1, source_target_pairs={{24,48},{56,80},{88,112},{120,144},{152,176},{184,208},{216,240},{... | collective-permute-start | bytes 393224 | tf_op jit(solution)/shard_map/ppermute | solution.py:164
  86.3 2.0 %collective-permute-start.13 = (f32[2,128,128]{2,1,0:T(8,128)S(1)}, f32[2,128,128]{2,1,0:T(8,128)S(1)}, u32[]{:S(2)}, u32[]{:S(2)}) collective-permute-start(f32[2,128,128]{2,1,0:T(8,128)S(1)} %fusion.18), channel_id=1, source_target_pairs={{24,40},{56,72},{88,104},{120,136},{152,168},{184,200},{216,232},{... | collective-permute-start | bytes 393224 | tf_op jit(solution)/shard_map/ppermute | solution.py:164
  87.0 36.6 %collective-permute-start.12 = (f32[2,128,128]{2,1,0:T(8,128)S(1)}, f32[2,128,128]{2,1,0:T(8,128)S(1)}, u32[]{:S(2)}, u32[]{:S(2)}) collective-permute-start(f32[2,128,128]{2,1,0:T(8,128)S(1)} %fusion.18), channel_id=1, source_target_pairs={{24,32},{56,64},{88,96},{120,128},{152,160},{184,192},{216,224},{2... | collective-permute-start | bytes 393224 | tf_op jit(solution)/shard_map/ppermute | solution.py:164
  124.0 13.5 %collective-permute-start.16 = (bf16[256,256]{0,1:T(8,128)(2,1)S(1)}, bf16[256,256]{0,1:T(8,128)(2,1)S(1)}, u32[]{:S(2)}, u32[]{:S(2)}) collective-permute-start(bf16[256,256]{0,1:T(8,128)(2,1)S(1)} %bitcast.170), channel_id=1, source_target_pairs={{0,40},{8,48},{16,56},{24,64},{32,72},{40,80},{48,88},{56,96},{64,... | collective-permute-start | bytes 393224 | tf_op jit(solution)/shard_map/ppermute | solution.py:18
  127.4 17.4 %collective-permute-start.20 = (bf16[256,256]{0,1:T(8,128)(2,1)S(1)}, bf16[256,256]{0,1:T(8,128)(2,1)S(1)}, u32[]{:S(2)}, u32[]{:S(2)}) collective-permute-start(bf16[256,256]{0,1:T(8,128)(2,1)S(1)} %bitcast.171), channel_id=1, source_target_pairs={{0,8},{8,16},{16,24},{24,32},{32,40},{40,48},{48,56},{56,64},{64,7... | collective-permute-start | bytes 393224 | tf_op jit(solution)/shard_map/ppermute | solution.py:18
  137.4 12.0 %collective-permute-start.17 = (bf16[256,256]{0,1:T(8,128)(2,1)S(1)}, bf16[256,256]{0,1:T(8,128)(2,1)S(1)}, u32[]{:S(2)}, u32[]{:S(2)}) collective-permute-start(bf16[256,256]{0,1:T(8,128)(2,1)S(1)} %collective-permute-done.16), channel_id=1, source_target_pairs={{0,8},{8,16},{16,24},{24,32},{32,40},{40,48},{48,56},{56,64},{64,7... | collective-permute-start | bytes 393224 | tf_op jit(solution)/shard_map/ppermute | solution.py:18
  144.8 7.8 %collective-permute-start.21 = (bf16[256,256]{0,1:T(8,128)(2,1)S(1)}, bf16[256,256]{0,1:T(8,128)(2,1)S(1)}, u32[]{:S(2)}, u32[]{:S(2)}) collective-permute-start(bf16[256,256]{0,1:T(8,128)(2,1)S(1)} %collective-permute-done.20), channel_id=1, source_target_pairs={{0,8},{8,16},{16,24},{24,32},{32,40},{40,48},{48,56},{56,64},{64,7... | collective-permute-start | bytes 393224 | tf_op jit(solution)/shard_map/ppermute | solution.py:18
  149.4 7.8 %collective-permute-start.18 = (bf16[256,256]{0,1:T(8,128)(2,1)S(1)}, bf16[256,256]{0,1:T(8,128)(2,1)S(1)}, u32[]{:S(2)}, u32[]{:S(2)}) collective-permute-start(bf16[256,256]{0,1:T(8,128)(2,1)S(1)} %collective-permute-done.17), channel_id=1, source_target_pairs={{0,8},{8,16},{16,24},{24,32},{32,40},{40,48},{48,56},{56,64},{64,7... | collective-permute-start | bytes 393224 | tf_op jit(solution)/shard_map/ppermute | solution.py:18
  152.6 11.5 %collective-permute-start.22 = (bf16[256,256]{0,1:T(8,128)(2,1)S(1)}, bf16[256,256]{0,1:T(8,128)(2,1)S(1)}, u32[]{:S(2)}, u32[]{:S(2)}) collective-permute-start(bf16[256,256]{0,1:T(8,128)(2,1)S(1)} %collective-permute-done.21), channel_id=1, source_target_pairs={{0,8},{8,16},{16,24},{24,32},{32,40},{40,48},{48,56},{56,64},{64,7... | collective-permute-start | bytes 393224 | tf_op jit(solution)/shard_map/ppermute | solution.py:18
  157.2 9.5 %collective-permute-start.19 = (bf16[256,256]{0,1:T(8,128)(2,1)S(1)}, bf16[256,256]{0,1:T(8,128)(2,1)S(1)}, u32[]{:S(2)}, u32[]{:S(2)}) collective-permute-start(bf16[256,256]{0,1:T(8,128)(2,1)S(1)} %collective-permute-done.18), channel_id=1, source_target_pairs={{0,8},{8,16},{16,24},{24,32},{32,40},{40,48},{48,56},{56,64},{64,7... | collective-permute-start | bytes 393224 | tf_op jit(solution)/shard_map/ppermute | solution.py:18
  164.2 8.0 %collective-permute-start.23 = (bf16[256,256]{0,1:T(8,128)(2,1)S(1)}, bf16[256,256]{0,1:T(8,128)(2,1)S(1)}, u32[]{:S(2)}, u32[]{:S(2)}) collective-permute-start(bf16[256,256]{0,1:T(8,128)(2,1)S(1)} %collective-permute-done.22), channel_id=1, source_target_pairs={{0,8},{8,16},{16,24},{24,32},{32,40},{40,48},{48,56},{56,64},{64,7... | collective-permute-start | bytes 393224 | tf_op jit(solution)/shard_map/ppermute | solution.py:18
  172.3 28.2 %copy-start.2 = (f32[256]{0:T(256)S(1)}, f32[256]{0:T(256)}, u32[]{:S(2)}) copy-start(f32[256]{0:T(256)} %param.13) | copy-start | bytes 3076

commit v13 on v8

--- a/solution.py
+++ b/solution.py
@@ -3,9 +3,10 @@
 import jax
 import jax.numpy as jnp
 from jax import lax
-from jax.sharding import PartitionSpec as P
+from jax.sharding import Mesh, PartitionSpec as P
 
 GROUP_TOKENS = 64
+SEQ = ("rows", "cols")
 WINDOW = 2048
 
 
@@ -105,14 +106,14 @@
         by_head(q_delta), by_head(k_delta), by_head(v_delta), write_rate.T
     )
     transit, carried = jax.vmap(local_pair)(k_unit, writes, updates)
-    position = lax.axis_index("seq")
-    seq_size = lax.axis_size("seq")
+    position = lax.axis_index(SEQ)
+    seq_size = lax.axis_size(SEQ)
     group = min(4, seq_size)
     rank = position % group
 
     def moved(value, by, sources):
         pairs = [(i, i + by) for i in sources if 0 <= i + by < seq_size]
-        return lax.ppermute(value, "seq", pairs)
+        return lax.ppermute(value, SEQ, pairs)
 
     identity = jnp.broadcast_to(jnp.eye(head_size, dtype=jnp.float32), transit.shape)
     before_transit = identity
@@ -165,16 +166,25 @@
         for lane in range(lanes):
             first = lane * lane_length + 1
             last = min(shard_reach, (lane + 1) * lane_length)
-            piece = shifted(own, "seq", first)
+            piece = shifted(own, SEQ, first)
             pieces.append(piece)
             for _ in range(first, last):
-                piece = shifted(piece, "seq", 1)
+                piece = shifted(piece, SEQ, 1)
                 pieces.append(piece)
         return jnp.concatenate(pieces[::-1] + [own], axis=0)
 
-    rows_all = (window_rows(k_attn, 2), window_rows(delta_out, 2))
+    row_count = lax.axis_size("rows")
+    col_count = lax.axis_size("cols")
+    prev_row = lax.ppermute(k_attn, "rows", [(i, i + 1) for i in range(row_count - 1)])
+    gathered = lax.all_gather(jnp.stack((prev_row, k_attn)), "cols")
+    flat = jnp.concatenate((gathered[:, 0], gathered[:, 1]), axis=0)
+    near = lax.dynamic_slice_in_dim(
+        flat, lax.axis_index("cols") + col_count - shard_reach, shard_reach, 0
+    )
+    key_rows = jnp.concatenate((near.reshape(shard_reach * tok_rows, features), k_attn), axis=0)
+    rows_all = (key_rows, window_rows(delta_out, 2))
     block_rows = min(512, tok_rows)
-    first_row = lax.axis_index("seq") * tok_rows
+    first_row = lax.axis_index(SEQ) * tok_rows
     score_scale = 1.0 / math.sqrt(head_size)
 
     def attend_block(block_start):
@@ -210,19 +220,25 @@
 
 
 def solution(mesh):
+    seq_devices = mesh.devices[:, 0]
+    cols = len({device.coords[-1] for device in seq_devices})
+    row_mesh = Mesh(
+        mesh.devices.reshape(mesh.shape["seq"] // cols, cols, mesh.shape["head"]),
+        ("rows", "cols", "head"),
+    )
     placed = (
-        P("seq", "head"),
-        P("seq", "head"),
-        P("seq", "head"),
-        P("seq", "head"),
-        P("seq", "head"),
-        P("seq", "head"),
+        P(SEQ, "head"),
+        P(SEQ, "head"),
+        P(SEQ, "head"),
+        P(SEQ, "head"),
+        P(SEQ, "head"),
+        P(SEQ, "head"),
         P("head"),
     )
     return jax.shard_map(
         on_device,
-        mesh=mesh,
+        mesh=row_mesh,
         in_specs=placed,
-        out_specs=(P("seq", "head"), P("seq", "head")),
+        out_specs=(P(SEQ, "head"), P(SEQ, "head")),
         check_vma=False,
     )

time: 195 us -> 225 us (1.15)
  waiting for transfers between devices: 61.9 us -> 106 us
  starting transfers between devices: 69.6 us -> 37 us
  local copies, waits for them, and re-layouts: 4.75 us -> 19.1 us
  between operations: 1.82 us -> 15 us
  blocking collectives: 24.3 us -> 17.3 us
  matrix products: 23.6 us -> 21.2 us
    ppermute x15 -> x16, waiting for transfers between devices: 26.4 us -> 76.7 us  [the longest x15 76.7 us: moved(): return lax.ppermute(value, SEQ, pairs)]
    ppermute x16 -> x8, starting transfers between devices: 49.3 us -> 15.3 us  [shifted(): return lax.ppermute(value, axis, pairs)]
    unnamed x44 -> x32, local copies, waits for them, and re-layouts: 3.3 us -> 11.3 us
    psum x1, blocking collectives: 24.3 us -> 17.3 us  [on_device(): total_sq = lax.psum(squares, 'head')]
    ppermute x16 -> x8, waiting for transfers between devices: 35.5 us -> 29.6 us  [shifted(): return lax.ppermute(value, axis, pairs)]
    slice x0 -> x1, local copies, waits for them, and re-layouts: none -> 5.06 us  [on_device(): flat = jnp.concatenate((gathered[:, 0], gathered[:, 1]), axis=0)]
    dot_general x1, matrix products: 2.93 us -> 0.51 us  [attend_block(): jnp.einsum('hqk,khd->qhd', weights, near_values, preferred_element_type=j...]
    ppermute x15 -> x16, starting transfers between devices: 20.3 us -> 21.7 us  [the longest x15 20.4 us: moved(): return lax.ppermute(value, SEQ, pairs)]
  transfers between devices with their start and end apart: 31 -> 25, of which waited for: 8 -> 8; matrix products, arithmetic and copies ran while one was open for 13% -> 12% of each run, Pallas kernels for 0% -> 0%
where the time goes in v13:
time: 225 us
  waiting for transfers between devices  106 us (47%)
  starting transfers between devices  37 us (16%)
  matrix products  21.2 us (9%)
  local copies, waits for them, and re-layouts  19.1 us (8%)
  blocking collectives  17.3 us (8%)
  between operations  15 us (7%)
  other arithmetic  8.24 us (4%)
    ppermute x15, waiting for transfers between devices, moved(): return lax.ppermute(value, SEQ, pairs)  76.7 us
    ppermute x8, waiting for transfers between devices, shifted(): return lax.ppermute(value, axis, pairs)  29.6 us
    ppermute x15, starting transfers between devices, moved(): return lax.ppermute(value, SEQ, pairs)  20.4 us
    psum x1, blocking collectives, on_device(): total_sq = lax.psum(squares, 'head')  17.3 us
    ppermute x8, starting transfers between devices, shifted(): return lax.ppermute(value, axis, pairs)  15.3 us
    unnamed x32, local copies, waits for them, and re-layouts  11.3 us
    slice x1, local copies, waits for them, and re-layouts, on_device(): flat = jnp.concatenate((gathered[:, 0], gathered[:, 1]), axis=0)  5.06 us
  transfers between devices with their start and end apart: 25, of which 8 were waited for; matrix products, arithmetic and copies ran while one was open for 12% of the time, Pallas kernels for 0%

profile of v13, /device:TPU:25, one launch (start us, length us, event | category | flops | bytes accessed | tf_op | source)
XLA Modules:
  0.0 224.5 jit_solution(3094908728327397991)
XLA Ops:
  7.2 1.3 collective-permute-start.23
  8.6 0.8 mul.84
  9.3 1.0 copy.69
  10.6 1.0 copy.71
  17.3 5.7 %while.30 = (s32[]{:T(128)}, f32[2,128,128]{2,1,0:T(8,128)S(1)}, f32[2,128,128]{2,1,0:T(8,128)S(1)}, f32[4,2,64,128]{3,2,1,0:T(8,128)S(1)}, f32[4,2,64,128]{3,2,...) while((s32[]{:T(128)}, f32[2,128,128]{2,1,0:T(8,128)S(1)}, ...), condition=%wide.region_2.3_spmd.clone, body=%wide.region_1.0_spmd.clone.sunk | while | flops 151126016 | bytes 1837159 | solution.py:75
  23.0 3.7 %collective-permute-start.5 = (f32[2,128,128]{2,1,0:T(8,128)S(1)}, f32[2,128,128]{2,1,0:T(8,128)S(1)}, u32[]{:S(2)}, u32[]{:S(2)}) collective-permute-start(f32[2,128,128]{2,1,0:T(8,128)S(1)} %get-tuple-element.101), channel_id=1, source_target_pairs={{0,8},{8,16},{16,24},{32,40},{40,48},{48,56},{64,72},{72,80},{80,8... | collective-permute-start | bytes 393224 | tf_op jit(solution)/shard_map/ppermute | solution.py:116
  26.6 3.6 %collective-permute-start = (f32[2,128,128]{2,1,0:T(8,128)S(1)}, f32[2,128,128]{2,1,0:T(8,128)S(1)}, u32[]{:S(2)}, u32[]{:S(2)}) collective-permute-start(f32[2,128,128]{2,1,0:T(8,128)S(1)} %get-tuple-element.100), channel_id=1, source_target_pairs={{0,8},{8,16},{16,24},{32,40},{40,48},{48,56},{64,72},{72,80},{80,8... | collective-permute-start | bytes 393224 | tf_op jit(solution)/shard_map/ppermute | solution.py:116
  31.2 0.7 pad_maximum_fusion
  32.2 3.3 %collective-permute-start.6 = (f32[2,128,128]{2,1,0:T(8,128)S(1)}, f32[2,128,128]{2,1,0:T(8,128)S(1)}, u32[]{:S(2)}, u32[]{:S(2)}) collective-permute-start(f32[2,128,128]{2,1,0:T(8,128)S(1)} %fusion.59), channel_id=1, source_target_pairs={{0,16},{8,24},{32,48},{40,56},{64,80},{72,88},{96,112},{104,120},{... | collective-permute-start | bytes 393224 | tf_op jit(solution)/shard_map/ppermute | solution.py:116
  35.8 1.7 collective-permute-start.1
  38.4 0.7 collective-permute-start.7
  39.0 1.2 collective-permute-done.1
  40.5 0.7 collective-permute-start.2
  41.8 0.7 collective-permute-start.8
  42.7 0.7 collective-permute-start.3
  43.7 0.7 collective-permute-start.9
  44.7 0.7 collective-permute-start.4
  45.6 0.7 collective-permute-start.10
  46.9 0.7 collective-permute-start.14
  47.6 0.7 collective-permute-start.13
  48.2 0.7 collective-permute-start.12
  48.9 1.5 collective-permute-start.11
  50.7 75.4 %collective-permute-done.11 = f32[2,128,128]{2,1,0:T(8,128)S(1)} collective-permute-done((f32[2,128,128]{2,1,0:T(8,128)S(1)}, f32[2,128,128]{2,1,0:T(8,128)S(1)}, u32[]{:S(2)}, u32[]{:S(2)}) %collective-permute-start.11) | collective-permute-done | bytes 131104 | tf_op jit(solution)/shard_map/ppermute | solution.py:116
  126.4 4.5 %while.29 = (s32[]{:T(128)}, f32[2,128,128]{2,1,0:T(8,128)S(1)}, bf16[4,2,64,128]{3,2,0,1:T(8,128)(2,1)S(1)}, f32[4,2,64,128]{3,2,1,0:T(8,128)S(1)}, f32[4,2,64,...) while((s32[]{:T(128)}, f32[2,128,128]{2,1,0:T(8,128)S(1)}, ...), condition=%wide.region_5.6_spmd, body=%wide.region_4.5_spmd.sunk | while | flops 88145920 | bytes 1247341 | solution.py:89
  131.1 1.9 collective-permute-start.15
  133.0 1.9 collective-permute-start.19
  134.9 13.7 %collective-permute-done.15 = bf16[256,256]{0,1:T(8,128)(2,1)S(1)} collective-permute-done((bf16[256,256]{0,1:T(8,128)(2,1)S(1)}, bf16[256,256]{0,1:T(8,128)(2,1)S(1)}, u32[]{:S(2)}, u32[]{:S(2)}) %collective-permute-start.15) | collective-permute-done | bytes 131104 | tf_op jit(solution)/shard_map/ppermute | solution.py:19
  148.6 1.9 collective-permute-start.16
  150.5 1.9 collective-permute-start.20
  152.5 4.0 %collective-permute-done.16 = bf16[256,256]{0,1:T(8,128)(2,1)S(1)} collective-permute-done((bf16[256,256]{0,1:T(8,128)(2,1)S(1)}, bf16[256,256]{0,1:T(8,128)(2,1)S(1)}, u32[]{:S(2)}, u32[]{:S(2)}) %collective-permute-start.16) | collective-permute-done | bytes 131104 | tf_op jit(solution)/shard_map/ppermute | solution.py:19
  156.4 1.9 collective-permute-start.17
  158.8 1.9 collective-permute-start.21
  160.7 5.0 %collective-permute-done.17 = bf16[256,256]{0,1:T(8,128)(2,1)S(1)} collective-permute-done((bf16[256,256]{0,1:T(8,128)(2,1)S(1)}, bf16[256,256]{0,1:T(8,128)(2,1)S(1)}, u32[]{:S(2)}, u32[]{:S(2)}) %collective-permute-start.17) | collective-permute-done | bytes 131104 | tf_op jit(solution)/shard_map/ppermute | solution.py:19
  165.7 1.9 collective-permute-start.18
  167.6 2.0 fusion.46
  169.8 0.8 copy.93
  170.6 1.9 collective-permute-start.22
  172.5 1.4 collective-permute-done.18
  173.9 5.2 %collective-permute-done.22 = bf16[256,256]{0,1:T(8,128)(2,1)S(1)} collective-permute-done((bf16[256,256]{0,1:T(8,128)(2,1)S(1)}, bf16[256,256]{0,1:T(8,128)(2,1)S(1)}, u32[]{:S(2)}, u32[]{:S(2)}) %collective-permute-start.22) | collective-permute-done | bytes 131104 | tf_op jit(solution)/shard_map/ppermute | solution.py:19
  179.2 5.1 %fusion.96 = (bf16[16,1,256,256]{3,2,1,0:T(8,128)(2,1)}, bf16[16,1,256,256]{3,2,1,0:T(8,128)(2,1)}) fusion(bf16[16,2,256,256]{3,2,1,0:T(8,128)(2,1)} %bitcast.203), kind=kLoop, calls=%fused_computation.149 | loop fusion | bytes 8388608 | tf_op jit(solution)/shard_map/slice | solution.py:180
  184.3 3.3 %copy.100 = bf16[16,1,256,256]{2,0,3,1:T(8,128)(2,1)S(1)} copy(bf16[16,1,256,256]{3,2,1,0:T(8,128)(2,1)} %get-tuple-element.214) | data formatting | bytes 4194304
  187.6 4.5 %copy.99 = bf16[16,1,256,256]{2,0,3,1:T(8,128)(2,1)} copy(bf16[16,1,256,256]{3,2,1,0:T(8,128)(2,1)} %get-tuple-element.215) | data formatting | bytes 4194304
  192.2 2.2 fusion.60
  194.9 0.7 copy.88
  195.6 0.8 fusion.39
  196.6 2.3 %fusion.97 = (f32[2,256]{1,0:T(2,128)S(1)}, f32[2,256,2304]{1,2,0:T(8,128)S(1)}) fusion(f32[2,256,2304]{1,2,0:T(8,128)S(1)} %fusion.39, pred[256,2304]{0,1:T(8,128)(4,1)S(1)} %copy-done.1), kind=kOutput, calls=%fused_computation.150 | output fusion | flops 4720895 | bytes 10029056 | tf_op jit(solution)/shard_map/while/body/eval_jaxpr/sub | solution.py:206
  199.5 17.3 %psum.7 = f32[256]{0:T(256)S(1)} all-reduce(f32[256]{0:T(256)S(1)} %get-tuple-element.218), channel_id=1, replica_groups=mesh['rows'=4,'cols'=16,'head'=8] {'head'}, use_global_device_ids=true, to_apply=%region_9.10 | all-reduce | flops 256 | bytes 2048 | tf_op jit(solution)/shard_map/psum | solution.py:216
  216.9 0.8 multiply_convert_fusion
  (143 shorter events, 23.2 us)
Async XLA Ops:
  7.2 188.4 %copy-start = (bf16[256,256]{1,0:T(8,128)(2,1)S(1)}, bf16[256,256]{1,0:T(8,128)(2,1)}, u32[]{:S(2)}) copy-start(bf16[256,256]{1,0:T(8,128)(2,1)} %param.15) | copy-start | bytes 393220
  7.2 172.0 %all-gather.3.cloned.1.call-start = ((), (), s32[]{:S(2)}) async-start(), calls=%async_computation | async-start | bytes 4456448 | tf_op jit(solution)/shard_map/all_gather | solution.py:179
  7.2 23.9 %collective-permute-start.23 = (bf16[256,256]{1,0:T(8,128)(2,1)}, bf16[256,256]{1,0:T(8,128)(2,1)S(1)}, u32[]{:S(2)}, u32[]{:S(2)}) collective-permute-start(bf16[256,256]{1,0:T(8,128)(2,1)} %param.16), channel_id=1, source_target_pairs={{0,128},{128,256},{256,384},{1,129},{129,257},{257,385},{2,130},{1... | collective-permute-start | bytes 393224 | tf_op jit(solution)/shard_map/ppermute | solution.py:178
  17.3 13.0 %copy-start.3 = (bf16[256,256]{1,0:T(8,128)(2,1)S(1)}, bf16[256,256]{1,0:T(8,128)(2,1)}, u32[]{:S(2)}) copy-start(bf16[256,256]{1,0:T(8,128)(2,1)} %param.11) | copy-start | bytes 393220
  22.9 8.2 %copy-start.2 = (bf16[256,256]{1,0:T(8,128)(2,1)S(1)}, bf16[256,256]{1,0:T(8,128)(2,1)}, u32[]{:S(2)}) copy-start(bf16[256,256]{1,0:T(8,128)(2,1)} %param.16) | copy-start | bytes 393220
  23.0 9.0 %collective-permute-start.5 = (f32[2,128,128]{2,1,0:T(8,128)S(1)}, f32[2,128,128]{2,1,0:T(8,128)S(1)}, u32[]{:S(2)}, u32[]{:S(2)}) collective-permute-start(f32[2,128,128]{2,1,0:T(8,128)S(1)} %get-tuple-element.101), channel_id=1, source_target_pairs={{0,8},{8,16},{16,24},{32,40},{40,48},{48,56},{64,72},{72,80},{80,8... | collective-permute-start | bytes 393224 | tf_op jit(solution)/shard_map/ppermute | solution.py:116
  26.6 8.9 %collective-permute-start = (f32[2,128,128]{2,1,0:T(8,128)S(1)}, f32[2,128,128]{2,1,0:T(8,128)S(1)}, u32[]{:S(2)}, u32[]{:S(2)}) collective-permute-start(f32[2,128,128]{2,1,0:T(8,128)S(1)} %get-tuple-element.100), channel_id=1, source_target_pairs={{0,8},{8,16},{16,24},{32,40},{40,48},{48,56},{64,72},{72,80},{80,8... | collective-permute-start | bytes 393224 | tf_op jit(solution)/shard_map/ppermute | solution.py:116
  32.2 5.8 %collective-permute-start.6 = (f32[2,128,128]{2,1,0:T(8,128)S(1)}, f32[2,128,128]{2,1,0:T(8,128)S(1)}, u32[]{:S(2)}, u32[]{:S(2)}) collective-permute-start(f32[2,128,128]{2,1,0:T(8,128)S(1)} %fusion.59), channel_id=1, source_target_pairs={{0,16},{8,24},{32,48},{40,56},{64,80},{72,88},{96,112},{104,120},{... | collective-permute-start | bytes 393224 | tf_op jit(solution)/shard_map/ppermute | solution.py:116
  35.8 4.5 %collective-permute-start.1 = (f32[2,128,128]{2,1,0:T(8,128)S(1)}, f32[2,128,128]{2,1,0:T(8,128)S(1)}, u32[]{:S(2)}, u32[]{:S(2)}) collective-permute-start(f32[2,128,128]{2,1,0:T(8,128)S(1)} %convolution_select_fusion.6), channel_id=1, source_target_pairs={{0,16},{8,24},{32,48},{40,56},{64,80},{72,88},{96,112},{104,120},{... | collective-permute-start | bytes 393224 | tf_op jit(solution)/shard_map/ppermute | solution.py:116
  38.4 3.1 %collective-permute-start.7 = (f32[2,128,128]{2,1,0:T(8,128)S(1)}, f32[2,128,128]{2,1,0:T(8,128)S(1)}, u32[]{:S(2)}, u32[]{:S(2)}) collective-permute-start(f32[2,128,128]{2,1,0:T(8,128)S(1)} %fusion.58), channel_id=1, source_target_pairs={{24,56},{56,88},{88,120},{120,152},{152,184},{184,216},{216,248},{... | collective-permute-start | bytes 393224 | tf_op jit(solution)/shard_map/ppermute | solution.py:116
  40.5 1.9 collective-permute-start.2
  41.8 1.6 collective-permute-start.8
  42.7 1.6 collective-permute-start.3
  43.7 1.6 collective-permute-start.9
  44.7 1.6 collective-permute-start.4
  45.6 1.0 collective-permute-start.10
  46.9 3.8 %collective-permute-start.14 = (f32[2,128,128]{2,1,0:T(8,128)S(1)}, f32[2,128,128]{2,1,0:T(8,128)S(1)}, u32[]{:S(2)}, u32[]{:S(2)}) collective-permute-start(f32[2,128,128]{2,1,0:T(8,128)S(1)} %fusion.54), channel_id=1, source_target_pairs={{24,56},{56,88},{88,120},{120,152},{152,184},{184,216},{216,248},{... | collective-permute-start | bytes 393224 | tf_op jit(solution)/shard_map/ppermute | solution.py:116
  47.6 3.1 %collective-permute-start.13 = (f32[2,128,128]{2,1,0:T(8,128)S(1)}, f32[2,128,128]{2,1,0:T(8,128)S(1)}, u32[]{:S(2)}, u32[]{:S(2)}) collective-permute-start(f32[2,128,128]{2,1,0:T(8,128)S(1)} %fusion.54), channel_id=1, source_target_pairs={{24,48},{56,80},{88,112},{120,144},{152,176},{184,208},{216,240},{... | collective-permute-start | bytes 393224 | tf_op jit(solution)/shard_map/ppermute | solution.py:116
  48.2 2.5 %collective-permute-start.12 = (f32[2,128,128]{2,1,0:T(8,128)S(1)}, f32[2,128,128]{2,1,0:T(8,128)S(1)}, u32[]{:S(2)}, u32[]{:S(2)}) collective-permute-start(f32[2,128,128]{2,1,0:T(8,128)S(1)} %fusion.54), channel_id=1, source_target_pairs={{24,40},{56,72},{88,104},{120,136},{152,168},{184,200},{216,232},{... | collective-permute-start | bytes 393224 | tf_op jit(solution)/shard_map/ppermute | solution.py:116
  48.9 77.2 %collective-permute-start.11 = (f32[2,128,128]{2,1,0:T(8,128)S(1)}, f32[2,128,128]{2,1,0:T(8,128)S(1)}, u32[]{:S(2)}, u32[]{:S(2)}) collective-permute-start(f32[2,128,128]{2,1,0:T(8,128)S(1)} %fusion.54), channel_id=1, source_target_pairs={{24,32},{56,64},{88,96},{120,128},{152,160},{184,192},{216,224},{2... | collective-permute-start | bytes 393224 | tf_op jit(solution)/shard_map/ppermute | solution.py:116
  131.1 17.5 %collective-permute-start.15 = (bf16[256,256]{0,1:T(8,128)(2,1)S(1)}, bf16[256,256]{0,1:T(8,128)(2,1)S(1)}, u32[]{:S(2)}, u32[]{:S(2)}) collective-permute-start(bf16[256,256]{0,1:T(8,128)(2,1)S(1)} %bitcast.208), channel_id=1, source_target_pairs={{0,40},{8,48},{16,56},{24,64},{32,72},{40,80},{48,88},{56,96},{64,... | collective-permute-start | bytes 393224 | tf_op jit(solution)/shard_map/ppermute | solution.py:19
  133.0 17.5 %collective-permute-start.19 = (bf16[256,256]{0,1:T(8,128)(2,1)S(1)}, bf16[256,256]{0,1:T(8,128)(2,1)S(1)}, u32[]{:S(2)}, u32[]{:S(2)}) collective-permute-start(bf16[256,256]{0,1:T(8,128)(2,1)S(1)} %bitcast.209), channel_id=1, source_target_pairs={{0,8},{8,16},{16,24},{24,32},{32,40},{40,48},{48,56},{56,64},{64,7... | collective-permute-start | bytes 393224 | tf_op jit(solution)/shard_map/ppermute | solution.py:19
  148.6 7.8 %collective-permute-start.16 = (bf16[256,256]{0,1:T(8,128)(2,1)S(1)}, bf16[256,256]{0,1:T(8,128)(2,1)S(1)}, u32[]{:S(2)}, u32[]{:S(2)}) collective-permute-start(bf16[256,256]{0,1:T(8,128)(2,1)S(1)} %collective-permute-done.15), channel_id=1, source_target_pairs={{0,8},{8,16},{16,24},{24,32},{32,40},{40,48},{48,56},{56,64},{64,7... | collective-permute-start | bytes 393224 | tf_op jit(solution)/shard_map/ppermute | solution.py:19
  150.5 8.3 %collective-permute-start.20 = (bf16[256,256]{0,1:T(8,128)(2,1)S(1)}, bf16[256,256]{0,1:T(8,128)(2,1)S(1)}, u32[]{:S(2)}, u32[]{:S(2)}) collective-permute-start(bf16[256,256]{0,1:T(8,128)(2,1)S(1)} %collective-permute-done.19), channel_id=1, source_target_pairs={{0,8},{8,16},{16,24},{24,32},{32,40},{40,48},{48,56},{56,64},{64,7... | collective-permute-start | bytes 393224 | tf_op jit(solution)/shard_map/ppermute | solution.py:19
  156.4 9.3 %collective-permute-start.17 = (bf16[256,256]{0,1:T(8,128)(2,1)S(1)}, bf16[256,256]{0,1:T(8,128)(2,1)S(1)}, u32[]{:S(2)}, u32[]{:S(2)}) collective-permute-start(bf16[256,256]{0,1:T(8,128)(2,1)S(1)} %collective-permute-done.16), channel_id=1, source_target_pairs={{0,8},{8,16},{16,24},{24,32},{32,40},{40,48},{48,56},{56,64},{64,7... | collective-permute-start | bytes 393224 | tf_op jit(solution)/shard_map/ppermute | solution.py:19
  158.8 11.8 %collective-permute-start.21 = (bf16[256,256]{0,1:T(8,128)(2,1)S(1)}, bf16[256,256]{0,1:T(8,128)(2,1)S(1)}, u32[]{:S(2)}, u32[]{:S(2)}) collective-permute-start(bf16[256,256]{0,1:T(8,128)(2,1)S(1)} %collective-permute-done.20), channel_id=1, source_target_pairs={{0,8},{8,16},{16,24},{24,32},{32,40},{40,48},{48,56},{56,64},{64,7... | collective-permute-start | bytes 393224 | tf_op jit(solution)/shard_map/ppermute | solution.py:19
  165.7 8.2 %collective-permute-start.18 = (bf16[256,256]{0,1:T(8,128)(2,1)S(1)}, bf16[256,256]{0,1:T(8,128)(2,1)S(1)}, u32[]{:S(2)}, u32[]{:S(2)}) collective-permute-start(bf16[256,256]{0,1:T(8,128)(2,1)S(1)} %collective-permute-done.17), channel_id=1, source_target_pairs={{0,8},{8,16},{16,24},{24,32},{32,40},{40,48},{48,56},{56,64},{64,7... | collective-permute-start | bytes 393224 | tf_op jit(solution)/shard_map/ppermute | solution.py:19
  170.6 8.5 %collective-permute-start.22 = (bf16[256,256]{0,1:T(8,128)(2,1)S(1)}, bf16[256,256]{0,1:T(8,128)(2,1)S(1)}, u32[]{:S(2)}, u32[]{:S(2)}) collective-permute-start(bf16[256,256]{0,1:T(8,128)(2,1)S(1)} %collective-permute-done.21), channel_id=1, source_target_pairs={{0,8},{8,16},{16,24},{24,32},{32,40},{40,48},{48,56},{56,64},{64,7... | collective-permute-start | bytes 393224 | tf_op jit(solution)/shard_map/ppermute | solution.py:19
  179.2 5.1 %copy-start.4 = (bf16[2304,256]{0,1:T(8,128)(2,1)}, bf16[2304,256]{0,1:T(8,128)(2,1)S(1)}, u32[]{:S(2)}) copy-start(bf16[2304,256]{0,1:T(8,128)(2,1)S(1)} %constant_dynamic-update-slice_fusion) | copy-start | bytes 3538948
  195.6 1.1 copy-start.1
  196.6 2.3 %copy-start.5 = (bf16[2304,256]{0,1:T(8,128)(2,1)S(1)}, bf16[2304,256]{0,1:T(8,128)(2,1)}, u32[]{:S(2)}) copy-start(bf16[2304,256]{0,1:T(8,128)(2,1)} %copy-done.4) | copy-start | bytes 3538948
  199.0 17.9 %copy-start.6 = (f32[256]{0:T(256)S(1)}, f32[256]{0:T(256)}, u32[]{:S(2)}) copy-start(f32[256]{0:T(256)} %param.17) | copy-start | bytes 3076
Sparse Core Ops, SparseCore 0:
  32.1 86.5 all-gather.2

commit v14 on v6

--- a/solution.py
+++ b/solution.py
@@ -107,7 +107,7 @@
     transit, carried = jax.vmap(local_pair)(k_unit, writes, updates)
     position = lax.axis_index("seq")
     seq_size = lax.axis_size("seq")
-    group = min(4, seq_size)
+    group = min(2, seq_size)
     rank = position % group
 
     def moved(value, by, sources):

time: 190 us -> 192 us (1.011)
  waiting for transfers between devices: 69.4 us -> 39.4 us
  starting transfers between devices: 63 us -> 92.7 us
    ppermute x16, starting transfers between devices: 40.9 us -> 79.9 us  [shifted(): return lax.ppermute(value, axis, pairs)]
    ppermute x16, waiting for transfers between devices: 58.4 us -> 35.2 us  [shifted(): return lax.ppermute(value, axis, pairs)]
    ppermute x15 -> x13, starting transfers between devices: 22.1 us -> 12.8 us  [moved(): return lax.ppermute(value, 'seq', pairs)]
    ppermute x15 -> x13, waiting for transfers between devices: 11.1 us -> 4.22 us  [moved(): return lax.ppermute(value, 'seq', pairs)]
    dot_general x16 -> x14, matrix products: 4.34 us -> 3.78 us  [batched_dot(): return jnp.einsum('hij,hjk->hik', left, right, precision=highest)]
  transfers between devices with their start and end apart: 31 -> 29, of which waited for: 12 -> 12; matrix products, arithmetic and copies ran while one was open for 15% -> 15% of each run, Pallas kernels for 0% -> 0%
where the time goes in v14:
time: 192 us; the launch traced here: 188 us
  starting transfers between devices  92.7 us (48%)
  waiting for transfers between devices  39.4 us (21%)
  blocking collectives  24.1 us (13%)
  matrix products  20.7 us (11%)
  local copies, waits for them, and re-layouts  4.72 us (2%)
  other arithmetic  4.65 us (2%)
    ppermute x16, starting transfers between devices, shifted(): return lax.ppermute(value, axis, pairs)  79.9 us
    ppermute x16, waiting for transfers between devices, shifted(): return lax.ppermute(value, axis, pairs)  35.2 us
    psum x1, blocking collectives, on_device(): total_sq = lax.psum(squares, 'head')  24.1 us
    ppermute x13, starting transfers between devices, moved(): return lax.ppermute(value, 'seq', pairs)  12.8 us
    ppermute x13, waiting for transfers between devices, moved(): return lax.ppermute(value, 'seq', pairs)  4.22 us
  transfers between devices with their start and end apart: 29, of which 12 were waited for; matrix products, arithmetic and copies ran while one was open for 15% of the time, Pallas kernels for 0%

profile of v14, /device:TPU:25, one launch (start us, length us, event | category | flops | bytes accessed | tf_op | source)
XLA Modules:
  0.0 188.4 jit_solution(11329359139611767912)
XLA Ops:
  0.7 1.1 copy.57
  1.7 3.5 %collective-permute-start.21 = (bf16[256,256]{0,1:T(8,128)(2,1)S(1)}, bf16[256,256]{0,1:T(8,128)(2,1)S(1)}, u32[]{:S(2)}, u32[]{:S(2)}) collective-permute-start(bf16[256,256]{0,1:T(8,128)(2,1)S(1)} %copy.57), channel_id=1, source_target_pairs={{0,8},{8,16},{16,24},{24,32},{32,40},{40,48},{48,56},{56,64},{64,7... | collective-permute-start | bytes 393224 | tf_op jit(solution)/shard_map/ppermute | solution.py:18
  5.3 0.8 mul.79
  6.1 1.0 copy.41
  13.1 5.7 %while.30 = (s32[]{:T(128)}, f32[2,128,128]{2,1,0:T(8,128)S(1)}, f32[2,128,128]{2,1,0:T(8,128)S(1)}, f32[4,2,64,128]{3,2,1,0:T(8,128)S(1)}, f32[4,2,64,128]{3,2,...) while((s32[]{:T(128)}, f32[2,128,128]{2,1,0:T(8,128)S(1)}, ...), condition=%wide.region_2.3_spmd.clone, body=%wide.region_1.0_spmd.clone.sunk | while | flops 151126016 | bytes 1837159 | solution.py:74
  18.8 3.6 %collective-permute-start.5 = (f32[2,128,128]{2,1,0:T(8,128)S(1)}, f32[2,128,128]{2,1,0:T(8,128)S(1)}, u32[]{:S(2)}, u32[]{:S(2)}) collective-permute-start(f32[2,128,128]{2,1,0:T(8,128)S(1)} %get-tuple-element.101), channel_id=1, source_target_pairs={{0,8},{16,24},{32,40},{48,56},{64,72},{80,88},{96,104},{112,120},{... | collective-permute-start | bytes 393224 | tf_op jit(solution)/shard_map/ppermute | solution.py:115
  22.3 1.3 collective-permute-start
  24.9 0.7 collective-permute-start.6
  25.6 1.4 collective-permute-done
  27.3 0.7 collective-permute-start.1
  27.9 11.7 %collective-permute-start.22 = (bf16[256,256]{0,1:T(8,128)(2,1)S(1)}, bf16[256,256]{0,1:T(8,128)(2,1)S(1)}, u32[]{:S(2)}, u32[]{:S(2)}) collective-permute-start(bf16[256,256]{0,1:T(8,128)(2,1)S(1)} %collective-permute-done.21), channel_id=1, source_target_pairs={{0,8},{8,16},{16,24},{24,32},{32,40},{40,48},{48,56},{56,64},{64,7... | collective-permute-start | bytes 393224 | tf_op jit(solution)/shard_map/ppermute | solution.py:18
  40.2 0.7 collective-permute-start.7
  41.2 0.7 collective-permute-start.2
  41.9 1.2 collective-permute-done.22
  43.0 10.5 %collective-permute-start.23 = (bf16[256,256]{0,1:T(8,128)(2,1)S(1)}, bf16[256,256]{0,1:T(8,128)(2,1)S(1)}, u32[]{:S(2)}, u32[]{:S(2)}) collective-permute-start(bf16[256,256]{0,1:T(8,128)(2,1)S(1)} %collective-permute-done.22), channel_id=1, source_target_pairs={{0,8},{8,16},{16,24},{24,32},{32,40},{40,48},{48,56},{56,64},{64,7... | collective-permute-start | bytes 393224 | tf_op jit(solution)/shard_map/ppermute | solution.py:18
  54.8 0.7 collective-permute-start.3
  55.4 7.9 %collective-permute-done.23 = bf16[256,256]{0,1:T(8,128)(2,1)S(1)} collective-permute-done((bf16[256,256]{0,1:T(8,128)(2,1)S(1)}, bf16[256,256]{0,1:T(8,128)(2,1)S(1)}, u32[]{:S(2)}, u32[]{:S(2)}) %collective-permute-start.23) | collective-permute-done | bytes 131104 | tf_op jit(solution)/shard_map/ppermute | solution.py:18
  63.4 2.5 %collective-permute-start.24 = (bf16[256,256]{0,1:T(8,128)(2,1)S(1)}, bf16[256,256]{0,1:T(8,128)(2,1)S(1)}, u32[]{:S(2)}, u32[]{:S(2)}) collective-permute-start(bf16[256,256]{0,1:T(8,128)(2,1)S(1)} %collective-permute-done.23), channel_id=1, source_target_pairs={{0,8},{8,16},{16,24},{24,32},{32,40},{40,48},{48,56},{56,64},{64,7... | collective-permute-start | bytes 393224 | tf_op jit(solution)/shard_map/ppermute | solution.py:18
  67.1 0.7 collective-permute-start.4
  67.8 5.5 %collective-permute-done.24 = bf16[256,256]{0,1:T(8,128)(2,1)S(1)} collective-permute-done((bf16[256,256]{0,1:T(8,128)(2,1)S(1)}, bf16[256,256]{0,1:T(8,128)(2,1)S(1)}, u32[]{:S(2)}, u32[]{:S(2)}) %collective-permute-start.24) | collective-permute-done | bytes 131104 | tf_op jit(solution)/shard_map/ppermute | solution.py:18
  73.2 16.5 %collective-permute-start.25 = (bf16[256,256]{0,1:T(8,128)(2,1)S(1)}, bf16[256,256]{0,1:T(8,128)(2,1)S(1)}, u32[]{:S(2)}, u32[]{:S(2)}) collective-permute-start(bf16[256,256]{0,1:T(8,128)(2,1)S(1)} %collective-permute-done.24), channel_id=1, source_target_pairs={{0,8},{8,16},{16,24},{24,32},{32,40},{40,48},{48,56},{56,64},{64,7... | collective-permute-start | bytes 393224 | tf_op jit(solution)/shard_map/ppermute | solution.py:18
  90.8 1.0 collective-permute-done.25
  91.7 4.1 %collective-permute-start.26 = (bf16[256,256]{0,1:T(8,128)(2,1)S(1)}, bf16[256,256]{0,1:T(8,128)(2,1)S(1)}, u32[]{:S(2)}, u32[]{:S(2)}) collective-permute-start(bf16[256,256]{0,1:T(8,128)(2,1)S(1)} %collective-permute-done.25), channel_id=1, source_target_pairs={{0,8},{8,16},{16,24},{24,32},{32,40},{40,48},{48,56},{56,64},{64,7... | collective-permute-start | bytes 393224 | tf_op jit(solution)/shard_map/ppermute | solution.py:18
  97.0 1.3 collective-permute-start.11
  98.6 0.9 collective-permute-done.26
  99.5 4.6 %collective-permute-start.27 = (bf16[256,256]{0,1:T(8,128)(2,1)S(1)}, bf16[256,256]{0,1:T(8,128)(2,1)S(1)}, u32[]{:S(2)}, u32[]{:S(2)}) collective-permute-start(bf16[256,256]{0,1:T(8,128)(2,1)S(1)} %collective-permute-done.26), channel_id=1, source_target_pairs={{0,8},{8,16},{16,24},{24,32},{32,40},{40,48},{48,56},{56,64},{64,7... | collective-permute-start | bytes 393224 | tf_op jit(solution)/shard_map/ppermute | solution.py:18
  104.1 2.8 %collective-permute-done.11 = f32[2,128,128]{2,1,0:T(8,128)S(1)} collective-permute-done((f32[2,128,128]{2,1,0:T(8,128)S(1)}, f32[2,128,128]{2,1,0:T(8,128)S(1)}, u32[]{:S(2)}, u32[]{:S(2)}) %collective-permute-start.11) | collective-permute-done | bytes 131104 | tf_op jit(solution)/shard_map/ppermute | solution.py:115
  107.2 4.5 %while.29 = (s32[]{:T(128)}, f32[2,128,128]{2,1,0:T(8,128)S(1)}, bf16[4,2,64,128]{3,2,0,1:T(8,128)(2,1)S(1)}, f32[4,2,64,128]{3,2,1,0:T(8,128)S(1)}, f32[4,2,64,...) while((s32[]{:T(128)}, f32[2,128,128]{2,1,0:T(8,128)S(1)}, ...), condition=%wide.region_5.6_spmd, body=%wide.region_4.5_spmd.sunk | while | flops 88145920 | bytes 1247341 | solution.py:88
  111.8 1.9 %collective-permute-start.17 = (bf16[256,256]{0,1:T(8,128)(2,1)S(1)}, bf16[256,256]{0,1:T(8,128)(2,1)S(1)}, u32[]{:S(2)}, u32[]{:S(2)}) collective-permute-start(bf16[256,256]{0,1:T(8,128)(2,1)S(1)} %bitcast.196), channel_id=1, source_target_pairs={{0,8},{8,16},{16,24},{24,32},{32,40},{40,48},{48,56},{56,64},{64,7... | collective-permute-start | bytes 393224 | tf_op jit(solution)/shard_map/ppermute | solution.py:18
  113.8 7.4 %collective-permute-start.13 = (bf16[256,256]{0,1:T(8,128)(2,1)S(1)}, bf16[256,256]{0,1:T(8,128)(2,1)S(1)}, u32[]{:S(2)}, u32[]{:S(2)}) collective-permute-start(bf16[256,256]{0,1:T(8,128)(2,1)S(1)} %bitcast.197), channel_id=1, source_target_pairs={{0,40},{8,48},{16,56},{24,64},{32,72},{40,80},{48,88},{56,96},{64,... | collective-permute-start | bytes 393224 | tf_op jit(solution)/shard_map/ppermute | solution.py:18
  121.2 1.9 %collective-permute-start.28 = (bf16[256,256]{0,1:T(8,128)(2,1)S(1)}, bf16[256,256]{0,1:T(8,128)(2,1)S(1)}, u32[]{:S(2)}, u32[]{:S(2)}) collective-permute-start(bf16[256,256]{0,1:T(8,128)(2,1)S(1)} %collective-permute-done.27), channel_id=1, source_target_pairs={{0,8},{8,16},{16,24},{24,32},{32,40},{40,48},{48,56},{56,64},{64,7... | collective-permute-start | bytes 393224 | tf_op jit(solution)/shard_map/ppermute | solution.py:18
  123.1 1.3 fusion.46
  124.3 0.8 copy.63
  125.1 4.6 %collective-permute-start.18 = (bf16[256,256]{0,1:T(8,128)(2,1)S(1)}, bf16[256,256]{0,1:T(8,128)(2,1)S(1)}, u32[]{:S(2)}, u32[]{:S(2)}) collective-permute-start(bf16[256,256]{0,1:T(8,128)(2,1)S(1)} %collective-permute-done.17), channel_id=1, source_target_pairs={{0,8},{8,16},{16,24},{24,32},{32,40},{40,48},{48,56},{56,64},{64,7... | collective-permute-start | bytes 393224 | tf_op jit(solution)/shard_map/ppermute | solution.py:18
  129.7 1.7 collective-permute-done.13
  131.4 1.9 %collective-permute-start.14 = (bf16[256,256]{0,1:T(8,128)(2,1)S(1)}, bf16[256,256]{0,1:T(8,128)(2,1)S(1)}, u32[]{:S(2)}, u32[]{:S(2)}) collective-permute-start(bf16[256,256]{0,1:T(8,128)(2,1)S(1)} %collective-permute-done.13), channel_id=1, source_target_pairs={{0,8},{8,16},{16,24},{24,32},{32,40},{40,48},{48,56},{56,64},{64,7... | collective-permute-start | bytes 393224 | tf_op jit(solution)/shard_map/ppermute | solution.py:18
  133.5 9.3 %collective-permute-done.14 = bf16[256,256]{0,1:T(8,128)(2,1)S(1)} collective-permute-done((bf16[256,256]{0,1:T(8,128)(2,1)S(1)}, bf16[256,256]{0,1:T(8,128)(2,1)S(1)}, u32[]{:S(2)}, u32[]{:S(2)}) %collective-permute-start.14) | collective-permute-done | bytes 131104 | tf_op jit(solution)/shard_map/ppermute | solution.py:18
  142.8 1.9 %collective-permute-start.15 = (bf16[256,256]{0,1:T(8,128)(2,1)S(1)}, bf16[256,256]{0,1:T(8,128)(2,1)S(1)}, u32[]{:S(2)}, u32[]{:S(2)}) collective-permute-start(bf16[256,256]{0,1:T(8,128)(2,1)S(1)} %collective-permute-done.14), channel_id=1, source_target_pairs={{0,8},{8,16},{16,24},{24,32},{32,40},{40,48},{48,56},{56,64},{64,7... | collective-permute-start | bytes 393224 | tf_op jit(solution)/shard_map/ppermute | solution.py:18
  144.7 0.8 fusion.39
  145.5 1.9 %collective-permute-start.19 = (bf16[256,256]{0,1:T(8,128)(2,1)S(1)}, bf16[256,256]{0,1:T(8,128)(2,1)S(1)}, u32[]{:S(2)}, u32[]{:S(2)}) collective-permute-start(bf16[256,256]{0,1:T(8,128)(2,1)S(1)} %collective-permute-done.18), channel_id=1, source_target_pairs={{0,8},{8,16},{16,24},{24,32},{32,40},{40,48},{48,56},{56,64},{64,7... | collective-permute-start | bytes 393224 | tf_op jit(solution)/shard_map/ppermute | solution.py:18
  147.5 3.1 %collective-permute-done.15 = bf16[256,256]{0,1:T(8,128)(2,1)S(1)} collective-permute-done((bf16[256,256]{0,1:T(8,128)(2,1)S(1)}, bf16[256,256]{0,1:T(8,128)(2,1)S(1)}, u32[]{:S(2)}, u32[]{:S(2)}) %collective-permute-start.15) | collective-permute-done | bytes 131104 | tf_op jit(solution)/shard_map/ppermute | solution.py:18
  150.6 1.9 %collective-permute-start.16 = (bf16[256,256]{0,1:T(8,128)(2,1)S(1)}, bf16[256,256]{0,1:T(8,128)(2,1)S(1)}, u32[]{:S(2)}, u32[]{:S(2)}) collective-permute-start(bf16[256,256]{0,1:T(8,128)(2,1)S(1)} %collective-permute-done.15), channel_id=1, source_target_pairs={{0,8},{8,16},{16,24},{24,32},{32,40},{40,48},{48,56},{56,64},{64,7... | collective-permute-start | bytes 393224 | tf_op jit(solution)/shard_map/ppermute | solution.py:18
  152.5 2.4 %fusion.88 = (f32[2,256]{1,0:T(2,128)S(1)}, f32[2,256,2304]{1,2,0:T(8,128)S(1)}) fusion(f32[2,256,2304]{1,2,0:T(8,128)S(1)} %fusion.39, pred[256,2304]{0,1:T(8,128)(4,1)S(1)} %fusion.46), kind=kOutput, calls=%fused_computation.145 | output fusion | flops 4720895 | bytes 10029056 | tf_op jit(solution)/shard_map/while/body/eval_jaxpr/sub | solution.py:196
  154.9 3.1 %collective-permute-start.20 = (bf16[256,256]{0,1:T(8,128)(2,1)S(1)}, bf16[256,256]{0,1:T(8,128)(2,1)S(1)}, u32[]{:S(2)}, u32[]{:S(2)}) collective-permute-start(bf16[256,256]{0,1:T(8,128)(2,1)S(1)} %collective-permute-done.19), channel_id=1, source_target_pairs={{0,8},{8,16},{16,24},{24,32},{32,40},{40,48},{48,56},{56,64},{64,7... | collective-permute-start | bytes 393224 | tf_op jit(solution)/shard_map/ppermute | solution.py:18
  158.0 1.4 collective-permute-done.16
  159.5 3.2 %collective-permute-done.20 = bf16[256,256]{0,1:T(8,128)(2,1)S(1)} collective-permute-done((bf16[256,256]{0,1:T(8,128)(2,1)S(1)}, bf16[256,256]{0,1:T(8,128)(2,1)S(1)}, u32[]{:S(2)}, u32[]{:S(2)}) %collective-permute-start.20) | collective-permute-done | bytes 131104 | tf_op jit(solution)/shard_map/ppermute | solution.py:18
  163.4 24.1 %psum.7 = f32[256]{0:T(256)S(1)} all-reduce(f32[256]{0:T(256)S(1)} %get-tuple-element.200), channel_id=1, replica_groups=mesh['seq'=64,'head'=8] {'head'}, use_global_device_ids=true, to_apply=%region_9.10 | all-reduce | flops 256 | bytes 2048 | tf_op jit(solution)/shard_map/psum | solution.py:206
  187.7 0.8 multiply_convert_fusion
  (143 shorter events, 24.0 us)
Async XLA Ops:
  0.6 144.1 %copy-start = (bf16[256,256]{1,0:T(8,128)(2,1)S(1)}, bf16[256,256]{1,0:T(8,128)(2,1)}, u32[]{:S(2)}) copy-start(bf16[256,256]{1,0:T(8,128)(2,1)} %param.15) | copy-start | bytes 393220
  0.6 6.7 %copy-start.1 = (bf16[256,256]{1,0:T(8,128)(2,1)S(1)}, bf16[256,256]{1,0:T(8,128)(2,1)}, u32[]{:S(2)}) copy-start(bf16[256,256]{1,0:T(8,128)(2,1)} %param.13) | copy-start | bytes 393220
  1.7 26.2 %collective-permute-start.21 = (bf16[256,256]{0,1:T(8,128)(2,1)S(1)}, bf16[256,256]{0,1:T(8,128)(2,1)S(1)}, u32[]{:S(2)}, u32[]{:S(2)}) collective-permute-start(bf16[256,256]{0,1:T(8,128)(2,1)S(1)} %copy.57), channel_id=1, source_target_pairs={{0,8},{8,16},{16,24},{24,32},{32,40},{40,48},{48,56},{56,64},{64,7... | collective-permute-start | bytes 393224 | tf_op jit(solution)/shard_map/ppermute | solution.py:18
  13.1 10.6 %copy-start.2 = (bf16[256,256]{1,0:T(8,128)(2,1)S(1)}, bf16[256,256]{1,0:T(8,128)(2,1)}, u32[]{:S(2)}) copy-start(bf16[256,256]{1,0:T(8,128)(2,1)} %param.11) | copy-start | bytes 393220
  18.8 5.8 %collective-permute-start.5 = (f32[2,128,128]{2,1,0:T(8,128)S(1)}, f32[2,128,128]{2,1,0:T(8,128)S(1)}, u32[]{:S(2)}, u32[]{:S(2)}) collective-permute-start(f32[2,128,128]{2,1,0:T(8,128)S(1)} %get-tuple-element.101), channel_id=1, source_target_pairs={{0,8},{16,24},{32,40},{48,56},{64,72},{80,88},{96,104},{112,120},{... | collective-permute-start | bytes 393224 | tf_op jit(solution)/shard_map/ppermute | solution.py:115
  22.3 4.6 %collective-permute-start = (f32[2,128,128]{2,1,0:T(8,128)S(1)}, f32[2,128,128]{2,1,0:T(8,128)S(1)}, u32[]{:S(2)}, u32[]{:S(2)}) collective-permute-start(f32[2,128,128]{2,1,0:T(8,128)S(1)} %get-tuple-element.100), channel_id=1, source_target_pairs={{0,8},{16,24},{32,40},{48,56},{64,72},{80,88},{96,104},{112,120},{... | collective-permute-start | bytes 393224 | tf_op jit(solution)/shard_map/ppermute | solution.py:115
  24.9 15.0 %collective-permute-start.6 = (f32[2,128,128]{2,1,0:T(8,128)S(1)}, f32[2,128,128]{2,1,0:T(8,128)S(1)}, u32[]{:S(2)}, u32[]{:S(2)}) collective-permute-start(f32[2,128,128]{2,1,0:T(8,128)S(1)} %fusion.55), channel_id=1, source_target_pairs={{8,24},{24,40},{40,56},{56,72},{72,88},{88,104},{104,120},{120,136... | collective-permute-start | bytes 393224 | tf_op jit(solution)/shard_map/ppermute | solution.py:115
  27.3 13.6 %collective-permute-start.1 = (f32[2,128,128]{2,1,0:T(8,128)S(1)}, f32[2,128,128]{2,1,0:T(8,128)S(1)}, u32[]{:S(2)}, u32[]{:S(2)}) collective-permute-start(f32[2,128,128]{2,1,0:T(8,128)S(1)} %convolution_select_fusion.5), channel_id=1, source_target_pairs={{8,24},{24,40},{40,56},{56,72},{72,88},{88,104},{104,120},{120,136... | collective-permute-start | bytes 393224 | tf_op jit(solution)/shard_map/ppermute | solution.py:115
  27.9 15.1 %collective-permute-start.22 = (bf16[256,256]{0,1:T(8,128)(2,1)S(1)}, bf16[256,256]{0,1:T(8,128)(2,1)S(1)}, u32[]{:S(2)}, u32[]{:S(2)}) collective-permute-start(bf16[256,256]{0,1:T(8,128)(2,1)S(1)} %collective-permute-done.21), channel_id=1, source_target_pairs={{0,8},{8,16},{16,24},{24,32},{32,40},{40,48},{48,56},{56,64},{64,7... | collective-permute-start | bytes 393224 | tf_op jit(solution)/shard_map/ppermute | solution.py:18
  40.2 13.3 %collective-permute-start.7 = (f32[2,128,128]{2,1,0:T(8,128)S(1)}, f32[2,128,128]{2,1,0:T(8,128)S(1)}, u32[]{:S(2)}, u32[]{:S(2)}) collective-permute-start(f32[2,128,128]{2,1,0:T(8,128)S(1)} %fusion.54), channel_id=1, source_target_pairs={{8,40},{24,56},{40,72},{56,88},{72,104},{88,120},{104,136},{120,15... | collective-permute-start | bytes 393224 | tf_op jit(solution)/shard_map/ppermute | solution.py:115
  41.2 13.3 %collective-permute-start.2 = (f32[2,128,128]{2,1,0:T(8,128)S(1)}, f32[2,128,128]{2,1,0:T(8,128)S(1)}, u32[]{:S(2)}, u32[]{:S(2)}) collective-permute-start(f32[2,128,128]{2,1,0:T(8,128)S(1)} %convolution_select_fusion.4), channel_id=1, source_target_pairs={{8,40},{24,56},{40,72},{56,88},{72,104},{88,120},{104,136},{120,15... | collective-permute-start | bytes 393224 | tf_op jit(solution)/shard_map/ppermute | solution.py:115
  43.0 20.3 %collective-permute-start.23 = (bf16[256,256]{0,1:T(8,128)(2,1)S(1)}, bf16[256,256]{0,1:T(8,128)(2,1)S(1)}, u32[]{:S(2)}, u32[]{:S(2)}) collective-permute-start(bf16[256,256]{0,1:T(8,128)(2,1)S(1)} %collective-permute-done.22), channel_id=1, source_target_pairs={{0,8},{8,16},{16,24},{24,32},{32,40},{40,48},{48,56},{56,64},{64,7... | collective-permute-start | bytes 393224 | tf_op jit(solution)/shard_map/ppermute | solution.py:18
  53.8 12.0 %collective-permute-start.8 = (f32[2,128,128]{2,1,0:T(8,128)S(1)}, f32[2,128,128]{2,1,0:T(8,128)S(1)}, u32[]{:S(2)}, u32[]{:S(2)}) collective-permute-start(f32[2,128,128]{2,1,0:T(8,128)S(1)} %fusion.53), channel_id=1, source_target_pairs={{8,72},{24,88},{40,104},{56,120},{72,136},{88,152},{104,168},{120,... | collective-permute-start | bytes 393224 | tf_op jit(solution)/shard_map/ppermute | solution.py:115
  54.8 12.0 %collective-permute-start.3 = (f32[2,128,128]{2,1,0:T(8,128)S(1)}, f32[2,128,128]{2,1,0:T(8,128)S(1)}, u32[]{:S(2)}, u32[]{:S(2)}) collective-permute-start(f32[2,128,128]{2,1,0:T(8,128)S(1)} %convolution_select_fusion.3), channel_id=1, source_target_pairs={{8,72},{24,88},{40,104},{56,120},{72,136},{88,152},{104,168},{120,... | collective-permute-start | bytes 393224 | tf_op jit(solution)/shard_map/ppermute | solution.py:115
  63.4 9.9 %collective-permute-start.24 = (bf16[256,256]{0,1:T(8,128)(2,1)S(1)}, bf16[256,256]{0,1:T(8,128)(2,1)S(1)}, u32[]{:S(2)}, u32[]{:S(2)}) collective-permute-start(bf16[256,256]{0,1:T(8,128)(2,1)S(1)} %collective-permute-done.23), channel_id=1, source_target_pairs={{0,8},{8,16},{16,24},{24,32},{32,40},{40,48},{48,56},{56,64},{64,7... | collective-permute-start | bytes 393224 | tf_op jit(solution)/shard_map/ppermute | solution.py:18
  66.1 23.7 %collective-permute-start.9 = (f32[2,128,128]{2,1,0:T(8,128)S(1)}, f32[2,128,128]{2,1,0:T(8,128)S(1)}, u32[]{:S(2)}, u32[]{:S(2)}) collective-permute-start(f32[2,128,128]{2,1,0:T(8,128)S(1)} %fusion.52), channel_id=1, source_target_pairs={{8,136},{24,152},{40,168},{56,184},{72,200},{88,216},{104,232},{12... | collective-permute-start | bytes 393224 | tf_op jit(solution)/shard_map/ppermute | solution.py:115
  67.1 28.7 %collective-permute-start.4 = (f32[2,128,128]{2,1,0:T(8,128)S(1)}, f32[2,128,128]{2,1,0:T(8,128)S(1)}, u32[]{:S(2)}, u32[]{:S(2)}) collective-permute-start(f32[2,128,128]{2,1,0:T(8,128)S(1)} %convolution_select_fusion.2), channel_id=1, source_target_pairs={{8,136},{24,152},{40,168},{56,184},{72,200},{88,216},{104,232},{12... | collective-permute-start | bytes 393224 | tf_op jit(solution)/shard_map/ppermute | solution.py:115
  73.2 18.5 %collective-permute-start.25 = (bf16[256,256]{0,1:T(8,128)(2,1)S(1)}, bf16[256,256]{0,1:T(8,128)(2,1)S(1)}, u32[]{:S(2)}, u32[]{:S(2)}) collective-permute-start(bf16[256,256]{0,1:T(8,128)(2,1)S(1)} %collective-permute-done.24), channel_id=1, source_target_pairs={{0,8},{8,16},{16,24},{24,32},{32,40},{40,48},{48,56},{56,64},{64,7... | collective-permute-start | bytes 393224 | tf_op jit(solution)/shard_map/ppermute | solution.py:18
  90.1 6.0 %collective-permute-start.10 = (f32[2,128,128]{2,1,0:T(8,128)S(1)}, f32[2,128,128]{2,1,0:T(8,128)S(1)}, u32[]{:S(2)}, u32[]{:S(2)}) collective-permute-start(f32[2,128,128]{2,1,0:T(8,128)S(1)} %fusion.51), channel_id=1, source_target_pairs={{8,264},{24,280},{40,296},{56,312},{72,328},{88,344},{104,360},{12... | collective-permute-start | bytes 393224 | tf_op jit(solution)/shard_map/ppermute | solution.py:115
  91.7 7.8 %collective-permute-start.26 = (bf16[256,256]{0,1:T(8,128)(2,1)S(1)}, bf16[256,256]{0,1:T(8,128)(2,1)S(1)}, u32[]{:S(2)}, u32[]{:S(2)}) collective-permute-start(bf16[256,256]{0,1:T(8,128)(2,1)S(1)} %collective-permute-done.25), channel_id=1, source_target_pairs={{0,8},{8,16},{16,24},{24,32},{32,40},{40,48},{48,56},{56,64},{64,7... | collective-permute-start | bytes 393224 | tf_op jit(solution)/shard_map/ppermute | solution.py:18
  96.4 7.8 %collective-permute-start.12 = (f32[2,128,128]{2,1,0:T(8,128)S(1)}, f32[2,128,128]{2,1,0:T(8,128)S(1)}, u32[]{:S(2)}, u32[]{:S(2)}) collective-permute-start(f32[2,128,128]{2,1,0:T(8,128)S(1)} %fusion.50), channel_id=1, source_target_pairs={{8,24},{24,40},{40,56},{56,72},{72,88},{88,104},{104,120},{120,136... | collective-permute-start | bytes 393224 | tf_op jit(solution)/shard_map/ppermute | solution.py:115
  97.0 9.9 %collective-permute-start.11 = (f32[2,128,128]{2,1,0:T(8,128)S(1)}, f32[2,128,128]{2,1,0:T(8,128)S(1)}, u32[]{:S(2)}, u32[]{:S(2)}) collective-permute-start(f32[2,128,128]{2,1,0:T(8,128)S(1)} %fusion.50), channel_id=1, source_target_pairs={{8,16},{24,32},{40,48},{56,64},{72,80},{88,96},{104,112},{120,128}... | collective-permute-start | bytes 393224 | tf_op jit(solution)/shard_map/ppermute | solution.py:115
  99.5 21.6 %collective-permute-start.27 = (bf16[256,256]{0,1:T(8,128)(2,1)S(1)}, bf16[256,256]{0,1:T(8,128)(2,1)S(1)}, u32[]{:S(2)}, u32[]{:S(2)}) collective-permute-start(bf16[256,256]{0,1:T(8,128)(2,1)S(1)} %collective-permute-done.26), channel_id=1, source_target_pairs={{0,8},{8,16},{16,24},{24,32},{32,40},{40,48},{48,56},{56,64},{64,7... | collective-permute-start | bytes 393224 | tf_op jit(solution)/shard_map/ppermute | solution.py:18
  111.8 13.3 %collective-permute-start.17 = (bf16[256,256]{0,1:T(8,128)(2,1)S(1)}, bf16[256,256]{0,1:T(8,128)(2,1)S(1)}, u32[]{:S(2)}, u32[]{:S(2)}) collective-permute-start(bf16[256,256]{0,1:T(8,128)(2,1)S(1)} %bitcast.196), channel_id=1, source_target_pairs={{0,8},{8,16},{16,24},{24,32},{32,40},{40,48},{48,56},{56,64},{64,7... | collective-permute-start | bytes 393224 | tf_op jit(solution)/shard_map/ppermute | solution.py:18
  113.8 17.7 %collective-permute-start.13 = (bf16[256,256]{0,1:T(8,128)(2,1)S(1)}, bf16[256,256]{0,1:T(8,128)(2,1)S(1)}, u32[]{:S(2)}, u32[]{:S(2)}) collective-permute-start(bf16[256,256]{0,1:T(8,128)(2,1)S(1)} %bitcast.197), channel_id=1, source_target_pairs={{0,40},{8,48},{16,56},{24,64},{32,72},{40,80},{48,88},{56,96},{64,... | collective-permute-start | bytes 393224 | tf_op jit(solution)/shard_map/ppermute | solution.py:18
  121.2 12.2 %collective-permute-start.28 = (bf16[256,256]{0,1:T(8,128)(2,1)S(1)}, bf16[256,256]{0,1:T(8,128)(2,1)S(1)}, u32[]{:S(2)}, u32[]{:S(2)}) collective-permute-start(bf16[256,256]{0,1:T(8,128)(2,1)S(1)} %collective-permute-done.27), channel_id=1, source_target_pairs={{0,8},{8,16},{16,24},{24,32},{32,40},{40,48},{48,56},{56,64},{64,7... | collective-permute-start | bytes 393224 | tf_op jit(solution)/shard_map/ppermute | solution.py:18
  125.1 20.4 %collective-permute-start.18 = (bf16[256,256]{0,1:T(8,128)(2,1)S(1)}, bf16[256,256]{0,1:T(8,128)(2,1)S(1)}, u32[]{:S(2)}, u32[]{:S(2)}) collective-permute-start(bf16[256,256]{0,1:T(8,128)(2,1)S(1)} %collective-permute-done.17), channel_id=1, source_target_pairs={{0,8},{8,16},{16,24},{24,32},{32,40},{40,48},{48,56},{56,64},{64,7... | collective-permute-start | bytes 393224 | tf_op jit(solution)/shard_map/ppermute | solution.py:18
  131.4 11.3 %collective-permute-start.14 = (bf16[256,256]{0,1:T(8,128)(2,1)S(1)}, bf16[256,256]{0,1:T(8,128)(2,1)S(1)}, u32[]{:S(2)}, u32[]{:S(2)}) collective-permute-start(bf16[256,256]{0,1:T(8,128)(2,1)S(1)} %collective-permute-done.13), channel_id=1, source_target_pairs={{0,8},{8,16},{16,24},{24,32},{32,40},{40,48},{48,56},{56,64},{64,7... | collective-permute-start | bytes 393224 | tf_op jit(solution)/shard_map/ppermute | solution.py:18
  142.8 7.8 %collective-permute-start.15 = (bf16[256,256]{0,1:T(8,128)(2,1)S(1)}, bf16[256,256]{0,1:T(8,128)(2,1)S(1)}, u32[]{:S(2)}, u32[]{:S(2)}) collective-permute-start(bf16[256,256]{0,1:T(8,128)(2,1)S(1)} %collective-permute-done.14), channel_id=1, source_target_pairs={{0,8},{8,16},{16,24},{24,32},{32,40},{40,48},{48,56},{56,64},{64,7... | collective-permute-start | bytes 393224 | tf_op jit(solution)/shard_map/ppermute | solution.py:18
  145.5 9.3 %collective-permute-start.19 = (bf16[256,256]{0,1:T(8,128)(2,1)S(1)}, bf16[256,256]{0,1:T(8,128)(2,1)S(1)}, u32[]{:S(2)}, u32[]{:S(2)}) collective-permute-start(bf16[256,256]{0,1:T(8,128)(2,1)S(1)} %collective-permute-done.18), channel_id=1, source_target_pairs={{0,8},{8,16},{16,24},{24,32},{32,40},{40,48},{48,56},{56,64},{64,7... | collective-permute-start | bytes 393224 | tf_op jit(solution)/shard_map/ppermute | solution.py:18
  150.6 8.8 %collective-permute-start.16 = (bf16[256,256]{0,1:T(8,128)(2,1)S(1)}, bf16[256,256]{0,1:T(8,128)(2,1)S(1)}, u32[]{:S(2)}, u32[]{:S(2)}) collective-permute-start(bf16[256,256]{0,1:T(8,128)(2,1)S(1)} %collective-permute-done.15), channel_id=1, source_target_pairs={{0,8},{8,16},{16,24},{24,32},{32,40},{40,48},{48,56},{56,64},{64,7... | collective-permute-start | bytes 393224 | tf_op jit(solution)/shard_map/ppermute | solution.py:18
  154.9 7.8 %collective-permute-start.20 = (bf16[256,256]{0,1:T(8,128)(2,1)S(1)}, bf16[256,256]{0,1:T(8,128)(2,1)S(1)}, u32[]{:S(2)}, u32[]{:S(2)}) collective-permute-start(bf16[256,256]{0,1:T(8,128)(2,1)S(1)} %collective-permute-done.19), channel_id=1, source_target_pairs={{0,8},{8,16},{16,24},{24,32},{32,40},{40,48},{48,56},{56,64},{64,7... | collective-permute-start | bytes 393224 | tf_op jit(solution)/shard_map/ppermute | solution.py:18
  162.8 24.9 %copy-start.3 = (f32[256]{0:T(256)S(1)}, f32[256]{0:T(256)}, u32[]{:S(2)}) copy-start(f32[256]{0:T(256)} %param.17) | copy-start | bytes 3076

commit v15 on v8

--- a/solution.py
+++ b/solution.py
@@ -172,7 +172,7 @@
                 pieces.append(piece)
         return jnp.concatenate(pieces[::-1] + [own], axis=0)
 
-    rows_all = (window_rows(k_attn, 2), window_rows(delta_out, 2))
+    rows_all = (window_rows(k_attn, 1), window_rows(delta_out, 3))
     block_rows = min(512, tok_rows)
     first_row = lax.axis_index("seq") * tok_rows
     score_scale = 1.0 / math.sqrt(head_size)

time: 195 us -> 197 us (1.010)
  waiting for transfers between devices: 61.9 us -> 66.4 us
  other arithmetic: 7.34 us -> 4.65 us
  matrix products: 23.6 us -> 21.3 us
    ppermute x16, waiting for transfers between devices: 35.5 us -> 66.4 us  [shifted(): return lax.ppermute(value, axis, pairs)]
    ppermute x15, waiting for transfers between devices: 26.4 us -> 0.04 us  [moved(): return lax.ppermute(value, 'seq', pairs)]
    dot_general x1, matrix products: 2.93 us -> 0.6 us  [attend_block(): jnp.einsum('hqk,khd->qhd', weights, near_values, preferred_element_type=j...]
    sub x1, other arithmetic: 4.34 us -> 2.35 us  [attend_block(): exps = jnp.exp(jnp.where(allowed[None], scores - row_top, -1e+30))]
    unnamed x44 -> x40, local copies, waits for them, and re-layouts: 3.3 us -> 5.1 us
  transfers between devices with their start and end apart: 31 -> 31, of which waited for: 8 -> 11; matrix products, arithmetic and copies ran while one was open for 13% -> 15% of each run, Pallas kernels for 0% -> 0%
where the time goes in v15:
time: 197 us; the launch traced here: 195 us
  starting transfers between devices  70.1 us (36%)
  waiting for transfers between devices  66.4 us (34%)
  blocking collectives  23.8 us (12%)
  matrix products  21.3 us (11%)
  local copies, waits for them, and re-layouts  6.55 us (3%)
  other arithmetic  4.65 us (2%)
    ppermute x16, waiting for transfers between devices, shifted(): return lax.ppermute(value, axis, pairs)  66.4 us
    ppermute x16, starting transfers between devices, shifted(): return lax.ppermute(value, axis, pairs)  49.1 us
    psum x1, blocking collectives, on_device(): total_sq = lax.psum(squares, 'head')  23.8 us
    ppermute x15, starting transfers between devices, moved(): return lax.ppermute(value, 'seq', pairs)  21 us
    unnamed x40, local copies, waits for them, and re-layouts  5.1 us
    dot_general x16, matrix products, batched_dot(): return jnp.einsum('hij,hjk->hik', left, right, precision=highest)  4.33 us
  transfers between devices with their start and end apart: 31, of which 11 were waited for; matrix products, arithmetic and copies ran while one was open for 15% of the time, Pallas kernels for 0%

profile of v15, /device:TPU:25, one launch (start us, length us, event | category | flops | bytes accessed | tf_op | source)
XLA Modules:
  0.0 195.0 jit_solution(8662063291414212076)
XLA Ops:
  0.7 1.1 copy.57
  1.7 3.5 %collective-permute-start.23 = (bf16[256,256]{0,1:T(8,128)(2,1)S(1)}, bf16[256,256]{0,1:T(8,128)(2,1)S(1)}, u32[]{:S(2)}, u32[]{:S(2)}) collective-permute-start(bf16[256,256]{0,1:T(8,128)(2,1)S(1)} %copy.57), channel_id=1, source_target_pairs={{0,8},{8,16},{16,24},{24,32},{32,40},{40,48},{48,56},{56,64},{64,7... | collective-permute-start | bytes 393224 | tf_op jit(solution)/shard_map/ppermute | solution.py:18
  5.3 0.8 mul.79
  6.1 1.0 copy.41
  13.1 5.7 %while.30 = (s32[]{:T(128)}, f32[2,128,128]{2,1,0:T(8,128)S(1)}, f32[2,128,128]{2,1,0:T(8,128)S(1)}, f32[4,2,64,128]{3,2,1,0:T(8,128)S(1)}, f32[4,2,64,128]{3,2,...) while((s32[]{:T(128)}, f32[2,128,128]{2,1,0:T(8,128)S(1)}, ...), condition=%wide.region_2.3_spmd.clone, body=%wide.region_1.0_spmd.clone.sunk | while | flops 151126016 | bytes 1837159 | solution.py:74
  18.8 3.6 %collective-permute-start.5 = (f32[2,128,128]{2,1,0:T(8,128)S(1)}, f32[2,128,128]{2,1,0:T(8,128)S(1)}, u32[]{:S(2)}, u32[]{:S(2)}) collective-permute-start(f32[2,128,128]{2,1,0:T(8,128)S(1)} %get-tuple-element.101), channel_id=1, source_target_pairs={{0,8},{8,16},{16,24},{32,40},{40,48},{48,56},{64,72},{72,80},{80,8... | collective-permute-start | bytes 393224 | tf_op jit(solution)/shard_map/ppermute | solution.py:115
  22.3 3.5 %collective-permute-start = (f32[2,128,128]{2,1,0:T(8,128)S(1)}, f32[2,128,128]{2,1,0:T(8,128)S(1)}, u32[]{:S(2)}, u32[]{:S(2)}) collective-permute-start(f32[2,128,128]{2,1,0:T(8,128)S(1)} %get-tuple-element.100), channel_id=1, source_target_pairs={{0,8},{8,16},{16,24},{32,40},{40,48},{48,56},{64,72},{72,80},{80,8... | collective-permute-start | bytes 393224 | tf_op jit(solution)/shard_map/ppermute | solution.py:115
  26.3 1.3 fusion.46
  28.4 4.5 %collective-permute-start.6 = (f32[2,128,128]{2,1,0:T(8,128)S(1)}, f32[2,128,128]{2,1,0:T(8,128)S(1)}, u32[]{:S(2)}, u32[]{:S(2)}) collective-permute-start(f32[2,128,128]{2,1,0:T(8,128)S(1)} %fusion.56), channel_id=1, source_target_pairs={{0,16},{8,24},{32,48},{40,56},{64,80},{72,88},{96,112},{104,120},{... | collective-permute-start | bytes 393224 | tf_op jit(solution)/shard_map/ppermute | solution.py:115
  33.2 1.3 collective-permute-start.1
  34.8 3.5 %collective-permute-start.24 = (bf16[256,256]{0,1:T(8,128)(2,1)S(1)}, bf16[256,256]{0,1:T(8,128)(2,1)S(1)}, u32[]{:S(2)}, u32[]{:S(2)}) collective-permute-start(bf16[256,256]{0,1:T(8,128)(2,1)S(1)} %collective-permute-done.23), channel_id=1, source_target_pairs={{0,8},{8,16},{16,24},{24,32},{32,40},{40,48},{48,56},{56,64},{64,7... | collective-permute-start | bytes 393224 | tf_op jit(solution)/shard_map/ppermute | solution.py:18
  38.9 0.7 collective-permute-start.7
  40.5 2.1 %collective-permute-done.24 = bf16[256,256]{0,1:T(8,128)(2,1)S(1)} collective-permute-done((bf16[256,256]{0,1:T(8,128)(2,1)S(1)}, bf16[256,256]{0,1:T(8,128)(2,1)S(1)}, u32[]{:S(2)}, u32[]{:S(2)}) %collective-permute-start.24) | collective-permute-done | bytes 131104 | tf_op jit(solution)/shard_map/ppermute | solution.py:18
  42.6 5.3 %collective-permute-start.25 = (bf16[256,256]{0,1:T(8,128)(2,1)S(1)}, bf16[256,256]{0,1:T(8,128)(2,1)S(1)}, u32[]{:S(2)}, u32[]{:S(2)}) collective-permute-start(bf16[256,256]{0,1:T(8,128)(2,1)S(1)} %collective-permute-done.24), channel_id=1, source_target_pairs={{0,8},{8,16},{16,24},{24,32},{32,40},{40,48},{48,56},{56,64},{64,7... | collective-permute-start | bytes 393224 | tf_op jit(solution)/shard_map/ppermute | solution.py:18
  50.1 8.2 %collective-permute-done.25 = bf16[256,256]{0,1:T(8,128)(2,1)S(1)} collective-permute-done((bf16[256,256]{0,1:T(8,128)(2,1)S(1)}, bf16[256,256]{0,1:T(8,128)(2,1)S(1)}, u32[]{:S(2)}, u32[]{:S(2)}) %collective-permute-start.25) | collective-permute-done | bytes 131104 | tf_op jit(solution)/shard_map/ppermute | solution.py:18
  58.4 1.9 collective-permute-start.26
  60.6 0.7 collective-permute-start.9
  62.2 10.9 %collective-permute-done.26 = bf16[256,256]{0,1:T(8,128)(2,1)S(1)} collective-permute-done((bf16[256,256]{0,1:T(8,128)(2,1)S(1)}, bf16[256,256]{0,1:T(8,128)(2,1)S(1)}, u32[]{:S(2)}, u32[]{:S(2)}) %collective-permute-start.26) | collective-permute-done | bytes 131104 | tf_op jit(solution)/shard_map/ppermute | solution.py:18
  73.1 1.9 collective-permute-start.27
  76.0 11.1 %collective-permute-done.27 = bf16[256,256]{0,1:T(8,128)(2,1)S(1)} collective-permute-done((bf16[256,256]{0,1:T(8,128)(2,1)S(1)}, bf16[256,256]{0,1:T(8,128)(2,1)S(1)}, u32[]{:S(2)}, u32[]{:S(2)}) %collective-permute-start.27) | collective-permute-done | bytes 131104 | tf_op jit(solution)/shard_map/ppermute | solution.py:18
  87.1 1.9 collective-permute-start.28
  91.0 0.8 collective-permute-start.12
  91.9 1.3 collective-permute-start.11
  93.2 2.0 %collective-permute-done.28 = bf16[256,256]{0,1:T(8,128)(2,1)S(1)} collective-permute-done((bf16[256,256]{0,1:T(8,128)(2,1)S(1)}, bf16[256,256]{0,1:T(8,128)(2,1)S(1)}, u32[]{:S(2)}, u32[]{:S(2)}) %collective-permute-start.28) | collective-permute-done | bytes 131104 | tf_op jit(solution)/shard_map/ppermute | solution.py:18
  95.1 1.9 collective-permute-start.29
  97.4 13.4 %collective-permute-done.29 = bf16[256,256]{0,1:T(8,128)(2,1)} collective-permute-done((bf16[256,256]{0,1:T(8,128)(2,1)S(1)}, bf16[256,256]{0,1:T(8,128)(2,1)}, u32[]{:S(2)}, u32[]{:S(2)}) %collective-permute-start.29) | collective-permute-done | bytes 131104 | tf_op jit(solution)/shard_map/ppermute | solution.py:18
  110.7 1.9 collective-permute-start.30
  113.0 4.5 %while.29 = (s32[]{:T(128)}, f32[2,128,128]{2,1,0:T(8,128)S(1)}, bf16[4,2,64,128]{3,2,0,1:T(8,128)(2,1)S(1)}, f32[4,2,64,128]{3,2,1,0:T(8,128)S(1)}, f32[4,2,64,...) while((s32[]{:T(128)}, f32[2,128,128]{2,1,0:T(8,128)S(1)}, ...), condition=%wide.region_5.6_spmd, body=%wide.region_4.5_spmd.sunk | while | flops 88145920 | bytes 1247341 | solution.py:88
  117.7 0.8 copy.63
  118.4 1.9 collective-permute-start.20
  120.3 3.3 %collective-permute-start.17 = (bf16[256,256]{0,1:T(8,128)(2,1)S(1)}, bf16[256,256]{0,1:T(8,128)(2,1)S(1)}, u32[]{:S(2)}, u32[]{:S(2)}) collective-permute-start(bf16[256,256]{0,1:T(8,128)(2,1)S(1)} %bitcast.202), channel_id=1, source_target_pairs={{0,32},{8,40},{16,48},{24,56},{32,64},{40,72},{48,80},{56,88},{64,... | collective-permute-start | bytes 393224 | tf_op jit(solution)/shard_map/ppermute | solution.py:18
  123.7 4.6 %collective-permute-start.15 = (bf16[256,256]{0,1:T(8,128)(2,1)S(1)}, bf16[256,256]{0,1:T(8,128)(2,1)S(1)}, u32[]{:S(2)}, u32[]{:S(2)}) collective-permute-start(bf16[256,256]{0,1:T(8,128)(2,1)S(1)} %bitcast.203), channel_id=1, source_target_pairs={{0,56},{8,64},{16,72},{24,80},{32,88},{40,96},{48,104},{56,112},{6... | collective-permute-start | bytes 393224 | tf_op jit(solution)/shard_map/ppermute | solution.py:18
  128.4 0.9 constant_dynamic-update-slice_fusion.17
  129.3 0.9 constant_dynamic-update-slice_fusion.16
  130.4 0.8 fusion.39
  131.2 1.9 collective-permute-start.21
  133.1 2.1 %collective-permute-done.17 = bf16[256,256]{0,1:T(8,128)(2,1)S(1)} collective-permute-done((bf16[256,256]{0,1:T(8,128)(2,1)S(1)}, bf16[256,256]{0,1:T(8,128)(2,1)S(1)}, u32[]{:S(2)}, u32[]{:S(2)}) %collective-permute-start.17) | collective-permute-done | bytes 131104 | tf_op jit(solution)/shard_map/ppermute | solution.py:18
  135.2 1.9 collective-permute-start.18
  137.1 6.9 %collective-permute-done.15 = bf16[256,256]{0,1:T(8,128)(2,1)S(1)} collective-permute-done((bf16[256,256]{0,1:T(8,128)(2,1)S(1)}, bf16[256,256]{0,1:T(8,128)(2,1)S(1)}, u32[]{:S(2)}, u32[]{:S(2)}) %collective-permute-start.15) | collective-permute-done | bytes 131104 | tf_op jit(solution)/shard_map/ppermute | solution.py:18
  144.0 9.6 %collective-permute-start.16 = (bf16[256,256]{0,1:T(8,128)(2,1)S(1)}, bf16[256,256]{0,1:T(8,128)(2,1)S(1)}, u32[]{:S(2)}, u32[]{:S(2)}) collective-permute-start(bf16[256,256]{0,1:T(8,128)(2,1)S(1)} %collective-permute-done.15), channel_id=1, source_target_pairs={{0,8},{8,16},{16,24},{24,32},{32,40},{40,48},{48,56},{56,64},{64,7... | collective-permute-start | bytes 393224 | tf_op jit(solution)/shard_map/ppermute | solution.py:18
  153.6 2.4 %fusion.91 = (f32[2,256]{1,0:T(2,128)S(1)}, f32[2,256,2304]{1,2,0:T(8,128)S(1)}) fusion(f32[2,256,2304]{1,2,0:T(8,128)S(1)} %fusion.39, pred[256,2304]{0,1:T(8,128)(4,1)S(1)} %fusion.46), kind=kOutput, calls=%fused_computation.150 | output fusion | flops 4720895 | bytes 10029056 | tf_op jit(solution)/shard_map/while/body/eval_jaxpr/sub | solution.py:196
  156.0 1.9 collective-permute-start.22
  157.9 3.2 %collective-permute-done.18 = bf16[256,256]{0,1:T(8,128)(2,1)S(1)} collective-permute-done((bf16[256,256]{0,1:T(8,128)(2,1)S(1)}, bf16[256,256]{0,1:T(8,128)(2,1)S(1)}, u32[]{:S(2)}, u32[]{:S(2)}) %collective-permute-start.18) | collective-permute-done | bytes 131104 | tf_op jit(solution)/shard_map/ppermute | solution.py:18
  161.1 1.9 collective-permute-start.19
  163.1 3.4 %collective-permute-done.16 = bf16[256,256]{0,1:T(8,128)(2,1)S(1)} collective-permute-done((bf16[256,256]{0,1:T(8,128)(2,1)S(1)}, bf16[256,256]{0,1:T(8,128)(2,1)S(1)}, u32[]{:S(2)}, u32[]{:S(2)}) %collective-permute-start.16) | collective-permute-done | bytes 131104 | tf_op jit(solution)/shard_map/ppermute | solution.py:18
  166.5 3.1 %collective-permute-done.19 = bf16[256,256]{0,1:T(8,128)(2,1)S(1)} collective-permute-done((bf16[256,256]{0,1:T(8,128)(2,1)S(1)}, bf16[256,256]{0,1:T(8,128)(2,1)S(1)}, u32[]{:S(2)}, u32[]{:S(2)}) %collective-permute-start.19) | collective-permute-done | bytes 131104 | tf_op jit(solution)/shard_map/ppermute | solution.py:18
  170.3 23.8 %psum.7 = f32[256]{0:T(256)S(1)} all-reduce(f32[256]{0:T(256)S(1)} %get-tuple-element.200), channel_id=1, replica_groups=mesh['seq'=64,'head'=8] {'head'}, use_global_device_ids=true, to_apply=%region_9.10 | all-reduce | flops 256 | bytes 2048 | tf_op jit(solution)/shard_map/psum | solution.py:206
  194.2 0.8 multiply_convert_fusion
  (157 shorter events, 26.6 us)
Async XLA Ops:
  0.6 129.7 %copy-start = (bf16[256,256]{1,0:T(8,128)(2,1)S(1)}, bf16[256,256]{1,0:T(8,128)(2,1)}, u32[]{:S(2)}) copy-start(bf16[256,256]{1,0:T(8,128)(2,1)} %param.15) | copy-start | bytes 393220
  0.6 6.7 %copy-start.1 = (bf16[256,256]{1,0:T(8,128)(2,1)S(1)}, bf16[256,256]{1,0:T(8,128)(2,1)}, u32[]{:S(2)}) copy-start(bf16[256,256]{1,0:T(8,128)(2,1)} %param.13) | copy-start | bytes 393220
  1.7 33.1 %collective-permute-start.23 = (bf16[256,256]{0,1:T(8,128)(2,1)S(1)}, bf16[256,256]{0,1:T(8,128)(2,1)S(1)}, u32[]{:S(2)}, u32[]{:S(2)}) collective-permute-start(bf16[256,256]{0,1:T(8,128)(2,1)S(1)} %copy.57), channel_id=1, source_target_pairs={{0,8},{8,16},{16,24},{24,32},{32,40},{40,48},{48,56},{56,64},{64,7... | collective-permute-start | bytes 393224 | tf_op jit(solution)/shard_map/ppermute | solution.py:18
  13.1 12.9 %copy-start.2 = (bf16[256,256]{1,0:T(8,128)(2,1)S(1)}, bf16[256,256]{1,0:T(8,128)(2,1)}, u32[]{:S(2)}) copy-start(bf16[256,256]{1,0:T(8,128)(2,1)} %param.11) | copy-start | bytes 393220
  18.8 9.4 %collective-permute-start.5 = (f32[2,128,128]{2,1,0:T(8,128)S(1)}, f32[2,128,128]{2,1,0:T(8,128)S(1)}, u32[]{:S(2)}, u32[]{:S(2)}) collective-permute-start(f32[2,128,128]{2,1,0:T(8,128)S(1)} %get-tuple-element.101), channel_id=1, source_target_pairs={{0,8},{8,16},{16,24},{32,40},{40,48},{48,56},{64,72},{72,80},{80,8... | collective-permute-start | bytes 393224 | tf_op jit(solution)/shard_map/ppermute | solution.py:115
  22.3 10.6 %collective-permute-start = (f32[2,128,128]{2,1,0:T(8,128)S(1)}, f32[2,128,128]{2,1,0:T(8,128)S(1)}, u32[]{:S(2)}, u32[]{:S(2)}) collective-permute-start(f32[2,128,128]{2,1,0:T(8,128)S(1)} %get-tuple-element.100), channel_id=1, source_target_pairs={{0,8},{8,16},{16,24},{32,40},{40,48},{48,56},{64,72},{72,80},{80,8... | collective-permute-start | bytes 393224 | tf_op jit(solution)/shard_map/ppermute | solution.py:115
  28.4 10.1 %collective-permute-start.6 = (f32[2,128,128]{2,1,0:T(8,128)S(1)}, f32[2,128,128]{2,1,0:T(8,128)S(1)}, u32[]{:S(2)}, u32[]{:S(2)}) collective-permute-start(f32[2,128,128]{2,1,0:T(8,128)S(1)} %fusion.56), channel_id=1, source_target_pairs={{0,16},{8,24},{32,48},{40,56},{64,80},{72,88},{96,112},{104,120},{... | collective-permute-start | bytes 393224 | tf_op jit(solution)/shard_map/ppermute | solution.py:115
  33.2 6.3 %collective-permute-start.1 = (f32[2,128,128]{2,1,0:T(8,128)S(1)}, f32[2,128,128]{2,1,0:T(8,128)S(1)}, u32[]{:S(2)}, u32[]{:S(2)}) collective-permute-start(f32[2,128,128]{2,1,0:T(8,128)S(1)} %convolution_select_fusion.6), channel_id=1, source_target_pairs={{0,16},{8,24},{32,48},{40,56},{64,80},{72,88},{96,112},{104,120},{... | collective-permute-start | bytes 393224 | tf_op jit(solution)/shard_map/ppermute | solution.py:115
  34.8 7.8 %collective-permute-start.24 = (bf16[256,256]{0,1:T(8,128)(2,1)S(1)}, bf16[256,256]{0,1:T(8,128)(2,1)S(1)}, u32[]{:S(2)}, u32[]{:S(2)}) collective-permute-start(bf16[256,256]{0,1:T(8,128)(2,1)S(1)} %collective-permute-done.23), channel_id=1, source_target_pairs={{0,8},{8,16},{16,24},{24,32},{32,40},{40,48},{48,56},{56,64},{64,7... | collective-permute-start | bytes 393224 | tf_op jit(solution)/shard_map/ppermute | solution.py:18
  38.9 9.3 %collective-permute-start.7 = (f32[2,128,128]{2,1,0:T(8,128)S(1)}, f32[2,128,128]{2,1,0:T(8,128)S(1)}, u32[]{:S(2)}, u32[]{:S(2)}) collective-permute-start(f32[2,128,128]{2,1,0:T(8,128)S(1)} %fusion.55), channel_id=1, source_target_pairs={{24,56},{56,88},{88,120},{120,152},{152,184},{184,216},{216,248},{... | collective-permute-start | bytes 393224 | tf_op jit(solution)/shard_map/ppermute | solution.py:115
  39.8 9.3 %collective-permute-start.2 = (f32[2,128,128]{2,1,0:T(8,128)S(1)}, f32[2,128,128]{2,1,0:T(8,128)S(1)}, u32[]{:S(2)}, u32[]{:S(2)}) collective-permute-start(f32[2,128,128]{2,1,0:T(8,128)S(1)} %convolution_select_fusion.4), channel_id=1, source_target_pairs={{24,56},{56,88},{88,120},{120,152},{152,184},{184,216},{216,248},{... | collective-permute-start | bytes 393224 | tf_op jit(solution)/shard_map/ppermute | solution.py:115
  42.6 15.7 %collective-permute-start.25 = (bf16[256,256]{0,1:T(8,128)(2,1)S(1)}, bf16[256,256]{0,1:T(8,128)(2,1)S(1)}, u32[]{:S(2)}, u32[]{:S(2)}) collective-permute-start(bf16[256,256]{0,1:T(8,128)(2,1)S(1)} %collective-permute-done.24), channel_id=1, source_target_pairs={{0,8},{8,16},{16,24},{24,32},{32,40},{40,48},{48,56},{56,64},{64,7... | collective-permute-start | bytes 393224 | tf_op jit(solution)/shard_map/ppermute | solution.py:18
  48.5 11.8 %collective-permute-start.8 = (f32[2,128,128]{2,1,0:T(8,128)S(1)}, f32[2,128,128]{2,1,0:T(8,128)S(1)}, u32[]{:S(2)}, u32[]{:S(2)}) collective-permute-start(f32[2,128,128]{2,1,0:T(8,128)S(1)} %fusion.54), channel_id=1, source_target_pairs={{24,88},{56,120},{88,152},{120,184},{152,216},{184,248},{216,280},... | collective-permute-start | bytes 393224 | tf_op jit(solution)/shard_map/ppermute | solution.py:115
  49.4 11.8 %collective-permute-start.3 = (f32[2,128,128]{2,1,0:T(8,128)S(1)}, f32[2,128,128]{2,1,0:T(8,128)S(1)}, u32[]{:S(2)}, u32[]{:S(2)}) collective-permute-start(f32[2,128,128]{2,1,0:T(8,128)S(1)} %convolution_select_fusion.3), channel_id=1, source_target_pairs={{24,88},{56,120},{88,152},{120,184},{152,216},{184,248},{216,280},... | collective-permute-start | bytes 393224 | tf_op jit(solution)/shard_map/ppermute | solution.py:115
  58.4 14.8 %collective-permute-start.26 = (bf16[256,256]{0,1:T(8,128)(2,1)S(1)}, bf16[256,256]{0,1:T(8,128)(2,1)S(1)}, u32[]{:S(2)}, u32[]{:S(2)}) collective-permute-start(bf16[256,256]{0,1:T(8,128)(2,1)S(1)} %collective-permute-done.25), channel_id=1, source_target_pairs={{0,8},{8,16},{16,24},{24,32},{32,40},{40,48},{48,56},{56,64},{64,7... | collective-permute-start | bytes 393224 | tf_op jit(solution)/shard_map/ppermute | solution.py:18
  60.6 14.5 %collective-permute-start.9 = (f32[2,128,128]{2,1,0:T(8,128)S(1)}, f32[2,128,128]{2,1,0:T(8,128)S(1)}, u32[]{:S(2)}, u32[]{:S(2)}) collective-permute-start(f32[2,128,128]{2,1,0:T(8,128)S(1)} %fusion.53), channel_id=1, source_target_pairs={{24,152},{56,184},{88,216},{120,248},{152,280},{184,312},{216,344}... | collective-permute-start | bytes 393224 | tf_op jit(solution)/shard_map/ppermute | solution.py:115
  61.5 27.5 %collective-permute-start.4 = (f32[2,128,128]{2,1,0:T(8,128)S(1)}, f32[2,128,128]{2,1,0:T(8,128)S(1)}, u32[]{:S(2)}, u32[]{:S(2)}) collective-permute-start(f32[2,128,128]{2,1,0:T(8,128)S(1)} %convolution_select_fusion.2), channel_id=1, source_target_pairs={{24,152},{56,184},{88,216},{120,248},{152,280},{184,312},{216,344}... | collective-permute-start | bytes 393224 | tf_op jit(solution)/shard_map/ppermute | solution.py:115
  73.1 14.0 %collective-permute-start.27 = (bf16[256,256]{0,1:T(8,128)(2,1)S(1)}, bf16[256,256]{0,1:T(8,128)(2,1)S(1)}, u32[]{:S(2)}, u32[]{:S(2)}) collective-permute-start(bf16[256,256]{0,1:T(8,128)(2,1)S(1)} %collective-permute-done.26), channel_id=1, source_target_pairs={{0,8},{8,16},{16,24},{24,32},{32,40},{40,48},{48,56},{56,64},{64,7... | collective-permute-start | bytes 393224 | tf_op jit(solution)/shard_map/ppermute | solution.py:18
  75.3 14.0 %collective-permute-start.10 = (f32[2,128,128]{2,1,0:T(8,128)S(1)}, f32[2,128,128]{2,1,0:T(8,128)S(1)}, u32[]{:S(2)}, u32[]{:S(2)}) collective-permute-start(f32[2,128,128]{2,1,0:T(8,128)S(1)} %fusion.52), channel_id=1, source_target_pairs={{24,280},{56,312},{88,344},{120,376},{152,408},{184,440},{216,472}... | collective-permute-start | bytes 393224 | tf_op jit(solution)/shard_map/ppermute | solution.py:115
  87.1 25.9 %copy-start.3 = (bf16[256,256]{0,1:T(8,128)(2,1)}, bf16[256,256]{0,1:T(8,128)(2,1)S(1)}, u32[]{:S(2)}) copy-start(bf16[256,256]{0,1:T(8,128)(2,1)S(1)} %collective-permute-done.27) | copy-start | bytes 393220
  87.1 8.0 %collective-permute-start.28 = (bf16[256,256]{0,1:T(8,128)(2,1)S(1)}, bf16[256,256]{0,1:T(8,128)(2,1)S(1)}, u32[]{:S(2)}, u32[]{:S(2)}) collective-permute-start(bf16[256,256]{0,1:T(8,128)(2,1)S(1)} %collective-permute-done.27), channel_id=1, source_target_pairs={{0,8},{8,16},{16,24},{24,32},{32,40},{40,48},{48,56},{56,64},{64,7... | collective-permute-start | bytes 393224 | tf_op jit(solution)/shard_map/ppermute | solution.py:18
  89.6 23.0 %collective-permute-start.14 = (f32[2,128,128]{2,1,0:T(8,128)S(1)}, f32[2,128,128]{2,1,0:T(8,128)S(1)}, u32[]{:S(2)}, u32[]{:S(2)}) collective-permute-start(f32[2,128,128]{2,1,0:T(8,128)S(1)} %fusion.51), channel_id=1, source_target_pairs={{24,56},{56,88},{88,120},{120,152},{152,184},{184,216},{216,248},{... | collective-permute-start | bytes 393224 | tf_op jit(solution)/shard_map/ppermute | solution.py:115
  90.3 22.4 %collective-permute-start.13 = (f32[2,128,128]{2,1,0:T(8,128)S(1)}, f32[2,128,128]{2,1,0:T(8,128)S(1)}, u32[]{:S(2)}, u32[]{:S(2)}) collective-permute-start(f32[2,128,128]{2,1,0:T(8,128)S(1)} %fusion.51), channel_id=1, source_target_pairs={{24,48},{56,80},{88,112},{120,144},{152,176},{184,208},{216,240},{... | collective-permute-start | bytes 393224 | tf_op jit(solution)/shard_map/ppermute | solution.py:115
  91.0 21.7 %collective-permute-start.12 = (f32[2,128,128]{2,1,0:T(8,128)S(1)}, f32[2,128,128]{2,1,0:T(8,128)S(1)}, u32[]{:S(2)}, u32[]{:S(2)}) collective-permute-start(f32[2,128,128]{2,1,0:T(8,128)S(1)} %fusion.51), channel_id=1, source_target_pairs={{24,40},{56,72},{88,104},{120,136},{152,168},{184,200},{216,232},{... | collective-permute-start | bytes 393224 | tf_op jit(solution)/shard_map/ppermute | solution.py:115
  91.9 20.8 %collective-permute-start.11 = (f32[2,128,128]{2,1,0:T(8,128)S(1)}, f32[2,128,128]{2,1,0:T(8,128)S(1)}, u32[]{:S(2)}, u32[]{:S(2)}) collective-permute-start(f32[2,128,128]{2,1,0:T(8,128)S(1)} %fusion.51), channel_id=1, source_target_pairs={{24,32},{56,64},{88,96},{120,128},{152,160},{184,192},{216,224},{2... | collective-permute-start | bytes 393224 | tf_op jit(solution)/shard_map/ppermute | solution.py:115
  95.1 17.9 %copy-start.5 = (bf16[256,256]{0,1:T(8,128)(2,1)}, bf16[256,256]{0,1:T(8,128)(2,1)S(1)}, u32[]{:S(2)}) copy-start(bf16[256,256]{0,1:T(8,128)(2,1)S(1)} %collective-permute-done.28) | copy-start | bytes 393220
  95.1 15.6 %collective-permute-start.29 = (bf16[256,256]{0,1:T(8,128)(2,1)S(1)}, bf16[256,256]{0,1:T(8,128)(2,1)}, u32[]{:S(2)}, u32[]{:S(2)}) collective-permute-start(bf16[256,256]{0,1:T(8,128)(2,1)S(1)} %collective-permute-done.28), channel_id=1, source_target_pairs={{0,8},{8,16},{16,24},{24,32},{32,40},{40,48},{48,56},{56,64},{64,7... | collective-permute-start | bytes 393224 | tf_op jit(solution)/shard_map/ppermute | solution.py:18
  110.7 17.6 %collective-permute-start.30 = (bf16[256,256]{0,1:T(8,128)(2,1)}, bf16[256,256]{0,1:T(8,128)(2,1)}, u32[]{:S(2)}, u32[]{:S(2)}) collective-permute-start(bf16[256,256]{0,1:T(8,128)(2,1)} %collective-permute-done.29), channel_id=1, source_target_pairs={{0,8},{8,16},{16,24},{24,32},{32,40},{40,48},{48,56},{56,64},{64,7... | collective-permute-start | bytes 393224 | tf_op jit(solution)/shard_map/ppermute | solution.py:18
  113.0 17.2 %copy-start.6 = (bf16[256,256]{0,1:T(8,128)(2,1)S(1)}, bf16[256,256]{0,1:T(8,128)(2,1)}, u32[]{:S(2)}) copy-start(bf16[256,256]{0,1:T(8,128)(2,1)} %copy-done.5) | copy-start | bytes 393220
  117.5 12.7 %copy-start.4 = (bf16[256,256]{0,1:T(8,128)(2,1)S(1)}, bf16[256,256]{0,1:T(8,128)(2,1)}, u32[]{:S(2)}) copy-start(bf16[256,256]{0,1:T(8,128)(2,1)} %copy-done.3) | copy-start | bytes 393220
  118.4 12.8 %collective-permute-start.20 = (bf16[256,256]{0,1:T(8,128)(2,1)S(1)}, bf16[256,256]{0,1:T(8,128)(2,1)S(1)}, u32[]{:S(2)}, u32[]{:S(2)}) collective-permute-start(bf16[256,256]{0,1:T(8,128)(2,1)S(1)} %bitcast.201), channel_id=1, source_target_pairs={{0,8},{8,16},{16,24},{24,32},{32,40},{40,48},{48,56},{56,64},{64,7... | collective-permute-start | bytes 393224 | tf_op jit(solution)/shard_map/ppermute | solution.py:18
  120.3 14.8 %collective-permute-start.17 = (bf16[256,256]{0,1:T(8,128)(2,1)S(1)}, bf16[256,256]{0,1:T(8,128)(2,1)S(1)}, u32[]{:S(2)}, u32[]{:S(2)}) collective-permute-start(bf16[256,256]{0,1:T(8,128)(2,1)S(1)} %bitcast.202), channel_id=1, source_target_pairs={{0,32},{8,40},{16,48},{24,56},{32,64},{40,72},{48,80},{56,88},{64,... | collective-permute-start | bytes 393224 | tf_op jit(solution)/shard_map/ppermute | solution.py:18
  123.7 20.3 %collective-permute-start.15 = (bf16[256,256]{0,1:T(8,128)(2,1)S(1)}, bf16[256,256]{0,1:T(8,128)(2,1)S(1)}, u32[]{:S(2)}, u32[]{:S(2)}) collective-permute-start(bf16[256,256]{0,1:T(8,128)(2,1)S(1)} %bitcast.203), channel_id=1, source_target_pairs={{0,56},{8,64},{16,72},{24,80},{32,88},{40,96},{48,104},{56,112},{6... | collective-permute-start | bytes 393224 | tf_op jit(solution)/shard_map/ppermute | solution.py:18
  131.2 24.8 %collective-permute-start.21 = (bf16[256,256]{0,1:T(8,128)(2,1)S(1)}, bf16[256,256]{0,1:T(8,128)(2,1)S(1)}, u32[]{:S(2)}, u32[]{:S(2)}) collective-permute-start(bf16[256,256]{0,1:T(8,128)(2,1)S(1)} %collective-permute-done.20), channel_id=1, source_target_pairs={{0,8},{8,16},{16,24},{24,32},{32,40},{40,48},{48,56},{56,64},{64,7... | collective-permute-start | bytes 393224 | tf_op jit(solution)/shard_map/ppermute | solution.py:18
  135.2 25.9 %collective-permute-start.18 = (bf16[256,256]{0,1:T(8,128)(2,1)S(1)}, bf16[256,256]{0,1:T(8,128)(2,1)S(1)}, u32[]{:S(2)}, u32[]{:S(2)}) collective-permute-start(bf16[256,256]{0,1:T(8,128)(2,1)S(1)} %collective-permute-done.17), channel_id=1, source_target_pairs={{0,8},{8,16},{16,24},{24,32},{32,40},{40,48},{48,56},{56,64},{64,7... | collective-permute-start | bytes 393224 | tf_op jit(solution)/shard_map/ppermute | solution.py:18
  144.0 22.4 %collective-permute-start.16 = (bf16[256,256]{0,1:T(8,128)(2,1)S(1)}, bf16[256,256]{0,1:T(8,128)(2,1)S(1)}, u32[]{:S(2)}, u32[]{:S(2)}) collective-permute-start(bf16[256,256]{0,1:T(8,128)(2,1)S(1)} %collective-permute-done.15), channel_id=1, source_target_pairs={{0,8},{8,16},{16,24},{24,32},{32,40},{40,48},{48,56},{56,64},{64,7... | collective-permute-start | bytes 393224 | tf_op jit(solution)/shard_map/ppermute | solution.py:18
  156.0 13.6 %collective-permute-start.22 = (bf16[256,256]{0,1:T(8,128)(2,1)S(1)}, bf16[256,256]{0,1:T(8,128)(2,1)S(1)}, u32[]{:S(2)}, u32[]{:S(2)}) collective-permute-start(bf16[256,256]{0,1:T(8,128)(2,1)S(1)} %collective-permute-done.21), channel_id=1, source_target_pairs={{0,8},{8,16},{16,24},{24,32},{32,40},{40,48},{48,56},{56,64},{64,7... | collective-permute-start | bytes 393224 | tf_op jit(solution)/shard_map/ppermute | solution.py:18
  161.1 8.4 %collective-permute-start.19 = (bf16[256,256]{0,1:T(8,128)(2,1)S(1)}, bf16[256,256]{0,1:T(8,128)(2,1)S(1)}, u32[]{:S(2)}, u32[]{:S(2)}) collective-permute-start(bf16[256,256]{0,1:T(8,128)(2,1)S(1)} %collective-permute-done.18), channel_id=1, source_target_pairs={{0,8},{8,16},{16,24},{24,32},{32,40},{40,48},{48,56},{56,64},{64,7... | collective-permute-start | bytes 393224 | tf_op jit(solution)/shard_map/ppermute | solution.py:18
  169.7 24.6 %copy-start.7 = (f32[256]{0:T(256)S(1)}, f32[256]{0:T(256)}, u32[]{:S(2)}) copy-start(f32[256]{0:T(256)} %param.17) | copy-start | bytes 3076

commit v16 on v6

--- a/solution.py
+++ b/solution.py
@@ -90,7 +90,7 @@
 
 
 def batched_dot(left, right):
-    return jnp.einsum("hij,hjk->hik", left, right, precision=highest)
+    return jnp.einsum("hij,hjk->hik", left, right, precision=lax.Precision.HIGH)
 
 
 def on_device(q_delta, k_delta, v_delta, write_rate, q_attn, k_attn, out_gain):

time: 190 us -> 189 us (level)
  transfers between devices with their start and end apart: 31 -> 31, of which waited for: 12 -> 12; matrix products, arithmetic and copies ran while one was open for 15% -> 14% of each run, Pallas kernels for 0% -> 0%
where the time goes in v16:
time: 189 us; the launch traced here: 187 us
  waiting for transfers between devices  69.8 us (37%)
  starting transfers between devices  63.2 us (33%)
  blocking collectives  22.8 us (12%)
  matrix products  20.1 us (11%)
  local copies, waits for them, and re-layouts  4.72 us (2%)
  other arithmetic  4.65 us (2%)
    ppermute x16, waiting for transfers between devices, shifted(): return lax.ppermute(value, axis, pairs)  58.7 us
    ppermute x16, starting transfers between devices, shifted(): return lax.ppermute(value, axis, pairs)  41.1 us
    psum x1, blocking collectives, on_device(): total_sq = lax.psum(squares, 'head')  22.8 us
    ppermute x15, starting transfers between devices, moved(): return lax.ppermute(value, 'seq', pairs)  22.1 us
    ppermute x15, waiting for transfers between devices, moved(): return lax.ppermute(value, 'seq', pairs)  11.1 us
  transfers between devices with their start and end apart: 31, of which 12 were waited for; matrix products, arithmetic and copies ran while one was open for 14% of the time, Pallas kernels for 0%

profile of v16, /device:TPU:25, one launch (start us, length us, event | category | flops | bytes accessed | tf_op | source)
XLA Modules:
  0.0 187.4 jit_solution(8739884173999950067)
XLA Ops:
  0.7 1.1 copy.57
  1.7 3.5 %collective-permute-start.23 = (bf16[256,256]{0,1:T(8,128)(2,1)S(1)}, bf16[256,256]{0,1:T(8,128)(2,1)S(1)}, u32[]{:S(2)}, u32[]{:S(2)}) collective-permute-start(bf16[256,256]{0,1:T(8,128)(2,1)S(1)} %copy.57), channel_id=1, source_target_pairs={{0,8},{8,16},{16,24},{24,32},{32,40},{40,48},{48,56},{56,64},{64,7... | collective-permute-start | bytes 393224 | tf_op jit(solution)/shard_map/ppermute | solution.py:18
  5.3 0.8 mul.79
  6.1 1.0 copy.41
  13.1 5.7 %while.30 = (s32[]{:T(128)}, f32[2,128,128]{2,1,0:T(8,128)S(1)}, f32[2,128,128]{2,1,0:T(8,128)S(1)}, f32[4,2,64,128]{3,2,1,0:T(8,128)S(1)}, f32[4,2,64,128]{3,2,...) while((s32[]{:T(128)}, f32[2,128,128]{2,1,0:T(8,128)S(1)}, ...), condition=%wide.region_2.3_spmd.clone, body=%wide.region_1.0_spmd.clone.sunk | while | flops 151126016 | bytes 1837159 | solution.py:74
  18.8 3.6 %collective-permute-start.5 = (f32[2,128,128]{2,1,0:T(8,128)S(1)}, f32[2,128,128]{2,1,0:T(8,128)S(1)}, u32[]{:S(2)}, u32[]{:S(2)}) collective-permute-start(f32[2,128,128]{2,1,0:T(8,128)S(1)} %get-tuple-element.101), channel_id=1, source_target_pairs={{0,8},{8,16},{16,24},{32,40},{40,48},{48,56},{64,72},{72,80},{80,8... | collective-permute-start | bytes 393224 | tf_op jit(solution)/shard_map/ppermute | solution.py:115
  22.3 3.5 %collective-permute-start = (f32[2,128,128]{2,1,0:T(8,128)S(1)}, f32[2,128,128]{2,1,0:T(8,128)S(1)}, u32[]{:S(2)}, u32[]{:S(2)}) collective-permute-start(f32[2,128,128]{2,1,0:T(8,128)S(1)} %get-tuple-element.100), channel_id=1, source_target_pairs={{0,8},{8,16},{16,24},{32,40},{40,48},{48,56},{64,72},{72,80},{80,8... | collective-permute-start | bytes 393224 | tf_op jit(solution)/shard_map/ppermute | solution.py:115
  27.1 4.5 %collective-permute-start.6 = (f32[2,128,128]{2,1,0:T(8,128)S(1)}, f32[2,128,128]{2,1,0:T(8,128)S(1)}, u32[]{:S(2)}, u32[]{:S(2)}) collective-permute-start(f32[2,128,128]{2,1,0:T(8,128)S(1)} %fusion.56), channel_id=1, source_target_pairs={{0,16},{8,24},{32,48},{40,56},{64,80},{72,88},{96,112},{104,120},{... | collective-permute-start | bytes 393224 | tf_op jit(solution)/shard_map/ppermute | solution.py:115
  31.8 2.6 %collective-permute-start.1 = (f32[2,128,128]{2,1,0:T(8,128)S(1)}, f32[2,128,128]{2,1,0:T(8,128)S(1)}, u32[]{:S(2)}, u32[]{:S(2)}) collective-permute-start(f32[2,128,128]{2,1,0:T(8,128)S(1)} %convolution_select_fusion.6), channel_id=1, source_target_pairs={{0,16},{8,24},{32,48},{40,56},{64,80},{72,88},{96,112},{104,120},{... | collective-permute-start | bytes 393224 | tf_op jit(solution)/shard_map/ppermute | solution.py:115
  34.6 3.5 %collective-permute-start.24 = (bf16[256,256]{0,1:T(8,128)(2,1)S(1)}, bf16[256,256]{0,1:T(8,128)(2,1)S(1)}, u32[]{:S(2)}, u32[]{:S(2)}) collective-permute-start(bf16[256,256]{0,1:T(8,128)(2,1)S(1)} %collective-permute-done.23), channel_id=1, source_target_pairs={{0,8},{8,16},{16,24},{24,32},{32,40},{40,48},{48,56},{56,64},{64,7... | collective-permute-start | bytes 393224 | tf_op jit(solution)/shard_map/ppermute | solution.py:18
  39.5 0.7 collective-permute-start.2
  40.2 2.3 %collective-permute-done.24 = bf16[256,256]{0,1:T(8,128)(2,1)S(1)} collective-permute-done((bf16[256,256]{0,1:T(8,128)(2,1)S(1)}, bf16[256,256]{0,1:T(8,128)(2,1)S(1)}, u32[]{:S(2)}, u32[]{:S(2)}) %collective-permute-start.24) | collective-permute-done | bytes 131104 | tf_op jit(solution)/shard_map/ppermute | solution.py:18
  42.4 5.2 %collective-permute-start.25 = (bf16[256,256]{0,1:T(8,128)(2,1)S(1)}, bf16[256,256]{0,1:T(8,128)(2,1)S(1)}, u32[]{:S(2)}, u32[]{:S(2)}) collective-permute-start(bf16[256,256]{0,1:T(8,128)(2,1)S(1)} %collective-permute-done.24), channel_id=1, source_target_pairs={{0,8},{8,16},{16,24},{24,32},{32,40},{40,48},{48,56},{56,64},{64,7... | collective-permute-start | bytes 393224 | tf_op jit(solution)/shard_map/ppermute | solution.py:18
  48.1 0.7 collective-permute-start.8
  49.7 10.5 %collective-permute-done.25 = bf16[256,256]{0,1:T(8,128)(2,1)S(1)} collective-permute-done((bf16[256,256]{0,1:T(8,128)(2,1)S(1)}, bf16[256,256]{0,1:T(8,128)(2,1)S(1)}, u32[]{:S(2)}, u32[]{:S(2)}) %collective-permute-start.25) | collective-permute-done | bytes 131104 | tf_op jit(solution)/shard_map/ppermute | solution.py:18
  60.2 1.9 %collective-permute-start.26 = (bf16[256,256]{0,1:T(8,128)(2,1)S(1)}, bf16[256,256]{0,1:T(8,128)(2,1)S(1)}, u32[]{:S(2)}, u32[]{:S(2)}) collective-permute-start(bf16[256,256]{0,1:T(8,128)(2,1)S(1)} %collective-permute-done.25), channel_id=1, source_target_pairs={{0,8},{8,16},{16,24},{24,32},{32,40},{40,48},{48,56},{56,64},{64,7... | collective-permute-start | bytes 393224 | tf_op jit(solution)/shard_map/ppermute | solution.py:18
  62.4 0.7 collective-permute-start.9
  64.0 9.1 %collective-permute-done.26 = bf16[256,256]{0,1:T(8,128)(2,1)S(1)} collective-permute-done((bf16[256,256]{0,1:T(8,128)(2,1)S(1)}, bf16[256,256]{0,1:T(8,128)(2,1)S(1)}, u32[]{:S(2)}, u32[]{:S(2)}) %collective-permute-start.26) | collective-permute-done | bytes 131104 | tf_op jit(solution)/shard_map/ppermute | solution.py:18
  73.0 1.9 %collective-permute-start.27 = (bf16[256,256]{0,1:T(8,128)(2,1)S(1)}, bf16[256,256]{0,1:T(8,128)(2,1)S(1)}, u32[]{:S(2)}, u32[]{:S(2)}) collective-permute-start(bf16[256,256]{0,1:T(8,128)(2,1)S(1)} %collective-permute-done.26), channel_id=1, source_target_pairs={{0,8},{8,16},{16,24},{24,32},{32,40},{40,48},{48,56},{56,64},{64,7... | collective-permute-start | bytes 393224 | tf_op jit(solution)/shard_map/ppermute | solution.py:18
  75.2 0.7 collective-permute-start.10
  75.9 10.9 %collective-permute-done.27 = bf16[256,256]{0,1:T(8,128)(2,1)S(1)} collective-permute-done((bf16[256,256]{0,1:T(8,128)(2,1)S(1)}, bf16[256,256]{0,1:T(8,128)(2,1)S(1)}, u32[]{:S(2)}, u32[]{:S(2)}) %collective-permute-start.27) | collective-permute-done | bytes 131104 | tf_op jit(solution)/shard_map/ppermute | solution.py:18
  86.8 1.9 %collective-permute-start.28 = (bf16[256,256]{0,1:T(8,128)(2,1)S(1)}, bf16[256,256]{0,1:T(8,128)(2,1)S(1)}, u32[]{:S(2)}, u32[]{:S(2)}) collective-permute-start(bf16[256,256]{0,1:T(8,128)(2,1)S(1)} %collective-permute-done.27), channel_id=1, source_target_pairs={{0,8},{8,16},{16,24},{24,32},{32,40},{40,48},{48,56},{56,64},{64,7... | collective-permute-start | bytes 393224 | tf_op jit(solution)/shard_map/ppermute | solution.py:18
  91.2 1.3 collective-permute-start.11
  92.7 2.1 %collective-permute-done.28 = bf16[256,256]{0,1:T(8,128)(2,1)S(1)} collective-permute-done((bf16[256,256]{0,1:T(8,128)(2,1)S(1)}, bf16[256,256]{0,1:T(8,128)(2,1)S(1)}, u32[]{:S(2)}, u32[]{:S(2)}) %collective-permute-start.28) | collective-permute-done | bytes 131104 | tf_op jit(solution)/shard_map/ppermute | solution.py:18
  94.7 1.9 %collective-permute-start.29 = (bf16[256,256]{0,1:T(8,128)(2,1)S(1)}, bf16[256,256]{0,1:T(8,128)(2,1)S(1)}, u32[]{:S(2)}, u32[]{:S(2)}) collective-permute-start(bf16[256,256]{0,1:T(8,128)(2,1)S(1)} %collective-permute-done.28), channel_id=1, source_target_pairs={{0,8},{8,16},{16,24},{24,32},{32,40},{40,48},{48,56},{56,64},{64,7... | collective-permute-start | bytes 393224 | tf_op jit(solution)/shard_map/ppermute | solution.py:18
  96.7 11.1 %collective-permute-done.11 = f32[2,128,128]{2,1,0:T(8,128)S(1)} collective-permute-done((f32[2,128,128]{2,1,0:T(8,128)S(1)}, f32[2,128,128]{2,1,0:T(8,128)S(1)}, u32[]{:S(2)}, u32[]{:S(2)}) %collective-permute-start.11) | collective-permute-done | bytes 131104 | tf_op jit(solution)/shard_map/ppermute | solution.py:115
  108.0 4.5 %while.29 = (s32[]{:T(128)}, f32[2,128,128]{2,1,0:T(8,128)S(1)}, bf16[4,2,64,128]{3,2,0,1:T(8,128)(2,1)S(1)}, f32[4,2,64,128]{3,2,1,0:T(8,128)S(1)}, f32[4,2,64,...) while((s32[]{:T(128)}, f32[2,128,128]{2,1,0:T(8,128)S(1)}, ...), condition=%wide.region_5.6_spmd, body=%wide.region_4.5_spmd.sunk | while | flops 88145920 | bytes 1247341 | solution.py:88
  112.6 1.9 %collective-permute-start.19 = (bf16[256,256]{0,1:T(8,128)(2,1)S(1)}, bf16[256,256]{0,1:T(8,128)(2,1)S(1)}, u32[]{:S(2)}, u32[]{:S(2)}) collective-permute-start(bf16[256,256]{0,1:T(8,128)(2,1)S(1)} %bitcast.200), channel_id=1, source_target_pairs={{0,8},{8,16},{16,24},{24,32},{32,40},{40,48},{48,56},{56,64},{64,7... | collective-permute-start | bytes 393224 | tf_op jit(solution)/shard_map/ppermute | solution.py:18
  114.5 1.9 %collective-permute-start.15 = (bf16[256,256]{0,1:T(8,128)(2,1)S(1)}, bf16[256,256]{0,1:T(8,128)(2,1)S(1)}, u32[]{:S(2)}, u32[]{:S(2)}) collective-permute-start(bf16[256,256]{0,1:T(8,128)(2,1)S(1)} %bitcast.201), channel_id=1, source_target_pairs={{0,40},{8,48},{16,56},{24,64},{32,72},{40,80},{48,88},{56,96},{64,... | collective-permute-start | bytes 393224 | tf_op jit(solution)/shard_map/ppermute | solution.py:18
  116.5 2.7 %collective-permute-start.30 = (bf16[256,256]{0,1:T(8,128)(2,1)S(1)}, bf16[256,256]{0,1:T(8,128)(2,1)S(1)}, u32[]{:S(2)}, u32[]{:S(2)}) collective-permute-start(bf16[256,256]{0,1:T(8,128)(2,1)S(1)} %collective-permute-done.29), channel_id=1, source_target_pairs={{0,8},{8,16},{16,24},{24,32},{32,40},{40,48},{48,56},{56,64},{64,7... | collective-permute-start | bytes 393224 | tf_op jit(solution)/shard_map/ppermute | solution.py:18
  119.1 1.3 fusion.46
  120.4 0.8 copy.63
  121.2 5.0 %collective-permute-start.20 = (bf16[256,256]{0,1:T(8,128)(2,1)S(1)}, bf16[256,256]{0,1:T(8,128)(2,1)S(1)}, u32[]{:S(2)}, u32[]{:S(2)}) collective-permute-start(bf16[256,256]{0,1:T(8,128)(2,1)S(1)} %collective-permute-done.19), channel_id=1, source_target_pairs={{0,8},{8,16},{16,24},{24,32},{32,40},{40,48},{48,56},{56,64},{64,7... | collective-permute-start | bytes 393224 | tf_op jit(solution)/shard_map/ppermute | solution.py:18
  126.2 3.5 %collective-permute-done.15 = bf16[256,256]{0,1:T(8,128)(2,1)S(1)} collective-permute-done((bf16[256,256]{0,1:T(8,128)(2,1)S(1)}, bf16[256,256]{0,1:T(8,128)(2,1)S(1)}, u32[]{:S(2)}, u32[]{:S(2)}) %collective-permute-start.15) | collective-permute-done | bytes 131104 | tf_op jit(solution)/shard_map/ppermute | solution.py:18
  129.7 1.9 %collective-permute-start.16 = (bf16[256,256]{0,1:T(8,128)(2,1)S(1)}, bf16[256,256]{0,1:T(8,128)(2,1)S(1)}, u32[]{:S(2)}, u32[]{:S(2)}) collective-permute-start(bf16[256,256]{0,1:T(8,128)(2,1)S(1)} %collective-permute-done.15), channel_id=1, source_target_pairs={{0,8},{8,16},{16,24},{24,32},{32,40},{40,48},{48,56},{56,64},{64,7... | collective-permute-start | bytes 393224 | tf_op jit(solution)/shard_map/ppermute | solution.py:18
  131.6 1.1 collective-permute-done.30
  132.9 9.8 %collective-permute-done.16 = bf16[256,256]{0,1:T(8,128)(2,1)S(1)} collective-permute-done((bf16[256,256]{0,1:T(8,128)(2,1)S(1)}, bf16[256,256]{0,1:T(8,128)(2,1)S(1)}, u32[]{:S(2)}, u32[]{:S(2)}) %collective-permute-start.16) | collective-permute-done | bytes 131104 | tf_op jit(solution)/shard_map/ppermute | solution.py:18
  142.7 1.9 %collective-permute-start.17 = (bf16[256,256]{0,1:T(8,128)(2,1)S(1)}, bf16[256,256]{0,1:T(8,128)(2,1)S(1)}, u32[]{:S(2)}, u32[]{:S(2)}) collective-permute-start(bf16[256,256]{0,1:T(8,128)(2,1)S(1)} %collective-permute-done.16), channel_id=1, source_target_pairs={{0,8},{8,16},{16,24},{24,32},{32,40},{40,48},{48,56},{56,64},{64,7... | collective-permute-start | bytes 393224 | tf_op jit(solution)/shard_map/ppermute | solution.py:18
  144.7 0.8 fusion.39
  145.5 1.9 %collective-permute-start.21 = (bf16[256,256]{0,1:T(8,128)(2,1)S(1)}, bf16[256,256]{0,1:T(8,128)(2,1)S(1)}, u32[]{:S(2)}, u32[]{:S(2)}) collective-permute-start(bf16[256,256]{0,1:T(8,128)(2,1)S(1)} %collective-permute-done.20), channel_id=1, source_target_pairs={{0,8},{8,16},{16,24},{24,32},{32,40},{40,48},{48,56},{56,64},{64,7... | collective-permute-start | bytes 393224 | tf_op jit(solution)/shard_map/ppermute | solution.py:18
  147.4 3.5 %collective-permute-done.17 = bf16[256,256]{0,1:T(8,128)(2,1)S(1)} collective-permute-done((bf16[256,256]{0,1:T(8,128)(2,1)S(1)}, bf16[256,256]{0,1:T(8,128)(2,1)S(1)}, u32[]{:S(2)}, u32[]{:S(2)}) %collective-permute-start.17) | collective-permute-done | bytes 131104 | tf_op jit(solution)/shard_map/ppermute | solution.py:18
  150.9 1.9 %collective-permute-start.18 = (bf16[256,256]{0,1:T(8,128)(2,1)S(1)}, bf16[256,256]{0,1:T(8,128)(2,1)S(1)}, u32[]{:S(2)}, u32[]{:S(2)}) collective-permute-start(bf16[256,256]{0,1:T(8,128)(2,1)S(1)} %collective-permute-done.17), channel_id=1, source_target_pairs={{0,8},{8,16},{16,24},{24,32},{32,40},{40,48},{48,56},{56,64},{64,7... | collective-permute-start | bytes 393224 | tf_op jit(solution)/shard_map/ppermute | solution.py:18
  152.9 2.4 %fusion.91 = (f32[2,256]{1,0:T(2,128)S(1)}, f32[2,256,2304]{1,2,0:T(8,128)S(1)}) fusion(f32[2,256,2304]{1,2,0:T(8,128)S(1)} %fusion.39, pred[256,2304]{0,1:T(8,128)(4,1)S(1)} %fusion.46), kind=kOutput, calls=%fused_computation.150 | output fusion | flops 4720895 | bytes 10029056 | tf_op jit(solution)/shard_map/while/body/eval_jaxpr/sub | solution.py:196
  155.2 1.9 %collective-permute-start.22 = (bf16[256,256]{0,1:T(8,128)(2,1)S(1)}, bf16[256,256]{0,1:T(8,128)(2,1)S(1)}, u32[]{:S(2)}, u32[]{:S(2)}) collective-permute-start(bf16[256,256]{0,1:T(8,128)(2,1)S(1)} %collective-permute-done.21), channel_id=1, source_target_pairs={{0,8},{8,16},{16,24},{24,32},{32,40},{40,48},{48,56},{56,64},{64,7... | collective-permute-start | bytes 393224 | tf_op jit(solution)/shard_map/ppermute | solution.py:18
  157.2 3.2 %collective-permute-done.18 = bf16[256,256]{0,1:T(8,128)(2,1)S(1)} collective-permute-done((bf16[256,256]{0,1:T(8,128)(2,1)S(1)}, bf16[256,256]{0,1:T(8,128)(2,1)S(1)}, u32[]{:S(2)}, u32[]{:S(2)}) %collective-permute-start.18) | collective-permute-done | bytes 131104 | tf_op jit(solution)/shard_map/ppermute | solution.py:18
  160.4 2.7 %collective-permute-done.22 = bf16[256,256]{0,1:T(8,128)(2,1)S(1)} collective-permute-done((bf16[256,256]{0,1:T(8,128)(2,1)S(1)}, bf16[256,256]{0,1:T(8,128)(2,1)S(1)}, u32[]{:S(2)}, u32[]{:S(2)}) %collective-permute-start.22) | collective-permute-done | bytes 131104 | tf_op jit(solution)/shard_map/ppermute | solution.py:18
  163.7 22.8 %psum.7 = f32[256]{0:T(256)S(1)} all-reduce(f32[256]{0:T(256)S(1)} %get-tuple-element.200), channel_id=1, replica_groups=mesh['seq'=64,'head'=8] {'head'}, use_global_device_ids=true, to_apply=%region_9.10 | all-reduce | flops 256 | bytes 2048 | tf_op jit(solution)/shard_map/psum | solution.py:206
  186.7 0.8 multiply_convert_fusion
  (149 shorter events, 24.8 us)
Async XLA Ops:
  0.6 144.0 %copy-start = (bf16[256,256]{1,0:T(8,128)(2,1)S(1)}, bf16[256,256]{1,0:T(8,128)(2,1)}, u32[]{:S(2)}) copy-start(bf16[256,256]{1,0:T(8,128)(2,1)} %param.15) | copy-start | bytes 393220
  0.6 6.7 %copy-start.1 = (bf16[256,256]{1,0:T(8,128)(2,1)S(1)}, bf16[256,256]{1,0:T(8,128)(2,1)}, u32[]{:S(2)}) copy-start(bf16[256,256]{1,0:T(8,128)(2,1)} %param.13) | copy-start | bytes 393220
  1.7 32.9 %collective-permute-start.23 = (bf16[256,256]{0,1:T(8,128)(2,1)S(1)}, bf16[256,256]{0,1:T(8,128)(2,1)S(1)}, u32[]{:S(2)}, u32[]{:S(2)}) collective-permute-start(bf16[256,256]{0,1:T(8,128)(2,1)S(1)} %copy.57), channel_id=1, source_target_pairs={{0,8},{8,16},{16,24},{24,32},{32,40},{40,48},{48,56},{56,64},{64,7... | collective-permute-start | bytes 393224 | tf_op jit(solution)/shard_map/ppermute | solution.py:18
  13.1 12.8 %copy-start.2 = (bf16[256,256]{1,0:T(8,128)(2,1)S(1)}, bf16[256,256]{1,0:T(8,128)(2,1)}, u32[]{:S(2)}) copy-start(bf16[256,256]{1,0:T(8,128)(2,1)} %param.11) | copy-start | bytes 393220
  18.8 8.1 %collective-permute-start.5 = (f32[2,128,128]{2,1,0:T(8,128)S(1)}, f32[2,128,128]{2,1,0:T(8,128)S(1)}, u32[]{:S(2)}, u32[]{:S(2)}) collective-permute-start(f32[2,128,128]{2,1,0:T(8,128)S(1)} %get-tuple-element.101), channel_id=1, source_target_pairs={{0,8},{8,16},{16,24},{32,40},{40,48},{48,56},{64,72},{72,80},{80,8... | collective-permute-start | bytes 393224 | tf_op jit(solution)/shard_map/ppermute | solution.py:115
  22.3 9.2 %collective-permute-start = (f32[2,128,128]{2,1,0:T(8,128)S(1)}, f32[2,128,128]{2,1,0:T(8,128)S(1)}, u32[]{:S(2)}, u32[]{:S(2)}) collective-permute-start(f32[2,128,128]{2,1,0:T(8,128)S(1)} %get-tuple-element.100), channel_id=1, source_target_pairs={{0,8},{8,16},{16,24},{32,40},{40,48},{48,56},{64,72},{72,80},{80,8... | collective-permute-start | bytes 393224 | tf_op jit(solution)/shard_map/ppermute | solution.py:115
  27.1 11.3 %collective-permute-start.6 = (f32[2,128,128]{2,1,0:T(8,128)S(1)}, f32[2,128,128]{2,1,0:T(8,128)S(1)}, u32[]{:S(2)}, u32[]{:S(2)}) collective-permute-start(f32[2,128,128]{2,1,0:T(8,128)S(1)} %fusion.56), channel_id=1, source_target_pairs={{0,16},{8,24},{32,48},{40,56},{64,80},{72,88},{96,112},{104,120},{... | collective-permute-start | bytes 393224 | tf_op jit(solution)/shard_map/ppermute | solution.py:115
  31.8 7.5 %collective-permute-start.1 = (f32[2,128,128]{2,1,0:T(8,128)S(1)}, f32[2,128,128]{2,1,0:T(8,128)S(1)}, u32[]{:S(2)}, u32[]{:S(2)}) collective-permute-start(f32[2,128,128]{2,1,0:T(8,128)S(1)} %convolution_select_fusion.6), channel_id=1, source_target_pairs={{0,16},{8,24},{32,48},{40,56},{64,80},{72,88},{96,112},{104,120},{... | collective-permute-start | bytes 393224 | tf_op jit(solution)/shard_map/ppermute | solution.py:115
  34.6 7.8 %collective-permute-start.24 = (bf16[256,256]{0,1:T(8,128)(2,1)S(1)}, bf16[256,256]{0,1:T(8,128)(2,1)S(1)}, u32[]{:S(2)}, u32[]{:S(2)}) collective-permute-start(bf16[256,256]{0,1:T(8,128)(2,1)S(1)} %collective-permute-done.23), channel_id=1, source_target_pairs={{0,8},{8,16},{16,24},{24,32},{32,40},{40,48},{48,56},{56,64},{64,7... | collective-permute-start | bytes 393224 | tf_op jit(solution)/shard_map/ppermute | solution.py:18
  38.6 9.3 %collective-permute-start.7 = (f32[2,128,128]{2,1,0:T(8,128)S(1)}, f32[2,128,128]{2,1,0:T(8,128)S(1)}, u32[]{:S(2)}, u32[]{:S(2)}) collective-permute-start(f32[2,128,128]{2,1,0:T(8,128)S(1)} %fusion.55), channel_id=1, source_target_pairs={{24,56},{56,88},{88,120},{120,152},{152,184},{184,216},{216,248},{... | collective-permute-start | bytes 393224 | tf_op jit(solution)/shard_map/ppermute | solution.py:115
  39.5 9.3 %collective-permute-start.2 = (f32[2,128,128]{2,1,0:T(8,128)S(1)}, f32[2,128,128]{2,1,0:T(8,128)S(1)}, u32[]{:S(2)}, u32[]{:S(2)}) collective-permute-start(f32[2,128,128]{2,1,0:T(8,128)S(1)} %convolution_select_fusion.4), channel_id=1, source_target_pairs={{24,56},{56,88},{88,120},{120,152},{152,184},{184,216},{216,248},{... | collective-permute-start | bytes 393224 | tf_op jit(solution)/shard_map/ppermute | solution.py:115
  42.4 17.8 %collective-permute-start.25 = (bf16[256,256]{0,1:T(8,128)(2,1)S(1)}, bf16[256,256]{0,1:T(8,128)(2,1)S(1)}, u32[]{:S(2)}, u32[]{:S(2)}) collective-permute-start(bf16[256,256]{0,1:T(8,128)(2,1)S(1)} %collective-permute-done.24), channel_id=1, source_target_pairs={{0,8},{8,16},{16,24},{24,32},{32,40},{40,48},{48,56},{56,64},{64,7... | collective-permute-start | bytes 393224 | tf_op jit(solution)/shard_map/ppermute | solution.py:18
  48.1 14.0 %collective-permute-start.8 = (f32[2,128,128]{2,1,0:T(8,128)S(1)}, f32[2,128,128]{2,1,0:T(8,128)S(1)}, u32[]{:S(2)}, u32[]{:S(2)}) collective-permute-start(f32[2,128,128]{2,1,0:T(8,128)S(1)} %fusion.54), channel_id=1, source_target_pairs={{24,88},{56,120},{88,152},{120,184},{152,216},{184,248},{216,280},... | collective-permute-start | bytes 393224 | tf_op jit(solution)/shard_map/ppermute | solution.py:115
  49.0 14.0 %collective-permute-start.3 = (f32[2,128,128]{2,1,0:T(8,128)S(1)}, f32[2,128,128]{2,1,0:T(8,128)S(1)}, u32[]{:S(2)}, u32[]{:S(2)}) collective-permute-start(f32[2,128,128]{2,1,0:T(8,128)S(1)} %convolution_select_fusion.3), channel_id=1, source_target_pairs={{24,88},{56,120},{88,152},{120,184},{152,216},{184,248},{216,280},... | collective-permute-start | bytes 393224 | tf_op jit(solution)/shard_map/ppermute | solution.py:115
  60.2 12.8 %collective-permute-start.26 = (bf16[256,256]{0,1:T(8,128)(2,1)S(1)}, bf16[256,256]{0,1:T(8,128)(2,1)S(1)}, u32[]{:S(2)}, u32[]{:S(2)}) collective-permute-start(bf16[256,256]{0,1:T(8,128)(2,1)S(1)} %collective-permute-done.25), channel_id=1, source_target_pairs={{0,8},{8,16},{16,24},{24,32},{32,40},{40,48},{48,56},{56,64},{64,7... | collective-permute-start | bytes 393224 | tf_op jit(solution)/shard_map/ppermute | solution.py:18
  62.4 12.6 %collective-permute-start.9 = (f32[2,128,128]{2,1,0:T(8,128)S(1)}, f32[2,128,128]{2,1,0:T(8,128)S(1)}, u32[]{:S(2)}, u32[]{:S(2)}) collective-permute-start(f32[2,128,128]{2,1,0:T(8,128)S(1)} %fusion.53), channel_id=1, source_target_pairs={{24,152},{56,184},{88,216},{120,248},{152,280},{184,312},{216,344}... | collective-permute-start | bytes 393224 | tf_op jit(solution)/shard_map/ppermute | solution.py:115
  63.3 25.4 %collective-permute-start.4 = (f32[2,128,128]{2,1,0:T(8,128)S(1)}, f32[2,128,128]{2,1,0:T(8,128)S(1)}, u32[]{:S(2)}, u32[]{:S(2)}) collective-permute-start(f32[2,128,128]{2,1,0:T(8,128)S(1)} %convolution_select_fusion.2), channel_id=1, source_target_pairs={{24,152},{56,184},{88,216},{120,248},{152,280},{184,312},{216,344}... | collective-permute-start | bytes 393224 | tf_op jit(solution)/shard_map/ppermute | solution.py:115
  73.0 13.7 %collective-permute-start.27 = (bf16[256,256]{0,1:T(8,128)(2,1)S(1)}, bf16[256,256]{0,1:T(8,128)(2,1)S(1)}, u32[]{:S(2)}, u32[]{:S(2)}) collective-permute-start(bf16[256,256]{0,1:T(8,128)(2,1)S(1)} %collective-permute-done.26), channel_id=1, source_target_pairs={{0,8},{8,16},{16,24},{24,32},{32,40},{40,48},{48,56},{56,64},{64,7... | collective-permute-start | bytes 393224 | tf_op jit(solution)/shard_map/ppermute | solution.py:18
  75.2 13.7 %collective-permute-start.10 = (f32[2,128,128]{2,1,0:T(8,128)S(1)}, f32[2,128,128]{2,1,0:T(8,128)S(1)}, u32[]{:S(2)}, u32[]{:S(2)}) collective-permute-start(f32[2,128,128]{2,1,0:T(8,128)S(1)} %fusion.52), channel_id=1, source_target_pairs={{24,280},{56,312},{88,344},{120,376},{152,408},{184,440},{216,472}... | collective-permute-start | bytes 393224 | tf_op jit(solution)/shard_map/ppermute | solution.py:115
  86.8 8.0 %collective-permute-start.28 = (bf16[256,256]{0,1:T(8,128)(2,1)S(1)}, bf16[256,256]{0,1:T(8,128)(2,1)S(1)}, u32[]{:S(2)}, u32[]{:S(2)}) collective-permute-start(bf16[256,256]{0,1:T(8,128)(2,1)S(1)} %collective-permute-done.27), channel_id=1, source_target_pairs={{0,8},{8,16},{16,24},{24,32},{32,40},{40,48},{48,56},{56,64},{64,7... | collective-permute-start | bytes 393224 | tf_op jit(solution)/shard_map/ppermute | solution.py:18
  89.1 7.5 %collective-permute-start.14 = (f32[2,128,128]{2,1,0:T(8,128)S(1)}, f32[2,128,128]{2,1,0:T(8,128)S(1)}, u32[]{:S(2)}, u32[]{:S(2)}) collective-permute-start(f32[2,128,128]{2,1,0:T(8,128)S(1)} %fusion.51), channel_id=1, source_target_pairs={{24,56},{56,88},{88,120},{120,152},{152,184},{184,216},{216,248},{... | collective-permute-start | bytes 393224 | tf_op jit(solution)/shard_map/ppermute | solution.py:115
  89.8 6.8 %collective-permute-start.13 = (f32[2,128,128]{2,1,0:T(8,128)S(1)}, f32[2,128,128]{2,1,0:T(8,128)S(1)}, u32[]{:S(2)}, u32[]{:S(2)}) collective-permute-start(f32[2,128,128]{2,1,0:T(8,128)S(1)} %fusion.51), channel_id=1, source_target_pairs={{24,48},{56,80},{88,112},{120,144},{152,176},{184,208},{216,240},{... | collective-permute-start | bytes 393224 | tf_op jit(solution)/shard_map/ppermute | solution.py:115
  90.5 6.2 %collective-permute-start.12 = (f32[2,128,128]{2,1,0:T(8,128)S(1)}, f32[2,128,128]{2,1,0:T(8,128)S(1)}, u32[]{:S(2)}, u32[]{:S(2)}) collective-permute-start(f32[2,128,128]{2,1,0:T(8,128)S(1)} %fusion.51), channel_id=1, source_target_pairs={{24,40},{56,72},{88,104},{120,136},{152,168},{184,200},{216,232},{... | collective-permute-start | bytes 393224 | tf_op jit(solution)/shard_map/ppermute | solution.py:115
  91.2 16.6 %collective-permute-start.11 = (f32[2,128,128]{2,1,0:T(8,128)S(1)}, f32[2,128,128]{2,1,0:T(8,128)S(1)}, u32[]{:S(2)}, u32[]{:S(2)}) collective-permute-start(f32[2,128,128]{2,1,0:T(8,128)S(1)} %fusion.51), channel_id=1, source_target_pairs={{24,32},{56,64},{88,96},{120,128},{152,160},{184,192},{216,224},{2... | collective-permute-start | bytes 393224 | tf_op jit(solution)/shard_map/ppermute | solution.py:115
  94.7 21.7 %collective-permute-start.29 = (bf16[256,256]{0,1:T(8,128)(2,1)S(1)}, bf16[256,256]{0,1:T(8,128)(2,1)S(1)}, u32[]{:S(2)}, u32[]{:S(2)}) collective-permute-start(bf16[256,256]{0,1:T(8,128)(2,1)S(1)} %collective-permute-done.28), channel_id=1, source_target_pairs={{0,8},{8,16},{16,24},{24,32},{32,40},{40,48},{48,56},{56,64},{64,7... | collective-permute-start | bytes 393224 | tf_op jit(solution)/shard_map/ppermute | solution.py:18
  112.6 8.6 %collective-permute-start.19 = (bf16[256,256]{0,1:T(8,128)(2,1)S(1)}, bf16[256,256]{0,1:T(8,128)(2,1)S(1)}, u32[]{:S(2)}, u32[]{:S(2)}) collective-permute-start(bf16[256,256]{0,1:T(8,128)(2,1)S(1)} %bitcast.200), channel_id=1, source_target_pairs={{0,8},{8,16},{16,24},{24,32},{32,40},{40,48},{48,56},{56,64},{64,7... | collective-permute-start | bytes 393224 | tf_op jit(solution)/shard_map/ppermute | solution.py:18
  114.5 15.2 %collective-permute-start.15 = (bf16[256,256]{0,1:T(8,128)(2,1)S(1)}, bf16[256,256]{0,1:T(8,128)(2,1)S(1)}, u32[]{:S(2)}, u32[]{:S(2)}) collective-permute-start(bf16[256,256]{0,1:T(8,128)(2,1)S(1)} %bitcast.201), channel_id=1, source_target_pairs={{0,40},{8,48},{16,56},{24,64},{32,72},{40,80},{48,88},{56,96},{64,... | collective-permute-start | bytes 393224 | tf_op jit(solution)/shard_map/ppermute | solution.py:18
  116.5 16.3 %collective-permute-start.30 = (bf16[256,256]{0,1:T(8,128)(2,1)S(1)}, bf16[256,256]{0,1:T(8,128)(2,1)S(1)}, u32[]{:S(2)}, u32[]{:S(2)}) collective-permute-start(bf16[256,256]{0,1:T(8,128)(2,1)S(1)} %collective-permute-done.29), channel_id=1, source_target_pairs={{0,8},{8,16},{16,24},{24,32},{32,40},{40,48},{48,56},{56,64},{64,7... | collective-permute-start | bytes 393224 | tf_op jit(solution)/shard_map/ppermute | solution.py:18
  121.2 24.3 %collective-permute-start.20 = (bf16[256,256]{0,1:T(8,128)(2,1)S(1)}, bf16[256,256]{0,1:T(8,128)(2,1)S(1)}, u32[]{:S(2)}, u32[]{:S(2)}) collective-permute-start(bf16[256,256]{0,1:T(8,128)(2,1)S(1)} %collective-permute-done.19), channel_id=1, source_target_pairs={{0,8},{8,16},{16,24},{24,32},{32,40},{40,48},{48,56},{56,64},{64,7... | collective-permute-start | bytes 393224 | tf_op jit(solution)/shard_map/ppermute | solution.py:18
  129.7 13.1 %collective-permute-start.16 = (bf16[256,256]{0,1:T(8,128)(2,1)S(1)}, bf16[256,256]{0,1:T(8,128)(2,1)S(1)}, u32[]{:S(2)}, u32[]{:S(2)}) collective-permute-start(bf16[256,256]{0,1:T(8,128)(2,1)S(1)} %collective-permute-done.15), channel_id=1, source_target_pairs={{0,8},{8,16},{16,24},{24,32},{32,40},{40,48},{48,56},{56,64},{64,7... | collective-permute-start | bytes 393224 | tf_op jit(solution)/shard_map/ppermute | solution.py:18
  142.7 8.2 %collective-permute-start.17 = (bf16[256,256]{0,1:T(8,128)(2,1)S(1)}, bf16[256,256]{0,1:T(8,128)(2,1)S(1)}, u32[]{:S(2)}, u32[]{:S(2)}) collective-permute-start(bf16[256,256]{0,1:T(8,128)(2,1)S(1)} %collective-permute-done.16), channel_id=1, source_target_pairs={{0,8},{8,16},{16,24},{24,32},{32,40},{40,48},{48,56},{56,64},{64,7... | collective-permute-start | bytes 393224 | tf_op jit(solution)/shard_map/ppermute | solution.py:18
  145.5 9.7 %collective-permute-start.21 = (bf16[256,256]{0,1:T(8,128)(2,1)S(1)}, bf16[256,256]{0,1:T(8,128)(2,1)S(1)}, u32[]{:S(2)}, u32[]{:S(2)}) collective-permute-start(bf16[256,256]{0,1:T(8,128)(2,1)S(1)} %collective-permute-done.20), channel_id=1, source_target_pairs={{0,8},{8,16},{16,24},{24,32},{32,40},{40,48},{48,56},{56,64},{64,7... | collective-permute-start | bytes 393224 | tf_op jit(solution)/shard_map/ppermute | solution.py:18
  150.9 9.4 %collective-permute-start.18 = (bf16[256,256]{0,1:T(8,128)(2,1)S(1)}, bf16[256,256]{0,1:T(8,128)(2,1)S(1)}, u32[]{:S(2)}, u32[]{:S(2)}) collective-permute-start(bf16[256,256]{0,1:T(8,128)(2,1)S(1)} %collective-permute-done.17), channel_id=1, source_target_pairs={{0,8},{8,16},{16,24},{24,32},{32,40},{40,48},{48,56},{56,64},{64,7... | collective-permute-start | bytes 393224 | tf_op jit(solution)/shard_map/ppermute | solution.py:18
  155.2 7.9 %collective-permute-start.22 = (bf16[256,256]{0,1:T(8,128)(2,1)S(1)}, bf16[256,256]{0,1:T(8,128)(2,1)S(1)}, u32[]{:S(2)}, u32[]{:S(2)}) collective-permute-start(bf16[256,256]{0,1:T(8,128)(2,1)S(1)} %collective-permute-done.21), channel_id=1, source_target_pairs={{0,8},{8,16},{16,24},{24,32},{32,40},{40,48},{48,56},{56,64},{64,7... | collective-permute-start | bytes 393224 | tf_op jit(solution)/shard_map/ppermute | solution.py:18
  163.2 23.5 %copy-start.3 = (f32[256]{0:T(256)S(1)}, f32[256]{0:T(256)}, u32[]{:S(2)}) copy-start(f32[256]{0:T(256)} %param.17) | copy-start | bytes 3076

commit v17 on v15

--- a/solution.py
+++ b/solution.py
@@ -172,7 +172,18 @@
                 pieces.append(piece)
         return jnp.concatenate(pieces[::-1] + [own], axis=0)
 
-    rows_all = (window_rows(k_attn, 1), window_rows(delta_out, 3))
+    def bypass_rows(own):
+        through = [i for i in range(seq_size) if i % group != group - 1]
+        skipping = [i for i in range(seq_size) if i % group == group - 2]
+        starts = rank == 0
+        pieces = [own, shifted(own, "seq", 1)]
+        for step in range(2, shard_reach + 1):
+            near = moved(pieces[step - 1], 1, through)
+            far = moved(pieces[step - 2], 2, skipping)
+            pieces.append(jnp.where(starts, far, near))
+        return jnp.concatenate(pieces[:0:-1] + [own], axis=0)
+
+    rows_all = (bypass_rows(k_attn), window_rows(delta_out, 2))
     block_rows = min(512, tok_rows)
     first_row = lax.axis_index("seq") * tok_rows
     score_scale = 1.0 / math.sqrt(head_size)

time: 197 us -> 193 us (0.980)
  starting transfers between devices: 70.1 us -> 87.5 us
  waiting for transfers between devices: 66.4 us -> 54.5 us
  blocking collectives: 23.8 us -> 16.7 us
  local copies, waits for them, and re-layouts: 6.55 us -> 4.03 us
    ppermute x15 -> x29, starting transfers between devices: 21 us -> 59.2 us  [moved(): return lax.ppermute(value, 'seq', pairs)]
    ppermute x16 -> x9, waiting for transfers between devices: 66.4 us -> 30.9 us  [shifted(): return lax.ppermute(value, axis, pairs)]
    ppermute x15 -> x29, waiting for transfers between devices: 0.04 us -> 23.6 us  [moved(): return lax.ppermute(value, 'seq', pairs)]
    ppermute x16 -> x9, starting transfers between devices: 49.1 us -> 28.2 us  [shifted(): return lax.ppermute(value, axis, pairs)]
    psum x1, blocking collectives: 23.8 us -> 16.7 us  [on_device(): total_sq = lax.psum(squares, 'head')]
    unnamed x40 -> x33, local copies, waits for them, and re-layouts: 5.1 us -> 3.27 us
  transfers between devices with their start and end apart: 31 -> 38, of which waited for: 11 -> 11; matrix products, arithmetic and copies ran while one was open for 15% -> 14% of each run, Pallas kernels for 0% -> 0%
where the time goes in v17:
time: 193 us; the launch traced here: 191 us
  starting transfers between devices  87.5 us (45%)
  waiting for transfers between devices  54.5 us (28%)
  matrix products  21.2 us (11%)
  blocking collectives  16.7 us (9%)
  other arithmetic  4.8 us (2%)
  local copies, waits for them, and re-layouts  4.03 us (2%)
    ppermute x29, starting transfers between devices, moved(): return lax.ppermute(value, 'seq', pairs)  59.2 us
    ppermute x9, waiting for transfers between devices, shifted(): return lax.ppermute(value, axis, pairs)  30.9 us
    ppermute x9, starting transfers between devices, shifted(): return lax.ppermute(value, axis, pairs)  28.2 us
    ppermute x29, waiting for transfers between devices, moved(): return lax.ppermute(value, 'seq', pairs)  23.6 us
    psum x1, blocking collectives, on_device(): total_sq = lax.psum(squares, 'head')  16.7 us
    dot_general x16, matrix products, batched_dot(): return jnp.einsum('hij,hjk->hik', left, right, precision=highest)  4.32 us
  transfers between devices with their start and end apart: 38, of which 11 were waited for; matrix products, arithmetic and copies ran while one was open for 14% of the time, Pallas kernels for 0%

profile of v17, /device:TPU:25, one launch (start us, length us, event | category | flops | bytes accessed | tf_op | source)
XLA Modules:
  0.0 191.0 jit_solution(9710460062720111501)
XLA Ops:
  0.7 1.0 copy.58
  1.7 3.5 %collective-permute-start.24 = (bf16[256,256]{0,1:T(8,128)(2,1)S(1)}, bf16[256,256]{0,1:T(8,128)(2,1)S(1)}, u32[]{:S(2)}, u32[]{:S(2)}) collective-permute-start(bf16[256,256]{0,1:T(8,128)(2,1)S(1)} %copy.58), channel_id=1, source_target_pairs={{0,8},{8,16},{16,24},{24,32},{32,40},{40,48},{48,56},{56,64},{64,7... | collective-permute-start | bytes 393224 | tf_op jit(solution)/shard_map/ppermute | solution.py:18
  5.3 1.3 collective-permute-start.23
  6.6 1.0 copy.42
  13.7 5.7 %while.30 = (s32[]{:T(128)}, f32[2,128,128]{2,1,0:T(8,128)S(1)}, f32[2,128,128]{2,1,0:T(8,128)S(1)}, f32[4,2,64,128]{3,2,1,0:T(8,128)S(1)}, f32[4,2,64,128]{3,2,...) while((s32[]{:T(128)}, f32[2,128,128]{2,1,0:T(8,128)S(1)}, ...), condition=%wide.region_2.3_spmd.clone, body=%wide.region_1.0_spmd.clone.sunk | while | flops 151126016 | bytes 1837151 | solution.py:74
  19.4 2.9 %collective-permute-start = (f32[2,128,128]{2,1,0:T(8,128)S(1)}, f32[2,128,128]{2,1,0:T(8,128)S(1)}, u32[]{:S(2)}, u32[]{:S(2)}) collective-permute-start(f32[2,128,128]{2,1,0:T(8,128)S(1)} %get-tuple-element.100), channel_id=1, source_target_pairs={{0,8},{8,16},{16,24},{32,40},{40,48},{48,56},{64,72},{72,80},{80,8... | collective-permute-start | bytes 393224 | tf_op jit(solution)/shard_map/ppermute | solution.py:115
  22.3 9.0 %collective-permute-start.5 = (f32[2,128,128]{2,1,0:T(8,128)S(1)}, f32[2,128,128]{2,1,0:T(8,128)S(1)}, u32[]{:S(2)}, u32[]{:S(2)}) collective-permute-start(f32[2,128,128]{2,1,0:T(8,128)S(1)} %get-tuple-element.101), channel_id=1, source_target_pairs={{0,8},{8,16},{16,24},{32,40},{40,48},{48,56},{64,72},{72,80},{80,8... | collective-permute-start | bytes 393224 | tf_op jit(solution)/shard_map/ppermute | solution.py:115
  31.8 1.3 fusion.46
  33.9 1.6 collective-permute-start.1
  35.8 2.9 %collective-permute-start.6 = (f32[2,128,128]{2,1,0:T(8,128)S(1)}, f32[2,128,128]{2,1,0:T(8,128)S(1)}, u32[]{:S(2)}, u32[]{:S(2)}) collective-permute-start(f32[2,128,128]{2,1,0:T(8,128)S(1)} %fusion.56), channel_id=1, source_target_pairs={{0,16},{8,24},{32,48},{40,56},{64,80},{72,88},{96,112},{104,120},{... | collective-permute-start | bytes 393224 | tf_op jit(solution)/shard_map/ppermute | solution.py:115
  38.8 1.9 collective-permute-start.25
  40.6 1.3 collective-permute-start.27
  42.5 2.1 %collective-permute-done.25 = bf16[256,256]{0,1:T(8,128)(2,1)S(1)} collective-permute-done((bf16[256,256]{0,1:T(8,128)(2,1)S(1)}, bf16[256,256]{0,1:T(8,128)(2,1)S(1)}, u32[]{:S(2)}, u32[]{:S(2)}) %collective-permute-start.25) | collective-permute-done | bytes 131104 | tf_op jit(solution)/shard_map/ppermute | solution.py:115
  44.6 6.3 %collective-permute-start.28 = (bf16[256,256]{0,1:T(8,128)(2,1)S(1)}, bf16[256,256]{0,1:T(8,128)(2,1)S(1)}, u32[]{:S(2)}, u32[]{:S(2)}) collective-permute-start(bf16[256,256]{0,1:T(8,128)(2,1)S(1)} %broadcast_select_fusion.5), channel_id=1, source_target_pairs={{0,8},{8,16},{16,24},{32,40},{40,48},{48,56},{64,72},{72,80},{80,8... | collective-permute-start | bytes 393224 | tf_op jit(solution)/shard_map/ppermute | solution.py:115
  51.0 1.3 collective-permute-start.26
  54.8 3.5 %collective-permute-start.29 = (bf16[256,256]{0,1:T(8,128)(2,1)S(1)}, bf16[256,256]{0,1:T(8,128)(2,1)S(1)}, u32[]{:S(2)}, u32[]{:S(2)}) collective-permute-start(bf16[256,256]{0,1:T(8,128)(2,1)S(1)} %broadcast_select_fusion.4), channel_id=1, source_target_pairs={{0,8},{8,16},{16,24},{32,40},{40,48},{48,56},{64,72},{72,80},{80,8... | collective-permute-start | bytes 393224 | tf_op jit(solution)/shard_map/ppermute | solution.py:115
  58.3 1.3 collective-permute-start.31
  61.5 4.1 %collective-permute-done.26 = bf16[256,256]{0,1:T(8,128)(2,1)S(1)} collective-permute-done((bf16[256,256]{0,1:T(8,128)(2,1)S(1)}, bf16[256,256]{0,1:T(8,128)(2,1)S(1)}, u32[]{:S(2)}, u32[]{:S(2)}) %collective-permute-start.26) | collective-permute-done | bytes 131104 | tf_op jit(solution)/shard_map/ppermute | solution.py:115
  65.7 2.8 %collective-permute-start.32 = (bf16[256,256]{0,1:T(8,128)(2,1)S(1)}, bf16[256,256]{0,1:T(8,128)(2,1)S(1)}, u32[]{:S(2)}, u32[]{:S(2)}) collective-permute-start(bf16[256,256]{0,1:T(8,128)(2,1)S(1)} %broadcast_select_fusion.3), channel_id=1, source_target_pairs={{0,8},{8,16},{16,24},{32,40},{40,48},{48,56},{64,72},{72,80},{80,8... | collective-permute-start | bytes 393224 | tf_op jit(solution)/shard_map/ppermute | solution.py:115
  68.5 1.3 collective-permute-start.30
  71.7 4.1 %collective-permute-start.33 = (bf16[256,256]{0,1:T(8,128)(2,1)S(1)}, bf16[256,256]{0,1:T(8,128)(2,1)S(1)}, u32[]{:S(2)}, u32[]{:S(2)}) collective-permute-start(bf16[256,256]{0,1:T(8,128)(2,1)S(1)} %broadcast_select_fusion.2), channel_id=1, source_target_pairs={{0,8},{8,16},{16,24},{32,40},{40,48},{48,56},{64,72},{72,80},{80,8... | collective-permute-start | bytes 393224 | tf_op jit(solution)/shard_map/ppermute | solution.py:115
  75.9 1.5 collective-permute-start.35
  78.6 2.3 %collective-permute-done.30 = bf16[256,256]{0,1:T(8,128)(2,1)S(1)} collective-permute-done((bf16[256,256]{0,1:T(8,128)(2,1)S(1)}, bf16[256,256]{0,1:T(8,128)(2,1)S(1)}, u32[]{:S(2)}, u32[]{:S(2)}) %collective-permute-start.30) | collective-permute-done | bytes 131104 | tf_op jit(solution)/shard_map/ppermute | solution.py:115
  81.0 5.1 %collective-permute-start.36 = (bf16[256,256]{0,1:T(8,128)(2,1)S(1)}, bf16[256,256]{0,1:T(8,128)(2,1)S(1)}, u32[]{:S(2)}, u32[]{:S(2)}) collective-permute-start(bf16[256,256]{0,1:T(8,128)(2,1)S(1)} %broadcast_select_fusion.1), channel_id=1, source_target_pairs={{0,8},{8,16},{16,24},{32,40},{40,48},{48,56},{64,72},{72,80},{80,8... | collective-permute-start | bytes 393224 | tf_op jit(solution)/shard_map/ppermute | solution.py:115
  86.0 1.3 collective-permute-start.34
  87.6 1.3 collective-permute-start.11
  89.6 6.4 %collective-permute-done.35 = bf16[256,256]{0,1:T(8,128)(2,1)S(1)} collective-permute-done((bf16[256,256]{0,1:T(8,128)(2,1)S(1)}, bf16[256,256]{0,1:T(8,128)(2,1)S(1)}, u32[]{:S(2)}, u32[]{:S(2)}) %collective-permute-start.35) | collective-permute-done | bytes 131104 | tf_op jit(solution)/shard_map/ppermute | solution.py:115
  97.4 8.6 %collective-permute-done.11 = f32[2,128,128]{2,1,0:T(8,128)S(1)} collective-permute-done((f32[2,128,128]{2,1,0:T(8,128)S(1)}, f32[2,128,128]{2,1,0:T(8,128)S(1)}, u32[]{:S(2)}, u32[]{:S(2)}) %collective-permute-start.11) | collective-permute-done | bytes 131104 | tf_op jit(solution)/shard_map/ppermute | solution.py:115
  106.0 1.9 %collective-permute-start.37 = (bf16[256,256]{0,1:T(8,128)(2,1)S(1)}, bf16[256,256]{0,1:T(8,128)(2,1)}, u32[]{:S(2)}, u32[]{:S(2)}) collective-permute-start(bf16[256,256]{0,1:T(8,128)(2,1)S(1)} %broadcast_select_fusion), channel_id=1, source_target_pairs={{0,8},{8,16},{16,24},{32,40},{40,48},{48,56},{64,72},{72,80},{80,8... | collective-permute-start | bytes 393224 | tf_op jit(solution)/shard_map/ppermute | solution.py:115
  108.2 4.5 %while.29 = (s32[]{:T(128)}, f32[2,128,128]{2,1,0:T(8,128)S(1)}, bf16[4,2,64,128]{3,2,0,1:T(8,128)(2,1)S(1)}, f32[4,2,64,128]{3,2,1,0:T(8,128)S(1)}, f32[4,2,64,...) while((s32[]{:T(128)}, f32[2,128,128]{2,1,0:T(8,128)S(1)}, ...), condition=%wide.region_5.6_spmd, body=%wide.region_4.5_spmd.sunk | while | flops 88145920 | bytes 1247333 | solution.py:88
  112.8 7.1 %collective-permute-start.15 = (bf16[256,256]{0,1:T(8,128)(2,1)S(1)}, bf16[256,256]{0,1:T(8,128)(2,1)S(1)}, u32[]{:S(2)}, u32[]{:S(2)}) collective-permute-start(bf16[256,256]{0,1:T(8,128)(2,1)S(1)} %bitcast.200), channel_id=1, source_target_pairs={{0,40},{8,48},{16,56},{24,64},{32,72},{40,80},{48,88},{56,96},{64,... | collective-permute-start | bytes 393224 | tf_op jit(solution)/shard_map/ppermute | solution.py:18
  120.0 6.1 %collective-permute-start.19 = (bf16[256,256]{0,1:T(8,128)(2,1)S(1)}, bf16[256,256]{0,1:T(8,128)(2,1)S(1)}, u32[]{:S(2)}, u32[]{:S(2)}) collective-permute-start(bf16[256,256]{0,1:T(8,128)(2,1)S(1)} %bitcast.201), channel_id=1, source_target_pairs={{0,8},{8,16},{16,24},{24,32},{32,40},{40,48},{48,56},{56,64},{64,7... | collective-permute-start | bytes 393224 | tf_op jit(solution)/shard_map/ppermute | solution.py:18
  126.1 0.8 copy.65
  127.0 16.3 %collective-permute-done.15 = bf16[256,256]{0,1:T(8,128)(2,1)S(1)} collective-permute-done((bf16[256,256]{0,1:T(8,128)(2,1)S(1)}, bf16[256,256]{0,1:T(8,128)(2,1)S(1)}, u32[]{:S(2)}, u32[]{:S(2)}) %collective-permute-start.15) | collective-permute-done | bytes 131104 | tf_op jit(solution)/shard_map/ppermute | solution.py:18
  143.3 1.9 collective-permute-start.16
  145.3 1.9 %collective-permute-start.20 = (bf16[256,256]{0,1:T(8,128)(2,1)S(1)}, bf16[256,256]{0,1:T(8,128)(2,1)S(1)}, u32[]{:S(2)}, u32[]{:S(2)}) collective-permute-start(bf16[256,256]{0,1:T(8,128)(2,1)S(1)} %collective-permute-done.19), channel_id=1, source_target_pairs={{0,8},{8,16},{16,24},{24,32},{32,40},{40,48},{48,56},{56,64},{64,7... | collective-permute-start | bytes 393224 | tf_op jit(solution)/shard_map/ppermute | solution.py:18
  147.2 4.6 %collective-permute-done.16 = bf16[256,256]{0,1:T(8,128)(2,1)S(1)} collective-permute-done((bf16[256,256]{0,1:T(8,128)(2,1)S(1)}, bf16[256,256]{0,1:T(8,128)(2,1)S(1)}, u32[]{:S(2)}, u32[]{:S(2)}) %collective-permute-start.16) | collective-permute-done | bytes 131104 | tf_op jit(solution)/shard_map/ppermute | solution.py:18
  151.8 1.9 collective-permute-start.17
  153.7 0.8 fusion.39
  154.5 1.9 %collective-permute-start.21 = (bf16[256,256]{0,1:T(8,128)(2,1)S(1)}, bf16[256,256]{0,1:T(8,128)(2,1)S(1)}, u32[]{:S(2)}, u32[]{:S(2)}) collective-permute-start(bf16[256,256]{0,1:T(8,128)(2,1)S(1)} %collective-permute-done.20), channel_id=1, source_target_pairs={{0,8},{8,16},{16,24},{24,32},{32,40},{40,48},{48,56},{56,64},{64,7... | collective-permute-start | bytes 393224 | tf_op jit(solution)/shard_map/ppermute | solution.py:18
  156.5 3.1 %collective-permute-done.17 = bf16[256,256]{0,1:T(8,128)(2,1)S(1)} collective-permute-done((bf16[256,256]{0,1:T(8,128)(2,1)S(1)}, bf16[256,256]{0,1:T(8,128)(2,1)S(1)}, u32[]{:S(2)}, u32[]{:S(2)}) %collective-permute-start.17) | collective-permute-done | bytes 131104 | tf_op jit(solution)/shard_map/ppermute | solution.py:18
  159.6 1.9 collective-permute-start.18
  161.5 2.4 %fusion.91 = (f32[2,256]{1,0:T(2,128)S(1)}, f32[2,256,2304]{1,2,0:T(8,128)S(1)}) fusion(f32[2,256,2304]{1,2,0:T(8,128)S(1)} %fusion.39, pred[256,2304]{0,1:T(8,128)(4,1)S(1)} %fusion.46), kind=kOutput, calls=%fused_computation.156 | output fusion | flops 4720895 | bytes 10029056 | tf_op jit(solution)/shard_map/while/body/eval_jaxpr/sub | solution.py:207
  164.1 1.9 collective-permute-start.22
  166.0 2.1 %collective-permute-done.18 = bf16[256,256]{0,1:T(8,128)(2,1)S(1)} collective-permute-done((bf16[256,256]{0,1:T(8,128)(2,1)S(1)}, bf16[256,256]{0,1:T(8,128)(2,1)S(1)}, u32[]{:S(2)}, u32[]{:S(2)}) %collective-permute-start.18) | collective-permute-done | bytes 131104 | tf_op jit(solution)/shard_map/ppermute | solution.py:18
  168.1 4.6 %collective-permute-done.22 = bf16[256,256]{0,1:T(8,128)(2,1)S(1)} collective-permute-done((bf16[256,256]{0,1:T(8,128)(2,1)S(1)}, bf16[256,256]{0,1:T(8,128)(2,1)S(1)}, u32[]{:S(2)}, u32[]{:S(2)}) %collective-permute-start.22) | collective-permute-done | bytes 131104 | tf_op jit(solution)/shard_map/ppermute | solution.py:18
  173.5 16.7 %psum.7 = f32[256]{0:T(256)S(1)} all-reduce(f32[256]{0:T(256)S(1)} %get-tuple-element.200), channel_id=1, replica_groups=mesh['seq'=64,'head'=8] {'head'}, use_global_device_ids=true, to_apply=%region_9.10 | all-reduce | flops 256 | bytes 2048 | tf_op jit(solution)/shard_map/psum | solution.py:217
  190.2 0.8 multiply_convert_fusion
  (171 shorter events, 28.9 us)
Async XLA Ops:
  0.6 153.1 %copy-start = (bf16[256,256]{1,0:T(8,128)(2,1)S(1)}, bf16[256,256]{1,0:T(8,128)(2,1)}, u32[]{:S(2)}) copy-start(bf16[256,256]{1,0:T(8,128)(2,1)} %param.15) | copy-start | bytes 393220
  0.6 7.2 %copy-start.3 = (f32[256,2]{0,1:T(2,128)S(1)}, f32[256,2]{0,1:T(2,128)}, u32[]{:S(2)}) copy-start(f32[256,2]{0,1:T(2,128)} %param.14) | copy-start | bytes 6148
  1.7 37.1 %collective-permute-start.24 = (bf16[256,256]{0,1:T(8,128)(2,1)S(1)}, bf16[256,256]{0,1:T(8,128)(2,1)S(1)}, u32[]{:S(2)}, u32[]{:S(2)}) collective-permute-start(bf16[256,256]{0,1:T(8,128)(2,1)S(1)} %copy.58), channel_id=1, source_target_pairs={{0,8},{8,16},{16,24},{24,32},{32,40},{40,48},{48,56},{56,64},{64,7... | collective-permute-start | bytes 393224 | tf_op jit(solution)/shard_map/ppermute | solution.py:18
  5.3 37.2 %collective-permute-start.23 = (bf16[256,256]{0,1:T(8,128)(2,1)S(1)}, bf16[256,256]{0,1:T(8,128)(2,1)S(1)}, u32[]{:S(2)}, u32[]{:S(2)}) collective-permute-start(bf16[256,256]{0,1:T(8,128)(2,1)S(1)} %copy.58), channel_id=1, source_target_pairs={{16,32},{48,64},{80,96},{112,128},{144,160},{176,192},{208,224},{2... | collective-permute-start | bytes 393224 | tf_op jit(solution)/shard_map/ppermute | solution.py:115
  12.0 0.9 copy-start.1
  13.7 17.7 %copy-start.2 = (bf16[256,256]{1,0:T(8,128)(2,1)S(1)}, bf16[256,256]{1,0:T(8,128)(2,1)}, u32[]{:S(2)}) copy-start(bf16[256,256]{1,0:T(8,128)(2,1)} %param.11) | copy-start | bytes 393220
  19.4 14.2 %collective-permute-start = (f32[2,128,128]{2,1,0:T(8,128)S(1)}, f32[2,128,128]{2,1,0:T(8,128)S(1)}, u32[]{:S(2)}, u32[]{:S(2)}) collective-permute-start(f32[2,128,128]{2,1,0:T(8,128)S(1)} %get-tuple-element.100), channel_id=1, source_target_pairs={{0,8},{8,16},{16,24},{32,40},{40,48},{48,56},{64,72},{72,80},{80,8... | collective-permute-start | bytes 393224 | tf_op jit(solution)/shard_map/ppermute | solution.py:115
  22.3 13.2 %collective-permute-start.5 = (f32[2,128,128]{2,1,0:T(8,128)S(1)}, f32[2,128,128]{2,1,0:T(8,128)S(1)}, u32[]{:S(2)}, u32[]{:S(2)}) collective-permute-start(f32[2,128,128]{2,1,0:T(8,128)S(1)} %get-tuple-element.101), channel_id=1, source_target_pairs={{0,8},{8,16},{16,24},{32,40},{40,48},{48,56},{64,72},{72,80},{80,8... | collective-permute-start | bytes 393224 | tf_op jit(solution)/shard_map/ppermute | solution.py:115
  33.9 18.4 %collective-permute-start.1 = (f32[2,128,128]{2,1,0:T(8,128)S(1)}, f32[2,128,128]{2,1,0:T(8,128)S(1)}, u32[]{:S(2)}, u32[]{:S(2)}) collective-permute-start(f32[2,128,128]{2,1,0:T(8,128)S(1)} %convolution_select_fusion.6), channel_id=1, source_target_pairs={{0,16},{8,24},{32,48},{40,56},{64,80},{72,88},{96,112},{104,120},{... | collective-permute-start | bytes 393224 | tf_op jit(solution)/shard_map/ppermute | solution.py:115
  35.8 17.4 %collective-permute-start.6 = (f32[2,128,128]{2,1,0:T(8,128)S(1)}, f32[2,128,128]{2,1,0:T(8,128)S(1)}, u32[]{:S(2)}, u32[]{:S(2)}) collective-permute-start(f32[2,128,128]{2,1,0:T(8,128)S(1)} %fusion.56), channel_id=1, source_target_pairs={{0,16},{8,24},{32,48},{40,56},{64,80},{72,88},{96,112},{104,120},{... | collective-permute-start | bytes 393224 | tf_op jit(solution)/shard_map/ppermute | solution.py:115
  38.8 5.8 %collective-permute-start.25 = (bf16[256,256]{0,1:T(8,128)(2,1)S(1)}, bf16[256,256]{0,1:T(8,128)(2,1)S(1)}, u32[]{:S(2)}, u32[]{:S(2)}) collective-permute-start(bf16[256,256]{0,1:T(8,128)(2,1)S(1)} %collective-permute-done.24), channel_id=1, source_target_pairs={{0,8},{8,16},{16,24},{32,40},{40,48},{48,56},{64,72},{72,80},{80,8... | collective-permute-start | bytes 393224 | tf_op jit(solution)/shard_map/ppermute | solution.py:115
  40.6 14.1 %collective-permute-start.27 = (bf16[256,256]{0,1:T(8,128)(2,1)S(1)}, bf16[256,256]{0,1:T(8,128)(2,1)S(1)}, u32[]{:S(2)}, u32[]{:S(2)}) collective-permute-start(bf16[256,256]{0,1:T(8,128)(2,1)S(1)} %collective-permute-done.24), channel_id=1, source_target_pairs={{16,32},{48,64},{80,96},{112,128},{144,160},{176,192},{208,224},{2... | collective-permute-start | bytes 393224 | tf_op jit(solution)/shard_map/ppermute | solution.py:115
  44.6 10.1 %collective-permute-start.28 = (bf16[256,256]{0,1:T(8,128)(2,1)S(1)}, bf16[256,256]{0,1:T(8,128)(2,1)S(1)}, u32[]{:S(2)}, u32[]{:S(2)}) collective-permute-start(bf16[256,256]{0,1:T(8,128)(2,1)S(1)} %broadcast_select_fusion.5), channel_id=1, source_target_pairs={{0,8},{8,16},{16,24},{32,40},{40,48},{48,56},{64,72},{72,80},{80,8... | collective-permute-start | bytes 393224 | tf_op jit(solution)/shard_map/ppermute | solution.py:115
  51.0 14.7 %collective-permute-start.26 = (bf16[256,256]{0,1:T(8,128)(2,1)S(1)}, bf16[256,256]{0,1:T(8,128)(2,1)S(1)}, u32[]{:S(2)}, u32[]{:S(2)}) collective-permute-start(bf16[256,256]{0,1:T(8,128)(2,1)S(1)} %broadcast_select_fusion.5), channel_id=1, source_target_pairs={{16,32},{48,64},{80,96},{112,128},{144,160},{176,192},{208,224},{2... | collective-permute-start | bytes 393224 | tf_op jit(solution)/shard_map/ppermute | solution.py:115
  52.5 7.0 %collective-permute-start.2 = (f32[2,128,128]{2,1,0:T(8,128)S(1)}, f32[2,128,128]{2,1,0:T(8,128)S(1)}, u32[]{:S(2)}, u32[]{:S(2)}) collective-permute-start(f32[2,128,128]{2,1,0:T(8,128)S(1)} %convolution_select_fusion.4), channel_id=1, source_target_pairs={{24,56},{56,88},{88,120},{120,152},{152,184},{184,216},{216,248},{... | collective-permute-start | bytes 393224 | tf_op jit(solution)/shard_map/ppermute | solution.py:115
  53.5 7.0 %collective-permute-start.7 = (f32[2,128,128]{2,1,0:T(8,128)S(1)}, f32[2,128,128]{2,1,0:T(8,128)S(1)}, u32[]{:S(2)}, u32[]{:S(2)}) collective-permute-start(f32[2,128,128]{2,1,0:T(8,128)S(1)} %fusion.55), channel_id=1, source_target_pairs={{24,56},{56,88},{88,120},{120,152},{152,184},{184,216},{216,248},{... | collective-permute-start | bytes 393224 | tf_op jit(solution)/shard_map/ppermute | solution.py:115
  54.8 10.9 %collective-permute-start.29 = (bf16[256,256]{0,1:T(8,128)(2,1)S(1)}, bf16[256,256]{0,1:T(8,128)(2,1)S(1)}, u32[]{:S(2)}, u32[]{:S(2)}) collective-permute-start(bf16[256,256]{0,1:T(8,128)(2,1)S(1)} %broadcast_select_fusion.4), channel_id=1, source_target_pairs={{0,8},{8,16},{16,24},{32,40},{40,48},{48,56},{64,72},{72,80},{80,8... | collective-permute-start | bytes 393224 | tf_op jit(solution)/shard_map/ppermute | solution.py:115
  58.3 13.4 %collective-permute-start.31 = (bf16[256,256]{0,1:T(8,128)(2,1)S(1)}, bf16[256,256]{0,1:T(8,128)(2,1)S(1)}, u32[]{:S(2)}, u32[]{:S(2)}) collective-permute-start(bf16[256,256]{0,1:T(8,128)(2,1)S(1)} %broadcast_select_fusion.4), channel_id=1, source_target_pairs={{16,32},{48,64},{80,96},{112,128},{144,160},{176,192},{208,224},{2... | collective-permute-start | bytes 393224 | tf_op jit(solution)/shard_map/ppermute | solution.py:115
  59.9 9.9 %collective-permute-start.3 = (f32[2,128,128]{2,1,0:T(8,128)S(1)}, f32[2,128,128]{2,1,0:T(8,128)S(1)}, u32[]{:S(2)}, u32[]{:S(2)}) collective-permute-start(f32[2,128,128]{2,1,0:T(8,128)S(1)} %convolution_select_fusion.3), channel_id=1, source_target_pairs={{24,88},{56,120},{88,152},{120,184},{152,216},{184,248},{216,280},... | collective-permute-start | bytes 393224 | tf_op jit(solution)/shard_map/ppermute | solution.py:115
  60.8 9.9 %collective-permute-start.8 = (f32[2,128,128]{2,1,0:T(8,128)S(1)}, f32[2,128,128]{2,1,0:T(8,128)S(1)}, u32[]{:S(2)}, u32[]{:S(2)}) collective-permute-start(f32[2,128,128]{2,1,0:T(8,128)S(1)} %fusion.54), channel_id=1, source_target_pairs={{24,88},{56,120},{88,152},{120,184},{152,216},{184,248},{216,280},... | collective-permute-start | bytes 393224 | tf_op jit(solution)/shard_map/ppermute | solution.py:115
  65.7 6.1 %collective-permute-start.32 = (bf16[256,256]{0,1:T(8,128)(2,1)S(1)}, bf16[256,256]{0,1:T(8,128)(2,1)S(1)}, u32[]{:S(2)}, u32[]{:S(2)}) collective-permute-start(bf16[256,256]{0,1:T(8,128)(2,1)S(1)} %broadcast_select_fusion.3), channel_id=1, source_target_pairs={{0,8},{8,16},{16,24},{32,40},{40,48},{48,56},{64,72},{72,80},{80,8... | collective-permute-start | bytes 393224 | tf_op jit(solution)/shard_map/ppermute | solution.py:115
  68.5 12.5 %collective-permute-start.30 = (bf16[256,256]{0,1:T(8,128)(2,1)S(1)}, bf16[256,256]{0,1:T(8,128)(2,1)S(1)}, u32[]{:S(2)}, u32[]{:S(2)}) collective-permute-start(bf16[256,256]{0,1:T(8,128)(2,1)S(1)} %broadcast_select_fusion.3), channel_id=1, source_target_pairs={{16,32},{48,64},{80,96},{112,128},{144,160},{176,192},{208,224},{2... | collective-permute-start | bytes 393224 | tf_op jit(solution)/shard_map/ppermute | solution.py:115
  70.1 8.3 %collective-permute-start.4 = (f32[2,128,128]{2,1,0:T(8,128)S(1)}, f32[2,128,128]{2,1,0:T(8,128)S(1)}, u32[]{:S(2)}, u32[]{:S(2)}) collective-permute-start(f32[2,128,128]{2,1,0:T(8,128)S(1)} %convolution_select_fusion.2), channel_id=1, source_target_pairs={{24,152},{56,184},{88,216},{120,248},{152,280},{184,312},{216,344}... | collective-permute-start | bytes 393224 | tf_op jit(solution)/shard_map/ppermute | solution.py:115
  71.0 6.3 %collective-permute-start.9 = (f32[2,128,128]{2,1,0:T(8,128)S(1)}, f32[2,128,128]{2,1,0:T(8,128)S(1)}, u32[]{:S(2)}, u32[]{:S(2)}) collective-permute-start(f32[2,128,128]{2,1,0:T(8,128)S(1)} %fusion.53), channel_id=1, source_target_pairs={{24,152},{56,184},{88,216},{120,248},{152,280},{184,312},{216,344}... | collective-permute-start | bytes 393224 | tf_op jit(solution)/shard_map/ppermute | solution.py:115
  71.7 9.2 %collective-permute-start.33 = (bf16[256,256]{0,1:T(8,128)(2,1)S(1)}, bf16[256,256]{0,1:T(8,128)(2,1)S(1)}, u32[]{:S(2)}, u32[]{:S(2)}) collective-permute-start(bf16[256,256]{0,1:T(8,128)(2,1)S(1)} %broadcast_select_fusion.2), channel_id=1, source_target_pairs={{0,8},{8,16},{16,24},{32,40},{40,48},{48,56},{64,72},{72,80},{80,8... | collective-permute-start | bytes 393224 | tf_op jit(solution)/shard_map/ppermute | solution.py:115
  75.9 20.2 %collective-permute-start.35 = (bf16[256,256]{0,1:T(8,128)(2,1)S(1)}, bf16[256,256]{0,1:T(8,128)(2,1)S(1)}, u32[]{:S(2)}, u32[]{:S(2)}) collective-permute-start(bf16[256,256]{0,1:T(8,128)(2,1)S(1)} %broadcast_select_fusion.2), channel_id=1, source_target_pairs={{16,32},{48,64},{80,96},{112,128},{144,160},{176,192},{208,224},{2... | collective-permute-start | bytes 393224 | tf_op jit(solution)/shard_map/ppermute | solution.py:115
  77.6 9.7 %collective-permute-start.10 = (f32[2,128,128]{2,1,0:T(8,128)S(1)}, f32[2,128,128]{2,1,0:T(8,128)S(1)}, u32[]{:S(2)}, u32[]{:S(2)}) collective-permute-start(f32[2,128,128]{2,1,0:T(8,128)S(1)} %fusion.52), channel_id=1, source_target_pairs={{24,280},{56,312},{88,344},{120,376},{152,408},{184,440},{216,472}... | collective-permute-start | bytes 393224 | tf_op jit(solution)/shard_map/ppermute | solution.py:115
  81.0 15.7 %collective-permute-start.36 = (bf16[256,256]{0,1:T(8,128)(2,1)S(1)}, bf16[256,256]{0,1:T(8,128)(2,1)S(1)}, u32[]{:S(2)}, u32[]{:S(2)}) collective-permute-start(bf16[256,256]{0,1:T(8,128)(2,1)S(1)} %broadcast_select_fusion.1), channel_id=1, source_target_pairs={{0,8},{8,16},{16,24},{32,40},{40,48},{48,56},{64,72},{72,80},{80,8... | collective-permute-start | bytes 393224 | tf_op jit(solution)/shard_map/ppermute | solution.py:115
  86.0 40.8 %collective-permute-start.34 = (bf16[256,256]{0,1:T(8,128)(2,1)S(1)}, bf16[256,256]{0,1:T(8,128)(2,1)S(1)}, u32[]{:S(2)}, u32[]{:S(2)}) collective-permute-start(bf16[256,256]{0,1:T(8,128)(2,1)S(1)} %broadcast_select_fusion.1), channel_id=1, source_target_pairs={{16,32},{48,64},{80,96},{112,128},{144,160},{176,192},{208,224},{2... | collective-permute-start | bytes 393224 | tf_op jit(solution)/shard_map/ppermute | solution.py:115
  87.6 18.4 %collective-permute-start.11 = (f32[2,128,128]{2,1,0:T(8,128)S(1)}, f32[2,128,128]{2,1,0:T(8,128)S(1)}, u32[]{:S(2)}, u32[]{:S(2)}) collective-permute-start(f32[2,128,128]{2,1,0:T(8,128)S(1)} %fusion.51), channel_id=1, source_target_pairs={{24,32},{56,64},{88,96},{120,128},{152,160},{184,192},{216,224},{2... | collective-permute-start | bytes 393224 | tf_op jit(solution)/shard_map/ppermute | solution.py:115
  88.9 19.0 %collective-permute-start.12 = (f32[2,128,128]{2,1,0:T(8,128)S(1)}, f32[2,128,128]{2,1,0:T(8,128)S(1)}, u32[]{:S(2)}, u32[]{:S(2)}) collective-permute-start(f32[2,128,128]{2,1,0:T(8,128)S(1)} %fusion.51), channel_id=1, source_target_pairs={{24,40},{56,72},{88,104},{120,136},{152,168},{184,200},{216,232},{... | collective-permute-start | bytes 393224 | tf_op jit(solution)/shard_map/ppermute | solution.py:115
  96.0 11.9 %collective-permute-start.13 = (f32[2,128,128]{2,1,0:T(8,128)S(1)}, f32[2,128,128]{2,1,0:T(8,128)S(1)}, u32[]{:S(2)}, u32[]{:S(2)}) collective-permute-start(f32[2,128,128]{2,1,0:T(8,128)S(1)} %fusion.51), channel_id=1, source_target_pairs={{24,48},{56,80},{88,112},{120,144},{152,176},{184,208},{216,240},{... | collective-permute-start | bytes 393224 | tf_op jit(solution)/shard_map/ppermute | solution.py:115
  96.7 11.2 %collective-permute-start.14 = (f32[2,128,128]{2,1,0:T(8,128)S(1)}, f32[2,128,128]{2,1,0:T(8,128)S(1)}, u32[]{:S(2)}, u32[]{:S(2)}) collective-permute-start(f32[2,128,128]{2,1,0:T(8,128)S(1)} %fusion.51), channel_id=1, source_target_pairs={{24,56},{56,88},{88,120},{120,152},{152,184},{184,216},{216,248},{... | collective-permute-start | bytes 393224 | tf_op jit(solution)/shard_map/ppermute | solution.py:115
  106.0 20.9 %collective-permute-start.37 = (bf16[256,256]{0,1:T(8,128)(2,1)S(1)}, bf16[256,256]{0,1:T(8,128)(2,1)}, u32[]{:S(2)}, u32[]{:S(2)}) collective-permute-start(bf16[256,256]{0,1:T(8,128)(2,1)S(1)} %broadcast_select_fusion), channel_id=1, source_target_pairs={{0,8},{8,16},{16,24},{32,40},{40,48},{48,56},{64,72},{72,80},{80,8... | collective-permute-start | bytes 393224 | tf_op jit(solution)/shard_map/ppermute | solution.py:115
  112.8 30.5 %collective-permute-start.15 = (bf16[256,256]{0,1:T(8,128)(2,1)S(1)}, bf16[256,256]{0,1:T(8,128)(2,1)S(1)}, u32[]{:S(2)}, u32[]{:S(2)}) collective-permute-start(bf16[256,256]{0,1:T(8,128)(2,1)S(1)} %bitcast.200), channel_id=1, source_target_pairs={{0,40},{8,48},{16,56},{24,64},{32,72},{40,80},{48,88},{56,96},{64,... | collective-permute-start | bytes 393224 | tf_op jit(solution)/shard_map/ppermute | solution.py:18
  120.0 25.3 %collective-permute-start.19 = (bf16[256,256]{0,1:T(8,128)(2,1)S(1)}, bf16[256,256]{0,1:T(8,128)(2,1)S(1)}, u32[]{:S(2)}, u32[]{:S(2)}) collective-permute-start(bf16[256,256]{0,1:T(8,128)(2,1)S(1)} %bitcast.201), channel_id=1, source_target_pairs={{0,8},{8,16},{16,24},{24,32},{32,40},{40,48},{48,56},{56,64},{64,7... | collective-permute-start | bytes 393224 | tf_op jit(solution)/shard_map/ppermute | solution.py:18
  143.3 8.5 %collective-permute-start.16 = (bf16[256,256]{0,1:T(8,128)(2,1)S(1)}, bf16[256,256]{0,1:T(8,128)(2,1)S(1)}, u32[]{:S(2)}, u32[]{:S(2)}) collective-permute-start(bf16[256,256]{0,1:T(8,128)(2,1)S(1)} %collective-permute-done.15), channel_id=1, source_target_pairs={{0,8},{8,16},{16,24},{24,32},{32,40},{40,48},{48,56},{56,64},{64,7... | collective-permute-start | bytes 393224 | tf_op jit(solution)/shard_map/ppermute | solution.py:18
  145.3 9.3 %collective-permute-start.20 = (bf16[256,256]{0,1:T(8,128)(2,1)S(1)}, bf16[256,256]{0,1:T(8,128)(2,1)S(1)}, u32[]{:S(2)}, u32[]{:S(2)}) collective-permute-start(bf16[256,256]{0,1:T(8,128)(2,1)S(1)} %collective-permute-done.19), channel_id=1, source_target_pairs={{0,8},{8,16},{16,24},{24,32},{32,40},{40,48},{48,56},{56,64},{64,7... | collective-permute-start | bytes 393224 | tf_op jit(solution)/shard_map/ppermute | solution.py:18
  151.8 7.8 %collective-permute-start.17 = (bf16[256,256]{0,1:T(8,128)(2,1)S(1)}, bf16[256,256]{0,1:T(8,128)(2,1)S(1)}, u32[]{:S(2)}, u32[]{:S(2)}) collective-permute-start(bf16[256,256]{0,1:T(8,128)(2,1)S(1)} %collective-permute-done.16), channel_id=1, source_target_pairs={{0,8},{8,16},{16,24},{24,32},{32,40},{40,48},{48,56},{56,64},{64,7... | collective-permute-start | bytes 393224 | tf_op jit(solution)/shard_map/ppermute | solution.py:18
  154.5 9.5 %collective-permute-start.21 = (bf16[256,256]{0,1:T(8,128)(2,1)S(1)}, bf16[256,256]{0,1:T(8,128)(2,1)S(1)}, u32[]{:S(2)}, u32[]{:S(2)}) collective-permute-start(bf16[256,256]{0,1:T(8,128)(2,1)S(1)} %collective-permute-done.20), channel_id=1, source_target_pairs={{0,8},{8,16},{16,24},{24,32},{32,40},{40,48},{48,56},{56,64},{64,7... | collective-permute-start | bytes 393224 | tf_op jit(solution)/shard_map/ppermute | solution.py:18
  159.6 8.5 %collective-permute-start.18 = (bf16[256,256]{0,1:T(8,128)(2,1)S(1)}, bf16[256,256]{0,1:T(8,128)(2,1)S(1)}, u32[]{:S(2)}, u32[]{:S(2)}) collective-permute-start(bf16[256,256]{0,1:T(8,128)(2,1)S(1)} %collective-permute-done.17), channel_id=1, source_target_pairs={{0,8},{8,16},{16,24},{24,32},{32,40},{40,48},{48,56},{56,64},{64,7... | collective-permute-start | bytes 393224 | tf_op jit(solution)/shard_map/ppermute | solution.py:18
  164.1 8.7 %collective-permute-start.22 = (bf16[256,256]{0,1:T(8,128)(2,1)S(1)}, bf16[256,256]{0,1:T(8,128)(2,1)S(1)}, u32[]{:S(2)}, u32[]{:S(2)}) collective-permute-start(bf16[256,256]{0,1:T(8,128)(2,1)S(1)} %collective-permute-done.21), channel_id=1, source_target_pairs={{0,8},{8,16},{16,24},{24,32},{32,40},{40,48},{48,56},{56,64},{64,7... | collective-permute-start | bytes 393224 | tf_op jit(solution)/shard_map/ppermute | solution.py:18
  172.8 17.4 %copy-start.4 = (f32[256]{0:T(256)S(1)}, f32[256]{0:T(256)}, u32[]{:S(2)}) copy-start(f32[256]{0:T(256)} %param.17) | copy-start | bytes 3076

commit v18 on v6

--- a/solution.py
+++ b/solution.py
@@ -203,7 +203,7 @@
     starts = jnp.arange(tok_rows // block_rows) * block_rows
     attended = lax.map(attend_block, starts).reshape(tok_rows, features)
     squares = jnp.sum(attended * attended, axis=1)
-    total_sq = lax.psum(squares, "head")
+    total_sq = jnp.sum(lax.all_gather(squares, "head"), axis=0)
     scale_rows = lax.rsqrt(total_sq / (features * lax.axis_size("head")) + 1e-06)
     normed_out = (attended * out_gain[None, :] * scale_rows[:, None]).astype(jnp.bfloat16)
     return (delta_out, normed_out)

time: 190 us -> 189 us (level)
    psum x1 -> x0, blocking collectives: 22.8 us -> none  [on_device(): total_sq = lax.psum(squares, 'head')]
    all_gather x0 -> x1, blocking collectives: none -> 21.4 us  [on_device(): total_sq = jnp.sum(lax.all_gather(squares, 'head'), axis=0)]
where the time goes in v18:
time: 189 us; the launch traced here: 187 us
  waiting for transfers between devices  69.4 us (37%)
  starting transfers between devices  63 us (33%)
  blocking collectives  21.4 us (11%)
  matrix products  21.2 us (11%)
  local copies, waits for them, and re-layouts  4.72 us (2%)
  other arithmetic  4.68 us (2%)
    ppermute x16, waiting for transfers between devices, shifted(): return lax.ppermute(value, axis, pairs)  58.4 us
    ppermute x16, starting transfers between devices, shifted(): return lax.ppermute(value, axis, pairs)  40.9 us
    ppermute x15, starting transfers between devices, moved(): return lax.ppermute(value, 'seq', pairs)  22.1 us
    all_gather x1, blocking collectives, on_device(): total_sq = jnp.sum(lax.all_gather(squares, 'head'), axis=0)  21.4 us
    ppermute x15, waiting for transfers between devices, moved(): return lax.ppermute(value, 'seq', pairs)  11.1 us
    dot_general x16, matrix products, batched_dot(): return jnp.einsum('hij,hjk->hik', left, right, precision=highest)  4.34 us
  transfers between devices with their start and end apart: 31, of which 12 were waited for; matrix products, arithmetic and copies ran while one was open for 15% of the time, Pallas kernels for 0%

profile of v18, /device:TPU:25, one launch (start us, length us, event | category | flops | bytes accessed | tf_op | source)
XLA Modules:
  0.0 186.5 jit_solution(11751023013375021027)
XLA Ops:
  0.7 1.1 copy.80
  1.7 3.5 %collective-permute-start.23 = (bf16[256,256]{0,1:T(8,128)(2,1)S(1)}, bf16[256,256]{0,1:T(8,128)(2,1)S(1)}, u32[]{:S(2)}, u32[]{:S(2)}) collective-permute-start(bf16[256,256]{0,1:T(8,128)(2,1)S(1)} %copy.80), channel_id=1, source_target_pairs={{0,8},{8,16},{16,24},{24,32},{32,40},{40,48},{48,56},{56,64},{64,7... | collective-permute-start | bytes 393224 | tf_op jit(solution)/shard_map/ppermute | solution.py:18
  5.3 0.8 mul.79
  6.1 1.0 copy.64
  13.1 5.7 %while.30 = (s32[]{:T(128)}, f32[2,128,128]{2,1,0:T(8,128)S(1)}, f32[2,128,128]{2,1,0:T(8,128)S(1)}, f32[4,2,64,128]{3,2,1,0:T(8,128)S(1)}, f32[4,2,64,128]{3,2,...) while((s32[]{:T(128)}, f32[2,128,128]{2,1,0:T(8,128)S(1)}, ...), condition=%wide.region_2.3_spmd.clone, body=%wide.region_1.0_spmd.clone.sunk | while | flops 151126016 | bytes 1837159 | solution.py:74
  18.8 3.6 %collective-permute-start.5 = (f32[2,128,128]{2,1,0:T(8,128)S(1)}, f32[2,128,128]{2,1,0:T(8,128)S(1)}, u32[]{:S(2)}, u32[]{:S(2)}) collective-permute-start(f32[2,128,128]{2,1,0:T(8,128)S(1)} %get-tuple-element.101), channel_id=1, source_target_pairs={{0,8},{8,16},{16,24},{32,40},{40,48},{48,56},{64,72},{72,80},{80,8... | collective-permute-start | bytes 393224 | tf_op jit(solution)/shard_map/ppermute | solution.py:115
  22.3 3.5 %collective-permute-start = (f32[2,128,128]{2,1,0:T(8,128)S(1)}, f32[2,128,128]{2,1,0:T(8,128)S(1)}, u32[]{:S(2)}, u32[]{:S(2)}) collective-permute-start(f32[2,128,128]{2,1,0:T(8,128)S(1)} %get-tuple-element.100), channel_id=1, source_target_pairs={{0,8},{8,16},{16,24},{32,40},{40,48},{48,56},{64,72},{72,80},{80,8... | collective-permute-start | bytes 393224 | tf_op jit(solution)/shard_map/ppermute | solution.py:115
  27.2 4.5 %collective-permute-start.6 = (f32[2,128,128]{2,1,0:T(8,128)S(1)}, f32[2,128,128]{2,1,0:T(8,128)S(1)}, u32[]{:S(2)}, u32[]{:S(2)}) collective-permute-start(f32[2,128,128]{2,1,0:T(8,128)S(1)} %fusion.56), channel_id=1, source_target_pairs={{0,16},{8,24},{32,48},{40,56},{64,80},{72,88},{96,112},{104,120},{... | collective-permute-start | bytes 393224 | tf_op jit(solution)/shard_map/ppermute | solution.py:115
  31.9 2.5 %collective-permute-start.1 = (f32[2,128,128]{2,1,0:T(8,128)S(1)}, f32[2,128,128]{2,1,0:T(8,128)S(1)}, u32[]{:S(2)}, u32[]{:S(2)}) collective-permute-start(f32[2,128,128]{2,1,0:T(8,128)S(1)} %convolution_select_fusion.6), channel_id=1, source_target_pairs={{0,16},{8,24},{32,48},{40,56},{64,80},{72,88},{96,112},{104,120},{... | collective-permute-start | bytes 393224 | tf_op jit(solution)/shard_map/ppermute | solution.py:115
  34.7 3.5 %collective-permute-start.24 = (bf16[256,256]{0,1:T(8,128)(2,1)S(1)}, bf16[256,256]{0,1:T(8,128)(2,1)S(1)}, u32[]{:S(2)}, u32[]{:S(2)}) collective-permute-start(bf16[256,256]{0,1:T(8,128)(2,1)S(1)} %collective-permute-done.23), channel_id=1, source_target_pairs={{0,8},{8,16},{16,24},{24,32},{32,40},{40,48},{48,56},{56,64},{64,7... | collective-permute-start | bytes 393224 | tf_op jit(solution)/shard_map/ppermute | solution.py:18
  38.9 0.7 collective-permute-start.7
  40.5 2.1 %collective-permute-done.24 = bf16[256,256]{0,1:T(8,128)(2,1)S(1)} collective-permute-done((bf16[256,256]{0,1:T(8,128)(2,1)S(1)}, bf16[256,256]{0,1:T(8,128)(2,1)S(1)}, u32[]{:S(2)}, u32[]{:S(2)}) %collective-permute-start.24) | collective-permute-done | bytes 131104 | tf_op jit(solution)/shard_map/ppermute | solution.py:18
  42.6 5.2 %collective-permute-start.25 = (bf16[256,256]{0,1:T(8,128)(2,1)S(1)}, bf16[256,256]{0,1:T(8,128)(2,1)S(1)}, u32[]{:S(2)}, u32[]{:S(2)}) collective-permute-start(bf16[256,256]{0,1:T(8,128)(2,1)S(1)} %collective-permute-done.24), channel_id=1, source_target_pairs={{0,8},{8,16},{16,24},{24,32},{32,40},{40,48},{48,56},{56,64},{64,7... | collective-permute-start | bytes 393224 | tf_op jit(solution)/shard_map/ppermute | solution.py:18
  48.3 0.7 collective-permute-start.8
  49.3 0.7 collective-permute-start.3
  50.0 10.5 %collective-permute-done.25 = bf16[256,256]{0,1:T(8,128)(2,1)S(1)} collective-permute-done((bf16[256,256]{0,1:T(8,128)(2,1)S(1)}, bf16[256,256]{0,1:T(8,128)(2,1)S(1)}, u32[]{:S(2)}, u32[]{:S(2)}) %collective-permute-start.25) | collective-permute-done | bytes 131104 | tf_op jit(solution)/shard_map/ppermute | solution.py:18
  60.4 1.9 %collective-permute-start.26 = (bf16[256,256]{0,1:T(8,128)(2,1)S(1)}, bf16[256,256]{0,1:T(8,128)(2,1)S(1)}, u32[]{:S(2)}, u32[]{:S(2)}) collective-permute-start(bf16[256,256]{0,1:T(8,128)(2,1)S(1)} %collective-permute-done.25), channel_id=1, source_target_pairs={{0,8},{8,16},{16,24},{24,32},{32,40},{40,48},{48,56},{56,64},{64,7... | collective-permute-start | bytes 393224 | tf_op jit(solution)/shard_map/ppermute | solution.py:18
  62.6 0.7 collective-permute-start.9
  64.3 9.0 %collective-permute-done.26 = bf16[256,256]{0,1:T(8,128)(2,1)S(1)} collective-permute-done((bf16[256,256]{0,1:T(8,128)(2,1)S(1)}, bf16[256,256]{0,1:T(8,128)(2,1)S(1)}, u32[]{:S(2)}, u32[]{:S(2)}) %collective-permute-start.26) | collective-permute-done | bytes 131104 | tf_op jit(solution)/shard_map/ppermute | solution.py:18
  73.2 1.9 %collective-permute-start.27 = (bf16[256,256]{0,1:T(8,128)(2,1)S(1)}, bf16[256,256]{0,1:T(8,128)(2,1)S(1)}, u32[]{:S(2)}, u32[]{:S(2)}) collective-permute-start(bf16[256,256]{0,1:T(8,128)(2,1)S(1)} %collective-permute-done.26), channel_id=1, source_target_pairs={{0,8},{8,16},{16,24},{24,32},{32,40},{40,48},{48,56},{56,64},{64,7... | collective-permute-start | bytes 393224 | tf_op jit(solution)/shard_map/ppermute | solution.py:18
  76.1 10.9 %collective-permute-done.27 = bf16[256,256]{0,1:T(8,128)(2,1)S(1)} collective-permute-done((bf16[256,256]{0,1:T(8,128)(2,1)S(1)}, bf16[256,256]{0,1:T(8,128)(2,1)S(1)}, u32[]{:S(2)}, u32[]{:S(2)}) %collective-permute-start.27) | collective-permute-done | bytes 131104 | tf_op jit(solution)/shard_map/ppermute | solution.py:18
  87.0 1.9 %collective-permute-start.28 = (bf16[256,256]{0,1:T(8,128)(2,1)S(1)}, bf16[256,256]{0,1:T(8,128)(2,1)S(1)}, u32[]{:S(2)}, u32[]{:S(2)}) collective-permute-start(bf16[256,256]{0,1:T(8,128)(2,1)S(1)} %collective-permute-done.27), channel_id=1, source_target_pairs={{0,8},{8,16},{16,24},{24,32},{32,40},{40,48},{48,56},{56,64},{64,7... | collective-permute-start | bytes 393224 | tf_op jit(solution)/shard_map/ppermute | solution.py:18
  91.6 1.3 collective-permute-start.11
  93.1 2.0 %collective-permute-done.28 = bf16[256,256]{0,1:T(8,128)(2,1)S(1)} collective-permute-done((bf16[256,256]{0,1:T(8,128)(2,1)S(1)}, bf16[256,256]{0,1:T(8,128)(2,1)S(1)}, u32[]{:S(2)}, u32[]{:S(2)}) %collective-permute-start.28) | collective-permute-done | bytes 131104 | tf_op jit(solution)/shard_map/ppermute | solution.py:18
  95.1 2.1 %collective-permute-start.29 = (bf16[256,256]{0,1:T(8,128)(2,1)S(1)}, bf16[256,256]{0,1:T(8,128)(2,1)S(1)}, u32[]{:S(2)}, u32[]{:S(2)}) collective-permute-start(bf16[256,256]{0,1:T(8,128)(2,1)S(1)} %collective-permute-done.28), channel_id=1, source_target_pairs={{0,8},{8,16},{16,24},{24,32},{32,40},{40,48},{48,56},{56,64},{64,7... | collective-permute-start | bytes 393224 | tf_op jit(solution)/shard_map/ppermute | solution.py:18
  97.3 11.0 %collective-permute-done.11 = f32[2,128,128]{2,1,0:T(8,128)S(1)} collective-permute-done((f32[2,128,128]{2,1,0:T(8,128)S(1)}, f32[2,128,128]{2,1,0:T(8,128)S(1)}, u32[]{:S(2)}, u32[]{:S(2)}) %collective-permute-start.11) | collective-permute-done | bytes 131104 | tf_op jit(solution)/shard_map/ppermute | solution.py:115
  108.6 4.5 %while.29 = (s32[]{:T(128)}, f32[2,128,128]{2,1,0:T(8,128)S(1)}, bf16[4,2,64,128]{3,2,0,1:T(8,128)(2,1)S(1)}, f32[4,2,64,128]{3,2,1,0:T(8,128)S(1)}, f32[4,2,64,...) while((s32[]{:T(128)}, f32[2,128,128]{2,1,0:T(8,128)S(1)}, ...), condition=%wide.region_5.6_spmd, body=%wide.region_4.5_spmd.sunk | while | flops 88145920 | bytes 1247341 | solution.py:88
  113.2 1.9 %collective-permute-start.19 = (bf16[256,256]{0,1:T(8,128)(2,1)S(1)}, bf16[256,256]{0,1:T(8,128)(2,1)S(1)}, u32[]{:S(2)}, u32[]{:S(2)}) collective-permute-start(bf16[256,256]{0,1:T(8,128)(2,1)S(1)} %bitcast.201), channel_id=1, source_target_pairs={{0,8},{8,16},{16,24},{24,32},{32,40},{40,48},{48,56},{56,64},{64,7... | collective-permute-start | bytes 393224 | tf_op jit(solution)/shard_map/ppermute | solution.py:18
  115.1 1.9 %collective-permute-start.15 = (bf16[256,256]{0,1:T(8,128)(2,1)S(1)}, bf16[256,256]{0,1:T(8,128)(2,1)S(1)}, u32[]{:S(2)}, u32[]{:S(2)}) collective-permute-start(bf16[256,256]{0,1:T(8,128)(2,1)S(1)} %bitcast.202), channel_id=1, source_target_pairs={{0,40},{8,48},{16,56},{24,64},{32,72},{40,80},{48,88},{56,96},{64,... | collective-permute-start | bytes 393224 | tf_op jit(solution)/shard_map/ppermute | solution.py:18
  117.1 2.4 %collective-permute-start.30 = (bf16[256,256]{0,1:T(8,128)(2,1)S(1)}, bf16[256,256]{0,1:T(8,128)(2,1)S(1)}, u32[]{:S(2)}, u32[]{:S(2)}) collective-permute-start(bf16[256,256]{0,1:T(8,128)(2,1)S(1)} %collective-permute-done.29), channel_id=1, source_target_pairs={{0,8},{8,16},{16,24},{24,32},{32,40},{40,48},{48,56},{56,64},{64,7... | collective-permute-start | bytes 393224 | tf_op jit(solution)/shard_map/ppermute | solution.py:18
  119.5 1.3 fusion.46
  120.8 0.8 copy.86
  121.5 5.0 %collective-permute-start.20 = (bf16[256,256]{0,1:T(8,128)(2,1)S(1)}, bf16[256,256]{0,1:T(8,128)(2,1)S(1)}, u32[]{:S(2)}, u32[]{:S(2)}) collective-permute-start(bf16[256,256]{0,1:T(8,128)(2,1)S(1)} %collective-permute-done.19), channel_id=1, source_target_pairs={{0,8},{8,16},{16,24},{24,32},{32,40},{40,48},{48,56},{56,64},{64,7... | collective-permute-start | bytes 393224 | tf_op jit(solution)/shard_map/ppermute | solution.py:18
  126.5 3.9 %collective-permute-done.15 = bf16[256,256]{0,1:T(8,128)(2,1)S(1)} collective-permute-done((bf16[256,256]{0,1:T(8,128)(2,1)S(1)}, bf16[256,256]{0,1:T(8,128)(2,1)S(1)}, u32[]{:S(2)}, u32[]{:S(2)}) %collective-permute-start.15) | collective-permute-done | bytes 131104 | tf_op jit(solution)/shard_map/ppermute | solution.py:18
  130.4 1.9 %collective-permute-start.16 = (bf16[256,256]{0,1:T(8,128)(2,1)S(1)}, bf16[256,256]{0,1:T(8,128)(2,1)S(1)}, u32[]{:S(2)}, u32[]{:S(2)}) collective-permute-start(bf16[256,256]{0,1:T(8,128)(2,1)S(1)} %collective-permute-done.15), channel_id=1, source_target_pairs={{0,8},{8,16},{16,24},{24,32},{32,40},{40,48},{48,56},{56,64},{64,7... | collective-permute-start | bytes 393224 | tf_op jit(solution)/shard_map/ppermute | solution.py:18
  132.3 1.1 collective-permute-done.30
  133.6 9.8 %collective-permute-done.16 = bf16[256,256]{0,1:T(8,128)(2,1)S(1)} collective-permute-done((bf16[256,256]{0,1:T(8,128)(2,1)S(1)}, bf16[256,256]{0,1:T(8,128)(2,1)S(1)}, u32[]{:S(2)}, u32[]{:S(2)}) %collective-permute-start.16) | collective-permute-done | bytes 131104 | tf_op jit(solution)/shard_map/ppermute | solution.py:18
  143.4 1.9 %collective-permute-start.17 = (bf16[256,256]{0,1:T(8,128)(2,1)S(1)}, bf16[256,256]{0,1:T(8,128)(2,1)S(1)}, u32[]{:S(2)}, u32[]{:S(2)}) collective-permute-start(bf16[256,256]{0,1:T(8,128)(2,1)S(1)} %collective-permute-done.16), channel_id=1, source_target_pairs={{0,8},{8,16},{16,24},{24,32},{32,40},{40,48},{48,56},{56,64},{64,7... | collective-permute-start | bytes 393224 | tf_op jit(solution)/shard_map/ppermute | solution.py:18
  145.3 0.8 fusion.39
  146.1 1.9 %collective-permute-start.21 = (bf16[256,256]{0,1:T(8,128)(2,1)S(1)}, bf16[256,256]{0,1:T(8,128)(2,1)S(1)}, u32[]{:S(2)}, u32[]{:S(2)}) collective-permute-start(bf16[256,256]{0,1:T(8,128)(2,1)S(1)} %collective-permute-done.20), channel_id=1, source_target_pairs={{0,8},{8,16},{16,24},{24,32},{32,40},{40,48},{48,56},{56,64},{64,7... | collective-permute-start | bytes 393224 | tf_op jit(solution)/shard_map/ppermute | solution.py:18
  148.0 3.4 %collective-permute-done.17 = bf16[256,256]{0,1:T(8,128)(2,1)S(1)} collective-permute-done((bf16[256,256]{0,1:T(8,128)(2,1)S(1)}, bf16[256,256]{0,1:T(8,128)(2,1)S(1)}, u32[]{:S(2)}, u32[]{:S(2)}) %collective-permute-start.17) | collective-permute-done | bytes 131104 | tf_op jit(solution)/shard_map/ppermute | solution.py:18
  151.5 1.9 %collective-permute-start.18 = (bf16[256,256]{0,1:T(8,128)(2,1)S(1)}, bf16[256,256]{0,1:T(8,128)(2,1)S(1)}, u32[]{:S(2)}, u32[]{:S(2)}) collective-permute-start(bf16[256,256]{0,1:T(8,128)(2,1)S(1)} %collective-permute-done.17), channel_id=1, source_target_pairs={{0,8},{8,16},{16,24},{24,32},{32,40},{40,48},{48,56},{56,64},{64,7... | collective-permute-start | bytes 393224 | tf_op jit(solution)/shard_map/ppermute | solution.py:18
  153.4 2.4 %fusion.91 = (f32[2,256]{1,0:T(2,128)S(1)}, f32[2,256,2304]{1,2,0:T(8,128)S(1)}) fusion(f32[2,256,2304]{1,2,0:T(8,128)S(1)} %fusion.39, pred[256,2304]{0,1:T(8,128)(4,1)S(1)} %fusion.46), kind=kOutput, calls=%fused_computation.150 | output fusion | flops 4720895 | bytes 10029056 | tf_op jit(solution)/shard_map/while/body/eval_jaxpr/sub | solution.py:196
  155.8 1.9 %collective-permute-start.22 = (bf16[256,256]{0,1:T(8,128)(2,1)S(1)}, bf16[256,256]{0,1:T(8,128)(2,1)S(1)}, u32[]{:S(2)}, u32[]{:S(2)}) collective-permute-start(bf16[256,256]{0,1:T(8,128)(2,1)S(1)} %collective-permute-done.21), channel_id=1, source_target_pairs={{0,8},{8,16},{16,24},{24,32},{32,40},{40,48},{48,56},{56,64},{64,7... | collective-permute-start | bytes 393224 | tf_op jit(solution)/shard_map/ppermute | solution.py:18
  157.7 3.3 %collective-permute-done.18 = bf16[256,256]{0,1:T(8,128)(2,1)S(1)} collective-permute-done((bf16[256,256]{0,1:T(8,128)(2,1)S(1)}, bf16[256,256]{0,1:T(8,128)(2,1)S(1)}, u32[]{:S(2)}, u32[]{:S(2)}) %collective-permute-start.18) | collective-permute-done | bytes 131104 | tf_op jit(solution)/shard_map/ppermute | solution.py:18
  161.0 2.6 %collective-permute-done.22 = bf16[256,256]{0,1:T(8,128)(2,1)S(1)} collective-permute-done((bf16[256,256]{0,1:T(8,128)(2,1)S(1)}, bf16[256,256]{0,1:T(8,128)(2,1)S(1)}, u32[]{:S(2)}, u32[]{:S(2)}) %collective-permute-start.22) | collective-permute-done | bytes 131104 | tf_op jit(solution)/shard_map/ppermute | solution.py:18
  164.3 21.4 %all-gather.1 = f32[8,1,256]{2,1,0:T(1,128)S(1)} all-gather(f32[1,1,256]{2,1,0:T(1,128)S(1)} %bitcast.211), channel_id=2, replica_groups=mesh['seq'=64,'head'=8] {'head'}, dimensions={0}, use_global_device_ids=true | all-gather | bytes 9216 | tf_op jit(solution)/shard_map/all_gather | solution.py:206
  185.8 0.8 multiply_convert_fusion
  (150 shorter events, 25.9 us)
Async XLA Ops:
  0.6 144.6 %copy-start = (bf16[256,256]{1,0:T(8,128)(2,1)S(1)}, bf16[256,256]{1,0:T(8,128)(2,1)}, u32[]{:S(2)}) copy-start(bf16[256,256]{1,0:T(8,128)(2,1)} %param.15) | copy-start | bytes 393220
  0.6 6.7 %copy-start.1 = (bf16[256,256]{1,0:T(8,128)(2,1)S(1)}, bf16[256,256]{1,0:T(8,128)(2,1)}, u32[]{:S(2)}) copy-start(bf16[256,256]{1,0:T(8,128)(2,1)} %param.13) | copy-start | bytes 393220
  1.7 33.0 %collective-permute-start.23 = (bf16[256,256]{0,1:T(8,128)(2,1)S(1)}, bf16[256,256]{0,1:T(8,128)(2,1)S(1)}, u32[]{:S(2)}, u32[]{:S(2)}) collective-permute-start(bf16[256,256]{0,1:T(8,128)(2,1)S(1)} %copy.80), channel_id=1, source_target_pairs={{0,8},{8,16},{16,24},{24,32},{32,40},{40,48},{48,56},{56,64},{64,7... | collective-permute-start | bytes 393224 | tf_op jit(solution)/shard_map/ppermute | solution.py:18
  13.1 12.8 %copy-start.2 = (bf16[256,256]{1,0:T(8,128)(2,1)S(1)}, bf16[256,256]{1,0:T(8,128)(2,1)}, u32[]{:S(2)}) copy-start(bf16[256,256]{1,0:T(8,128)(2,1)} %param.11) | copy-start | bytes 393220
  18.8 8.1 %collective-permute-start.5 = (f32[2,128,128]{2,1,0:T(8,128)S(1)}, f32[2,128,128]{2,1,0:T(8,128)S(1)}, u32[]{:S(2)}, u32[]{:S(2)}) collective-permute-start(f32[2,128,128]{2,1,0:T(8,128)S(1)} %get-tuple-element.101), channel_id=1, source_target_pairs={{0,8},{8,16},{16,24},{32,40},{40,48},{48,56},{64,72},{72,80},{80,8... | collective-permute-start | bytes 393224 | tf_op jit(solution)/shard_map/ppermute | solution.py:115
  22.3 9.3 %collective-permute-start = (f32[2,128,128]{2,1,0:T(8,128)S(1)}, f32[2,128,128]{2,1,0:T(8,128)S(1)}, u32[]{:S(2)}, u32[]{:S(2)}) collective-permute-start(f32[2,128,128]{2,1,0:T(8,128)S(1)} %get-tuple-element.100), channel_id=1, source_target_pairs={{0,8},{8,16},{16,24},{32,40},{40,48},{48,56},{64,72},{72,80},{80,8... | collective-permute-start | bytes 393224 | tf_op jit(solution)/shard_map/ppermute | solution.py:115
  27.2 11.4 %collective-permute-start.6 = (f32[2,128,128]{2,1,0:T(8,128)S(1)}, f32[2,128,128]{2,1,0:T(8,128)S(1)}, u32[]{:S(2)}, u32[]{:S(2)}) collective-permute-start(f32[2,128,128]{2,1,0:T(8,128)S(1)} %fusion.56), channel_id=1, source_target_pairs={{0,16},{8,24},{32,48},{40,56},{64,80},{72,88},{96,112},{104,120},{... | collective-permute-start | bytes 393224 | tf_op jit(solution)/shard_map/ppermute | solution.py:115
  31.9 7.6 %collective-permute-start.1 = (f32[2,128,128]{2,1,0:T(8,128)S(1)}, f32[2,128,128]{2,1,0:T(8,128)S(1)}, u32[]{:S(2)}, u32[]{:S(2)}) collective-permute-start(f32[2,128,128]{2,1,0:T(8,128)S(1)} %convolution_select_fusion.6), channel_id=1, source_target_pairs={{0,16},{8,24},{32,48},{40,56},{64,80},{72,88},{96,112},{104,120},{... | collective-permute-start | bytes 393224 | tf_op jit(solution)/shard_map/ppermute | solution.py:115
  34.7 7.8 %collective-permute-start.24 = (bf16[256,256]{0,1:T(8,128)(2,1)S(1)}, bf16[256,256]{0,1:T(8,128)(2,1)S(1)}, u32[]{:S(2)}, u32[]{:S(2)}) collective-permute-start(bf16[256,256]{0,1:T(8,128)(2,1)S(1)} %collective-permute-done.23), channel_id=1, source_target_pairs={{0,8},{8,16},{16,24},{24,32},{32,40},{40,48},{48,56},{56,64},{64,7... | collective-permute-start | bytes 393224 | tf_op jit(solution)/shard_map/ppermute | solution.py:18
  38.9 9.2 %collective-permute-start.7 = (f32[2,128,128]{2,1,0:T(8,128)S(1)}, f32[2,128,128]{2,1,0:T(8,128)S(1)}, u32[]{:S(2)}, u32[]{:S(2)}) collective-permute-start(f32[2,128,128]{2,1,0:T(8,128)S(1)} %fusion.55), channel_id=1, source_target_pairs={{24,56},{56,88},{88,120},{120,152},{152,184},{184,216},{216,248},{... | collective-permute-start | bytes 393224 | tf_op jit(solution)/shard_map/ppermute | solution.py:115
  39.8 9.2 %collective-permute-start.2 = (f32[2,128,128]{2,1,0:T(8,128)S(1)}, f32[2,128,128]{2,1,0:T(8,128)S(1)}, u32[]{:S(2)}, u32[]{:S(2)}) collective-permute-start(f32[2,128,128]{2,1,0:T(8,128)S(1)} %convolution_select_fusion.4), channel_id=1, source_target_pairs={{24,56},{56,88},{88,120},{120,152},{152,184},{184,216},{216,248},{... | collective-permute-start | bytes 393224 | tf_op jit(solution)/shard_map/ppermute | solution.py:115
  42.6 17.9 %collective-permute-start.25 = (bf16[256,256]{0,1:T(8,128)(2,1)S(1)}, bf16[256,256]{0,1:T(8,128)(2,1)S(1)}, u32[]{:S(2)}, u32[]{:S(2)}) collective-permute-start(bf16[256,256]{0,1:T(8,128)(2,1)S(1)} %collective-permute-done.24), channel_id=1, source_target_pairs={{0,8},{8,16},{16,24},{24,32},{32,40},{40,48},{48,56},{56,64},{64,7... | collective-permute-start | bytes 393224 | tf_op jit(solution)/shard_map/ppermute | solution.py:18
  48.3 14.0 %collective-permute-start.8 = (f32[2,128,128]{2,1,0:T(8,128)S(1)}, f32[2,128,128]{2,1,0:T(8,128)S(1)}, u32[]{:S(2)}, u32[]{:S(2)}) collective-permute-start(f32[2,128,128]{2,1,0:T(8,128)S(1)} %fusion.54), channel_id=1, source_target_pairs={{24,88},{56,120},{88,152},{120,184},{152,216},{184,248},{216,280},... | collective-permute-start | bytes 393224 | tf_op jit(solution)/shard_map/ppermute | solution.py:115
  49.3 14.0 %collective-permute-start.3 = (f32[2,128,128]{2,1,0:T(8,128)S(1)}, f32[2,128,128]{2,1,0:T(8,128)S(1)}, u32[]{:S(2)}, u32[]{:S(2)}) collective-permute-start(f32[2,128,128]{2,1,0:T(8,128)S(1)} %convolution_select_fusion.3), channel_id=1, source_target_pairs={{24,88},{56,120},{88,152},{120,184},{152,216},{184,248},{216,280},... | collective-permute-start | bytes 393224 | tf_op jit(solution)/shard_map/ppermute | solution.py:115
  60.4 12.8 %collective-permute-start.26 = (bf16[256,256]{0,1:T(8,128)(2,1)S(1)}, bf16[256,256]{0,1:T(8,128)(2,1)S(1)}, u32[]{:S(2)}, u32[]{:S(2)}) collective-permute-start(bf16[256,256]{0,1:T(8,128)(2,1)S(1)} %collective-permute-done.25), channel_id=1, source_target_pairs={{0,8},{8,16},{16,24},{24,32},{32,40},{40,48},{48,56},{56,64},{64,7... | collective-permute-start | bytes 393224 | tf_op jit(solution)/shard_map/ppermute | solution.py:18
  62.6 12.5 %collective-permute-start.9 = (f32[2,128,128]{2,1,0:T(8,128)S(1)}, f32[2,128,128]{2,1,0:T(8,128)S(1)}, u32[]{:S(2)}, u32[]{:S(2)}) collective-permute-start(f32[2,128,128]{2,1,0:T(8,128)S(1)} %fusion.53), channel_id=1, source_target_pairs={{24,152},{56,184},{88,216},{120,248},{152,280},{184,312},{216,344}... | collective-permute-start | bytes 393224 | tf_op jit(solution)/shard_map/ppermute | solution.py:115
  63.6 25.3 %collective-permute-start.4 = (f32[2,128,128]{2,1,0:T(8,128)S(1)}, f32[2,128,128]{2,1,0:T(8,128)S(1)}, u32[]{:S(2)}, u32[]{:S(2)}) collective-permute-start(f32[2,128,128]{2,1,0:T(8,128)S(1)} %convolution_select_fusion.2), channel_id=1, source_target_pairs={{24,152},{56,184},{88,216},{120,248},{152,280},{184,312},{216,344}... | collective-permute-start | bytes 393224 | tf_op jit(solution)/shard_map/ppermute | solution.py:115
  73.2 13.8 %collective-permute-start.27 = (bf16[256,256]{0,1:T(8,128)(2,1)S(1)}, bf16[256,256]{0,1:T(8,128)(2,1)S(1)}, u32[]{:S(2)}, u32[]{:S(2)}) collective-permute-start(bf16[256,256]{0,1:T(8,128)(2,1)S(1)} %collective-permute-done.26), channel_id=1, source_target_pairs={{0,8},{8,16},{16,24},{24,32},{32,40},{40,48},{48,56},{56,64},{64,7... | collective-permute-start | bytes 393224 | tf_op jit(solution)/shard_map/ppermute | solution.py:18
  75.4 13.8 %collective-permute-start.10 = (f32[2,128,128]{2,1,0:T(8,128)S(1)}, f32[2,128,128]{2,1,0:T(8,128)S(1)}, u32[]{:S(2)}, u32[]{:S(2)}) collective-permute-start(f32[2,128,128]{2,1,0:T(8,128)S(1)} %fusion.52), channel_id=1, source_target_pairs={{24,280},{56,312},{88,344},{120,376},{152,408},{184,440},{216,472}... | collective-permute-start | bytes 393224 | tf_op jit(solution)/shard_map/ppermute | solution.py:115
  87.0 8.1 %collective-permute-start.28 = (bf16[256,256]{0,1:T(8,128)(2,1)S(1)}, bf16[256,256]{0,1:T(8,128)(2,1)S(1)}, u32[]{:S(2)}, u32[]{:S(2)}) collective-permute-start(bf16[256,256]{0,1:T(8,128)(2,1)S(1)} %collective-permute-done.27), channel_id=1, source_target_pairs={{0,8},{8,16},{16,24},{24,32},{32,40},{40,48},{48,56},{56,64},{64,7... | collective-permute-start | bytes 393224 | tf_op jit(solution)/shard_map/ppermute | solution.py:18
  89.5 7.7 %collective-permute-start.14 = (f32[2,128,128]{2,1,0:T(8,128)S(1)}, f32[2,128,128]{2,1,0:T(8,128)S(1)}, u32[]{:S(2)}, u32[]{:S(2)}) collective-permute-start(f32[2,128,128]{2,1,0:T(8,128)S(1)} %fusion.51), channel_id=1, source_target_pairs={{24,56},{56,88},{88,120},{120,152},{152,184},{184,216},{216,248},{... | collective-permute-start | bytes 393224 | tf_op jit(solution)/shard_map/ppermute | solution.py:115
  90.2 7.0 %collective-permute-start.13 = (f32[2,128,128]{2,1,0:T(8,128)S(1)}, f32[2,128,128]{2,1,0:T(8,128)S(1)}, u32[]{:S(2)}, u32[]{:S(2)}) collective-permute-start(f32[2,128,128]{2,1,0:T(8,128)S(1)} %fusion.51), channel_id=1, source_target_pairs={{24,48},{56,80},{88,112},{120,144},{152,176},{184,208},{216,240},{... | collective-permute-start | bytes 393224 | tf_op jit(solution)/shard_map/ppermute | solution.py:115
  90.9 6.4 %collective-permute-start.12 = (f32[2,128,128]{2,1,0:T(8,128)S(1)}, f32[2,128,128]{2,1,0:T(8,128)S(1)}, u32[]{:S(2)}, u32[]{:S(2)}) collective-permute-start(f32[2,128,128]{2,1,0:T(8,128)S(1)} %fusion.51), channel_id=1, source_target_pairs={{24,40},{56,72},{88,104},{120,136},{152,168},{184,200},{216,232},{... | collective-permute-start | bytes 393224 | tf_op jit(solution)/shard_map/ppermute | solution.py:115
  91.6 16.7 %collective-permute-start.11 = (f32[2,128,128]{2,1,0:T(8,128)S(1)}, f32[2,128,128]{2,1,0:T(8,128)S(1)}, u32[]{:S(2)}, u32[]{:S(2)}) collective-permute-start(f32[2,128,128]{2,1,0:T(8,128)S(1)} %fusion.51), channel_id=1, source_target_pairs={{24,32},{56,64},{88,96},{120,128},{152,160},{184,192},{216,224},{2... | collective-permute-start | bytes 393224 | tf_op jit(solution)/shard_map/ppermute | solution.py:115
  95.1 21.9 %collective-permute-start.29 = (bf16[256,256]{0,1:T(8,128)(2,1)S(1)}, bf16[256,256]{0,1:T(8,128)(2,1)S(1)}, u32[]{:S(2)}, u32[]{:S(2)}) collective-permute-start(bf16[256,256]{0,1:T(8,128)(2,1)S(1)} %collective-permute-done.28), channel_id=1, source_target_pairs={{0,8},{8,16},{16,24},{24,32},{32,40},{40,48},{48,56},{56,64},{64,7... | collective-permute-start | bytes 393224 | tf_op jit(solution)/shard_map/ppermute | solution.py:18
  113.2 8.3 %collective-permute-start.19 = (bf16[256,256]{0,1:T(8,128)(2,1)S(1)}, bf16[256,256]{0,1:T(8,128)(2,1)S(1)}, u32[]{:S(2)}, u32[]{:S(2)}) collective-permute-start(bf16[256,256]{0,1:T(8,128)(2,1)S(1)} %bitcast.201), channel_id=1, source_target_pairs={{0,8},{8,16},{16,24},{24,32},{32,40},{40,48},{48,56},{56,64},{64,7... | collective-permute-start | bytes 393224 | tf_op jit(solution)/shard_map/ppermute | solution.py:18
  115.1 15.3 %collective-permute-start.15 = (bf16[256,256]{0,1:T(8,128)(2,1)S(1)}, bf16[256,256]{0,1:T(8,128)(2,1)S(1)}, u32[]{:S(2)}, u32[]{:S(2)}) collective-permute-start(bf16[256,256]{0,1:T(8,128)(2,1)S(1)} %bitcast.202), channel_id=1, source_target_pairs={{0,40},{8,48},{16,56},{24,64},{32,72},{40,80},{48,88},{56,96},{64,... | collective-permute-start | bytes 393224 | tf_op jit(solution)/shard_map/ppermute | solution.py:18
  117.1 16.3 %collective-permute-start.30 = (bf16[256,256]{0,1:T(8,128)(2,1)S(1)}, bf16[256,256]{0,1:T(8,128)(2,1)S(1)}, u32[]{:S(2)}, u32[]{:S(2)}) collective-permute-start(bf16[256,256]{0,1:T(8,128)(2,1)S(1)} %collective-permute-done.29), channel_id=1, source_target_pairs={{0,8},{8,16},{16,24},{24,32},{32,40},{40,48},{48,56},{56,64},{64,7... | collective-permute-start | bytes 393224 | tf_op jit(solution)/shard_map/ppermute | solution.py:18
  121.5 24.6 %collective-permute-start.20 = (bf16[256,256]{0,1:T(8,128)(2,1)S(1)}, bf16[256,256]{0,1:T(8,128)(2,1)S(1)}, u32[]{:S(2)}, u32[]{:S(2)}) collective-permute-start(bf16[256,256]{0,1:T(8,128)(2,1)S(1)} %collective-permute-done.19), channel_id=1, source_target_pairs={{0,8},{8,16},{16,24},{24,32},{32,40},{40,48},{48,56},{56,64},{64,7... | collective-permute-start | bytes 393224 | tf_op jit(solution)/shard_map/ppermute | solution.py:18
  130.4 12.9 %collective-permute-start.16 = (bf16[256,256]{0,1:T(8,128)(2,1)S(1)}, bf16[256,256]{0,1:T(8,128)(2,1)S(1)}, u32[]{:S(2)}, u32[]{:S(2)}) collective-permute-start(bf16[256,256]{0,1:T(8,128)(2,1)S(1)} %collective-permute-done.15), channel_id=1, source_target_pairs={{0,8},{8,16},{16,24},{24,32},{32,40},{40,48},{48,56},{56,64},{64,7... | collective-permute-start | bytes 393224 | tf_op jit(solution)/shard_map/ppermute | solution.py:18
  143.4 8.1 %collective-permute-start.17 = (bf16[256,256]{0,1:T(8,128)(2,1)S(1)}, bf16[256,256]{0,1:T(8,128)(2,1)S(1)}, u32[]{:S(2)}, u32[]{:S(2)}) collective-permute-start(bf16[256,256]{0,1:T(8,128)(2,1)S(1)} %collective-permute-done.16), channel_id=1, source_target_pairs={{0,8},{8,16},{16,24},{24,32},{32,40},{40,48},{48,56},{56,64},{64,7... | collective-permute-start | bytes 393224 | tf_op jit(solution)/shard_map/ppermute | solution.py:18
  146.1 9.6 %collective-permute-start.21 = (bf16[256,256]{0,1:T(8,128)(2,1)S(1)}, bf16[256,256]{0,1:T(8,128)(2,1)S(1)}, u32[]{:S(2)}, u32[]{:S(2)}) collective-permute-start(bf16[256,256]{0,1:T(8,128)(2,1)S(1)} %collective-permute-done.20), channel_id=1, source_target_pairs={{0,8},{8,16},{16,24},{24,32},{32,40},{40,48},{48,56},{56,64},{64,7... | collective-permute-start | bytes 393224 | tf_op jit(solution)/shard_map/ppermute | solution.py:18
  151.5 9.5 %collective-permute-start.18 = (bf16[256,256]{0,1:T(8,128)(2,1)S(1)}, bf16[256,256]{0,1:T(8,128)(2,1)S(1)}, u32[]{:S(2)}, u32[]{:S(2)}) collective-permute-start(bf16[256,256]{0,1:T(8,128)(2,1)S(1)} %collective-permute-done.17), channel_id=1, source_target_pairs={{0,8},{8,16},{16,24},{24,32},{32,40},{40,48},{48,56},{56,64},{64,7... | collective-permute-start | bytes 393224 | tf_op jit(solution)/shard_map/ppermute | solution.py:18
  155.8 7.8 %collective-permute-start.22 = (bf16[256,256]{0,1:T(8,128)(2,1)S(1)}, bf16[256,256]{0,1:T(8,128)(2,1)S(1)}, u32[]{:S(2)}, u32[]{:S(2)}) collective-permute-start(bf16[256,256]{0,1:T(8,128)(2,1)S(1)} %collective-permute-done.21), channel_id=1, source_target_pairs={{0,8},{8,16},{16,24},{24,32},{32,40},{40,48},{48,56},{56,64},{64,7... | collective-permute-start | bytes 393224 | tf_op jit(solution)/shard_map/ppermute | solution.py:18
  163.7 22.1 %copy-start.3 = (f32[256]{0:T(256)S(1)}, f32[256]{0:T(256)}, u32[]{:S(2)}) copy-start(f32[256]{0:T(256)} %param.17) | copy-start | bytes 3076

commit v19 on v10

--- a/solution.py
+++ b/solution.py
@@ -235,7 +235,7 @@
     starts = jnp.arange(tok_rows // block_rows) * block_rows
     attended = lax.map(attend_block, starts).reshape(tok_rows, features)
     squares = jnp.sum(attended * attended, axis=1)
-    total_sq = lax.psum(squares, "head")
+    total_sq = jnp.sum(lax.all_gather(squares, "head"), axis=0)
     scale_rows = lax.rsqrt(total_sq / (features * lax.axis_size("head")) + 1e-06)
     normed_out = (attended * out_gain[None, :] * scale_rows[:, None]).astype(jnp.bfloat16)
     return (delta_out, normed_out)

time: 190 us -> 188 us (0.989)
    psum x1 -> x0, blocking collectives: 22.1 us -> none  [on_device(): total_sq = lax.psum(squares, 'head')]
    all_gather x0 -> x1, blocking collectives: none -> 20.7 us  [on_device(): total_sq = jnp.sum(lax.all_gather(squares, 'head'), axis=0)]
where the time goes in v19:
time: 188 us
  waiting for transfers between devices  75.3 us (40%)
  starting transfers between devices  61.6 us (33%)
  blocking collectives  20.7 us (11%)
  matrix products  18.5 us (10%)
  other arithmetic  5.45 us (3%)
  local copies, waits for them, and re-layouts  4.24 us (2%)
    ppermute x16, waiting for transfers between devices, shifted(): return lax.ppermute(value, axis, pairs)  66.3 us
    ppermute x16, starting transfers between devices, shifted(): return lax.ppermute(value, axis, pairs)  40.5 us
    ppermute x15, starting transfers between devices, moved(): return lax.ppermute(value, 'seq', pairs)  21 us
    all_gather x1, blocking collectives, on_device(): total_sq = jnp.sum(lax.all_gather(squares, 'head'), axis=0)  20.7 us
    ppermute x15, waiting for transfers between devices, moved(): return lax.ppermute(value, 'seq', pairs)  9.06 us
    dot_general x18, matrix products, batched_dot(): return jnp.einsum('hij,hjk->hik', left, right, precision=highest)  5.25 us
  transfers between devices with their start and end apart: 31, of which 12 were waited for; matrix products, arithmetic and copies ran while one was open for 14% of the time, Pallas kernels for 0%

profile of v19, /device:TPU:9, one launch (start us, length us, event | category | flops | bytes accessed | tf_op | source)
XLA Modules:
  0.0 187.6 jit_solution(13105093165839897908)
XLA Ops:
  0.6 1.0 copy.90
  1.7 3.5 %collective-permute-start.23 = (bf16[256,256]{0,1:T(8,128)(2,1)S(1)}, bf16[256,256]{0,1:T(8,128)(2,1)S(1)}, u32[]{:S(2)}, u32[]{:S(2)}) collective-permute-start(bf16[256,256]{0,1:T(8,128)(2,1)S(1)} %copy.90), channel_id=1, source_target_pairs={{0,8},{8,16},{16,24},{24,32},{32,40},{40,48},{48,56},{56,64},{64,7... | collective-permute-start | bytes 393224 | tf_op jit(solution)/shard_map/ppermute | solution.py:18
  5.3 0.8 mul.82
  6.1 1.0 reshape.162
  12.8 1.0 convolution_subtract_fusion
  14.8 3.6 %collective-permute-start = (f32[2,128,128]{2,1,0:T(8,128)S(1)}, f32[2,128,128]{2,1,0:T(8,128)S(1)}, u32[]{:S(2)}, u32[]{:S(2)}) collective-permute-start(f32[2,128,128]{2,1,0:T(8,128)S(1)} %fusion.67), channel_id=1, source_target_pairs={{0,8},{8,16},{16,24},{32,40},{40,48},{48,56},{64,72},{72,80},{80,8... | collective-permute-start | bytes 393224 | tf_op jit(solution)/shard_map/ppermute | solution.py:146
  19.0 1.0 fusion.32
  21.1 3.7 %collective-permute-start.5 = (f32[2,128,128]{2,1,0:T(8,128)S(1)}, f32[2,128,128]{2,1,0:T(8,128)S(1)}, u32[]{:S(2)}, u32[]{:S(2)}) collective-permute-start(f32[2,128,128]{2,1,0:T(8,128)S(1)} %convolution_add_fusion.12), channel_id=1, source_target_pairs={{0,8},{8,16},{16,24},{32,40},{40,48},{48,56},{64,72},{72,80},{80,8... | collective-permute-start | bytes 393224 | tf_op jit(solution)/shard_map/ppermute | solution.py:146
  28.3 4.5 %collective-permute-start.1 = (f32[2,128,128]{2,1,0:T(8,128)S(1)}, f32[2,128,128]{2,1,0:T(8,128)S(1)}, u32[]{:S(2)}, u32[]{:S(2)}) collective-permute-start(f32[2,128,128]{2,1,0:T(8,128)S(1)} %convolution_select_fusion.6), channel_id=1, source_target_pairs={{0,16},{8,24},{32,48},{40,56},{64,80},{72,88},{96,112},{104,120},{... | collective-permute-start | bytes 393224 | tf_op jit(solution)/shard_map/ppermute | solution.py:146
  33.1 1.3 collective-permute-start.6
  34.7 1.9 %collective-permute-start.24 = (bf16[256,256]{0,1:T(8,128)(2,1)S(1)}, bf16[256,256]{0,1:T(8,128)(2,1)S(1)}, u32[]{:S(2)}, u32[]{:S(2)}) collective-permute-start(bf16[256,256]{0,1:T(8,128)(2,1)S(1)} %collective-permute-done.23), channel_id=1, source_target_pairs={{0,8},{8,16},{16,24},{24,32},{32,40},{40,48},{48,56},{56,64},{64,7... | collective-permute-start | bytes 393224 | tf_op jit(solution)/shard_map/ppermute | solution.py:18
  37.1 0.7 collective-permute-start.2
  39.5 3.0 %collective-permute-done.24 = bf16[256,256]{0,1:T(8,128)(2,1)S(1)} collective-permute-done((bf16[256,256]{0,1:T(8,128)(2,1)S(1)}, bf16[256,256]{0,1:T(8,128)(2,1)S(1)}, u32[]{:S(2)}, u32[]{:S(2)}) %collective-permute-start.24) | collective-permute-done | bytes 131104 | tf_op jit(solution)/shard_map/ppermute | solution.py:18
  42.5 5.1 %collective-permute-start.25 = (bf16[256,256]{0,1:T(8,128)(2,1)S(1)}, bf16[256,256]{0,1:T(8,128)(2,1)S(1)}, u32[]{:S(2)}, u32[]{:S(2)}) collective-permute-start(bf16[256,256]{0,1:T(8,128)(2,1)S(1)} %collective-permute-done.24), channel_id=1, source_target_pairs={{0,8},{8,16},{16,24},{24,32},{32,40},{40,48},{48,56},{56,64},{64,7... | collective-permute-start | bytes 393224 | tf_op jit(solution)/shard_map/ppermute | solution.py:18
  49.8 9.0 %collective-permute-done.25 = bf16[256,256]{0,1:T(8,128)(2,1)S(1)} collective-permute-done((bf16[256,256]{0,1:T(8,128)(2,1)S(1)}, bf16[256,256]{0,1:T(8,128)(2,1)S(1)}, u32[]{:S(2)}, u32[]{:S(2)}) %collective-permute-start.25) | collective-permute-done | bytes 131104 | tf_op jit(solution)/shard_map/ppermute | solution.py:18
  58.8 1.9 %collective-permute-start.26 = (bf16[256,256]{0,1:T(8,128)(2,1)S(1)}, bf16[256,256]{0,1:T(8,128)(2,1)S(1)}, u32[]{:S(2)}, u32[]{:S(2)}) collective-permute-start(bf16[256,256]{0,1:T(8,128)(2,1)S(1)} %collective-permute-done.25), channel_id=1, source_target_pairs={{0,8},{8,16},{16,24},{24,32},{32,40},{40,48},{48,56},{56,64},{64,7... | collective-permute-start | bytes 393224 | tf_op jit(solution)/shard_map/ppermute | solution.py:18
  62.0 0.7 collective-permute-start.4
  62.7 16.9 %collective-permute-done.26 = bf16[256,256]{0,1:T(8,128)(2,1)S(1)} collective-permute-done((bf16[256,256]{0,1:T(8,128)(2,1)S(1)}, bf16[256,256]{0,1:T(8,128)(2,1)S(1)}, u32[]{:S(2)}, u32[]{:S(2)}) %collective-permute-start.26) | collective-permute-done | bytes 131104 | tf_op jit(solution)/shard_map/ppermute | solution.py:18
  79.6 1.9 %collective-permute-start.27 = (bf16[256,256]{0,1:T(8,128)(2,1)S(1)}, bf16[256,256]{0,1:T(8,128)(2,1)S(1)}, u32[]{:S(2)}, u32[]{:S(2)}) collective-permute-start(bf16[256,256]{0,1:T(8,128)(2,1)S(1)} %collective-permute-done.26), channel_id=1, source_target_pairs={{0,8},{8,16},{16,24},{24,32},{32,40},{40,48},{48,56},{56,64},{64,7... | collective-permute-start | bytes 393224 | tf_op jit(solution)/shard_map/ppermute | solution.py:18
  82.5 8.6 %collective-permute-done.27 = bf16[256,256]{0,1:T(8,128)(2,1)S(1)} collective-permute-done((bf16[256,256]{0,1:T(8,128)(2,1)S(1)}, bf16[256,256]{0,1:T(8,128)(2,1)S(1)}, u32[]{:S(2)}, u32[]{:S(2)}) %collective-permute-start.27) | collective-permute-done | bytes 131104 | tf_op jit(solution)/shard_map/ppermute | solution.py:18
  91.0 1.9 %collective-permute-start.28 = (bf16[256,256]{0,1:T(8,128)(2,1)S(1)}, bf16[256,256]{0,1:T(8,128)(2,1)S(1)}, u32[]{:S(2)}, u32[]{:S(2)}) collective-permute-start(bf16[256,256]{0,1:T(8,128)(2,1)S(1)} %collective-permute-done.27), channel_id=1, source_target_pairs={{0,8},{8,16},{16,24},{24,32},{32,40},{40,48},{48,56},{56,64},{64,7... | collective-permute-start | bytes 393224 | tf_op jit(solution)/shard_map/ppermute | solution.py:18
  93.5 0.7 collective-permute-start.14
  94.2 0.7 collective-permute-start.13
  95.5 1.3 collective-permute-start.11
  97.2 2.5 %collective-permute-done.28 = bf16[256,256]{0,1:T(8,128)(2,1)S(1)} collective-permute-done((bf16[256,256]{0,1:T(8,128)(2,1)S(1)}, bf16[256,256]{0,1:T(8,128)(2,1)S(1)}, u32[]{:S(2)}, u32[]{:S(2)}) %collective-permute-start.28) | collective-permute-done | bytes 131104 | tf_op jit(solution)/shard_map/ppermute | solution.py:18
  99.8 1.9 %collective-permute-start.29 = (bf16[256,256]{0,1:T(8,128)(2,1)S(1)}, bf16[256,256]{0,1:T(8,128)(2,1)S(1)}, u32[]{:S(2)}, u32[]{:S(2)}) collective-permute-start(bf16[256,256]{0,1:T(8,128)(2,1)S(1)} %collective-permute-done.28), channel_id=1, source_target_pairs={{0,8},{8,16},{16,24},{24,32},{32,40},{40,48},{48,56},{56,64},{64,7... | collective-permute-start | bytes 393224 | tf_op jit(solution)/shard_map/ppermute | solution.py:18
  101.7 9.0 %collective-permute-done.11 = f32[2,128,128]{2,1,0:T(8,128)S(1)} collective-permute-done((f32[2,128,128]{2,1,0:T(8,128)S(1)}, f32[2,128,128]{2,1,0:T(8,128)S(1)}, u32[]{:S(2)}, u32[]{:S(2)}) %collective-permute-start.11) | collective-permute-done | bytes 131104 | tf_op jit(solution)/shard_map/ppermute | solution.py:146
  111.2 1.9 %collective-permute-start.19 = (bf16[256,256]{0,1:T(8,128)(2,1)S(1)}, bf16[256,256]{0,1:T(8,128)(2,1)S(1)}, u32[]{:S(2)}, u32[]{:S(2)}) collective-permute-start(bf16[256,256]{0,1:T(8,128)(2,1)S(1)} %bitcast.171), channel_id=1, source_target_pairs={{0,8},{8,16},{16,24},{24,32},{32,40},{40,48},{48,56},{56,64},{64,7... | collective-permute-start | bytes 393224 | tf_op jit(solution)/shard_map/ppermute | solution.py:18
  113.1 5.0 %collective-permute-start.15 = (bf16[256,256]{0,1:T(8,128)(2,1)S(1)}, bf16[256,256]{0,1:T(8,128)(2,1)S(1)}, u32[]{:S(2)}, u32[]{:S(2)}) collective-permute-start(bf16[256,256]{0,1:T(8,128)(2,1)S(1)} %bitcast.172), channel_id=1, source_target_pairs={{0,40},{8,48},{16,56},{24,64},{32,72},{40,80},{48,88},{56,96},{64,... | collective-permute-start | bytes 393224 | tf_op jit(solution)/shard_map/ppermute | solution.py:18
  118.1 1.9 %collective-permute-start.30 = (bf16[256,256]{0,1:T(8,128)(2,1)S(1)}, bf16[256,256]{0,1:T(8,128)(2,1)S(1)}, u32[]{:S(2)}, u32[]{:S(2)}) collective-permute-start(bf16[256,256]{0,1:T(8,128)(2,1)S(1)} %collective-permute-done.29), channel_id=1, source_target_pairs={{0,8},{8,16},{16,24},{24,32},{32,40},{40,48},{48,56},{56,64},{64,7... | collective-permute-start | bytes 393224 | tf_op jit(solution)/shard_map/ppermute | solution.py:18
  120.0 1.3 fusion.13
  121.3 0.8 copy.96
  122.0 2.9 %collective-permute-start.20 = (bf16[256,256]{0,1:T(8,128)(2,1)S(1)}, bf16[256,256]{0,1:T(8,128)(2,1)S(1)}, u32[]{:S(2)}, u32[]{:S(2)}) collective-permute-start(bf16[256,256]{0,1:T(8,128)(2,1)S(1)} %collective-permute-done.19), channel_id=1, source_target_pairs={{0,8},{8,16},{16,24},{24,32},{32,40},{40,48},{48,56},{56,64},{64,7... | collective-permute-start | bytes 393224 | tf_op jit(solution)/shard_map/ppermute | solution.py:18
  124.9 2.3 %collective-permute-done.15 = bf16[256,256]{0,1:T(8,128)(2,1)S(1)} collective-permute-done((bf16[256,256]{0,1:T(8,128)(2,1)S(1)}, bf16[256,256]{0,1:T(8,128)(2,1)S(1)}, u32[]{:S(2)}, u32[]{:S(2)}) %collective-permute-start.15) | collective-permute-done | bytes 131104 | tf_op jit(solution)/shard_map/ppermute | solution.py:18
  127.3 1.9 %collective-permute-start.16 = (bf16[256,256]{0,1:T(8,128)(2,1)S(1)}, bf16[256,256]{0,1:T(8,128)(2,1)S(1)}, u32[]{:S(2)}, u32[]{:S(2)}) collective-permute-start(bf16[256,256]{0,1:T(8,128)(2,1)S(1)} %collective-permute-done.15), channel_id=1, source_target_pairs={{0,8},{8,16},{16,24},{24,32},{32,40},{40,48},{48,56},{56,64},{64,7... | collective-permute-start | bytes 393224 | tf_op jit(solution)/shard_map/ppermute | solution.py:18
  129.2 6.2 %collective-permute-done.30 = bf16[256,256]{0,1:T(8,128)(2,1)S(1)} collective-permute-done((bf16[256,256]{0,1:T(8,128)(2,1)S(1)}, bf16[256,256]{0,1:T(8,128)(2,1)S(1)}, u32[]{:S(2)}, u32[]{:S(2)}) %collective-permute-start.30) | collective-permute-done | bytes 131104 | tf_op jit(solution)/shard_map/ppermute | solution.py:18
  135.5 8.1 %collective-permute-done.16 = bf16[256,256]{0,1:T(8,128)(2,1)S(1)} collective-permute-done((bf16[256,256]{0,1:T(8,128)(2,1)S(1)}, bf16[256,256]{0,1:T(8,128)(2,1)S(1)}, u32[]{:S(2)}, u32[]{:S(2)}) %collective-permute-start.16) | collective-permute-done | bytes 131104 | tf_op jit(solution)/shard_map/ppermute | solution.py:18
  143.6 1.9 %collective-permute-start.17 = (bf16[256,256]{0,1:T(8,128)(2,1)S(1)}, bf16[256,256]{0,1:T(8,128)(2,1)S(1)}, u32[]{:S(2)}, u32[]{:S(2)}) collective-permute-start(bf16[256,256]{0,1:T(8,128)(2,1)S(1)} %collective-permute-done.16), channel_id=1, source_target_pairs={{0,8},{8,16},{16,24},{24,32},{32,40},{40,48},{48,56},{56,64},{64,7... | collective-permute-start | bytes 393224 | tf_op jit(solution)/shard_map/ppermute | solution.py:18
  145.5 0.8 fusion.6
  146.4 2.6 %collective-permute-start.21 = (bf16[256,256]{0,1:T(8,128)(2,1)S(1)}, bf16[256,256]{0,1:T(8,128)(2,1)S(1)}, u32[]{:S(2)}, u32[]{:S(2)}) collective-permute-start(bf16[256,256]{0,1:T(8,128)(2,1)S(1)} %collective-permute-done.20), channel_id=1, source_target_pairs={{0,8},{8,16},{16,24},{24,32},{32,40},{40,48},{48,56},{56,64},{64,7... | collective-permute-start | bytes 393224 | tf_op jit(solution)/shard_map/ppermute | solution.py:18
  149.0 3.5 %collective-permute-done.17 = bf16[256,256]{0,1:T(8,128)(2,1)S(1)} collective-permute-done((bf16[256,256]{0,1:T(8,128)(2,1)S(1)}, bf16[256,256]{0,1:T(8,128)(2,1)S(1)}, u32[]{:S(2)}, u32[]{:S(2)}) %collective-permute-start.17) | collective-permute-done | bytes 131104 | tf_op jit(solution)/shard_map/ppermute | solution.py:18
  152.5 1.9 %collective-permute-start.18 = (bf16[256,256]{0,1:T(8,128)(2,1)S(1)}, bf16[256,256]{0,1:T(8,128)(2,1)S(1)}, u32[]{:S(2)}, u32[]{:S(2)}) collective-permute-start(bf16[256,256]{0,1:T(8,128)(2,1)S(1)} %collective-permute-done.17), channel_id=1, source_target_pairs={{0,8},{8,16},{16,24},{24,32},{32,40},{40,48},{48,56},{56,64},{64,7... | collective-permute-start | bytes 393224 | tf_op jit(solution)/shard_map/ppermute | solution.py:18
  154.4 2.4 %fusion.77 = (f32[2,256]{1,0:T(2,128)S(1)}, f32[2,256,2304]{1,2,0:T(8,128)S(1)}) fusion(f32[2,256,2304]{1,2,0:T(8,128)S(1)} %fusion.6, pred[256,2304]{0,1:T(8,128)(4,1)S(1)} %fusion.13), kind=kOutput, calls=%fused_computation.147 | output fusion | flops 4720895 | bytes 10029056 | tf_op jit(solution)/shard_map/while/body/eval_jaxpr/sub | solution.py:228
  156.7 2.3 %collective-permute-start.22 = (bf16[256,256]{0,1:T(8,128)(2,1)S(1)}, bf16[256,256]{0,1:T(8,128)(2,1)S(1)}, u32[]{:S(2)}, u32[]{:S(2)}) collective-permute-start(bf16[256,256]{0,1:T(8,128)(2,1)S(1)} %collective-permute-done.21), channel_id=1, source_target_pairs={{0,8},{8,16},{16,24},{24,32},{32,40},{40,48},{48,56},{56,64},{64,7... | collective-permute-start | bytes 393224 | tf_op jit(solution)/shard_map/ppermute | solution.py:18
  159.0 2.1 %collective-permute-done.18 = bf16[256,256]{0,1:T(8,128)(2,1)S(1)} collective-permute-done((bf16[256,256]{0,1:T(8,128)(2,1)S(1)}, bf16[256,256]{0,1:T(8,128)(2,1)S(1)}, u32[]{:S(2)}, u32[]{:S(2)}) %collective-permute-start.18) | collective-permute-done | bytes 131104 | tf_op jit(solution)/shard_map/ppermute | solution.py:18
  161.2 4.1 %collective-permute-done.22 = bf16[256,256]{0,1:T(8,128)(2,1)S(1)} collective-permute-done((bf16[256,256]{0,1:T(8,128)(2,1)S(1)}, bf16[256,256]{0,1:T(8,128)(2,1)S(1)}, u32[]{:S(2)}, u32[]{:S(2)}) %collective-permute-start.22) | collective-permute-done | bytes 131104 | tf_op jit(solution)/shard_map/ppermute | solution.py:18
  166.1 20.7 %all-gather.1 = f32[8,1,256]{2,1,0:T(1,128)S(1)} all-gather(f32[1,1,256]{2,1,0:T(1,128)S(1)} %bitcast.187), channel_id=2, replica_groups=mesh['seq'=64,'head'=8] {'head'}, dimensions={0}, use_global_device_ids=true | all-gather | bytes 9216 | tf_op jit(solution)/shard_map/all_gather | solution.py:238
  186.8 0.8 multiply_convert_fusion
  (116 shorter events, 21.5 us)
Async XLA Ops:
  0.6 144.9 %copy-start = (bf16[256,256]{1,0:T(8,128)(2,1)S(1)}, bf16[256,256]{1,0:T(8,128)(2,1)}, u32[]{:S(2)}) copy-start(bf16[256,256]{1,0:T(8,128)(2,1)} %param.11) | copy-start | bytes 393220
  1.7 33.0 %collective-permute-start.23 = (bf16[256,256]{0,1:T(8,128)(2,1)S(1)}, bf16[256,256]{0,1:T(8,128)(2,1)S(1)}, u32[]{:S(2)}, u32[]{:S(2)}) collective-permute-start(bf16[256,256]{0,1:T(8,128)(2,1)S(1)} %copy.90), channel_id=1, source_target_pairs={{0,8},{8,16},{16,24},{24,32},{32,40},{40,48},{48,56},{56,64},{64,7... | collective-permute-start | bytes 393224 | tf_op jit(solution)/shard_map/ppermute | solution.py:18
  12.8 5.6 %copy-start.2 = (bf16[256,256]{1,0:T(8,128)(2,1)S(1)}, bf16[256,256]{1,0:T(8,128)(2,1)}, u32[]{:S(2)}) copy-start(bf16[256,256]{1,0:T(8,128)(2,1)} %param.9) | copy-start | bytes 393220
  14.8 13.2 %collective-permute-start = (f32[2,128,128]{2,1,0:T(8,128)S(1)}, f32[2,128,128]{2,1,0:T(8,128)S(1)}, u32[]{:S(2)}, u32[]{:S(2)}) collective-permute-start(f32[2,128,128]{2,1,0:T(8,128)S(1)} %fusion.67), channel_id=1, source_target_pairs={{0,8},{8,16},{16,24},{32,40},{40,48},{48,56},{64,72},{72,80},{80,8... | collective-permute-start | bytes 393224 | tf_op jit(solution)/shard_map/ppermute | solution.py:146
  20.0 4.8 %copy-start.1 = (bf16[256,256]{1,0:T(8,128)(2,1)S(1)}, bf16[256,256]{1,0:T(8,128)(2,1)}, u32[]{:S(2)}) copy-start(bf16[256,256]{1,0:T(8,128)(2,1)} %param.7) | copy-start | bytes 393220
  21.1 11.6 %collective-permute-start.5 = (f32[2,128,128]{2,1,0:T(8,128)S(1)}, f32[2,128,128]{2,1,0:T(8,128)S(1)}, u32[]{:S(2)}, u32[]{:S(2)}) collective-permute-start(f32[2,128,128]{2,1,0:T(8,128)S(1)} %convolution_add_fusion.12), channel_id=1, source_target_pairs={{0,8},{8,16},{16,24},{32,40},{40,48},{48,56},{64,72},{72,80},{80,8... | collective-permute-start | bytes 393224 | tf_op jit(solution)/shard_map/ppermute | solution.py:146
  28.3 8.6 %collective-permute-start.1 = (f32[2,128,128]{2,1,0:T(8,128)S(1)}, f32[2,128,128]{2,1,0:T(8,128)S(1)}, u32[]{:S(2)}, u32[]{:S(2)}) collective-permute-start(f32[2,128,128]{2,1,0:T(8,128)S(1)} %convolution_select_fusion.6), channel_id=1, source_target_pairs={{0,16},{8,24},{32,48},{40,56},{64,80},{72,88},{96,112},{104,120},{... | collective-permute-start | bytes 393224 | tf_op jit(solution)/shard_map/ppermute | solution.py:146
  33.1 4.8 %collective-permute-start.6 = (f32[2,128,128]{2,1,0:T(8,128)S(1)}, f32[2,128,128]{2,1,0:T(8,128)S(1)}, u32[]{:S(2)}, u32[]{:S(2)}) collective-permute-start(f32[2,128,128]{2,1,0:T(8,128)S(1)} %fusion.23), channel_id=1, source_target_pairs={{0,16},{8,24},{32,48},{40,56},{64,80},{72,88},{96,112},{104,120},{... | collective-permute-start | bytes 393224 | tf_op jit(solution)/shard_map/ppermute | solution.py:146
  34.7 7.8 %collective-permute-start.24 = (bf16[256,256]{0,1:T(8,128)(2,1)S(1)}, bf16[256,256]{0,1:T(8,128)(2,1)S(1)}, u32[]{:S(2)}, u32[]{:S(2)}) collective-permute-start(bf16[256,256]{0,1:T(8,128)(2,1)S(1)} %collective-permute-done.23), channel_id=1, source_target_pairs={{0,8},{8,16},{16,24},{24,32},{32,40},{40,48},{48,56},{56,64},{64,7... | collective-permute-start | bytes 393224 | tf_op jit(solution)/shard_map/ppermute | solution.py:18
  37.1 11.7 %collective-permute-start.2 = (f32[2,128,128]{2,1,0:T(8,128)S(1)}, f32[2,128,128]{2,1,0:T(8,128)S(1)}, u32[]{:S(2)}, u32[]{:S(2)}) collective-permute-start(f32[2,128,128]{2,1,0:T(8,128)S(1)} %convolution_select_fusion.4), channel_id=1, source_target_pairs={{24,56},{56,88},{88,120},{120,152},{152,184},{184,216},{216,248},{... | collective-permute-start | bytes 393224 | tf_op jit(solution)/shard_map/ppermute | solution.py:146
  38.1 9.7 %collective-permute-start.7 = (f32[2,128,128]{2,1,0:T(8,128)S(1)}, f32[2,128,128]{2,1,0:T(8,128)S(1)}, u32[]{:S(2)}, u32[]{:S(2)}) collective-permute-start(f32[2,128,128]{2,1,0:T(8,128)S(1)} %fusion.22), channel_id=1, source_target_pairs={{24,56},{56,88},{88,120},{120,152},{152,184},{184,216},{216,248},{... | collective-permute-start | bytes 393224 | tf_op jit(solution)/shard_map/ppermute | solution.py:146
  42.5 16.3 %collective-permute-start.25 = (bf16[256,256]{0,1:T(8,128)(2,1)S(1)}, bf16[256,256]{0,1:T(8,128)(2,1)S(1)}, u32[]{:S(2)}, u32[]{:S(2)}) collective-permute-start(bf16[256,256]{0,1:T(8,128)(2,1)S(1)} %collective-permute-done.24), channel_id=1, source_target_pairs={{0,8},{8,16},{16,24},{24,32},{32,40},{40,48},{48,56},{56,64},{64,7... | collective-permute-start | bytes 393224 | tf_op jit(solution)/shard_map/ppermute | solution.py:18
  48.1 12.6 %collective-permute-start.8 = (f32[2,128,128]{2,1,0:T(8,128)S(1)}, f32[2,128,128]{2,1,0:T(8,128)S(1)}, u32[]{:S(2)}, u32[]{:S(2)}) collective-permute-start(f32[2,128,128]{2,1,0:T(8,128)S(1)} %fusion.21), channel_id=1, source_target_pairs={{24,88},{56,120},{88,152},{120,184},{152,216},{184,248},{216,280},... | collective-permute-start | bytes 393224 | tf_op jit(solution)/shard_map/ppermute | solution.py:146
  49.1 12.6 %collective-permute-start.3 = (f32[2,128,128]{2,1,0:T(8,128)S(1)}, f32[2,128,128]{2,1,0:T(8,128)S(1)}, u32[]{:S(2)}, u32[]{:S(2)}) collective-permute-start(f32[2,128,128]{2,1,0:T(8,128)S(1)} %convolution_select_fusion.3), channel_id=1, source_target_pairs={{24,88},{56,120},{88,152},{120,184},{152,216},{184,248},{216,280},... | collective-permute-start | bytes 393224 | tf_op jit(solution)/shard_map/ppermute | solution.py:146
  58.8 20.8 %collective-permute-start.26 = (bf16[256,256]{0,1:T(8,128)(2,1)S(1)}, bf16[256,256]{0,1:T(8,128)(2,1)S(1)}, u32[]{:S(2)}, u32[]{:S(2)}) collective-permute-start(bf16[256,256]{0,1:T(8,128)(2,1)S(1)} %collective-permute-done.25), channel_id=1, source_target_pairs={{0,8},{8,16},{16,24},{24,32},{32,40},{40,48},{48,56},{56,64},{64,7... | collective-permute-start | bytes 393224 | tf_op jit(solution)/shard_map/ppermute | solution.py:18
  61.0 20.5 %collective-permute-start.9 = (f32[2,128,128]{2,1,0:T(8,128)S(1)}, f32[2,128,128]{2,1,0:T(8,128)S(1)}, u32[]{:S(2)}, u32[]{:S(2)}) collective-permute-start(f32[2,128,128]{2,1,0:T(8,128)S(1)} %fusion.20), channel_id=1, source_target_pairs={{24,152},{56,184},{88,216},{120,248},{152,280},{184,312},{216,344}... | collective-permute-start | bytes 393224 | tf_op jit(solution)/shard_map/ppermute | solution.py:146
  62.0 30.9 %collective-permute-start.4 = (f32[2,128,128]{2,1,0:T(8,128)S(1)}, f32[2,128,128]{2,1,0:T(8,128)S(1)}, u32[]{:S(2)}, u32[]{:S(2)}) collective-permute-start(f32[2,128,128]{2,1,0:T(8,128)S(1)} %convolution_select_fusion.2), channel_id=1, source_target_pairs={{24,152},{56,184},{88,216},{120,248},{152,280},{184,312},{216,344}... | collective-permute-start | bytes 393224 | tf_op jit(solution)/shard_map/ppermute | solution.py:146
  79.6 11.4 %collective-permute-start.27 = (bf16[256,256]{0,1:T(8,128)(2,1)S(1)}, bf16[256,256]{0,1:T(8,128)(2,1)S(1)}, u32[]{:S(2)}, u32[]{:S(2)}) collective-permute-start(bf16[256,256]{0,1:T(8,128)(2,1)S(1)} %collective-permute-done.26), channel_id=1, source_target_pairs={{0,8},{8,16},{16,24},{24,32},{32,40},{40,48},{48,56},{56,64},{64,7... | collective-permute-start | bytes 393224 | tf_op jit(solution)/shard_map/ppermute | solution.py:18
  81.8 11.4 %collective-permute-start.10 = (f32[2,128,128]{2,1,0:T(8,128)S(1)}, f32[2,128,128]{2,1,0:T(8,128)S(1)}, u32[]{:S(2)}, u32[]{:S(2)}) collective-permute-start(f32[2,128,128]{2,1,0:T(8,128)S(1)} %fusion.19), channel_id=1, source_target_pairs={{24,280},{56,312},{88,344},{120,376},{152,408},{184,440},{216,472}... | collective-permute-start | bytes 393224 | tf_op jit(solution)/shard_map/ppermute | solution.py:146
  91.0 8.7 %collective-permute-start.28 = (bf16[256,256]{0,1:T(8,128)(2,1)S(1)}, bf16[256,256]{0,1:T(8,128)(2,1)S(1)}, u32[]{:S(2)}, u32[]{:S(2)}) collective-permute-start(bf16[256,256]{0,1:T(8,128)(2,1)S(1)} %collective-permute-done.27), channel_id=1, source_target_pairs={{0,8},{8,16},{16,24},{24,32},{32,40},{40,48},{48,56},{56,64},{64,7... | collective-permute-start | bytes 393224 | tf_op jit(solution)/shard_map/ppermute | solution.py:18
  93.5 8.2 %collective-permute-start.14 = (f32[2,128,128]{2,1,0:T(8,128)S(1)}, f32[2,128,128]{2,1,0:T(8,128)S(1)}, u32[]{:S(2)}, u32[]{:S(2)}) collective-permute-start(f32[2,128,128]{2,1,0:T(8,128)S(1)} %fusion.18), channel_id=1, source_target_pairs={{24,56},{56,88},{88,120},{120,152},{152,184},{184,216},{216,248},{... | collective-permute-start | bytes 393224 | tf_op jit(solution)/shard_map/ppermute | solution.py:146
  94.2 7.5 %collective-permute-start.13 = (f32[2,128,128]{2,1,0:T(8,128)S(1)}, f32[2,128,128]{2,1,0:T(8,128)S(1)}, u32[]{:S(2)}, u32[]{:S(2)}) collective-permute-start(f32[2,128,128]{2,1,0:T(8,128)S(1)} %fusion.18), channel_id=1, source_target_pairs={{24,48},{56,80},{88,112},{120,144},{152,176},{184,208},{216,240},{... | collective-permute-start | bytes 393224 | tf_op jit(solution)/shard_map/ppermute | solution.py:146
  94.9 6.8 %collective-permute-start.12 = (f32[2,128,128]{2,1,0:T(8,128)S(1)}, f32[2,128,128]{2,1,0:T(8,128)S(1)}, u32[]{:S(2)}, u32[]{:S(2)}) collective-permute-start(f32[2,128,128]{2,1,0:T(8,128)S(1)} %fusion.18), channel_id=1, source_target_pairs={{24,40},{56,72},{88,104},{120,136},{152,168},{184,200},{216,232},{... | collective-permute-start | bytes 393224 | tf_op jit(solution)/shard_map/ppermute | solution.py:146
  95.5 15.2 %collective-permute-start.11 = (f32[2,128,128]{2,1,0:T(8,128)S(1)}, f32[2,128,128]{2,1,0:T(8,128)S(1)}, u32[]{:S(2)}, u32[]{:S(2)}) collective-permute-start(f32[2,128,128]{2,1,0:T(8,128)S(1)} %fusion.18), channel_id=1, source_target_pairs={{24,32},{56,64},{88,96},{120,128},{152,160},{184,192},{216,224},{2... | collective-permute-start | bytes 393224 | tf_op jit(solution)/shard_map/ppermute | solution.py:146
  99.8 18.3 %collective-permute-start.29 = (bf16[256,256]{0,1:T(8,128)(2,1)S(1)}, bf16[256,256]{0,1:T(8,128)(2,1)S(1)}, u32[]{:S(2)}, u32[]{:S(2)}) collective-permute-start(bf16[256,256]{0,1:T(8,128)(2,1)S(1)} %collective-permute-done.28), channel_id=1, source_target_pairs={{0,8},{8,16},{16,24},{24,32},{32,40},{40,48},{48,56},{56,64},{64,7... | collective-permute-start | bytes 393224 | tf_op jit(solution)/shard_map/ppermute | solution.py:18
  111.2 10.9 %collective-permute-start.19 = (bf16[256,256]{0,1:T(8,128)(2,1)S(1)}, bf16[256,256]{0,1:T(8,128)(2,1)S(1)}, u32[]{:S(2)}, u32[]{:S(2)}) collective-permute-start(bf16[256,256]{0,1:T(8,128)(2,1)S(1)} %bitcast.171), channel_id=1, source_target_pairs={{0,8},{8,16},{16,24},{24,32},{32,40},{40,48},{48,56},{56,64},{64,7... | collective-permute-start | bytes 393224 | tf_op jit(solution)/shard_map/ppermute | solution.py:18
  113.1 14.2 %collective-permute-start.15 = (bf16[256,256]{0,1:T(8,128)(2,1)S(1)}, bf16[256,256]{0,1:T(8,128)(2,1)S(1)}, u32[]{:S(2)}, u32[]{:S(2)}) collective-permute-start(bf16[256,256]{0,1:T(8,128)(2,1)S(1)} %bitcast.172), channel_id=1, source_target_pairs={{0,40},{8,48},{16,56},{24,64},{32,72},{40,80},{48,88},{56,96},{64,... | collective-permute-start | bytes 393224 | tf_op jit(solution)/shard_map/ppermute | solution.py:18
  118.1 17.3 %collective-permute-start.30 = (bf16[256,256]{0,1:T(8,128)(2,1)S(1)}, bf16[256,256]{0,1:T(8,128)(2,1)S(1)}, u32[]{:S(2)}, u32[]{:S(2)}) collective-permute-start(bf16[256,256]{0,1:T(8,128)(2,1)S(1)} %collective-permute-done.29), channel_id=1, source_target_pairs={{0,8},{8,16},{16,24},{24,32},{32,40},{40,48},{48,56},{56,64},{64,7... | collective-permute-start | bytes 393224 | tf_op jit(solution)/shard_map/ppermute | solution.py:18
  122.0 24.3 %collective-permute-start.20 = (bf16[256,256]{0,1:T(8,128)(2,1)S(1)}, bf16[256,256]{0,1:T(8,128)(2,1)S(1)}, u32[]{:S(2)}, u32[]{:S(2)}) collective-permute-start(bf16[256,256]{0,1:T(8,128)(2,1)S(1)} %collective-permute-done.19), channel_id=1, source_target_pairs={{0,8},{8,16},{16,24},{24,32},{32,40},{40,48},{48,56},{56,64},{64,7... | collective-permute-start | bytes 393224 | tf_op jit(solution)/shard_map/ppermute | solution.py:18
  127.3 16.3 %collective-permute-start.16 = (bf16[256,256]{0,1:T(8,128)(2,1)S(1)}, bf16[256,256]{0,1:T(8,128)(2,1)S(1)}, u32[]{:S(2)}, u32[]{:S(2)}) collective-permute-start(bf16[256,256]{0,1:T(8,128)(2,1)S(1)} %collective-permute-done.15), channel_id=1, source_target_pairs={{0,8},{8,16},{16,24},{24,32},{32,40},{40,48},{48,56},{56,64},{64,7... | collective-permute-start | bytes 393224 | tf_op jit(solution)/shard_map/ppermute | solution.py:18
  143.6 8.9 %collective-permute-start.17 = (bf16[256,256]{0,1:T(8,128)(2,1)S(1)}, bf16[256,256]{0,1:T(8,128)(2,1)S(1)}, u32[]{:S(2)}, u32[]{:S(2)}) collective-permute-start(bf16[256,256]{0,1:T(8,128)(2,1)S(1)} %collective-permute-done.16), channel_id=1, source_target_pairs={{0,8},{8,16},{16,24},{24,32},{32,40},{40,48},{48,56},{56,64},{64,7... | collective-permute-start | bytes 393224 | tf_op jit(solution)/shard_map/ppermute | solution.py:18
  146.4 10.4 %collective-permute-start.21 = (bf16[256,256]{0,1:T(8,128)(2,1)S(1)}, bf16[256,256]{0,1:T(8,128)(2,1)S(1)}, u32[]{:S(2)}, u32[]{:S(2)}) collective-permute-start(bf16[256,256]{0,1:T(8,128)(2,1)S(1)} %collective-permute-done.20), channel_id=1, source_target_pairs={{0,8},{8,16},{16,24},{24,32},{32,40},{40,48},{48,56},{56,64},{64,7... | collective-permute-start | bytes 393224 | tf_op jit(solution)/shard_map/ppermute | solution.py:18
  152.5 8.7 %collective-permute-start.18 = (bf16[256,256]{0,1:T(8,128)(2,1)S(1)}, bf16[256,256]{0,1:T(8,128)(2,1)S(1)}, u32[]{:S(2)}, u32[]{:S(2)}) collective-permute-start(bf16[256,256]{0,1:T(8,128)(2,1)S(1)} %collective-permute-done.17), channel_id=1, source_target_pairs={{0,8},{8,16},{16,24},{24,32},{32,40},{40,48},{48,56},{56,64},{64,7... | collective-permute-start | bytes 393224 | tf_op jit(solution)/shard_map/ppermute | solution.py:18
  156.7 8.6 %collective-permute-start.22 = (bf16[256,256]{0,1:T(8,128)(2,1)S(1)}, bf16[256,256]{0,1:T(8,128)(2,1)S(1)}, u32[]{:S(2)}, u32[]{:S(2)}) collective-permute-start(bf16[256,256]{0,1:T(8,128)(2,1)S(1)} %collective-permute-done.21), channel_id=1, source_target_pairs={{0,8},{8,16},{16,24},{24,32},{32,40},{40,48},{48,56},{56,64},{64,7... | collective-permute-start | bytes 393224 | tf_op jit(solution)/shard_map/ppermute | solution.py:18
  165.4 21.4 %copy-start.3 = (f32[256]{0:T(256)S(1)}, f32[256]{0:T(256)}, u32[]{:S(2)}) copy-start(f32[256]{0:T(256)} %param.13) | copy-start | bytes 3076
